TPU v7x, 32 devices: a whole 2x2x4 slice. The times are simulated.
32 devices in a mesh: seq: 8 (over z, core), tp: 4 (over y, x).
Axes of the slice: x: 2, y: 2, z: 4, core: 2. Of those that a mesh axis runs over, the one named last changes fastest.
Arguments:
- tokens: bfloat16 [8, 512, 2048], P('seq', None, 'tp'), may hold values from -6 to 6
- segment_ids: int32 [8, 512], P('seq'), may hold values from 0 to 15, as said below
- shard_map: int32 [32], replicated, may hold values from 0 to 31, each once
- trainer_qkv: float32 [2, 2048, 6144], P(None, ('seq', 'tp')), may hold values from -0.125 to 0.125
- trainer_up: float32 [2, 2048, 8192], P(None, ('seq', 'tp')), may hold values from -0.125 to 0.125
- qkv_bias: bfloat16 [2, 6144], P(None, 'tp'), may hold values from -4 to 4
- up_bias: bfloat16 [2, 8192], P(None, 'tp'), may hold values from -3 to 3
- dense_w: bfloat16 [2, 2048, 2048], P(None, 'tp'), may hold values from -0.125 to 0.125
- down_w: bfloat16 [2, 8192, 2048], P(None, 'tp'), may hold values from -0.0625 to 0.0625
- out_bias: float32 [2, 2048], P(None, 'tp'), may hold values from -3 to 3
- norm_gain: float32 [2, 2, 2048], replicated, may hold values from 0.1 to 1.9
- norm_shift: float32 [2, 2, 2048], replicated, may hold values from -3 to 3
Outputs:
- result: bfloat16 [8, 512, 2048], P('seq', None, 'tp')
Inputs may be any that keep to these rules, and one draw needn't show every extreme that they name: `shard_map`: each trainer shard number appears exactly once. `segment_ids`: along a row the numbers start at 0 and rise by 0 or 1 from token to token; a row holds one prompt of 512 tokens or several packed prompts.
All inputs are finite; a program needn't handle non-finite values.
Results may differ from a plain program's by a relative error of at most 0.015.
Values may be sent and summed in bfloat16 or wider, within the bound.
No kernel may reach another device: no remote copies, remote signals or barrier semaphores. Data moves between devices by JAX's collectives and lax.ppermute only.
A program may use at most 192 MiB of HBM per device.

v0:
```python
import jax
import jax.numpy as jnp
import numpy as np
from jax import lax
from jax.sharding import PartitionSpec as P

HD = 256
ROT = 64
LAYERS = 2


def layer_norm(values, gain, shift):
    mean = jnp.mean(values, axis=-1, keepdims=True)
    centred = values - mean
    var = jnp.mean(centred * centred, axis=-1, keepdims=True)
    return centred * lax.rsqrt(var + 1e-05) * gain + shift


def positions(segs):
    length = segs.shape[-1]
    index = jnp.broadcast_to(jnp.arange(length, dtype=jnp.int32), segs.shape)
    first = jnp.ones(segs.shape[:-1] + (1,), dtype=bool)
    flag = jnp.concatenate([first, segs[..., 1:] != segs[..., :-1]], axis=-1)
    start = lax.cummax(jnp.where(flag, index, 0), axis=segs.ndim - 1)
    return index - start


def rotate(values, pos):
    half = ROT // 2
    inverse = 10000.0 ** (-(jnp.arange(half, dtype=jnp.float32) * 2.0 / ROT))
    angle = pos[..., None].astype(jnp.float32) * inverse
    cosine = jnp.cos(angle)[..., None, :]
    sine = jnp.sin(angle)[..., None, :]
    first = values[..., :half]
    second = values[..., half:ROT]
    return jnp.concatenate(
        [first * cosine - second * sine, second * cosine + first * sine, values[..., ROT:]], axis=-1
    )


def shards(
    tokens,
    segment_ids,
    shard_map,
    trainer_qkv,
    trainer_up,
    qkv_bias,
    up_bias,
    dense_w,
    down_w,
    out_bias,
    norm_gain,
    norm_shift,
):
    n_seq = lax.axis_size("seq")
    n_tp = lax.axis_size("tp")
    devices = n_seq * n_tp
    rows, length, _ = tokens.shape
    block = trainer_qkv.shape[1]
    full_width = block * devices
    heads_here = qkv_bias.shape[1] // (3 * HD)
    counter = np.arange(devices)
    source_of = counter % n_seq * n_tp + counter // n_seq
    arrived_block = jnp.take(shard_map, jnp.asarray(source_of, dtype=jnp.int32))
    slot_ids = jnp.arange(devices, dtype=jnp.int32)
    onehot = arrived_block[None, :] == slot_ids[:, None]
    arrival_of = jnp.sum(jnp.where(onehot, slot_ids[None, :], 0), axis=1)
    pos = positions(segment_ids)
    index = jnp.arange(length, dtype=jnp.int32)
    mask = (index[None, :] <= index[:, None])[None] & (
        segment_ids[:, :, None] == segment_ids[:, None, :]
    )
    mask = mask[:, None]
    stream = tokens
    for layer in range(LAYERS):
        whole = lax.all_gather(stream, "tp", axis=2, tiled=True).astype(jnp.float32)
        attn_in = layer_norm(whole, norm_gain[layer, 0], norm_shift[layer, 0]).astype(jnp.bfloat16)
        mlp_in = layer_norm(whole, norm_gain[layer, 1], norm_shift[layer, 1]).astype(jnp.bfloat16)
        qkv_piece = trainer_qkv[layer].astype(jnp.bfloat16)
        up_piece = trainer_up[layer].astype(jnp.bfloat16)
        qkv_arr, up_arr = (
            lax.all_gather(qkv_piece, "seq", axis=0, tiled=True),
            lax.all_gather(up_piece, "seq", axis=0, tiled=True),
        )
        qkv_arr, up_arr = (
            lax.all_to_all(qkv_arr, "tp", split_axis=1, concat_axis=0, tiled=True),
            lax.all_to_all(up_arr, "tp", split_axis=1, concat_axis=0, tiled=True),
        )
        qkv_mat = qkv_arr.reshape(devices, block, -1)[arrival_of].reshape(full_width, -1)
        up_mat = up_arr.reshape(devices, block, -1)[arrival_of].reshape(full_width, -1)
        left_attn = attn_in.reshape(rows * length, full_width)
        left_mlp = mlp_in.reshape(rows * length, full_width)
        qkv = jnp.dot(left_attn, qkv_mat, preferred_element_type=jnp.float32) + qkv_bias[
            layer
        ].astype(jnp.float32)
        qkv = qkv.reshape(rows, length, heads_here, 3, HD)
        query = rotate(qkv[:, :, :, 0], pos).astype(jnp.bfloat16)
        keys = rotate(qkv[:, :, :, 1], pos).astype(jnp.bfloat16)
        vals = qkv[:, :, :, 2].astype(jnp.bfloat16)
        scores = jnp.einsum(
            "rqhd,rkhd->rhqk", query, keys, preferred_element_type=jnp.float32
        ) / jnp.sqrt(jnp.float32(HD))
        scores = jnp.where(mask, scores, -jnp.inf)
        probs = jax.nn.softmax(scores, axis=-1).astype(jnp.bfloat16)
        ctx = jnp.einsum("rhqk,rkhd->rqhd", probs, vals, preferred_element_type=jnp.float32).astype(
            jnp.bfloat16
        )
        ctx = ctx.reshape(rows * length, heads_here * HD)
        up = jnp.dot(left_mlp, up_mat, preferred_element_type=jnp.float32) + up_bias[layer].astype(
            jnp.float32
        )
        hidden_units = jax.nn.gelu(up, approximate=False).astype(jnp.bfloat16)
        partial_terms = jnp.dot(ctx, dense_w[layer], preferred_element_type=jnp.float32) + jnp.dot(
            hidden_units, down_w[layer], preferred_element_type=jnp.float32
        )
        summed = lax.psum_scatter(
            partial_terms.astype(jnp.bfloat16), "tp", scatter_dimension=1, tiled=True
        ).astype(jnp.float32)
        flat_stream = stream.astype(jnp.float32).reshape(rows * length, -1)
        stream = (
            (flat_stream + summed + out_bias[layer]).astype(jnp.bfloat16).reshape(rows, length, -1)
        )
    return stream


def solution(mesh):
    in_specs = (
        P("seq", None, "tp"),
        P("seq", None),
        P(),
        P(None, ("seq", "tp"), None),
        P(None, ("seq", "tp"), None),
        P(None, "tp"),
        P(None, "tp"),
        P(None, "tp", None),
        P(None, "tp", None),
        P(None, "tp"),
        P(),
        P(),
    )
    out_specs = P("seq", None, "tp")
    return jax.shard_map(shards, mesh=mesh, in_specs=in_specs, out_specs=out_specs, check_vma=False)
```

profile of v0, /device:TPU:0, one launch (start us, length us, event | category | flops | bytes accessed | tf_op | source)
XLA Modules:
  0.0 689.4 jit_solution(17803890025388998924)
XLA Ops:
  6.5 2.1 convert.71
  8.6 1.3 fusion.277
  10.0 2.4 convert.79
  12.4 1.4 fusion.276
  13.9 0.7 all-gather.12.cloned.1.call-update
  14.7 0.5 all-gather.20.cloned.1.call-update
  15.2 62.3 %all-gather.14.cloned.1.call-done = bf16[1,512,6144]{2,1,0:T(8,128)(2,1)} async-done(((bf16[1,64,6144]{2,1,0:T(8,128)(2,1)}), bf16[1,512,6144]{2,1,0:T(8,128)(2,1)}) %all-gather.14.cloned.1.call-update) | async-done | bytes 6291472 | tf_op jit(solution)/shard_map/all_gather | solution.py:82
  77.5 8.6 %copy.64 = bf16[1,512,6144]{1,2,0:T(8,128)(2,1)} copy(bf16[1,512,6144]{2,1,0:T(8,128)(2,1)} %all-gather.14.cloned.1.call-done) | data formatting | bytes 12582912 | tf_op jit(solution)/shard_map/all_gather | solution.py:82
  86.2 5.4 all-to-all-start
  91.6 0.5 all-gather.22.cloned.1.call-update
  92.1 0.7 gather_fusion
  93.0 0.3 reduce-window.6
  93.6 66.2 %all-gather.16.cloned.1.call-done = bf16[1,512,8192]{2,1,0:T(8,128)(2,1)} async-done(((bf16[1,64,8192]{2,1,0:T(8,128)(2,1)}), bf16[1,512,8192]{2,1,0:T(8,128)(2,1)}) %all-gather.16.cloned.1.call-update) | async-done | bytes 8388624 | tf_op jit(solution)/shard_map/all_gather | solution.py:83
  159.9 12.1 %copy.71 = bf16[1,512,8192]{1,2,0:T(8,128)(2,1)} copy(bf16[1,512,8192]{2,1,0:T(8,128)(2,1)} %all-gather.16.cloned.1.call-done) | data formatting | bytes 16777216 | tf_op jit(solution)/shard_map/all_gather | solution.py:83
  172.0 5.8 all-to-all-start.1
  178.1 0.9 fusion.135
  179.0 1.7 multiply_cosine_fusion
  180.9 68.5 %all-gather.12.cloned.1.call-done = bf16[1,512,2048]{2,1,0:T(8,128)(2,1)} async-done(((bf16[1,512,512]{2,1,0:T(8,128)(2,1)}), bf16[1,512,2048]{2,1,0:T(8,128)(2,1)}) %all-gather.12.cloned.1.call-update) | async-done | bytes 2097168 | tf_op jit(solution)/shard_map/all_gather | solution.py:76
  249.4 1.9 convert_reduce_fusion.1
  251.4 2.3 fusion.16
  253.7 58.9 %all-gather.20.cloned.1.call-done = bf16[1,512,6144]{2,1,0:T(8,128)(2,1)} async-done(((bf16[1,64,6144]{2,1,0:T(8,128)(2,1)}), bf16[1,512,6144]{2,1,0:T(8,128)(2,1)}) %all-gather.20.cloned.1.call-update) | async-done | bytes 6291472 | tf_op jit(solution)/shard_map/all_gather | solution.py:82
  312.5 8.6 %copy.73 = bf16[1,512,6144]{1,2,0:T(8,128)(2,1)} copy(bf16[1,512,6144]{2,1,0:T(8,128)(2,1)} %all-gather.20.cloned.1.call-done) | data formatting | bytes 12582912 | tf_op jit(solution)/shard_map/all_gather | solution.py:82
  321.1 8.4 %copy.65 = bf16[4,512,1536]{2,1,0:T(8,128)(2,1)} copy(bf16[4,512,1536]{1,2,0:T(8,128)(2,1)} %bitcast.5) | data formatting | bytes 12582912 | tf_op jit(solution)/shard_map/all_to_all | solution.py:86
  329.6 6.5 gather_fusion.1
  336.1 8.0 %convolution_add_fusion.1 = f32[512,1536]{1,0:T(8,128)} fusion(bf16[2048,1536]{1,0:T(8,128)(2,1)} %bitcast.183, bf16[1,512,2048]{2,1,0:T(8,128)(2,1)S(1)} %copy-done.2, f32[2048]{0:T(1024)S(1)} %bitcast.199, f32[2048]{0:T(1024)S(1)} %bitcast.198, f32[512]{0:T(512)S(1)} %add_rsqrt_fusion.1, f32[512]{0:T(512)S(1)} %broadcast_multiply_fusion.1, ...), kind=kOutput, calls=%fused_computation.77 | convolution fusion | flops 3228303360 | bytes 11560960 | tf_op jit(solution)/shard_map/dot_general | solution.py:93
  344.1 2.4 copy.66
  346.5 1.5 fusion.275
  348.0 2.5 copy.84
  350.5 2.5 copy.85
  353.1 3.2 fusion.171
  356.2 2.9 fusion.139
  359.1 4.3 fusion.281
  363.5 2.9 convolution_convert_fusion.1
  366.4 5.2 all-to-all-start.2
  371.7 11.5 %copy.72 = bf16[4,512,2048]{2,1,0:T(8,128)(2,1)} copy(bf16[4,512,2048]{1,2,0:T(8,128)(2,1)} %bitcast.32) | data formatting | bytes 16777216 | tf_op jit(solution)/shard_map/all_to_all | solution.py:87
  383.1 9.1 %gather_fusion.2 = bf16[32,64,2048]{2,1,0:T(8,128)(2,1)} fusion(bf16[32,64,2048]{2,1,0:T(8,128)(2,1)} %bitcast.161, s32[1024]{0:T(1024)S(1)} %pad_clamp_fusion), kind=kCustom, calls=%fused_computation.2 | custom fusion | bytes 16777344 | tf_op jit(solution)/shard_map/gather | solution.py:90
  392.2 23.5 %fusion.4 = f32[512,2048]{1,0:T(8,128)} fusion(bf16[2,2048,2048]{2,1,0:T(8,128)(2,1)} %param.21, bf16[2048,2048]{1,0:T(8,128)(2,1)} %bitcast.173, bf16[1,512,2048]{2,1,0:T(8,128)(2,1)S(1)} %copy-done.3, f32[2048]{0:T(1024)S(1)} %bitcast.191, f32[2048]{0:T(1024)S(1)} %bitcast.197, f32[2048]{0:T(1024)S(1)} %bitcast.196, f32[512]{0:T(512)S(1)} %add_rsqrt_fusion.1, ...), kind=kOutput, calls=%fused_computation.9 | convolution fusion | flops 8665432064 | bytes 23097344 | tf_op jit(solution)/shard_map/dot_general | solution.py:113
  415.8 5.5 add_convert_fusion.1
  421.3 12.0 %copy.80 = bf16[1,512,8192]{1,2,0:T(8,128)(2,1)} copy(bf16[1,512,8192]{2,1,0:T(8,128)(2,1)} %all-gather.22.cloned.1.call-done) | data formatting | bytes 16777216 | tf_op jit(solution)/shard_map/all_gather | solution.py:83
  433.2 20.6 %all-to-all-done.2 = bf16[512,4,1536]{0,2,1:T(8,128)(2,1)} async-done(((bf16[512,4,1536]{0,2,1:T(8,128)(2,1)}), bf16[512,4,1536]{0,2,1:T(8,128)(2,1)}, u32[]{:S(2)}, u32[]{:S(2)}) %all-to-all-start.2) | async-done | bytes 6291488 | tf_op jit(solution)/shard_map/all_to_all | solution.py:86
  453.8 5.8 all-to-all-start.3
  459.7 54.8 %reduce-scatter.3.cloned.1.call-done = bf16[512,512]{1,0:T(8,128)(2,1)} async-done(((bf16[512,2048]{1,0:T(8,128)(2,1)}), bf16[512,512]{1,0:T(8,128)(2,1)}) %reduce-scatter.3.cloned.1.call-update) | async-done | bytes 524304 | tf_op jit(solution)/shard_map/reduce_scatter | solution.py:116
  514.5 2.0 fusion.130
  516.6 8.7 %copy.74 = bf16[4,512,1536]{2,1,0:T(8,128)(2,1)} copy(bf16[4,512,1536]{1,2,0:T(8,128)(2,1)} %bitcast.43) | data formatting | bytes 12582912 | tf_op jit(solution)/shard_map/all_to_all | solution.py:86
  525.3 6.5 gather_fusion.3
  531.7 29.2 %all-to-all-done.3 = bf16[512,4,2048]{0,2,1:T(8,128)(2,1)} async-done(((bf16[512,4,2048]{0,2,1:T(8,128)(2,1)}), bf16[512,4,2048]{0,2,1:T(8,128)(2,1)}, u32[]{:S(2)}, u32[]{:S(2)}) %all-to-all-start.3) | async-done | bytes 8388640 | tf_op jit(solution)/shard_map/all_to_all | solution.py:87
  560.9 11.5 %copy.81 = bf16[4,512,2048]{2,1,0:T(8,128)(2,1)} copy(bf16[4,512,2048]{1,2,0:T(8,128)(2,1)} %bitcast.64) | data formatting | bytes 16777216 | tf_op jit(solution)/shard_map/all_to_all | solution.py:87
  572.4 8.4 %gather_fusion.4 = bf16[32,64,2048]{2,1,0:T(8,128)(2,1)} fusion(bf16[32,64,2048]{2,1,0:T(8,128)(2,1)} %bitcast.160, s32[1024]{0:T(1024)S(1)} %pad_clamp_fusion), kind=kCustom, calls=%fused_computation.4 | custom fusion | bytes 16777344 | tf_op jit(solution)/shard_map/gather | solution.py:90
  580.8 2.1 convert_reduce_fusion
  582.9 2.3 fusion.26
  585.2 8.0 %convolution_add_fusion = f32[512,1536]{1,0:T(8,128)} fusion(bf16[2048,1536]{1,0:T(8,128)(2,1)} %bitcast.182, bf16[512,2048]{1,0:T(8,128)(2,1)S(1)} %copy-done.4, f32[2048]{0:T(1024)S(1)} %bitcast.195, f32[2048]{0:T(1024)S(1)} %bitcast.194, f32[512]{0:T(512)S(1)} %add_rsqrt_fusion, f32[512]{0:T(512)S(1)} %broadcast_multiply_fusion, ...), kind=kOutput, calls=%fused_computation.76 | convolution fusion | flops 3228303360 | bytes 11560960 | tf_op jit(solution)/shard_map/dot_general | solution.py:93
  593.2 2.6 copy.75
  595.8 1.5 fusion.274
  597.3 2.6 copy.86
  599.9 2.5 copy.87
  602.5 2.3 fusion.141
  604.8 3.1 fusion.175
  607.9 1.0 fusion.142
  608.9 4.4 fusion.286
  613.3 2.9 convolution_convert_fusion
  616.2 24.1 %fusion.2 = f32[512,2048]{1,0:T(8,128)} fusion(bf16[2,2048,2048]{2,1,0:T(8,128)(2,1)} %param.21, bf16[2048,2048]{1,0:T(8,128)(2,1)} %bitcast.172, bf16[512,2048]{1,0:T(8,128)(2,1)} %all-gather.18.cloned.1.call-done, f32[2048]{0:T(1024)S(1)} %bitcast.190, f32[2048]{0:T(1024)S(1)} %bitcast.193, f32[2048]{0:T(1024)S(1)} %bitcast.192, ...), kind=kOutput, calls=%fused_computation.7 | convolution fusion | flops 8665432064 | bytes 23097344 | tf_op jit(solution)/shard_map/dot_general | solution.py:113
  640.4 5.5 add_convert_fusion
  645.9 34.2 %reduce-scatter.5.cloned.1.call-done = bf16[512,512]{1,0:T(8,128)(2,1)} async-done(((bf16[512,2048]{1,0:T(8,128)(2,1)}), bf16[512,512]{1,0:T(8,128)(2,1)}) %reduce-scatter.5.cloned.1.call-update) | async-done | bytes 524304 | tf_op jit(solution)/shard_map/reduce_scatter | solution.py:116
  680.1 2.0 fusion.138
  (73 shorter events, 1.4 us)
Async XLA Ops:
  6.5 85.6 %copy-start = (s32[32]{0:T(128)S(1)}, s32[32]{0:T(128)}, u32[]{:S(2)}) copy-start(s32[32]{0:T(128)} %param.15) | copy-start | bytes 388
  6.5 71.0 %all-gather.14.cloned.1.call-start = ((), (), s32[]{:S(2)}) async-start(), calls=%async_computation.9 | async-start | bytes 7077888 | tf_op jit(solution)/shard_map/all_gather | solution.py:82
  9.9 150.0 %all-gather.16.cloned.1.call-start = ((), (), s32[]{:S(2)}) async-start(), calls=%async_computation.10 | async-start | bytes 9437184 | tf_op jit(solution)/shard_map/all_gather | solution.py:83
  13.9 235.5 %all-gather.12.cloned.1.call-start = ((), (), s32[]{:S(2)}) async-start(), calls=%async_computation.6 | async-start | bytes 2621440 | tf_op jit(solution)/shard_map/all_gather | solution.py:76
  14.6 297.9 %all-gather.20.cloned.1.call-start = ((), (), s32[]{:S(2)}) async-start(), calls=%async_computation.12 | async-start | bytes 7077888 | tf_op jit(solution)/shard_map/all_gather | solution.py:82
  86.1 6.0 copy-start.16
  86.1 6.7 copy-start.10
  86.2 85.8 %all-to-all-start = ((bf16[512,4,1536]{0,2,1:T(8,128)(2,1)}), bf16[512,4,1536]{0,2,1:T(8,128)(2,1)}, u32[]{:S(2)}, u32[]{:S(2)}) async-start(bf16[512,4,1536]{0,2,1:T(8,128)(2,1)} %bitcast.165), calls=%async_computation | async-start | bytes 12582912 | tf_op jit(solution)/shard_map/all_to_all | solution.py:86
  91.5 329.8 %all-gather.22.cloned.1.call-start = ((), (), s32[]{:S(2)}) async-start(), calls=%async_computation.13 | async-start | bytes 9437184 | tf_op jit(solution)/shard_map/all_gather | solution.py:83
  171.9 6.1 copy-start.14
  171.9 8.8 %copy-start.13 = (bf16[2,2048]{1,0:T(2,128)(2,1)S(1)}, bf16[2,2048]{1,0:T(2,128)(2,1)}, u32[]{:S(2)}) copy-start(bf16[2,2048]{1,0:T(2,128)(2,1)} %param.19) | copy-start | bytes 24580
  171.9 8.9 %copy-start.11 = (f32[2,2,2048]{2,1,0:T(2,128)S(1)}, f32[2,2,2048]{2,1,0:T(2,128)}, u32[]{:S(2)}) copy-start(f32[2,2,2048]{2,1,0:T(2,128)} %param.23) | copy-start | bytes 98308
  172.0 8.9 %copy-start.12 = (f32[2,2,2048]{2,1,0:T(2,128)S(1)}, f32[2,2,2048]{2,1,0:T(2,128)}, u32[]{:S(2)}) copy-start(f32[2,2,2048]{2,1,0:T(2,128)} %param.24) | copy-start | bytes 98308
  172.0 194.4 %all-to-all-start.1 = ((bf16[512,4,2048]{0,2,1:T(8,128)(2,1)}), bf16[512,4,2048]{0,2,1:T(8,128)(2,1)}, u32[]{:S(2)}, u32[]{:S(2)}) async-start(bf16[512,4,2048]{0,2,1:T(8,128)(2,1)} %bitcast.162), calls=%async_computation.1 | async-start | bytes 16777216 | tf_op jit(solution)/shard_map/all_to_all | solution.py:87
  329.6 6.5 copy-start.2
  366.4 87.5 %all-to-all-start.2 = ((bf16[512,4,1536]{0,2,1:T(8,128)(2,1)}), bf16[512,4,1536]{0,2,1:T(8,128)(2,1)}, u32[]{:S(2)}, u32[]{:S(2)}) async-start(bf16[512,4,1536]{0,2,1:T(8,128)(2,1)} %bitcast.164), calls=%async_computation.3 | async-start | bytes 12582912 | tf_op jit(solution)/shard_map/all_to_all | solution.py:86
  371.6 142.8 %reduce-scatter.3.cloned.1.call-start = ((), (), s32[]{:S(2)}) async-start(), calls=%async_computation.7 | async-start | bytes 2621440 | tf_op jit(solution)/shard_map/reduce_scatter | solution.py:116
  383.1 9.1 %copy-start.3 = (bf16[1,512,2048]{2,1,0:T(8,128)(2,1)S(1)}, bf16[1,512,2048]{2,1,0:T(8,128)(2,1)}, u32[]{:S(2)}) copy-start(bf16[1,512,2048]{2,1,0:T(8,128)(2,1)} %all-gather.12.cloned.1.call-done) | copy-start | bytes 6291460
  392.2 23.5 %copy-start.8 = (bf16[2,256,512]{2,1,0:T(8,128)(2,1)S(1)}, bf16[2,256,512]{2,1,0:T(8,128)(2,1)}, u32[]{:S(2)}) copy-start(bf16[2,256,512]{2,1,0:T(8,128)(2,1)} %convolution_convert_fusion.1) | copy-start | bytes 1572868
  453.8 5.8 copy-start.15
  453.8 60.6 %copy-start.7 = (bf16[1,512,512]{2,1,0:T(8,128)(2,1)S(1)}, bf16[1,512,512]{2,1,0:T(8,128)(2,1)}, u32[]{:S(2)}) copy-start(bf16[1,512,512]{2,1,0:T(8,128)(2,1)} %param.13) | copy-start | bytes 1572868
  453.8 107.1 %all-to-all-start.3 = ((bf16[512,4,2048]{0,2,1:T(8,128)(2,1)}), bf16[512,4,2048]{0,2,1:T(8,128)(2,1)}, u32[]{:S(2)}, u32[]{:S(2)}) async-start(bf16[512,4,2048]{0,2,1:T(8,128)(2,1)} %bitcast.163), calls=%async_computation.4 | async-start | bytes 16777216 | tf_op jit(solution)/shard_map/all_to_all | solution.py:87
  459.6 121.2 %all-gather.18.cloned.1.call-start = ((), (), s32[]{:S(2)}) async-start(), calls=%async_computation.11 | async-start | bytes 2621440 | tf_op jit(solution)/shard_map/all_gather | solution.py:76
  516.5 163.6 %reduce-scatter.5.cloned.1.call-start = ((), (), s32[]{:S(2)}) async-start(), calls=%async_computation.8 | async-start | bytes 2621440 | tf_op jit(solution)/shard_map/reduce_scatter | solution.py:116
  580.8 4.4 copy-start.4
  602.5 5.5 copy-start.5
  616.2 24.1 %copy-start.9 = (bf16[2,256,512]{2,1,0:T(8,128)(2,1)S(1)}, bf16[2,256,512]{2,1,0:T(8,128)(2,1)}, u32[]{:S(2)}) copy-start(bf16[2,256,512]{2,1,0:T(8,128)(2,1)} %convolution_convert_fusion) | copy-start | bytes 1572868
  640.4 41.7 %copy-start.1 = (s32[32]{0:T(128)S(1)}, s32[32]{0:T(128)}, u32[]{:S(2)}) copy-start(s32[32]{0:T(128)} %param.15) | copy-start | bytes 388
  640.4 39.7 %copy-start.6 = (bf16[512,512]{1,0:T(8,128)(2,1)S(1)}, bf16[512,512]{1,0:T(8,128)(2,1)}, u32[]{:S(2)}) copy-start(bf16[512,512]{1,0:T(8,128)(2,1)} %fusion.130) | copy-start | bytes 1572868
Sparse Core Ops, SparseCore 0:
  10.0 67.4 all-gather.13
  79.1 80.6 all-gather.15
  161.7 87.6 all-gather.11
  250.9 61.5 all-gather.19
  314.0 80.6 all-gather.21
  421.4 93.0 reduce-scatter.2
  516.6 61.9 all-gather.17
  646.0 34.0 reduce-scatter.4
where the time goes:
time: 702 us; the launch traced here: 689 us
  waiting for transfers between devices  397 us (57%)
  local copies, waits for them, and re-layouts  140 us (20%)
  matrix products  89.2 us (13%)
  other arithmetic  27 us (4%)
  starting transfers between devices  22.5 us (3%)
  between operations  14.2 us (2%)
    all_gather x2, waiting for transfers between devices, shards(): lax.all_gather(qkv_piece, 'seq', axis=0, tiled=True)  121 us
    reduce_scatter x2, waiting for transfers between devices, shards(): lax.psum_scatter(partial_terms.astype(jnp.bfloat16), 'tp', scatter_dimens...  89 us
    all_gather x2, waiting for transfers between devices, shards(): whole = lax.all_gather(stream, 'tp', axis=2, tiled=True).astype(jnp.float32)  68.5 us
    all_gather x2, waiting for transfers between devices, shards(): lax.all_gather(up_piece, 'seq', axis=0, tiled=True)  66.3 us
    dot_general x2, matrix products, shards(): jnp.dot(hidden_units, down_w[layer], preferred_element_type=jnp.float32)  47.7 us
    all_to_all x2, waiting for transfers between devices, shards(): lax.all_to_all(up_arr, 'tp', split_axis=1, concat_axis=0, tiled=True)  29.2 us
    all_gather x2, local copies, waits for them, and re-layouts, shards(): lax.all_gather(up_piece, 'seq', axis=0, tiled=True)  24 us
    all_to_all x2, local copies, waits for them, and re-layouts, shards(): lax.all_to_all(up_arr, 'tp', split_axis=1, concat_axis=0, tiled=True)  23 us
  transfers between devices with their start and end apart: 12, of which 8 were waited for; matrix products, arithmetic and copies ran while one was open for 27% of the time, Pallas kernels for 0%

commit v1 on v0

v1 whole, which is shorter than its diff:
```python
import jax
import jax.numpy as jnp
import numpy as np
from jax import lax
from jax.sharding import Mesh
from jax.sharding import PartitionSpec as P

HD = 256
ROT = 64
LAYERS = 2
HEADS = 8


def layer_norm(values, gain, shift):
    mean = jnp.mean(values, axis=-1, keepdims=True)
    centred = values - mean
    var = jnp.mean(centred * centred, axis=-1, keepdims=True)
    return centred * lax.rsqrt(var + 1e-05) * gain + shift


def positions(segs):
    length = segs.shape[-1]
    index = jnp.broadcast_to(jnp.arange(length, dtype=jnp.int32), segs.shape)
    first = jnp.ones(segs.shape[:-1] + (1,), dtype=bool)
    flag = jnp.concatenate([first, segs[..., 1:] != segs[..., :-1]], axis=-1)
    start = lax.cummax(jnp.where(flag, index, 0), axis=segs.ndim - 1)
    return index - start


def rotate(values, pos):
    half = ROT // 2
    inverse = 10000.0 ** (-(jnp.arange(half, dtype=jnp.float32) * 2.0 / ROT))
    angle = pos[..., None].astype(jnp.float32) * inverse
    cosine = jnp.cos(angle)[..., None, :]
    sine = jnp.sin(angle)[..., None, :]
    first = values[..., :half]
    second = values[..., half:ROT]
    return jnp.concatenate(
        [first * cosine - second * sine, second * cosine + first * sine, values[..., ROT:]], axis=-1
    )


def attention(qkv, pos, mask):
    query = rotate(qkv[:, :, :, 0], pos).astype(jnp.bfloat16)
    keys = rotate(qkv[:, :, :, 1], pos).astype(jnp.bfloat16)
    vals = qkv[:, :, :, 2].astype(jnp.bfloat16)
    scores = jnp.einsum("rqhd,rkhd->rhqk", query, keys, preferred_element_type=jnp.float32) / jnp.sqrt(
        jnp.float32(HD)
    )
    scores = jnp.where(mask, scores, -jnp.inf)
    probs = jax.nn.softmax(scores, axis=-1).astype(jnp.bfloat16)
    ctx = jnp.einsum("rhqk,rkhd->rqhd", probs, vals, preferred_element_type=jnp.float32)
    return ctx.astype(jnp.bfloat16)


def shards(
    tokens,
    segment_ids,
    shard_map,
    trainer_qkv,
    trainer_up,
    qkv_bias,
    up_bias,
    dense_w,
    down_w,
    out_bias,
    norm_gain,
    norm_shift,
):
    n_zz = lax.axis_size("zz")
    n_core = lax.axis_size("core")
    n_tp = lax.axis_size("tp")
    core = lax.axis_index("core")
    _, length, _ = tokens.shape
    block = trainer_qkv.shape[1]
    full_width = trainer_qkv.shape[1] * n_zz * n_core * n_tp
    n_blocks = full_width // block
    heads_group = qkv_bias.shape[1] // (3 * HD)
    ff_group = up_bias.shape[1]
    ff_here = ff_group // n_core
    split_heads = heads_group % n_core == 0
    heads_here = heads_group // n_core if split_heads else heads_group
    qkv_cols = heads_here * 3 * HD
    n_dest = n_tp * n_core

    wq = trainer_qkv.astype(jnp.bfloat16)
    wu = trainer_up.astype(jnp.bfloat16)
    if split_heads:
        wq = wq.reshape(LAYERS, block, n_dest, qkv_cols)
    else:
        wq = wq.reshape(LAYERS, block, n_tp, 1, qkv_cols)
        wq = jnp.broadcast_to(wq, (LAYERS, block, n_tp, n_core, qkv_cols))
        wq = wq.reshape(LAYERS, block, n_dest, qkv_cols)
    wu = wu.reshape(LAYERS, block, n_dest, ff_here)
    packed = jnp.concatenate([wq, wu], axis=-1)
    packed = lax.all_to_all(packed, ("tp", "core"), split_axis=2, concat_axis=1, tiled=True)

    zz_i, t_i, c_i = np.meshgrid(np.arange(n_zz), np.arange(n_tp), np.arange(n_core), indexing="ij")
    source = ((zz_i * n_core + c_i) * n_tp + t_i).reshape(-1)
    feature_block = jnp.take(shard_map, jnp.asarray(source, dtype=jnp.int32))

    segs = lax.all_gather(segment_ids, "core", axis=0, tiled=True)
    rows = segs.shape[0]
    pos = positions(segs)
    index = jnp.arange(length, dtype=jnp.int32)
    mask = (index[None, :] <= index[:, None])[None] & (segs[:, :, None] == segs[:, None, :])
    mask = mask[:, None]
    bias_full = lax.all_gather(out_bias, "tp", axis=1, tiled=True)

    stream = lax.all_gather(tokens, "tp", axis=2, tiled=True)
    stream = lax.all_gather(stream, "core", axis=0, tiled=True)
    for layer in range(LAYERS):
        weights = lax.all_gather(packed[layer].reshape(n_dest * block, -1), "zz", axis=0, tiled=True)
        w_qkv = weights[:, :qkv_cols]
        w_up = weights[:, qkv_cols:]
        flt = stream.astype(jnp.float32)
        permuted = jnp.take(stream.reshape(rows, length, n_blocks, block), feature_block, axis=2)
        permuted = permuted.reshape(rows * length, full_width).astype(jnp.float32)

        def norm_of(i):
            gain = jnp.take(norm_gain[layer, i].reshape(n_blocks, block), feature_block, axis=0)
            shift = jnp.take(norm_shift[layer, i].reshape(n_blocks, block), feature_block, axis=0)
            return layer_norm(permuted, gain.reshape(-1), shift.reshape(-1)).astype(jnp.bfloat16)

        attn_in = norm_of(0)
        mlp_in = norm_of(1)

        if split_heads:
            q_bias = lax.dynamic_slice_in_dim(qkv_bias[layer], core * qkv_cols, qkv_cols)
            qkv = jnp.dot(attn_in, w_qkv, preferred_element_type=jnp.float32) + q_bias.astype(jnp.float32)
            ctx = attention(qkv.reshape(rows, length, heads_here, 3, HD), pos, mask)
            ctx = ctx.reshape(rows * length, heads_here * HD)
            d_rows = lax.dynamic_slice_in_dim(dense_w[layer], core * heads_here * HD, heads_here * HD)
            attn_out = jnp.dot(ctx, d_rows, preferred_element_type=jnp.float32)
        else:
            own = lax.dynamic_slice_in_dim(attn_in.reshape(rows, length, -1), core, 1, axis=0)
            qkv = jnp.dot(own.reshape(length, -1), w_qkv, preferred_element_type=jnp.float32)
            qkv = qkv + qkv_bias[layer].astype(jnp.float32)
            own_pos = lax.dynamic_slice_in_dim(pos, core, 1, axis=0)
            own_mask = lax.dynamic_slice_in_dim(mask, core, 1, axis=0)
            ctx = attention(qkv.reshape(1, length, heads_here, 3, HD), own_pos, own_mask)
            attn_out = jnp.dot(ctx.reshape(length, -1), dense_w[layer], preferred_element_type=jnp.float32)
            here = (jnp.arange(rows) == core)[:, None, None]
            attn_out = jnp.where(here, attn_out[None], 0.0).reshape(rows * length, -1)

        u_bias = lax.dynamic_slice_in_dim(up_bias[layer], core * ff_here, ff_here)
        up = jnp.dot(mlp_in, w_up, preferred_element_type=jnp.float32) + u_bias.astype(jnp.float32)
        hidden_units = jax.nn.gelu(up, approximate=False).astype(jnp.bfloat16)
        m_rows = lax.dynamic_slice_in_dim(down_w[layer], core * ff_here, ff_here)
        partial_terms = attn_out + jnp.dot(hidden_units, m_rows, preferred_element_type=jnp.float32)
        partial_terms = partial_terms.astype(jnp.bfloat16).reshape(rows, length, full_width)
        if layer + 1 < LAYERS:
            summed = lax.psum(partial_terms, ("core", "tp")).astype(jnp.float32)
            stream = (flt + summed + bias_full[layer]).astype(jnp.bfloat16)
        else:
            summed = lax.psum_scatter(partial_terms, "core", scatter_dimension=0, tiled=True)
            summed = lax.psum_scatter(summed, "tp", scatter_dimension=2, tiled=True).astype(jnp.float32)
            width_here = full_width // n_tp
            own_stream = lax.dynamic_slice_in_dim(flt, core, 1, axis=0)
            own_stream = lax.dynamic_slice_in_dim(own_stream, lax.axis_index("tp") * width_here, width_here, axis=2)
            stream = (own_stream + summed + out_bias[layer]).astype(jnp.bfloat16)
    return stream


def solution(mesh):
    n_seq = mesh.shape["seq"]
    n_tp = mesh.shape["tp"]
    devices = np.asarray(mesh.devices).reshape(n_seq // 2, 2, n_tp)
    grid = Mesh(devices, ("zz", "core", "tp"))
    seq = ("zz", "core")
    in_specs = (
        P(seq, None, "tp"),
        P(seq, None),
        P(),
        P(None, ("zz", "core", "tp"), None),
        P(None, ("zz", "core", "tp"), None),
        P(None, "tp"),
        P(None, "tp"),
        P(None, "tp", None),
        P(None, "tp", None),
        P(None, "tp"),
        P(),
        P(),
    )
    out_specs = P(seq, None, "tp")
    return jax.shard_map(shards, mesh=grid, in_specs=in_specs, out_specs=out_specs, check_vma=False)
```

time: 702 us -> 650 us (0.926)
  waiting for transfers between devices: 397 us -> 330 us
  blocking collectives: 0 us -> 56.2 us
  starting transfers between devices: 22.5 us -> 0.24 us
  local copies, waits for them, and re-layouts: 140 us -> 119 us
    psum x0 -> x1, waiting for transfers between devices: none -> 70.2 us  [shards(): summed = lax.psum(partial_terms, ('core', 'tp')).astype(jnp.float32)]
    all_to_all x4 -> x0, waiting for transfers between devices: 49.8 us -> none  [the longest x2 29.2 us: shards(): lax.all_to_all(up_arr, 'tp', split_axis=1, concat_axis=0, tiled=True)]
    all_gather x6 -> x4, waiting for transfers between devices: 256 us -> 209 us  [the longest x2 169 us: shards(): lax.all_gather(packed[layer].reshape(n_dest * block, -1), 'zz', axis=0, t...]
    all_to_all x0 -> x1, blocking collectives: none -> 46 us  [shards(): lax.all_to_all(packed, ('tp', 'core'), split_axis=2, concat_axis=1, tiled...]
    all_to_all x4 -> x1, local copies, waits for them, and re-layouts: 40.1 us -> 0.29 us  [shards(): lax.all_to_all(packed, ('tp', 'core'), split_axis=2, concat_axis=1, tiled...]
    reduce_scatter x2, waiting for transfers between devices: 89 us -> 49.8 us  [the longest x1 39.4 us: shards(): lax.psum_scatter(summed, 'tp', scatter_dimension=2, tiled=True)]
    all_gather x4 -> x1, local copies, waits for them, and re-layouts: 41.2 us -> 6.25 us  [shards(): stream = lax.all_gather(stream, 'core', axis=0, tiled=True)]
    convert_element_type x0 -> x5, local copies, waits for them, and re-layouts: none -> 26.1 us  [the longest x2 24.7 us: shards(): permuted = permuted.reshape(rows * length, full_width).astype(jnp.float32)]
  transfers between devices with their start and end apart: 12 -> 7, of which waited for: 8 -> 6; matrix products, arithmetic and copies ran while one was open for 27% -> 16% of each run, Pallas kernels for 0% -> 0%
where the time goes in v1:
time: 650 us; the launch traced here: 640 us
  waiting for transfers between devices  330 us (51%)
  local copies, waits for them, and re-layouts  119 us (18%)
  matrix products  89.4 us (14%)
  blocking collectives  56.2 us (9%)
  other arithmetic  30.2 us (5%)
  between operations  14.2 us (2%)
    all_gather x2, waiting for transfers between devices, shards(): lax.all_gather(packed[layer].reshape(n_dest * block, -1), 'zz', axis=0, t...  169 us
    psum x1, waiting for transfers between devices, shards(): summed = lax.psum(partial_terms, ('core', 'tp')).astype(jnp.float32)  70.2 us
    all_to_all x1, blocking collectives, shards(): lax.all_to_all(packed, ('tp', 'core'), split_axis=2, concat_axis=1, tiled...  46 us
    all_gather x1, waiting for transfers between devices, shards(): stream = lax.all_gather(tokens, 'tp', axis=2, tiled=True)  39.8 us
    reduce_scatter x1, waiting for transfers between devices, shards(): lax.psum_scatter(summed, 'tp', scatter_dimension=2, tiled=True)  39.4 us
    dot_general x2, matrix products, shards(): jnp.dot(mlp_in, w_up, preferred_element_type=jnp.float32)  37.4 us
    convert_element_type x2, local copies, waits for them, and re-layouts, shards(): permuted = permuted.reshape(rows * length, full_width).astype(jnp.float32)  24.7 us
    dot_general x2, matrix products, shards(): jnp.dot(attn_in, w_qkv, preferred_element_type=jnp.float32)  19.9 us
  transfers between devices with their start and end apart: 7, of which 6 were waited for; matrix products, arithmetic and copies ran while one was open for 16% of the time, Pallas kernels for 0%

profile of v1, /device:TPU:0, one launch (start us, length us, event | category | flops | bytes accessed | tf_op | source)
XLA Modules:
  0.0 639.9 jit_solution(1780125768389264380)
XLA Ops:
  6.5 0.7 all-gather.6.cloned.1.call-update
  7.3 39.8 %all-gather.6.cloned.1.call-done = bf16[1,512,2048]{2,1,0:T(8,128)(2,1)} async-done(((bf16[1,512,512]{2,1,0:T(8,128)(2,1)}), bf16[1,512,2048]{2,1,0:T(8,128)(2,1)}) %all-gather.6.cloned.1.call-update) | async-done | bytes 2097168 | tf_op jit(solution)/shard_map/all_gather | solution.py:110
  47.2 2.6 convert_element_type.149
  49.8 1.4 copy.92
  52.0 0.7 copy.61
  52.8 46.0 %all_to_all.15 = bf16[2,64,8,1792]{3,1,0,2:T(8,128)(2,1)S(1)} all-to-all(bf16[2,64,8,1792]{3,1,0,2:T(8,128)(2,1)S(1)} %copy.61), channel_id=1, replica_groups=mesh['zz'=4,'core'=2,'tp'=4] {'tp','core'}, dimensions={2} | all-to-all | bytes 7340032 | tf_op jit(solution)/shard_map/all_to_all | solution.py:96
  99.1 2.2 fusion.303
  101.7 0.7 gather_fusion
  102.5 0.6 gather_fusion.2
  106.3 0.6 gather_fusion.9
  107.7 2.0 all-gather
  109.9 0.6 reduce-window.6
  111.3 5.2 fusion.302
  116.5 11.9 %fusion.301 = (bf16[1,2048,2048]{2,1,0:T(8,128)(2,1)}, bf16[1,2048,2048]{2,1,0:T(8,128)(2,1)}) fusion(bf16[2,2048,2048]{2,1,0:T(8,128)(2,1)} %param.25), kind=kLoop, calls=%fused_computation.367 | loop fusion | bytes 33554432 | tf_op jit(solution)/shard_map/slice | solution.py:149
  128.4 6.3 copy.58
  134.7 5.0 gather_fusion.1
  139.6 3.6 fusion.19
  143.3 1.6 multiply_reduce_fusion.1
  144.9 0.6 bitcast_convert_fusion.1
  145.5 12.4 %copy.60 = f32[2,512,32,64]{1,0,3,2:T(2,128)S(1)} copy(f32[2,512,32,64]{1,3,0,2:T(8,128)S(1)} %bitcast_convert_fusion.1) | data formatting | bytes 16777216 | tf_op jit(solution)/shard_map/convert_element_type | solution.py:118
  157.9 5.3 copy.88
  163.2 69.9 %all-gather.10.cloned.1.call-done = bf16[2048,1792]{1,0:T(8,128)(2,1)} async-done(((bf16[512,1792]{1,0:T(8,128)(2,1)}), bf16[2048,1792]{1,0:T(8,128)(2,1)}) %all-gather.10.cloned.1.call-update) | async-done | bytes 7340048 | tf_op jit(solution)/shard_map/all_gather | solution.py:113
  233.1 9.9 %fusion.121 = f32[1024,768]{1,0:T(8,128)} fusion(bf16[2048,1792]{1,0:T(8,128)(2,1)} %all-gather.10.cloned.1.call-done, f32[1024,2048]{0,1:T(8,128)} %bitcast.146, f32[2048]{0:T(1024)S(1)} %add.208, f32[2048]{0:T(1024)S(1)} %mul.210, f32[1024]{0:T(1024)S(1)} %bitcast.172, f32[1024]{0:T(1024)S(1)} %bitcast.174, f32[768]{0:T(1024)S(1)} %convert_reduce_fusion.1), kind=kOutput, calls=%fused_computation.170 | convolution fusion | flops 3232497664 | bytes 14707712 | tf_op jit(solution)/shard_map/dot_general | solution.py:130
  243.0 2.8 copy.63
  245.8 3.8 reshape.330
  249.5 2.3 fusion.305
  251.8 2.4 slice.216
  254.2 0.6 copy.83
  254.8 0.6 copy.82
  255.9 3.3 fusion.195
  259.2 4.3 fusion.308
  263.5 2.0 fusion.124
  265.7 18.7 %fusion.333 = bf16[1024,1024]{1,0:T(8,128)(2,1)S(1)} fusion(f32[1024]{0:T(1024)S(1)} %bitcast.168, bf16[2048,1792]{1,0:T(8,128)(2,1)} %all-gather.10.cloned.1.call-done, f32[1024,2048]{0,1:T(8,128)} %bitcast.147, f32[2048]{0:T(1024)S(1)} %add.219, f32[2048]{0:T(1024)S(1)} %mul.226, f32[1024]{0:T(1024)S(1)} %bitcast.173, f32[1024]{0:T(1024)S(1)} %bitcast.175), kind=kOutput, calls=%fused_computation.28.clone.clone | convolution fusion | flops 4374659072 | bytes 14708736 | tf_op jit(solution)/shard_map/dot_general | solution.py:147
  284.4 6.5 %fusion.17 = f32[1024,2048]{1,0:T(8,128)S(1)} fusion(bf16[1,2048,2048]{2,1,0:T(8,128)(2,1)} %get-tuple-element.15, s32[]{:T(128)S(6)} %select_n.65, bf16[1024,1024]{1,0:T(8,128)(2,1)S(1)} %fusion.333), kind=kOutput, calls=%fused_computation.42 | convolution fusion | flops 4294967296 | bytes 14680068 | tf_op jit(solution)/shard_map/dot_general | solution.py:150
  291.0 3.4 add_convert_fusion.4
  294.3 6.3 copy.69
  301.3 8.2 %all_gather.22 = f32[2,2048]{1,0:T(2,128)S(1)} all-gather(f32[2,512]{1,0:T(2,128)S(1)} %copy-done.12), channel_id=1, replica_groups=mesh['zz'=4,'core'=2,'tp'=4] {'tp'}, dimensions={1}, use_global_device_ids=true | all-gather | bytes 20480 | tf_op jit(solution)/shard_map/all_gather | solution.py:108
  309.9 70.2 %all-reduce.3.cloned.1.call-done = bf16[2,512,2048]{1,2,0:T(8,128)(2,1)} async-done(((bf16[2,512,2048]{1,2,0:T(8,128)(2,1)}), bf16[2,512,2048]{1,2,0:T(8,128)(2,1)}) %all-reduce.3.cloned.1.call-update) | async-done | bytes 4194320 | tf_op jit(solution)/shard_map/psum | solution.py:153
  380.0 5.6 add_convert_fusion.3
  385.7 5.0 gather_fusion.6
  390.7 3.9 fusion.16
  394.8 1.6 multiply_reduce_fusion
  396.5 0.6 bitcast_convert_fusion
  397.1 12.4 %copy.70 = f32[2,512,32,64]{1,0,3,2:T(2,128)S(1)} copy(f32[2,512,32,64]{1,3,0,2:T(8,128)S(1)} %bitcast_convert_fusion) | data formatting | bytes 16777216 | tf_op jit(solution)/shard_map/convert_element_type | solution.py:118
  409.4 5.3 copy.94
  414.7 99.4 %all-gather.12.cloned.1.call-done = bf16[2048,1792]{1,0:T(8,128)(2,1)} async-done(((bf16[512,1792]{1,0:T(8,128)(2,1)}), bf16[2048,1792]{1,0:T(8,128)(2,1)}) %all-gather.12.cloned.1.call-update) | async-done | bytes 7340048 | tf_op jit(solution)/shard_map/all_gather | solution.py:113
  514.1 10.0 %fusion.118 = f32[1024,768]{1,0:T(8,128)} fusion(bf16[2048,1792]{1,0:T(8,128)(2,1)} %all-gather.12.cloned.1.call-done, f32[1024,2048]{0,1:T(8,128)} %bitcast.144, f32[2048]{0:T(1024)S(1)} %add.235, f32[2048]{0:T(1024)S(1)} %mul.237, f32[1024]{0:T(1024)S(1)} %bitcast.170, f32[1024]{0:T(1024)S(1)} %bitcast.176, f32[768]{0:T(1024)S(1)} %convert_reduce_fusion), kind=kOutput, calls=%fused_computation.169 | convolution fusion | flops 3232497664 | bytes 14707712 | tf_op jit(solution)/shard_map/dot_general | solution.py:130
  524.1 2.4 copy.71
  526.5 3.7 reshape.336
  530.2 2.3 fusion.304
  532.5 0.6 copy.84
  533.1 0.6 copy.85
  534.0 3.5 fusion.191
  537.8 1.6 slice.232
  539.4 4.0 fusion.313
  543.4 2.0 fusion.125
  545.7 18.7 %fusion.330 = bf16[1024,1024]{1,0:T(8,128)(2,1)S(1)} fusion(f32[1024]{0:T(1024)S(1)} %bitcast.169, bf16[2048,1792]{1,0:T(8,128)(2,1)} %all-gather.12.cloned.1.call-done, f32[1024,2048]{0,1:T(8,128)} %bitcast.145, f32[2048]{0:T(1024)S(1)} %add.244, f32[2048]{0:T(1024)S(1)} %mul.248, f32[1024]{0:T(1024)S(1)} %bitcast.171, f32[1024]{0:T(1024)S(1)} %bitcast.177), kind=kOutput, calls=%fused_computation.31.clone.clone.2 | convolution fusion | flops 4374659072 | bytes 14708736 | tf_op jit(solution)/shard_map/dot_general | solution.py:147
  564.4 6.5 %fusion.14 = f32[1024,2048]{1,0:T(8,128)S(1)} fusion(bf16[1,2048,2048]{2,1,0:T(8,128)(2,1)} %get-tuple-element.16, s32[]{:T(128)S(6)} %select_n.65, bf16[1024,1024]{1,0:T(8,128)(2,1)S(1)} %fusion.330), kind=kOutput, calls=%fused_computation.38 | convolution fusion | flops 4294967296 | bytes 14680068 | tf_op jit(solution)/shard_map/dot_general | solution.py:150
  570.9 3.4 add_convert_fusion
  574.3 6.2 copy.77
  580.6 10.4 %reduce-scatter.3.cloned.1.call-done = bf16[1,512,2048]{1,2,0:T(8,128)(2,1)} async-done(((bf16[2,512,2048]{1,2,0:T(8,128)(2,1)}), bf16[1,512,2048]{1,2,0:T(8,128)(2,1)}) %reduce-scatter.3.cloned.1.call-update) | async-done | bytes 2097168 | tf_op jit(solution)/shard_map/reduce_scatter | solution.py:156
  591.0 39.4 %reduce-scatter.5.cloned.1.call-done = bf16[1,512,512]{1,2,0:T(8,128)(2,1)} async-done(((bf16[1,512,2048]{1,2,0:T(8,128)(2,1)}), bf16[1,512,512]{1,2,0:T(8,128)(2,1)}) %reduce-scatter.5.cloned.1.call-update) | async-done | bytes 524304 | tf_op jit(solution)/shard_map/reduce_scatter | solution.py:157
  630.4 1.4 add_convert_fusion.15
  631.9 1.0 copy.78
  (108 shorter events, 9.3 us)
Async XLA Ops:
  6.5 95.2 %copy-start = (s32[32]{0:T(128)S(1)}, s32[32]{0:T(128)}, u32[]{:S(2)}) copy-start(s32[32]{0:T(128)} %param.19) | copy-start | bytes 388
  6.5 40.5 %all-gather.6.cloned.1.call-start = ((), (), s32[]{:S(2)}) async-start(), calls=%async_computation.3 | async-start | bytes 2621440 | tf_op jit(solution)/shard_map/all_gather | solution.py:110
  7.3 121.2 %all-gather.8.cloned.1.call-start = ((), (), s32[]{:S(2)}) async-start(), calls=%async_computation.4 | async-start | bytes 6291456 | tf_op jit(solution)/shard_map/all_gather | solution.py:111
  47.1 4.1 copy-start.6
  47.1 186.0 %all-gather.10.cloned.1.call-start = ((), (), s32[]{:S(2)}) async-start(), calls=%async_computation.5 | async-start | bytes 9175040 | tf_op jit(solution)/shard_map/all_gather | solution.py:113
  99.1 2.3 copy-start.9
  99.1 2.3 copy-start.10
  99.1 2.6 copy-start.14
  99.1 8.6 %copy-start.13 = (s32[1,512]{1,0:T(1,128)S(1)}, s32[1,512]{1,0:T(1,128)}, u32[]{:S(2)}) copy-start(s32[1,512]{1,0:T(1,128)} %param.18) | copy-start | bytes 6148
  99.1 11.9 %copy-start.11 = (bf16[2,1536]{1,0:T(2,128)(2,1)S(1)}, bf16[2,1536]{1,0:T(2,128)(2,1)}, u32[]{:S(2)}) copy-start(bf16[2,1536]{1,0:T(2,128)(2,1)} %param.22) | copy-start | bytes 18436
  99.1 12.0 %copy-start.8 = (bf16[2,2048]{1,0:T(2,128)(2,1)S(1)}, bf16[2,2048]{1,0:T(2,128)(2,1)}, u32[]{:S(2)}) copy-start(bf16[2,2048]{1,0:T(2,128)(2,1)} %param.23) | copy-start | bytes 24580
  101.3 278.7 %all-reduce.3.cloned.1.call-start = ((), (), s32[]{:S(2)}) async-start(), calls=%async_computation.6 | async-start | bytes 8388608 | tf_op jit(solution)/shard_map/psum | solution.py:153
  139.6 3.6 copy-start.2
  259.2 4.3 copy-start.7
  284.4 6.5 %copy-start.5 = (bf16[1,512,2048]{2,1,0:T(8,128)(2,1)S(1)}, bf16[1,512,2048]{2,1,0:T(8,128)(2,1)}, u32[]{:S(2)}) copy-start(bf16[1,512,2048]{2,1,0:T(8,128)(2,1)} %get-tuple-element.18) | copy-start | bytes 6291460
  300.6 0.7 copy-start.12
  300.6 213.5 %all-gather.12.cloned.1.call-start = ((), (), s32[]{:S(2)}) async-start(), calls=%async_computation.7 | async-start | bytes 9175040 | tf_op jit(solution)/shard_map/all_gather | solution.py:113
  301.2 289.7 %reduce-scatter.3.cloned.1.call-start = ((), (), s32[]{:S(2)}) async-start(), calls=%async_computation.8 | async-start | bytes 6291456 | tf_op jit(solution)/shard_map/reduce_scatter | solution.py:156
  390.7 4.1 copy-start.3
  564.4 6.5 %copy-start.4 = (bf16[1,512,2048]{2,1,0:T(8,128)(2,1)S(1)}, bf16[1,512,2048]{2,1,0:T(8,128)(2,1)}, u32[]{:S(2)}) copy-start(bf16[1,512,2048]{2,1,0:T(8,128)(2,1)} %get-tuple-element.17) | copy-start | bytes 6291460
  580.5 52.4 %copy-start.1 = (s32[32]{0:T(128)S(1)}, s32[32]{0:T(128)}, u32[]{:S(2)}) copy-start(s32[32]{0:T(128)} %param.19) | copy-start | bytes 388
  580.5 49.9 %reduce-scatter.5.cloned.1.call-start = ((), (), s32[]{:S(2)}) async-start(), calls=%async_computation.9 | async-start | bytes 2621440 | tf_op jit(solution)/shard_map/reduce_scatter | solution.py:157
Sparse Core Ops, SparseCore 0:
  9.2 37.8 all-gather.5
  48.6 13.6 all-gather.7
  101.5 131.5 all-gather.9
  300.7 79.2 all-reduce.2
  381.5 132.5 all-gather.11
  580.6 10.2 reduce-scatter.2
  593.9 36.4 reduce-scatter.4

commit v2 on v1

--- a/solution.py
+++ b/solution.py
@@ -95,9 +95,16 @@
     packed = jnp.concatenate([wq, wu], axis=-1)
     packed = lax.all_to_all(packed, ("tp", "core"), split_axis=2, concat_axis=1, tiled=True)
 
-    zz_i, t_i, c_i = np.meshgrid(np.arange(n_zz), np.arange(n_tp), np.arange(n_core), indexing="ij")
-    source = ((zz_i * n_core + c_i) * n_tp + t_i).reshape(-1)
-    feature_block = jnp.take(shard_map, jnp.asarray(source, dtype=jnp.int32))
+    k_i, t_i, c_i = np.meshgrid(np.arange(n_zz), np.arange(n_tp), np.arange(n_core), indexing="ij")
+    src_zz = (lax.axis_index("zz") + n_zz - jnp.asarray(k_i.reshape(-1), dtype=jnp.int32)) % n_zz
+    source = (src_zz * n_core + jnp.asarray(c_i.reshape(-1))) * n_tp + jnp.asarray(t_i.reshape(-1))
+    feature_block = jnp.take(shard_map, source.astype(jnp.int32))
+
+    def gather_zz(piece):
+        pieces = [piece]
+        for k in range(1, n_zz):
+            pieces.append(lax.ppermute(piece, "zz", perm=[(i, (i + k) % n_zz) for i in range(n_zz)]))
+        return jnp.concatenate(pieces, axis=0)
 
     segs = lax.all_gather(segment_ids, "core", axis=0, tiled=True)
     rows = segs.shape[0]
@@ -110,7 +117,7 @@
     stream = lax.all_gather(tokens, "tp", axis=2, tiled=True)
     stream = lax.all_gather(stream, "core", axis=0, tiled=True)
     for layer in range(LAYERS):
-        weights = lax.all_gather(packed[layer].reshape(n_dest * block, -1), "zz", axis=0, tiled=True)
+        weights = gather_zz(packed[layer].reshape(n_dest * block, -1))
         w_qkv = weights[:, :qkv_cols]
         w_up = weights[:, qkv_cols:]
         flt = stream.astype(jnp.float32)

time: 650 us -> 624 us (0.960)
  starting transfers between devices: 0.24 us -> 53.5 us
  blocking collectives: 56.2 us -> 16.4 us
  waiting for transfers between devices: 330 us -> 303 us
    all_gather x2 -> x0, waiting for transfers between devices: 169 us -> none  [shards(): lax.all_gather(packed[layer].reshape(n_dest * block, -1), 'zz', axis=0, t...]
    ppermute x0 -> x6, waiting for transfers between devices: none -> 102 us  [gather_zz(): lax.ppermute(piece, 'zz', perm=[(i, (i + k) % n_zz) for i in range(n_zz)])]
    ppermute x0 -> x6, starting transfers between devices: none -> 48 us  [gather_zz(): lax.ppermute(piece, 'zz', perm=[(i, (i + k) % n_zz) for i in range(n_zz)])]
    all_to_all x1 -> x0, blocking collectives: 46 us -> none  [shards(): lax.all_to_all(packed, ('tp', 'core'), split_axis=2, concat_axis=1, tiled...]
    reduce_scatter x1, waiting for transfers between devices: 10.4 us -> 50.3 us  [shards(): lax.psum_scatter(partial_terms, 'core', scatter_dimension=0, tiled=True)]
    unnamed x43 -> x59, local copies, waits for them, and re-layouts: 15.2 us -> 9.15 us
  transfers between devices with their start and end apart: 7 -> 12, of which waited for: 6 -> 7; matrix products, arithmetic and copies ran while one was open for 16% -> 16% of each run, Pallas kernels for 0% -> 0%
where the time goes in v2:
time: 624 us; the launch traced here: 618 us
  waiting for transfers between devices  303 us (49%)
  local copies, waits for them, and re-layouts  117 us (19%)
  matrix products  84.7 us (14%)
  starting transfers between devices  53.5 us (9%)
  other arithmetic  29.8 us (5%)
  blocking collectives  16.4 us (3%)
  between operations  14.2 us (2%)
    ppermute x6, waiting for transfers between devices, gather_zz(): lax.ppermute(piece, 'zz', perm=[(i, (i + k) % n_zz) for i in range(n_zz)])  102 us
    psum x1, waiting for transfers between devices, shards(): summed = lax.psum(partial_terms, ('core', 'tp')).astype(jnp.float32)  67.1 us
    reduce_scatter x1, waiting for transfers between devices, shards(): lax.psum_scatter(partial_terms, 'core', scatter_dimension=0, tiled=True)  50.3 us
    ppermute x6, starting transfers between devices, gather_zz(): lax.ppermute(piece, 'zz', perm=[(i, (i + k) % n_zz) for i in range(n_zz)])  48 us
    all_gather x1, waiting for transfers between devices, shards(): stream = lax.all_gather(tokens, 'tp', axis=2, tiled=True)  43.6 us
    reduce_scatter x1, waiting for transfers between devices, shards(): lax.psum_scatter(summed, 'tp', scatter_dimension=2, tiled=True)  39.3 us
    dot_general x2, matrix products, shards(): jnp.dot(mlp_in, w_up, preferred_element_type=jnp.float32)  37.1 us
    convert_element_type x2, local copies, waits for them, and re-layouts, shards(): permuted = permuted.reshape(rows * length, full_width).astype(jnp.float32)  24.7 us
  transfers between devices with their start and end apart: 12, of which 7 were waited for; matrix products, arithmetic and copies ran while one was open for 16% of the time, Pallas kernels for 0%

profile of v2, /device:TPU:0, one launch (start us, length us, event | category | flops | bytes accessed | tf_op | source)
XLA Modules:
  0.0 618.5 jit_solution(3810582457018060437)
XLA Ops:
  6.5 0.7 all-gather.4.cloned.1.call-update
  7.3 2.6 convert_element_type.149
  9.9 1.4 copy.94
  12.1 2.7 copy.63
  14.8 5.3 all-to-all-start
  20.6 0.7 gather_fusion
  26.6 1.9 all-gather
  28.6 43.6 %all-gather.4.cloned.1.call-done = bf16[1,512,2048]{2,1,0:T(8,128)(2,1)} async-done(((bf16[1,512,512]{2,1,0:T(8,128)(2,1)}), bf16[1,512,2048]{2,1,0:T(8,128)(2,1)}) %all-gather.4.cloned.1.call-update) | async-done | bytes 2097168 | tf_op jit(solution)/shard_map/all_gather | solution.py:117
  73.8 4.8 fusion.191
  78.5 12.6 %fusion.190 = (bf16[1,2048,2048]{2,1,0:T(8,128)(2,1)}, bf16[1,2048,2048]{2,1,0:T(8,128)(2,1)}) fusion(bf16[2,2048,2048]{2,1,0:T(8,128)(2,1)} %param.27), kind=kLoop, calls=%fused_computation.277 | loop fusion | bytes 33554432 | tf_op jit(solution)/shard_map/slice | solution.py:156
  91.2 2.5 copy.110
  93.7 1.5 fusion.192
  95.2 1.6 collective-permute-start
  96.8 2.4 collective-permute-start.1
  99.3 1.6 collective-permute-start.2
  100.8 6.3 %copy.60 = bf16[2,512,2048]{1,2,0:T(8,128)(2,1)} copy(bf16[2,512,2048]{2,1,0:T(8,128)(2,1)} %all-gather.6.cloned.1.call-done) | data formatting | bytes 8388608 | tf_op jit(solution)/shard_map/all_gather | solution.py:118
  107.1 4.9 gather_fusion.1
  112.1 3.6 fusion.19
  115.6 1.6 multiply_reduce_fusion.1
  117.9 12.4 %copy.62 = f32[2,512,32,64]{1,0,3,2:T(2,128)S(1)} copy(f32[2,512,32,64]{1,3,0,2:T(8,128)S(1)} %bitcast_convert_fusion.1) | data formatting | bytes 16777216 | tf_op jit(solution)/shard_map/convert_element_type | solution.py:125
  130.3 2.1 copy.90
  132.4 7.8 %collective-permute-done = bf16[512,1792]{1,0:T(8,128)(2,1)} collective-permute-done((bf16[512,1792]{1,0:T(8,128)(2,1)S(1)}, bf16[512,1792]{1,0:T(8,128)(2,1)}, u32[]{:S(2)}, u32[]{:S(2)}) %collective-permute-start) | collective-permute-done | bytes 1835040 | tf_op jit(solution)/shard_map/ppermute | solution.py:106
  140.2 77.8 %collective-permute-done.1 = bf16[512,1792]{1,0:T(8,128)(2,1)} collective-permute-done((bf16[512,1792]{1,0:T(8,128)(2,1)S(1)}, bf16[512,1792]{1,0:T(8,128)(2,1)}, u32[]{:S(2)}, u32[]{:S(2)}) %collective-permute-start.1) | collective-permute-done | bytes 1835040 | tf_op jit(solution)/shard_map/ppermute | solution.py:106
  218.0 7.7 %fusion.69 = f32[1024,768]{1,0:T(8,128)} fusion(bf16[512,1792]{1,0:T(8,128)(2,1)} %collective-permute-done.2, bf16[512,1792]{1,0:T(8,128)(2,1)} %collective-permute-done.1, bf16[512,1792]{1,0:T(8,128)(2,1)} %collective-permute-done, bf16[512,1792]{1,0:T(8,128)(2,1)S(1)} %bitcast.165, f32[1024,2048]{0,1:T(8,128)S(1)} %bitcast.143, f32[2048]{0:T(1024)S(1)} %add.227, ...), kind=kOutput, calls=%fused_computation.126 | convolution fusion | flops 3245080576 | bytes 18902016 | tf_op jit(solution)/shard_map/dot_general | solution.py:137
  225.7 2.4 copy.65
  228.1 3.8 reshape.330
  231.9 2.3 fusion.194
  234.1 2.4 slice.215
  237.1 0.6 copy.84
  238.2 3.5 fusion.143
  241.7 4.3 fusion.197
  246.0 2.2 fusion.72
  248.4 18.6 %fusion.4 = bf16[1024,1024]{1,0:T(8,128)(2,1)S(1)} fusion(bf16[512,1792]{1,0:T(8,128)(2,1)} %collective-permute-done.2, bf16[512,1792]{1,0:T(8,128)(2,1)} %collective-permute-done.1, bf16[512,1792]{1,0:T(8,128)(2,1)} %collective-permute-done, bf16[512,1792]{1,0:T(8,128)(2,1)S(1)} %bitcast.166, f32[1024,2048]{0,1:T(8,128)} %bitcast.144, f32[2048]{0:T(1024)S(1)} %add.238, ...), kind=kOutput, calls=%fused_computation.28 | convolution fusion | flops 4391436288 | bytes 17854464 | tf_op jit(solution)/shard_map/dot_general | solution.py:154
  267.0 6.5 %fusion.17 = f32[1024,2048]{1,0:T(8,128)S(1)} fusion(bf16[1024,1024]{1,0:T(8,128)(2,1)S(1)} %fusion.4, bf16[1,2048,2048]{2,1,0:T(8,128)(2,1)} %get-tuple-element.18, s32[]{:T(128)S(6)} %select_n.72), kind=kOutput, calls=%fused_computation.48 | convolution fusion | flops 4294967296 | bytes 14680068 | tf_op jit(solution)/shard_map/dot_general | solution.py:157
  273.5 3.4 add_convert_fusion.4
  276.9 6.3 %copy.71 = bf16[2,512,2048]{1,2,0:T(8,128)(2,1)} copy(bf16[2,512,2048]{2,1,0:T(8,128)(2,1)} %bitcast.137) | data formatting | bytes 8388608 | tf_op jit(solution)/shard_map/reshape | solution.py:158
  283.8 14.5 %all_gather.15 = f32[2,2048]{1,0:T(2,128)S(1)} all-gather(f32[2,512]{1,0:T(2,128)S(1)} %copy-done.18), channel_id=1, replica_groups=mesh['zz'=4,'core'=2,'tp'=4] {'tp'}, dimensions={1}, use_global_device_ids=true | all-gather | bytes 20480 | tf_op jit(solution)/shard_map/all_gather | solution.py:115
  298.6 40.0 %collective-permute-start.3 = (bf16[512,1792]{1,0:T(8,128)(2,1)S(1)}, bf16[512,1792]{1,0:T(8,128)(2,1)}, u32[]{:S(2)}, u32[]{:S(2)}) collective-permute-start(bf16[512,1792]{1,0:T(8,128)(2,1)S(1)} %bitcast.157), channel_id=1, source_target_pairs={{0,8},{8,16},{16,24},{24,0},{1,9},{9,17},{17,25},{25,1},{2,10},{10... | collective-permute-start | bytes 5505032 | tf_op jit(solution)/shard_map/ppermute | solution.py:106
  338.6 1.4 collective-permute-start.4
  340.0 1.1 collective-permute-start.5
  341.1 67.1 %all-reduce.3.cloned.1.call-done = bf16[2,512,2048]{1,2,0:T(8,128)(2,1)} async-done(((bf16[2,512,2048]{1,2,0:T(8,128)(2,1)}), bf16[2,512,2048]{1,2,0:T(8,128)(2,1)}) %all-reduce.3.cloned.1.call-update) | async-done | bytes 4194320 | tf_op jit(solution)/shard_map/psum | solution.py:160
  408.2 5.5 add_convert_fusion.3
  413.7 5.0 gather_fusion.6
  418.7 3.6 fusion.16
  422.3 1.6 multiply_reduce_fusion
  424.5 12.4 %copy.72 = f32[2,512,32,64]{1,0,3,2:T(2,128)S(1)} copy(f32[2,512,32,64]{1,3,0,2:T(8,128)S(1)} %bitcast_convert_fusion) | data formatting | bytes 16777216 | tf_op jit(solution)/shard_map/convert_element_type | solution.py:125
  436.9 2.1 copy.96
  439.0 16.6 %collective-permute-done.4 = bf16[512,1792]{1,0:T(8,128)(2,1)} collective-permute-done((bf16[512,1792]{1,0:T(8,128)(2,1)S(1)}, bf16[512,1792]{1,0:T(8,128)(2,1)}, u32[]{:S(2)}, u32[]{:S(2)}) %collective-permute-start.4) | collective-permute-done | bytes 1835040 | tf_op jit(solution)/shard_map/ppermute | solution.py:106
  455.6 7.7 %fusion.66 = f32[1024,768]{1,0:T(8,128)} fusion(bf16[512,1792]{1,0:T(8,128)(2,1)} %collective-permute-done.5, bf16[512,1792]{1,0:T(8,128)(2,1)} %collective-permute-done.4, bf16[512,1792]{1,0:T(8,128)(2,1)} %collective-permute-done.3, bf16[512,1792]{1,0:T(8,128)(2,1)S(1)} %bitcast.160, f32[1024,2048]{0,1:T(8,128)S(1)} %bitcast.141, f32[2048]{0:T(1024)S(1)} %add.254, ...), kind=kOutput, calls=%fused_computation.125 | convolution fusion | flops 3245080576 | bytes 18902016 | tf_op jit(solution)/shard_map/dot_general | solution.py:137
  463.3 2.4 copy.73
  465.7 3.8 reshape.336
  469.4 2.3 fusion.193
  473.2 3.4 fusion.139
  476.8 1.6 slice.229
  478.4 4.0 fusion.202
  482.4 2.2 fusion.73
  484.8 18.5 %fusion.7 = bf16[1024,1024]{1,0:T(8,128)(2,1)S(1)} fusion(bf16[512,1792]{1,0:T(8,128)(2,1)} %collective-permute-done.5, bf16[512,1792]{1,0:T(8,128)(2,1)} %collective-permute-done.4, bf16[512,1792]{1,0:T(8,128)(2,1)} %collective-permute-done.3, bf16[512,1792]{1,0:T(8,128)(2,1)S(1)} %bitcast.161, f32[1024,2048]{0,1:T(8,128)} %bitcast.142, ...), kind=kOutput, calls=%fused_computation.31 | convolution fusion | flops 4391436288 | bytes 17854464 | tf_op jit(solution)/shard_map/dot_general | solution.py:154
  503.3 6.5 %fusion.14 = f32[1024,2048]{1,0:T(8,128)S(1)} fusion(bf16[1024,1024]{1,0:T(8,128)(2,1)S(1)} %fusion.7, bf16[1,2048,2048]{2,1,0:T(8,128)(2,1)} %get-tuple-element.17, s32[]{:T(128)S(6)} %select_n.72), kind=kOutput, calls=%fused_computation.44 | convolution fusion | flops 4294967296 | bytes 14680068 | tf_op jit(solution)/shard_map/dot_general | solution.py:157
  509.8 3.4 add_convert_fusion
  513.1 6.2 %copy.79 = bf16[2,512,2048]{1,2,0:T(8,128)(2,1)} copy(bf16[2,512,2048]{2,1,0:T(8,128)(2,1)} %bitcast.136) | data formatting | bytes 8388608 | tf_op jit(solution)/shard_map/reshape | solution.py:158
  519.4 50.3 %reduce-scatter.3.cloned.1.call-done = bf16[1,512,2048]{1,2,0:T(8,128)(2,1)} async-done(((bf16[2,512,2048]{1,2,0:T(8,128)(2,1)}), bf16[1,512,2048]{1,2,0:T(8,128)(2,1)}) %reduce-scatter.3.cloned.1.call-update) | async-done | bytes 2097168 | tf_op jit(solution)/shard_map/reduce_scatter | solution.py:163
  569.8 39.3 %reduce-scatter.5.cloned.1.call-done = bf16[1,512,512]{1,2,0:T(8,128)(2,1)} async-done(((bf16[1,512,2048]{1,2,0:T(8,128)(2,1)}), bf16[1,512,512]{1,2,0:T(8,128)(2,1)}) %reduce-scatter.5.cloned.1.call-update) | async-done | bytes 524304 | tf_op jit(solution)/shard_map/reduce_scatter | solution.py:164
  609.0 1.4 add_convert_fusion.19
  610.5 1.0 copy.80
  (131 shorter events, 13.6 us)
Async XLA Ops:
  6.5 14.1 %copy-start = (s32[32]{0:T(128)S(1)}, s32[32]{0:T(128)}, u32[]{:S(2)}) copy-start(s32[32]{0:T(128)} %param.21) | copy-start | bytes 388
  6.5 65.6 %all-gather.4.cloned.1.call-start = ((), (), s32[]{:S(2)}) async-start(), calls=%async_computation.3 | async-start | bytes 2621440 | tf_op jit(solution)/shard_map/all_gather | solution.py:117
  7.3 4.0 copy-start.8
  14.8 5.4 copy-start.15
  14.8 5.4 copy-start.16
  14.8 5.8 copy-start.20
  14.8 5.8 copy-start.21
  14.8 5.8 copy-start.22
  14.8 11.8 %copy-start.19 = (s32[1,512]{1,0:T(1,128)S(1)}, s32[1,512]{1,0:T(1,128)}, u32[]{:S(2)}) copy-start(s32[1,512]{1,0:T(1,128)} %param.20) | copy-start | bytes 6148
  14.8 13.8 %copy-start.17 = (bf16[2,1536]{1,0:T(2,128)(2,1)S(1)}, bf16[2,1536]{1,0:T(2,128)(2,1)}, u32[]{:S(2)}) copy-start(bf16[2,1536]{1,0:T(2,128)(2,1)} %param.24) | copy-start | bytes 18436
  14.8 58.7 %copy-start.14 = (bf16[2,2048]{1,0:T(2,128)(2,1)S(1)}, bf16[2,2048]{1,0:T(2,128)(2,1)}, u32[]{:S(2)}) copy-start(bf16[2,2048]{1,0:T(2,128)(2,1)} %param.25) | copy-start | bytes 24580
  14.8 76.3 %all-to-all-start = ((bf16[2,64,8,1792]{3,1,0,2:T(8,128)(2,1)}), bf16[2,64,8,1792]{3,1,0,2:T(8,128)(2,1)}, u32[]{:S(2)}, u32[]{:S(2)}) async-start(bf16[2,64,8,1792]{3,1,0,2:T(8,128)(2,1)} %copy.63), calls=%async_computation | async-start | bytes 7340032 | tf_op jit(solution)/shard_map/all_to_all | solution.py:96
  20.2 80.7 %all-gather.6.cloned.1.call-start = ((), (), s32[]{:S(2)}) async-start(), calls=%async_computation.4 | async-start | bytes 6291456 | tf_op jit(solution)/shard_map/all_gather | solution.py:118
  72.2 336.0 %all-reduce.3.cloned.1.call-start = ((), (), s32[]{:S(2)}) async-start(), calls=%async_computation.5 | async-start | bytes 8388608 | tf_op jit(solution)/shard_map/psum | solution.py:160
  95.2 122.7 %copy-start.11 = (bf16[1,8,64,1,1792]{4,2,1,3,0:T(8,128)(2,1)}, bf16[1,8,64,1,1792]{4,2,1,3,0:T(8,128)(2,1)S(1)}, u32[]{:S(2)}) copy-start(bf16[1,8,64,1,1792]{4,2,1,3,0:T(8,128)(2,1)S(1)} %get-tuple-element.21) | copy-start | bytes 5505028
  95.2 44.9 %collective-permute-start = (bf16[512,1792]{1,0:T(8,128)(2,1)S(1)}, bf16[512,1792]{1,0:T(8,128)(2,1)}, u32[]{:S(2)}, u32[]{:S(2)}) collective-permute-start(bf16[512,1792]{1,0:T(8,128)(2,1)S(1)} %bitcast.162), channel_id=1, source_target_pairs={{0,8},{8,16},{16,24},{24,0},{1,9},{9,17},{17,25},{25,1},{2,10},{10... | collective-permute-start | bytes 5505032 | tf_op jit(solution)/shard_map/ppermute | solution.py:106
  96.8 121.1 %collective-permute-start.1 = (bf16[512,1792]{1,0:T(8,128)(2,1)S(1)}, bf16[512,1792]{1,0:T(8,128)(2,1)}, u32[]{:S(2)}, u32[]{:S(2)}) collective-permute-start(bf16[512,1792]{1,0:T(8,128)(2,1)S(1)} %bitcast.163), channel_id=1, source_target_pairs={{0,16},{8,24},{16,0},{24,8},{1,17},{9,25},{17,1},{25,9},{2,18},{10... | collective-permute-start | bytes 5505032 | tf_op jit(solution)/shard_map/ppermute | solution.py:106
  99.3 118.7 %collective-permute-start.2 = (bf16[512,1792]{1,0:T(8,128)(2,1)S(1)}, bf16[512,1792]{1,0:T(8,128)(2,1)}, u32[]{:S(2)}, u32[]{:S(2)}) collective-permute-start(bf16[512,1792]{1,0:T(8,128)(2,1)S(1)} %bitcast.164), channel_id=1, source_target_pairs={{0,24},{8,0},{16,8},{24,16},{1,25},{9,1},{17,9},{25,17},{2,26},{10... | collective-permute-start | bytes 5505032 | tf_op jit(solution)/shard_map/ppermute | solution.py:106
  112.0 3.6 copy-start.2
  132.4 85.6 %copy-start.5 = (f32[256,8,2,512]{3,1,2,0:T(8,128)}, f32[256,8,2,512]{3,1,2,0:T(8,128)S(1)}, u32[]{:S(2)}) copy-start(f32[256,8,2,512]{3,1,2,0:T(8,128)S(1)} %copy.90) | copy-start | bytes 25165828
  241.7 4.3 copy-start.13
  246.0 2.4 copy-start.12
  267.0 6.5 %copy-start.7 = (bf16[1,512,2048]{2,1,0:T(8,128)(2,1)S(1)}, bf16[1,512,2048]{2,1,0:T(8,128)(2,1)}, u32[]{:S(2)}) copy-start(bf16[1,512,2048]{2,1,0:T(8,128)(2,1)} %get-tuple-element.20) | copy-start | bytes 6291460
  283.1 0.7 copy-start.18
  283.1 15.5 %copy-start.9 = (bf16[1,8,64,1,1792]{4,2,1,3,0:T(8,128)(2,1)S(1)}, bf16[1,8,64,1,1792]{4,2,1,3,0:T(8,128)(2,1)}, u32[]{:S(2)}) copy-start(bf16[1,8,64,1,1792]{4,2,1,3,0:T(8,128)(2,1)} %get-tuple-element.22) | copy-start | bytes 5505028
  283.1 286.6 %reduce-scatter.3.cloned.1.call-start = ((), (), s32[]{:S(2)}) async-start(), calls=%async_computation.6 | async-start | bytes 6291456 | tf_op jit(solution)/shard_map/reduce_scatter | solution.py:163
  298.6 140.4 %collective-permute-start.3 = (bf16[512,1792]{1,0:T(8,128)(2,1)S(1)}, bf16[512,1792]{1,0:T(8,128)(2,1)}, u32[]{:S(2)}, u32[]{:S(2)}) collective-permute-start(bf16[512,1792]{1,0:T(8,128)(2,1)S(1)} %bitcast.157), channel_id=1, source_target_pairs={{0,8},{8,16},{16,24},{24,0},{1,9},{9,17},{17,25},{25,1},{2,10},{10... | collective-permute-start | bytes 5505032 | tf_op jit(solution)/shard_map/ppermute | solution.py:106
  338.6 117.0 %collective-permute-start.4 = (bf16[512,1792]{1,0:T(8,128)(2,1)S(1)}, bf16[512,1792]{1,0:T(8,128)(2,1)}, u32[]{:S(2)}, u32[]{:S(2)}) collective-permute-start(bf16[512,1792]{1,0:T(8,128)(2,1)S(1)} %bitcast.158), channel_id=1, source_target_pairs={{0,16},{8,24},{16,0},{24,8},{1,17},{9,25},{17,1},{25,9},{2,18},{10... | collective-permute-start | bytes 5505032 | tf_op jit(solution)/shard_map/ppermute | solution.py:106
  340.0 115.7 %collective-permute-start.5 = (bf16[512,1792]{1,0:T(8,128)(2,1)S(1)}, bf16[512,1792]{1,0:T(8,128)(2,1)}, u32[]{:S(2)}, u32[]{:S(2)}) collective-permute-start(bf16[512,1792]{1,0:T(8,128)(2,1)S(1)} %bitcast.159), channel_id=1, source_target_pairs={{0,24},{8,0},{16,8},{24,16},{1,25},{9,1},{17,9},{25,17},{2,26},{10... | collective-permute-start | bytes 5505032 | tf_op jit(solution)/shard_map/ppermute | solution.py:106
  418.7 3.6 copy-start.3
  439.0 16.6 %copy-start.4 = (f32[256,8,2,512]{3,1,2,0:T(8,128)}, f32[256,8,2,512]{3,1,2,0:T(8,128)S(1)}, u32[]{:S(2)}) copy-start(f32[256,8,2,512]{3,1,2,0:T(8,128)S(1)} %copy.96) | copy-start | bytes 25165828
  482.4 2.4 copy-start.10
  503.3 6.5 %copy-start.6 = (bf16[1,512,2048]{2,1,0:T(8,128)(2,1)S(1)}, bf16[1,512,2048]{2,1,0:T(8,128)(2,1)}, u32[]{:S(2)}) copy-start(bf16[1,512,2048]{2,1,0:T(8,128)(2,1)} %get-tuple-element.19) | copy-start | bytes 6291460
  519.3 92.2 %copy-start.1 = (s32[32]{0:T(128)S(1)}, s32[32]{0:T(128)}, u32[]{:S(2)}) copy-start(s32[32]{0:T(128)} %param.21) | copy-start | bytes 388
  519.4 89.7 %reduce-scatter.5.cloned.1.call-start = ((), (), s32[]{:S(2)}) async-start(), calls=%async_computation.7 | async-start | bytes 2621440 | tf_op jit(solution)/shard_map/reduce_scatter | solution.py:164
Sparse Core Ops, SparseCore 0:
  9.2 62.9 all-gather.3
  73.7 20.2 all-gather.5
  283.3 124.8 all-reduce.2
  519.5 50.1 reduce-scatter.2
  572.5 36.4 reduce-scatter.4

commit v3 on v2

--- a/solution.py
+++ b/solution.py
@@ -106,21 +106,47 @@
             pieces.append(lax.ppermute(piece, "zz", perm=[(i, (i + k) % n_zz) for i in range(n_zz)]))
         return jnp.concatenate(pieces, axis=0)
 
-    segs = lax.all_gather(segment_ids, "core", axis=0, tiled=True)
-    rows = segs.shape[0]
+    n_plane = n_core * n_tp
+    me_plane = core * n_tp + lax.axis_index("tp")
+    shifts = range(1, n_plane)
+
+    def plane_perm(piece, k):
+        return lax.ppermute(piece, ("core", "tp"), perm=[(i, (i + k) % n_plane) for i in range(n_plane)])
+
+    def gather_plane(piece):
+        width = piece.shape[2]
+        whole = jnp.zeros((n_core, length, n_tp * width), piece.dtype)
+        whole = lax.dynamic_update_slice(whole, piece, (core, 0, lax.axis_index("tp") * width))
+        for k in shifts:
+            src = (me_plane + n_plane - k) % n_plane
+            got = plane_perm(piece, k)
+            whole = lax.dynamic_update_slice(whole, got, (src // n_tp, 0, src % n_tp * width))
+        return whole
+
+    def scatter_plane(terms):
+        width = terms.shape[2] // n_tp
+        def block_of(dest):
+            return lax.dynamic_slice(terms, (dest // n_tp, 0, dest % n_tp * width), (1, length, width))
+        total = block_of(me_plane).astype(jnp.float32)
+        for k in shifts:
+            dest = (me_plane + k) % n_plane
+            total = total + plane_perm(block_of(dest), k).astype(jnp.float32)
+        return total
+
+    segs = gather_plane(segment_ids[:, :, None])[:, :, 0::1].reshape(n_core, length * n_tp)
+    segs = segs.reshape(n_core, length, n_tp)[:, :, 0]
+    rows = n_core
     pos = positions(segs)
     index = jnp.arange(length, dtype=jnp.int32)
     mask = (index[None, :] <= index[:, None])[None] & (segs[:, :, None] == segs[:, None, :])
     mask = mask[:, None]
-    bias_full = lax.all_gather(out_bias, "tp", axis=1, tiled=True)
-
-    stream = lax.all_gather(tokens, "tp", axis=2, tiled=True)
-    stream = lax.all_gather(stream, "core", axis=0, tiled=True)
+
+    local = tokens
     for layer in range(LAYERS):
+        stream = gather_plane(local)
         weights = gather_zz(packed[layer].reshape(n_dest * block, -1))
         w_qkv = weights[:, :qkv_cols]
         w_up = weights[:, qkv_cols:]
-        flt = stream.astype(jnp.float32)
         permuted = jnp.take(stream.reshape(rows, length, n_blocks, block), feature_block, axis=2)
         permuted = permuted.reshape(rows * length, full_width).astype(jnp.float32)
 
@@ -156,16 +182,9 @@
         m_rows = lax.dynamic_slice_in_dim(down_w[layer], core * ff_here, ff_here)
         partial_terms = attn_out + jnp.dot(hidden_units, m_rows, preferred_element_type=jnp.float32)
         partial_terms = partial_terms.astype(jnp.bfloat16).reshape(rows, length, full_width)
-        if layer + 1 < LAYERS:
-            summed = lax.psum(partial_terms, ("core", "tp")).astype(jnp.float32)
-            stream = (flt + summed + bias_full[layer]).astype(jnp.bfloat16)
-        else:
-            summed = lax.psum_scatter(partial_terms, "core", scatter_dimension=0, tiled=True)
-            summed = lax.psum_scatter(summed, "tp", scatter_dimension=2, tiled=True).astype(jnp.float32)
-            width_here = full_width // n_tp
-            own_stream = lax.dynamic_slice_in_dim(flt, core, 1, axis=0)
-            own_stream = lax.dynamic_slice_in_dim(own_stream, lax.axis_index("tp") * width_here, width_here, axis=2)
-            stream = (own_stream + summed + out_bias[layer]).astype(jnp.bfloat16)
+        summed = scatter_plane(partial_terms)
+        local = (local.astype(jnp.float32) + summed + out_bias[layer]).astype(jnp.bfloat16)
+    stream = local
     return stream
 
 

time: 624 us -> 703 us (1.13)
  the two profiles are of different devices: /device:TPU:0 before, /device:TPU:15 now
where the time goes in v3:
time: 703 us; the launch traced here: 695 us
  waiting for transfers between devices  385 us (55%)
  local copies, waits for them, and re-layouts  141 us (20%)
  matrix products  79.5 us (11%)
  starting transfers between devices  60.2 us (9%)
  other arithmetic  28 us (4%)
    ppermute x6, waiting for transfers between devices, gather_zz(): lax.ppermute(piece, 'zz', perm=[(i, (i + k) % n_zz) for i in range(n_zz)])  252 us
    ppermute x35, waiting for transfers between devices, plane_perm(): lax.ppermute(piece, ('core', 'tp'), perm=[(i, (i + k) % n_plane) for i in...  133 us
    ppermute x35, starting transfers between devices, plane_perm(): lax.ppermute(piece, ('core', 'tp'), perm=[(i, (i + k) % n_plane) for i in...  50.5 us
    dot_general x2, matrix products, shards(): jnp.dot(mlp_in, w_up, preferred_element_type=jnp.float32)  36.8 us
    unnamed x103, local copies, waits for them, and re-layouts  29.4 us
    convert_element_type x2, local copies, waits for them, and re-layouts, shards(): permuted = permuted.reshape(rows * length, full_width).astype(jnp.float32)  24.7 us
    dynamic_update_slice x21, local copies, waits for them, and re-layouts, gather_plane(): lax.dynamic_update_slice(whole, got, (src // n_tp, 0, src % n_tp * width))  15.7 us
    dot_general x2, matrix products, shards(): jnp.dot(attn_in, w_qkv, preferred_element_type=jnp.float32)  14.3 us
  transfers between devices with their start and end apart: 42, of which 20 were waited for; matrix products, arithmetic and copies ran while one was open for 17% of the time, Pallas kernels for 0%

profile of v3, /device:TPU:15, one launch (start us, length us, event | category | flops | bytes accessed | tf_op | source)
XLA Modules:
  0.0 694.6 jit_solution(3019054406566338283)
XLA Ops:
  4.7 2.4 convert_element_type.191
  9.3 2.5 copy.114
  11.9 5.5 all-to-all-start
  24.5 4.8 fusion.197
  29.9 2.3 broadcast.283.clone
  33.2 11.9 %fusion.196 = (bf16[1,2048,2048]{2,1,0:T(8,128)(2,1)}, bf16[1,2048,2048]{2,1,0:T(8,128)(2,1)}) fusion(bf16[2,2048,2048]{2,1,0:T(8,128)(2,1)} %param.27), kind=kLoop, calls=%fused_computation.315 | loop fusion | bytes 33554432 | tf_op jit(solution)/shard_map/slice | solution.py:182
  46.9 2.2 collective-permute-start
  51.1 7.3 %collective-permute-done.15 = s32[1,512,1]{1,0,2:T(1,128)S(1)} collective-permute-done((s32[1,512,1]{1,0,2:T(1,128)S(1)}, s32[1,512,1]{1,0,2:T(1,128)S(1)}, u32[]{:S(2)}, u32[]{:S(2)}) %collective-permute-start.15) | collective-permute-done | bytes 2080 | tf_op jit(solution)/shard_map/ppermute | solution.py:114
  61.4 8.0 %collective-permute-done = bf16[1,512,512]{1,2,0:T(8,128)(2,1)S(1)} collective-permute-done((bf16[1,512,512]{1,2,0:T(8,128)(2,1)S(1)}, bf16[1,512,512]{1,2,0:T(8,128)(2,1)S(1)}, u32[]{:S(2)}, u32[]{:S(2)}) %collective-permute-start) | collective-permute-done | bytes 524320 | tf_op jit(solution)/shard_map/ppermute | solution.py:114
  70.6 11.8 %collective-permute-start.6 = (bf16[1,512,512]{1,2,0:T(8,128)(2,1)S(1)}, bf16[1,512,512]{1,2,0:T(8,128)(2,1)S(1)}, u32[]{:S(2)}, u32[]{:S(2)}) collective-permute-start(bf16[1,512,512]{1,2,0:T(8,128)(2,1)S(1)} %copy.104), channel_id=1, source_target_pairs={{0,7},{1,0},{2,1},{3,2},{4,3},{5,4},{6,5},{7,6},{8,15},{9,8},{10,9... | collective-permute-start | bytes 1572872 | tf_op jit(solution)/shard_map/ppermute | solution.py:114
  84.9 8.0 %collective-permute-done.4 = bf16[1,512,512]{1,2,0:T(8,128)(2,1)S(1)} collective-permute-done((bf16[1,512,512]{1,2,0:T(8,128)(2,1)S(1)}, bf16[1,512,512]{1,2,0:T(8,128)(2,1)S(1)}, u32[]{:S(2)}, u32[]{:S(2)}) %collective-permute-start.4) | collective-permute-done | bytes 524320 | tf_op jit(solution)/shard_map/ppermute | solution.py:114
  94.5 8.6 %collective-permute-done.6 = bf16[1,512,512]{1,2,0:T(8,128)(2,1)S(1)} collective-permute-done((bf16[1,512,512]{1,2,0:T(8,128)(2,1)S(1)}, bf16[1,512,512]{1,2,0:T(8,128)(2,1)S(1)}, u32[]{:S(2)}, u32[]{:S(2)}) %collective-permute-start.6) | collective-permute-done | bytes 524320 | tf_op jit(solution)/shard_map/ppermute | solution.py:114
  104.0 5.0 gather_fusion.1
  109.0 2.3 copy.189
  120.4 12.4 %copy.113 = f32[2,512,32,64]{1,0,3,2:T(2,128)S(1)} copy(f32[2,512,32,64]{1,3,0,2:T(8,128)S(1)} %bitcast_convert_fusion.1) | data formatting | bytes 16777216 | tf_op jit(solution)/shard_map/convert_element_type | solution.py:151
  132.7 2.1 copy.170
  134.9 19.2 %collective-permute-done.7 = bf16[512,1792]{1,0:T(8,128)(2,1)S(1)} collective-permute-done((bf16[512,1792]{1,0:T(8,128)(2,1)S(1)}, bf16[512,1792]{1,0:T(8,128)(2,1)S(1)}, u32[]{:S(2)}, u32[]{:S(2)}) %collective-permute-start.7) | collective-permute-done | bytes 1835040 | tf_op jit(solution)/shard_map/ppermute | solution.py:106
  154.0 117.1 %collective-permute-done.8 = bf16[512,1792]{1,0:T(8,128)(2,1)} collective-permute-done((bf16[512,1792]{1,0:T(8,128)(2,1)S(1)}, bf16[512,1792]{1,0:T(8,128)(2,1)}, u32[]{:S(2)}, u32[]{:S(2)}) %collective-permute-start.8) | collective-permute-done | bytes 1835040 | tf_op jit(solution)/shard_map/ppermute | solution.py:106
  271.1 2.6 collective-permute-done.9
  273.8 7.0 %fusion.69 = f32[1024,768]{1,0:T(8,128)} fusion(bf16[512,1792]{1,0:T(8,128)(2,1)} %collective-permute-done.9, bf16[512,1792]{1,0:T(8,128)(2,1)} %collective-permute-done.8, bf16[512,1792]{1,0:T(8,128)(2,1)S(1)} %collective-permute-done.7, bf16[512,1792]{1,0:T(8,128)(2,1)S(1)} %bitcast.162, f32[1024,2048]{0,1:T(8,128)S(1)} %bitcast.140, ...), kind=kOutput, calls=%fused_computation.125 | convolution fusion | flops 3245080576 | bytes 18902016 | tf_op jit(solution)/shard_map/dot_general | solution.py:163
  280.8 2.4 copy.116
  283.2 3.8 reshape.331
  287.0 2.3 fusion.200
  289.2 2.4 slice.219
  293.3 3.7 fusion.143
  297.0 4.3 fusion.204
  301.3 2.2 fusion.72
  303.7 18.4 %fusion.4 = bf16[1024,1024]{1,0:T(8,128)(2,1)S(1)} fusion(bf16[512,1792]{1,0:T(8,128)(2,1)} %collective-permute-done.9, bf16[512,1792]{1,0:T(8,128)(2,1)} %collective-permute-done.8, bf16[512,1792]{1,0:T(8,128)(2,1)} %copy-done.36, bf16[512,1792]{1,0:T(8,128)(2,1)S(1)} %bitcast.163, f32[1024,2048]{0,1:T(8,128)} %bitcast.141, f32[2048]{0:T(1024)S(1)} %add.613, ...), kind=kOutput, calls=%fused_computation.27 | convolution fusion | flops 4391436288 | bytes 17854464 | tf_op jit(solution)/shard_map/dot_general | solution.py:180
  322.1 6.5 fusion.17
  331.5 2.1 copy.151
  333.6 3.6 collective-permute-start.17
  337.2 2.1 copy.152
  343.0 2.3 collective-permute-start.21
  349.3 15.1 %collective-permute-done.18 = bf16[1,512,512]{1,2,0:T(8,128)(2,1)} collective-permute-done((bf16[1,512,512]{1,2,0:T(8,128)(2,1)}, bf16[1,512,512]{1,2,0:T(8,128)(2,1)}, u32[]{:S(2)}, u32[]{:S(2)}) %collective-permute-start.18) | collective-permute-done | bytes 524320 | tf_op jit(solution)/shard_map/ppermute | solution.py:114
  364.6 7.2 %collective-permute-done.21 = bf16[1,512,512]{1,2,0:T(8,128)(2,1)S(1)} collective-permute-done((bf16[1,512,512]{1,2,0:T(8,128)(2,1)}, bf16[1,512,512]{1,2,0:T(8,128)(2,1)S(1)}, u32[]{:S(2)}, u32[]{:S(2)}) %collective-permute-start.21) | collective-permute-done | bytes 524320 | tf_op jit(solution)/shard_map/ppermute | solution.py:114
  371.9 15.0 %collective-permute-done.22 = bf16[1,512,512]{1,2,0:T(8,128)(2,1)S(1)} collective-permute-done((bf16[1,512,512]{1,2,0:T(8,128)(2,1)}, bf16[1,512,512]{1,2,0:T(8,128)(2,1)S(1)}, u32[]{:S(2)}, u32[]{:S(2)}) %collective-permute-start.22) | collective-permute-done | bytes 524320 | tf_op jit(solution)/shard_map/ppermute | solution.py:114
  387.7 2.3 broadcast.283
  389.9 3.6 constant_dynamic-update-slice_fusion.7
  398.0 8.9 %collective-permute-done.24 = bf16[1,512,512]{1,2,0:T(8,128)(2,1)} collective-permute-done((bf16[1,512,512]{1,2,0:T(8,128)(2,1)S(1)}, bf16[1,512,512]{1,2,0:T(8,128)(2,1)}, u32[]{:S(2)}, u32[]{:S(2)}) %collective-permute-start.24) | collective-permute-done | bytes 524320 | tf_op jit(solution)/shard_map/ppermute | solution.py:114
  409.3 10.2 %collective-permute-start.30 = (bf16[1,512,512]{1,2,0:T(8,128)(2,1)S(1)}, bf16[1,512,512]{1,2,0:T(8,128)(2,1)S(1)}, u32[]{:S(2)}, u32[]{:S(2)}) collective-permute-start(bf16[1,512,512]{1,2,0:T(8,128)(2,1)S(1)} %get-tuple-element.16), channel_id=1, source_target_pairs={{0,7},{1,0},{2,1},{3,2},{4,3},{5,4},{6,5},{7,6},{8,15},{9,8},{10,9... | collective-permute-start | bytes 1572872 | tf_op jit(solution)/shard_map/ppermute | solution.py:114
  424.3 6.5 collective-permute-done.28
  432.4 8.9 %collective-permute-done.30 = bf16[1,512,512]{1,2,0:T(8,128)(2,1)S(1)} collective-permute-done((bf16[1,512,512]{1,2,0:T(8,128)(2,1)S(1)}, bf16[1,512,512]{1,2,0:T(8,128)(2,1)S(1)}, u32[]{:S(2)}, u32[]{:S(2)}) %collective-permute-start.30) | collective-permute-done | bytes 524320 | tf_op jit(solution)/shard_map/ppermute | solution.py:114
  442.2 4.9 gather_fusion.6
  447.1 3.6 fusion.16
  452.9 12.4 %copy.130 = f32[2,512,32,64]{1,0,3,2:T(2,128)S(1)} copy(f32[2,512,32,64]{1,3,0,2:T(8,128)S(1)} %bitcast_convert_fusion) | data formatting | bytes 16777216 | tf_op jit(solution)/shard_map/convert_element_type | solution.py:151
  465.3 2.1 copy.176
  467.4 110.5 %collective-permute-done.32 = bf16[512,1792]{1,0:T(8,128)(2,1)} collective-permute-done((bf16[512,1792]{1,0:T(8,128)(2,1)S(1)}, bf16[512,1792]{1,0:T(8,128)(2,1)}, u32[]{:S(2)}, u32[]{:S(2)}) %collective-permute-start.32) | collective-permute-done | bytes 1835040 | tf_op jit(solution)/shard_map/ppermute | solution.py:106
  577.9 2.2 collective-permute-done.33
  580.2 7.3 %fusion.66 = f32[1024,768]{1,0:T(8,128)} fusion(bf16[512,1792]{1,0:T(8,128)(2,1)} %collective-permute-done.33, bf16[512,1792]{1,0:T(8,128)(2,1)} %collective-permute-done.32, bf16[512,1792]{1,0:T(8,128)(2,1)} %collective-permute-done.31, bf16[512,1792]{1,0:T(8,128)(2,1)S(1)} %bitcast.157, f32[1024,2048]{0,1:T(8,128)S(1)} %bitcast.138, f32[2048]{0:T(1024)S(1)} %add.637, ...), kind=kOutput, calls=%fused_computation.124 | convolution fusion | flops 3245080576 | bytes 18902016 | tf_op jit(solution)/shard_map/dot_general | solution.py:163
  587.4 2.4 copy.131
  589.8 3.8 reshape.337
  593.6 2.3 fusion.199
  597.4 3.3 fusion.139
  602.5 4.0 fusion.209
  606.5 2.2 fusion.73
  608.9 18.4 %fusion.7 = bf16[1024,1024]{1,0:T(8,128)(2,1)S(1)} fusion(bf16[512,1792]{1,0:T(8,128)(2,1)} %collective-permute-done.33, bf16[512,1792]{1,0:T(8,128)(2,1)} %collective-permute-done.32, bf16[512,1792]{1,0:T(8,128)(2,1)} %collective-permute-done.31, bf16[512,1792]{1,0:T(8,128)(2,1)S(1)} %bitcast.158, f32[1024,2048]{0,1:T(8,128)} %bitcast.139, ...), kind=kOutput, calls=%fused_computation.30 | convolution fusion | flops 4391436288 | bytes 17854464 | tf_op jit(solution)/shard_map/dot_general | solution.py:180
  627.4 6.5 fusion.14
  636.7 2.1 copy.161
  638.8 2.7 collective-permute-start.34
  641.5 2.1 copy.162
  654.4 14.3 %collective-permute-done.35 = bf16[1,512,512]{1,2,0:T(8,128)(2,1)} collective-permute-done((bf16[1,512,512]{1,2,0:T(8,128)(2,1)}, bf16[1,512,512]{1,2,0:T(8,128)(2,1)}, u32[]{:S(2)}, u32[]{:S(2)}) %collective-permute-start.35) | collective-permute-done | bytes 524320 | tf_op jit(solution)/shard_map/ppermute | solution.py:114
  668.9 7.5 %collective-permute-done.38 = bf16[1,512,512]{1,2,0:T(8,128)(2,1)S(1)} collective-permute-done((bf16[1,512,512]{1,2,0:T(8,128)(2,1)}, bf16[1,512,512]{1,2,0:T(8,128)(2,1)S(1)}, u32[]{:S(2)}, u32[]{:S(2)}) %collective-permute-start.38) | collective-permute-done | bytes 524320 | tf_op jit(solution)/shard_map/ppermute | solution.py:114
  676.4 14.7 %collective-permute-done.39 = bf16[1,512,512]{1,2,0:T(8,128)(2,1)S(1)} collective-permute-done((bf16[1,512,512]{1,2,0:T(8,128)(2,1)}, bf16[1,512,512]{1,2,0:T(8,128)(2,1)S(1)}, u32[]{:S(2)}, u32[]{:S(2)}) %collective-permute-start.39) | collective-permute-done | bytes 524320 | tf_op jit(solution)/shard_map/ppermute | solution.py:114
  691.2 2.2 add_convert_fusion.18
  (253 shorter events, 85.7 us)
Async XLA Ops:
  0.0 18.4 %copy-start = (s32[32]{0:T(128)S(1)}, s32[32]{0:T(128)}, u32[]{:S(2)}) copy-start(s32[32]{0:T(128)} %param.21) | copy-start | bytes 388
  0.0 8.5 %copy-start.10 = (f32[2,64,6144]{2,1,0:T(8,128)S(1)}, f32[2,64,6144]{2,1,0:T(8,128)}, u32[]{:S(2)}) copy-start(f32[2,64,6144]{2,1,0:T(8,128)} %param.22) | copy-start | bytes 9437188
  0.0 45.4 %collective-permute-start.10 = (s32[1,512,1]{1,0,2:T(1,128)}, s32[1,512,1]{1,0,2:T(1,128)S(1)}, u32[]{:S(2)}, u32[]{:S(2)}) collective-permute-start(s32[1,512,1]{1,0,2:T(1,128)} %bitcast.177), channel_id=1, source_target_pairs={{0,1},{1,2},{2,3},{3,4},{4,5},{5,6},{6,7},{7,0},{8,9},{9,10},{10,1... | collective-permute-start | bytes 6152 | tf_op jit(solution)/shard_map/ppermute | solution.py:114
  0.8 44.9 %collective-permute-start.11 = (s32[1,512,1]{1,0,2:T(1,128)}, s32[1,512,1]{1,0,2:T(1,128)S(1)}, u32[]{:S(2)}, u32[]{:S(2)}) collective-permute-start(s32[1,512,1]{1,0,2:T(1,128)} %bitcast.178), channel_id=1, source_target_pairs={{0,2},{1,3},{2,4},{3,5},{4,6},{5,7},{6,0},{7,1},{8,10},{9,11},{10,... | collective-permute-start | bytes 6152 | tf_op jit(solution)/shard_map/ppermute | solution.py:114
  2.3 44.6 %collective-permute-start.12 = (s32[1,512,1]{1,0,2:T(1,128)}, s32[1,512,1]{1,0,2:T(1,128)S(1)}, u32[]{:S(2)}, u32[]{:S(2)}) collective-permute-start(s32[1,512,1]{1,0,2:T(1,128)} %bitcast.179), channel_id=1, source_target_pairs={{0,3},{1,4},{2,5},{3,6},{4,7},{5,0},{6,1},{7,2},{8,11},{9,12},{10,... | collective-permute-start | bytes 6152 | tf_op jit(solution)/shard_map/ppermute | solution.py:114
  2.3 46.8 %collective-permute-start.13 = (s32[1,512,1]{1,0,2:T(1,128)}, s32[1,512,1]{1,0,2:T(1,128)S(1)}, u32[]{:S(2)}, u32[]{:S(2)}) collective-permute-start(s32[1,512,1]{1,0,2:T(1,128)} %bitcast.180), channel_id=1, source_target_pairs={{0,4},{1,5},{2,6},{3,7},{4,0},{5,1},{6,2},{7,3},{8,12},{9,13},{10,... | collective-permute-start | bytes 6152 | tf_op jit(solution)/shard_map/ppermute | solution.py:114
  2.9 48.1 %collective-permute-start.14 = (s32[1,512,1]{1,0,2:T(1,128)}, s32[1,512,1]{1,0,2:T(1,128)S(1)}, u32[]{:S(2)}, u32[]{:S(2)}) collective-permute-start(s32[1,512,1]{1,0,2:T(1,128)} %bitcast.181), channel_id=1, source_target_pairs={{0,5},{1,6},{2,7},{3,0},{4,1},{5,2},{6,3},{7,4},{8,13},{9,14},{10,... | collective-permute-start | bytes 6152 | tf_op jit(solution)/shard_map/ppermute | solution.py:114
  11.9 7.2 %copy-start.25 = (f32[2,2,2048]{2,1,0:T(2,128)S(1)}, f32[2,2,2048]{2,1,0:T(2,128)}, u32[]{:S(2)}) copy-start(f32[2,2,2048]{2,1,0:T(2,128)} %param.30) | copy-start | bytes 98308
  11.9 7.2 %copy-start.26 = (f32[2,2,2048]{2,1,0:T(2,128)S(1)}, f32[2,2,2048]{2,1,0:T(2,128)}, u32[]{:S(2)}) copy-start(f32[2,2,2048]{2,1,0:T(2,128)} %param.29) | copy-start | bytes 98308
  11.9 12.5 %copy-start.27 = (bf16[2,1536]{1,0:T(2,128)(2,1)S(1)}, bf16[2,1536]{1,0:T(2,128)(2,1)}, u32[]{:S(2)}) copy-start(bf16[2,1536]{1,0:T(2,128)(2,1)} %param.24) | copy-start | bytes 18436
  11.9 12.6 %copy-start.24 = (bf16[2,2048]{1,0:T(2,128)(2,1)S(1)}, bf16[2,2048]{1,0:T(2,128)(2,1)}, u32[]{:S(2)}) copy-start(bf16[2,2048]{1,0:T(2,128)(2,1)} %param.25) | copy-start | bytes 24580
  11.9 97.0 %all-to-all-start = ((bf16[2,64,8,1792]{3,1,0,2:T(8,128)(2,1)}), bf16[2,64,8,1792]{3,1,0,2:T(8,128)(2,1)}, u32[]{:S(2)}, u32[]{:S(2)}) async-start(bf16[2,64,8,1792]{3,1,0,2:T(8,128)(2,1)} %copy.114), calls=%async_computation | async-start | bytes 7340032 | tf_op jit(solution)/shard_map/all_to_all | solution.py:96
  18.1 279.0 %copy-start.22 = (pred[512,512]{0,1:T(8,128)(4,1)}, pred[512,512]{0,1:T(8,128)(4,1)S(1)}, u32[]{:S(2)}) copy-start(pred[512,512]{0,1:T(8,128)(4,1)S(1)} %iota_compare_fusion) | copy-start | bytes 786436
  18.3 52.3 %copy-start.6 = (bf16[1,512,512]{1,2,0:T(8,128)(2,1)}, bf16[1,512,512]{1,2,0:T(8,128)(2,1)S(1)}, u32[]{:S(2)}) copy-start(bf16[1,512,512]{1,2,0:T(8,128)(2,1)S(1)} %copy.104) | copy-start | bytes 1572868
  33.2 12.2 %copy-start.31 = (s32[1,512]{1,0:T(1,128)S(1)}, s32[1,512]{1,0:T(1,128)}, u32[]{:S(2)}) copy-start(s32[1,512]{1,0:T(1,128)} %param.20) | copy-start | bytes 6148
  45.4 13.1 %collective-permute-start.15 = (s32[1,512,1]{1,0,2:T(1,128)S(1)}, s32[1,512,1]{1,0,2:T(1,128)S(1)}, u32[]{:S(2)}, u32[]{:S(2)}) collective-permute-start(s32[1,512,1]{1,0,2:T(1,128)S(1)} %bitcast.183), channel_id=1, source_target_pairs={{0,6},{1,7},{2,0},{3,1},{4,2},{5,3},{6,4},{7,5},{8,14},{9,15},{10,... | collective-permute-start | bytes 6152 | tf_op jit(solution)/shard_map/ppermute | solution.py:114
  45.7 13.0 %collective-permute-start.16 = (s32[1,512,1]{1,0,2:T(1,128)S(1)}, s32[1,512,1]{1,0,2:T(1,128)}, u32[]{:S(2)}, u32[]{:S(2)}) collective-permute-start(s32[1,512,1]{1,0,2:T(1,128)S(1)} %bitcast.184), channel_id=1, source_target_pairs={{0,7},{1,0},{2,1},{3,2},{4,3},{5,4},{6,5},{7,6},{8,15},{9,8},{10,9... | collective-permute-start | bytes 6152 | tf_op jit(solution)/shard_map/ppermute | solution.py:114
  46.9 22.5 %collective-permute-start = (bf16[1,512,512]{1,2,0:T(8,128)(2,1)S(1)}, bf16[1,512,512]{1,2,0:T(8,128)(2,1)S(1)}, u32[]{:S(2)}, u32[]{:S(2)}) collective-permute-start(bf16[1,512,512]{1,2,0:T(8,128)(2,1)S(1)} %copy.104), channel_id=1, source_target_pairs={{0,1},{1,2},{2,3},{3,4},{4,5},{5,6},{6,7},{7,0},{8,9},{9,10},{10,1... | collective-permute-start | bytes 1572872 | tf_op jit(solution)/shard_map/ppermute | solution.py:114
  49.1 21.5 %collective-permute-start.1 = (bf16[1,512,512]{1,2,0:T(8,128)(2,1)S(1)}, bf16[1,512,512]{1,2,0:T(8,128)(2,1)S(1)}, u32[]{:S(2)}, u32[]{:S(2)}) collective-permute-start(bf16[1,512,512]{1,2,0:T(8,128)(2,1)S(1)} %copy.104), channel_id=1, source_target_pairs={{0,2},{1,3},{2,4},{3,5},{4,6},{5,7},{6,0},{7,1},{8,10},{9,11},{10,... | collective-permute-start | bytes 1572872 | tf_op jit(solution)/shard_map/ppermute | solution.py:114
  51.0 32.2 %collective-permute-start.2 = (bf16[1,512,512]{1,2,0:T(8,128)(2,1)S(1)}, bf16[1,512,512]{1,2,0:T(8,128)(2,1)S(1)}, u32[]{:S(2)}, u32[]{:S(2)}) collective-permute-start(bf16[1,512,512]{1,2,0:T(8,128)(2,1)S(1)} %copy.104), channel_id=1, source_target_pairs={{0,3},{1,4},{2,5},{3,6},{4,7},{5,0},{6,1},{7,2},{8,11},{9,12},{10,... | collective-permute-start | bytes 1572872 | tf_op jit(solution)/shard_map/ppermute | solution.py:114
  58.5 25.6 %collective-permute-start.3 = (bf16[1,512,512]{1,2,0:T(8,128)(2,1)S(1)}, bf16[1,512,512]{1,2,0:T(8,128)(2,1)S(1)}, u32[]{:S(2)}, u32[]{:S(2)}) collective-permute-start(bf16[1,512,512]{1,2,0:T(8,128)(2,1)S(1)} %copy.104), channel_id=1, source_target_pairs={{0,4},{1,5},{2,6},{3,7},{4,0},{5,1},{6,2},{7,3},{8,12},{9,13},{10,... | collective-permute-start | bytes 1572872 | tf_op jit(solution)/shard_map/ppermute | solution.py:114
  58.7 34.1 %collective-permute-start.4 = (bf16[1,512,512]{1,2,0:T(8,128)(2,1)S(1)}, bf16[1,512,512]{1,2,0:T(8,128)(2,1)S(1)}, u32[]{:S(2)}, u32[]{:S(2)}) collective-permute-start(bf16[1,512,512]{1,2,0:T(8,128)(2,1)S(1)} %copy.104), channel_id=1, source_target_pairs={{0,5},{1,6},{2,7},{3,0},{4,1},{5,2},{6,3},{7,4},{8,13},{9,14},{10,... | collective-permute-start | bytes 1572872 | tf_op jit(solution)/shard_map/ppermute | solution.py:114
  69.4 24.3 %collective-permute-start.5 = (bf16[1,512,512]{1,2,0:T(8,128)(2,1)S(1)}, bf16[1,512,512]{1,2,0:T(8,128)(2,1)S(1)}, u32[]{:S(2)}, u32[]{:S(2)}) collective-permute-start(bf16[1,512,512]{1,2,0:T(8,128)(2,1)S(1)} %copy.104), channel_id=1, source_target_pairs={{0,6},{1,7},{2,0},{3,1},{4,2},{5,3},{6,4},{7,5},{8,14},{9,15},{10,... | collective-permute-start | bytes 1572872 | tf_op jit(solution)/shard_map/ppermute | solution.py:114
  70.6 32.6 %collective-permute-start.6 = (bf16[1,512,512]{1,2,0:T(8,128)(2,1)S(1)}, bf16[1,512,512]{1,2,0:T(8,128)(2,1)S(1)}, u32[]{:S(2)}, u32[]{:S(2)}) collective-permute-start(bf16[1,512,512]{1,2,0:T(8,128)(2,1)S(1)} %copy.104), channel_id=1, source_target_pairs={{0,7},{1,0},{2,1},{3,2},{4,3},{5,4},{6,5},{7,6},{8,15},{9,8},{10,9... | collective-permute-start | bytes 1572872 | tf_op jit(solution)/shard_map/ppermute | solution.py:114
  112.8 160.9 %copy-start.15 = (bf16[1,8,64,1,1792]{4,2,1,3,0:T(8,128)(2,1)}, bf16[1,8,64,1,1792]{4,2,1,3,0:T(8,128)(2,1)S(1)}, u32[]{:S(2)}) copy-start(bf16[1,8,64,1,1792]{4,2,1,3,0:T(8,128)(2,1)S(1)} %get-tuple-element.39) | copy-start | bytes 5505028
  112.8 41.2 %collective-permute-start.7 = (bf16[512,1792]{1,0:T(8,128)(2,1)S(1)}, bf16[512,1792]{1,0:T(8,128)(2,1)S(1)}, u32[]{:S(2)}, u32[]{:S(2)}) collective-permute-start(bf16[512,1792]{1,0:T(8,128)(2,1)S(1)} %bitcast.159), channel_id=1, source_target_pairs={{0,8},{8,16},{16,24},{24,0},{1,9},{9,17},{17,25},{25,1},{2,10},{10... | collective-permute-start | bytes 5505032 | tf_op jit(solution)/shard_map/ppermute | solution.py:106
  114.1 157.0 %collective-permute-start.8 = (bf16[512,1792]{1,0:T(8,128)(2,1)S(1)}, bf16[512,1792]{1,0:T(8,128)(2,1)}, u32[]{:S(2)}, u32[]{:S(2)}) collective-permute-start(bf16[512,1792]{1,0:T(8,128)(2,1)S(1)} %bitcast.160), channel_id=1, source_target_pairs={{0,16},{8,24},{16,0},{24,8},{1,17},{9,25},{17,1},{25,9},{2,18},{10... | collective-permute-start | bytes 5505032 | tf_op jit(solution)/shard_map/ppermute | solution.py:106
  115.2 158.6 %collective-permute-start.9 = (bf16[512,1792]{1,0:T(8,128)(2,1)S(1)}, bf16[512,1792]{1,0:T(8,128)(2,1)}, u32[]{:S(2)}, u32[]{:S(2)}) collective-permute-start(bf16[512,1792]{1,0:T(8,128)(2,1)S(1)} %bitcast.161), channel_id=1, source_target_pairs={{0,24},{8,0},{16,8},{24,16},{1,25},{9,1},{17,9},{25,17},{2,26},{10... | collective-permute-start | bytes 5505032 | tf_op jit(solution)/shard_map/ppermute | solution.py:106
  132.7 141.0 %copy-start.30 = (f32[768]{0:T(1024)S(1)}, f32[768]{0:T(1024)}, u32[]{:S(2)}) copy-start(f32[768]{0:T(1024)} %fusion.162) | copy-start | bytes 9220
  134.8 138.9 %copy-start.5 = (f32[256,8,2,512]{3,1,2,0:T(8,128)}, f32[256,8,2,512]{3,1,2,0:T(8,128)S(1)}, u32[]{:S(2)}) copy-start(f32[256,8,2,512]{3,1,2,0:T(8,128)S(1)} %copy.170) | copy-start | bytes 25165828
  154.0 119.7 %copy-start.36 = (bf16[512,1792]{1,0:T(8,128)(2,1)}, bf16[512,1792]{1,0:T(8,128)(2,1)S(1)}, u32[]{:S(2)}) copy-start(bf16[512,1792]{1,0:T(8,128)(2,1)S(1)} %collective-permute-done.7) | copy-start | bytes 5505028
  331.5 32.9 %copy-start.28 = (f32[2,512]{1,0:T(2,128)S(1)}, f32[2,512]{1,0:T(2,128)}, u32[]{:S(2)}) copy-start(f32[2,512]{1,0:T(2,128)} %param.28) | copy-start | bytes 12292
  333.6 15.5 %collective-permute-start.17 = (bf16[1,512,512]{1,2,0:T(8,128)(2,1)}, bf16[1,512,512]{1,2,0:T(8,128)(2,1)}, u32[]{:S(2)}, u32[]{:S(2)}) collective-permute-start(bf16[1,512,512]{1,2,0:T(8,128)(2,1)} %copy.151), channel_id=1, source_target_pairs={{0,1},{1,2},{2,3},{3,4},{4,5},{5,6},{6,7},{7,0},{8,9},{9,10},{10,1... | collective-permute-start | bytes 1572872 | tf_op jit(solution)/shard_map/ppermute | solution.py:114
  339.3 25.1 %collective-permute-start.18 = (bf16[1,512,512]{1,2,0:T(8,128)(2,1)}, bf16[1,512,512]{1,2,0:T(8,128)(2,1)}, u32[]{:S(2)}, u32[]{:S(2)}) collective-permute-start(bf16[1,512,512]{1,2,0:T(8,128)(2,1)} %copy.152), channel_id=1, source_target_pairs={{0,2},{1,3},{2,4},{3,5},{4,6},{5,7},{6,0},{7,1},{8,10},{9,11},{10,... | collective-permute-start | bytes 1572872 | tf_op jit(solution)/shard_map/ppermute | solution.py:114
  340.9 23.8 %collective-permute-start.19 = (bf16[1,512,512]{1,2,0:T(8,128)(2,1)}, bf16[1,512,512]{1,2,0:T(8,128)(2,1)S(1)}, u32[]{:S(2)}, u32[]{:S(2)}) collective-permute-start(bf16[1,512,512]{1,2,0:T(8,128)(2,1)} %copy.153), channel_id=1, source_target_pairs={{0,3},{1,4},{2,5},{3,6},{4,7},{5,0},{6,1},{7,2},{8,11},{9,12},{10,... | collective-permute-start | bytes 1572872 | tf_op jit(solution)/shard_map/ppermute | solution.py:114
  341.9 22.8 %collective-permute-start.20 = (bf16[1,512,512]{1,2,0:T(8,128)(2,1)}, bf16[1,512,512]{1,2,0:T(8,128)(2,1)}, u32[]{:S(2)}, u32[]{:S(2)}) collective-permute-start(bf16[1,512,512]{1,2,0:T(8,128)(2,1)} %copy.154), channel_id=1, source_target_pairs={{0,4},{1,5},{2,6},{3,7},{4,0},{5,1},{6,2},{7,3},{8,12},{9,13},{10,... | collective-permute-start | bytes 1572872 | tf_op jit(solution)/shard_map/ppermute | solution.py:114
  342.0 47.9 %copy-start.7 = (bf16[1,512,512]{1,2,0:T(8,128)(2,1)S(1)}, bf16[1,512,512]{1,2,0:T(8,128)(2,1)}, u32[]{:S(2)}) copy-start(bf16[1,512,512]{1,2,0:T(8,128)(2,1)} %copy-done.6) | copy-start | bytes 1572868
  343.0 28.9 %collective-permute-start.21 = (bf16[1,512,512]{1,2,0:T(8,128)(2,1)}, bf16[1,512,512]{1,2,0:T(8,128)(2,1)S(1)}, u32[]{:S(2)}, u32[]{:S(2)}) collective-permute-start(bf16[1,512,512]{1,2,0:T(8,128)(2,1)} %copy.155), channel_id=1, source_target_pairs={{0,5},{1,6},{2,7},{3,0},{4,1},{5,2},{6,3},{7,4},{8,13},{9,14},{10,... | collective-permute-start | bytes 1572872 | tf_op jit(solution)/shard_map/ppermute | solution.py:114
  349.1 37.7 %collective-permute-start.22 = (bf16[1,512,512]{1,2,0:T(8,128)(2,1)}, bf16[1,512,512]{1,2,0:T(8,128)(2,1)S(1)}, u32[]{:S(2)}, u32[]{:S(2)}) collective-permute-start(bf16[1,512,512]{1,2,0:T(8,128)(2,1)} %copy.156), channel_id=1, source_target_pairs={{0,6},{1,7},{2,0},{3,1},{4,2},{5,3},{6,4},{7,5},{8,14},{9,15},{10,... | collective-permute-start | bytes 1572872 | tf_op jit(solution)/shard_map/ppermute | solution.py:114
  364.4 22.5 %collective-permute-start.23 = (bf16[1,512,512]{1,2,0:T(8,128)(2,1)}, bf16[1,512,512]{1,2,0:T(8,128)(2,1)}, u32[]{:S(2)}, u32[]{:S(2)}) collective-permute-start(bf16[1,512,512]{1,2,0:T(8,128)(2,1)} %copy.157), channel_id=1, source_target_pairs={{0,7},{1,0},{2,1},{3,2},{4,3},{5,4},{6,5},{7,6},{8,15},{9,8},{10,9... | collective-permute-start | bytes 1572872 | tf_op jit(solution)/shard_map/ppermute | solution.py:114
  364.6 22.2 %copy-start.17 = (bf16[1,512,512]{1,2,0:T(8,128)(2,1)}, bf16[1,512,512]{1,2,0:T(8,128)(2,1)S(1)}, u32[]{:S(2)}) copy-start(bf16[1,512,512]{1,2,0:T(8,128)(2,1)S(1)} %collective-permute-done.19) | copy-start | bytes 1572868
  371.9 15.0 %copy-start.18 = (bf16[1,512,512]{1,2,0:T(8,128)(2,1)}, bf16[1,512,512]{1,2,0:T(8,128)(2,1)S(1)}, u32[]{:S(2)}) copy-start(bf16[1,512,512]{1,2,0:T(8,128)(2,1)S(1)} %collective-permute-done.21) | copy-start | bytes 1572868
  389.9 31.4 %copy-start.13 = (bf16[1,8,64,1,1792]{4,2,1,3,0:T(8,128)(2,1)S(1)}, bf16[1,8,64,1,1792]{4,2,1,3,0:T(8,128)(2,1)}, u32[]{:S(2)}) copy-start(bf16[1,8,64,1,1792]{4,2,1,3,0:T(8,128)(2,1)} %get-tuple-element.40) | copy-start | bytes 5505028
  393.5 53.6 %copy-start.11 = (bf16[1,512,512]{1,2,0:T(8,128)(2,1)}, bf16[1,512,512]{1,2,0:T(8,128)(2,1)S(1)}, u32[]{:S(2)}) copy-start(bf16[1,512,512]{1,2,0:T(8,128)(2,1)S(1)} %get-tuple-element.16) | copy-start | bytes 1572868
  393.5 13.3 %collective-permute-start.24 = (bf16[1,512,512]{1,2,0:T(8,128)(2,1)S(1)}, bf16[1,512,512]{1,2,0:T(8,128)(2,1)}, u32[]{:S(2)}, u32[]{:S(2)}) collective-permute-start(bf16[1,512,512]{1,2,0:T(8,128)(2,1)S(1)} %get-tuple-element.16), channel_id=1, source_target_pairs={{0,1},{1,2},{2,3},{3,4},{4,5},{5,6},{6,7},{7,0},{8,9},{9,10},{10,1... | collective-permute-start | bytes 1572872 | tf_op jit(solution)/shard_map/ppermute | solution.py:114
  393.5 15.8 %collective-permute-start.25 = (bf16[1,512,512]{1,2,0:T(8,128)(2,1)S(1)}, bf16[1,512,512]{1,2,0:T(8,128)(2,1)}, u32[]{:S(2)}, u32[]{:S(2)}) collective-permute-start(bf16[1,512,512]{1,2,0:T(8,128)(2,1)S(1)} %get-tuple-element.16), channel_id=1, source_target_pairs={{0,2},{1,3},{2,4},{3,5},{4,6},{5,7},{6,0},{7,1},{8,10},{9,11},{10,... | collective-permute-start | bytes 1572872 | tf_op jit(solution)/shard_map/ppermute | solution.py:114
  394.5 26.8 %collective-permute-start.26 = (bf16[1,512,512]{1,2,0:T(8,128)(2,1)S(1)}, bf16[1,512,512]{1,2,0:T(8,128)(2,1)}, u32[]{:S(2)}, u32[]{:S(2)}) collective-permute-start(bf16[1,512,512]{1,2,0:T(8,128)(2,1)S(1)} %get-tuple-element.16), channel_id=1, source_target_pairs={{0,3},{1,4},{2,5},{3,6},{4,7},{5,0},{6,1},{7,2},{8,11},{9,12},{10,... | collective-permute-start | bytes 1572872 | tf_op jit(solution)/shard_map/ppermute | solution.py:114
  396.0 27.3 %collective-permute-start.27 = (bf16[1,512,512]{1,2,0:T(8,128)(2,1)S(1)}, bf16[1,512,512]{1,2,0:T(8,128)(2,1)S(1)}, u32[]{:S(2)}, u32[]{:S(2)}) collective-permute-start(bf16[1,512,512]{1,2,0:T(8,128)(2,1)S(1)} %get-tuple-element.16), channel_id=1, source_target_pairs={{0,4},{1,5},{2,6},{3,7},{4,0},{5,1},{6,2},{7,3},{8,12},{9,13},{10,... | collective-permute-start | bytes 1572872 | tf_op jit(solution)/shard_map/ppermute | solution.py:114
  396.6 34.2 %collective-permute-start.28 = (bf16[1,512,512]{1,2,0:T(8,128)(2,1)S(1)}, bf16[1,512,512]{1,2,0:T(8,128)(2,1)S(1)}, u32[]{:S(2)}, u32[]{:S(2)}) collective-permute-start(bf16[1,512,512]{1,2,0:T(8,128)(2,1)S(1)} %get-tuple-element.16), channel_id=1, source_target_pairs={{0,5},{1,6},{2,7},{3,0},{4,1},{5,2},{6,3},{7,4},{8,13},{9,14},{10,... | collective-permute-start | bytes 1572872 | tf_op jit(solution)/shard_map/ppermute | solution.py:114
  406.9 24.7 %collective-permute-start.29 = (bf16[1,512,512]{1,2,0:T(8,128)(2,1)S(1)}, bf16[1,512,512]{1,2,0:T(8,128)(2,1)S(1)}, u32[]{:S(2)}, u32[]{:S(2)}) collective-permute-start(bf16[1,512,512]{1,2,0:T(8,128)(2,1)S(1)} %get-tuple-element.16), channel_id=1, source_target_pairs={{0,6},{1,7},{2,0},{3,1},{4,2},{5,3},{6,4},{7,5},{8,14},{9,15},{10,... | collective-permute-start | bytes 1572872 | tf_op jit(solution)/shard_map/ppermute | solution.py:114
  409.3 32.0 %collective-permute-start.30 = (bf16[1,512,512]{1,2,0:T(8,128)(2,1)S(1)}, bf16[1,512,512]{1,2,0:T(8,128)(2,1)S(1)}, u32[]{:S(2)}, u32[]{:S(2)}) collective-permute-start(bf16[1,512,512]{1,2,0:T(8,128)(2,1)S(1)} %get-tuple-element.16), channel_id=1, source_target_pairs={{0,7},{1,0},{2,1},{3,2},{4,3},{5,4},{6,5},{7,6},{8,15},{9,8},{10,9... | collective-permute-start | bytes 1572872 | tf_op jit(solution)/shard_map/ppermute | solution.py:114
  421.4 46.1 %collective-permute-start.31 = (bf16[512,1792]{1,0:T(8,128)(2,1)S(1)}, bf16[512,1792]{1,0:T(8,128)(2,1)}, u32[]{:S(2)}, u32[]{:S(2)}) collective-permute-start(bf16[512,1792]{1,0:T(8,128)(2,1)S(1)} %bitcast.154), channel_id=1, source_target_pairs={{0,8},{8,16},{16,24},{24,0},{1,9},{9,17},{17,25},{25,1},{2,10},{10... | collective-permute-start | bytes 5505032 | tf_op jit(solution)/shard_map/ppermute | solution.py:106
  423.2 154.7 %collective-permute-start.32 = (bf16[512,1792]{1,0:T(8,128)(2,1)S(1)}, bf16[512,1792]{1,0:T(8,128)(2,1)}, u32[]{:S(2)}, u32[]{:S(2)}) collective-permute-start(bf16[512,1792]{1,0:T(8,128)(2,1)S(1)} %bitcast.155), channel_id=1, source_target_pairs={{0,16},{8,24},{16,0},{24,8},{1,17},{9,25},{17,1},{25,9},{2,18},{10... | collective-permute-start | bytes 5505032 | tf_op jit(solution)/shard_map/ppermute | solution.py:106
  430.8 149.4 %collective-permute-start.33 = (bf16[512,1792]{1,0:T(8,128)(2,1)S(1)}, bf16[512,1792]{1,0:T(8,128)(2,1)}, u32[]{:S(2)}, u32[]{:S(2)}) collective-permute-start(bf16[512,1792]{1,0:T(8,128)(2,1)S(1)} %bitcast.156), channel_id=1, source_target_pairs={{0,24},{8,0},{16,8},{24,16},{1,25},{9,1},{17,9},{25,17},{2,26},{10... | collective-permute-start | bytes 5505032 | tf_op jit(solution)/shard_map/ppermute | solution.py:106
  467.4 112.7 %copy-start.4 = (f32[256,8,2,512]{3,1,2,0:T(8,128)}, f32[256,8,2,512]{3,1,2,0:T(8,128)S(1)}, u32[]{:S(2)}) copy-start(f32[256,8,2,512]{3,1,2,0:T(8,128)S(1)} %copy.176) | copy-start | bytes 25165828
  636.7 54.4 %copy-start.12 = (bf16[1,512,512]{1,2,0:T(8,128)(2,1)S(1)}, bf16[1,512,512]{1,2,0:T(8,128)(2,1)}, u32[]{:S(2)}) copy-start(bf16[1,512,512]{1,2,0:T(8,128)(2,1)} %copy-done.11) | copy-start | bytes 1572868
  638.8 14.6 %collective-permute-start.34 = (bf16[1,512,512]{1,2,0:T(8,128)(2,1)}, bf16[1,512,512]{1,2,0:T(8,128)(2,1)}, u32[]{:S(2)}, u32[]{:S(2)}) collective-permute-start(bf16[1,512,512]{1,2,0:T(8,128)(2,1)} %copy.161), channel_id=1, source_target_pairs={{0,1},{1,2},{2,3},{3,4},{4,5},{5,6},{6,7},{7,0},{8,9},{9,10},{10,1... | collective-permute-start | bytes 1572872 | tf_op jit(solution)/shard_map/ppermute | solution.py:114
  643.6 25.1 %collective-permute-start.35 = (bf16[1,512,512]{1,2,0:T(8,128)(2,1)}, bf16[1,512,512]{1,2,0:T(8,128)(2,1)}, u32[]{:S(2)}, u32[]{:S(2)}) collective-permute-start(bf16[1,512,512]{1,2,0:T(8,128)(2,1)} %copy.162), channel_id=1, source_target_pairs={{0,2},{1,3},{2,4},{3,5},{4,6},{5,7},{6,0},{7,1},{8,10},{9,11},{10,... | collective-permute-start | bytes 1572872 | tf_op jit(solution)/shard_map/ppermute | solution.py:114
  645.6 23.3 %collective-permute-start.36 = (bf16[1,512,512]{1,2,0:T(8,128)(2,1)}, bf16[1,512,512]{1,2,0:T(8,128)(2,1)}, u32[]{:S(2)}, u32[]{:S(2)}) collective-permute-start(bf16[1,512,512]{1,2,0:T(8,128)(2,1)} %copy.163), channel_id=1, source_target_pairs={{0,3},{1,4},{2,5},{3,6},{4,7},{5,0},{6,1},{7,2},{8,11},{9,12},{10,... | collective-permute-start | bytes 1572872 | tf_op jit(solution)/shard_map/ppermute | solution.py:114
  647.9 21.0 %collective-permute-start.37 = (bf16[1,512,512]{1,2,0:T(8,128)(2,1)}, bf16[1,512,512]{1,2,0:T(8,128)(2,1)S(1)}, u32[]{:S(2)}, u32[]{:S(2)}) collective-permute-start(bf16[1,512,512]{1,2,0:T(8,128)(2,1)} %copy.164), channel_id=1, source_target_pairs={{0,4},{1,5},{2,6},{3,7},{4,0},{5,1},{6,2},{7,3},{8,12},{9,13},{10,... | collective-permute-start | bytes 1572872 | tf_op jit(solution)/shard_map/ppermute | solution.py:114
  649.7 26.7 %collective-permute-start.38 = (bf16[1,512,512]{1,2,0:T(8,128)(2,1)}, bf16[1,512,512]{1,2,0:T(8,128)(2,1)S(1)}, u32[]{:S(2)}, u32[]{:S(2)}) collective-permute-start(bf16[1,512,512]{1,2,0:T(8,128)(2,1)} %copy.165), channel_id=1, source_target_pairs={{0,5},{1,6},{2,7},{3,0},{4,1},{5,2},{6,3},{7,4},{8,13},{9,14},{10,... | collective-permute-start | bytes 1572872 | tf_op jit(solution)/shard_map/ppermute | solution.py:114
  651.4 43.0 %copy-start.1 = (s32[32]{0:T(128)S(1)}, s32[32]{0:T(128)}, u32[]{:S(2)}) copy-start(s32[32]{0:T(128)} %param.21) | copy-start | bytes 388
  653.4 37.7 %collective-permute-start.39 = (bf16[1,512,512]{1,2,0:T(8,128)(2,1)}, bf16[1,512,512]{1,2,0:T(8,128)(2,1)S(1)}, u32[]{:S(2)}, u32[]{:S(2)}) collective-permute-start(bf16[1,512,512]{1,2,0:T(8,128)(2,1)} %copy.166), channel_id=1, source_target_pairs={{0,6},{1,7},{2,0},{3,1},{4,2},{5,3},{6,4},{7,5},{8,14},{9,15},{10,... | collective-permute-start | bytes 1572872 | tf_op jit(solution)/shard_map/ppermute | solution.py:114
  668.7 22.5 %collective-permute-start.40 = (bf16[1,512,512]{1,2,0:T(8,128)(2,1)}, bf16[1,512,512]{1,2,0:T(8,128)(2,1)}, u32[]{:S(2)}, u32[]{:S(2)}) collective-permute-start(bf16[1,512,512]{1,2,0:T(8,128)(2,1)} %copy.167), channel_id=1, source_target_pairs={{0,7},{1,0},{2,1},{3,2},{4,3},{5,4},{6,5},{7,6},{8,15},{9,8},{10,9... | collective-permute-start | bytes 1572872 | tf_op jit(solution)/shard_map/ppermute | solution.py:114
  (15 other events, 70.0 us)

commit v4 on v3

--- a/solution.py
+++ b/solution.py
@@ -107,34 +107,24 @@
         return jnp.concatenate(pieces, axis=0)
 
     n_plane = n_core * n_tp
-    me_plane = core * n_tp + lax.axis_index("tp")
-    shifts = range(1, n_plane)
-
-    def plane_perm(piece, k):
-        return lax.ppermute(piece, ("core", "tp"), perm=[(i, (i + k) % n_plane) for i in range(n_plane)])
+    plane = ("core", "tp")
 
     def gather_plane(piece):
         width = piece.shape[2]
-        whole = jnp.zeros((n_core, length, n_tp * width), piece.dtype)
-        whole = lax.dynamic_update_slice(whole, piece, (core, 0, lax.axis_index("tp") * width))
-        for k in shifts:
-            src = (me_plane + n_plane - k) % n_plane
-            got = plane_perm(piece, k)
-            whole = lax.dynamic_update_slice(whole, got, (src // n_tp, 0, src % n_tp * width))
-        return whole
+        spread = jnp.broadcast_to(piece, (n_plane, length, width))
+        got = lax.all_to_all(spread, plane, split_axis=0, concat_axis=0, tiled=True)
+        got = got.reshape(n_core, n_tp, length, width).transpose(0, 2, 1, 3)
+        return got.reshape(n_core, length, n_tp * width)
 
     def scatter_plane(terms):
         width = terms.shape[2] // n_tp
-        def block_of(dest):
-            return lax.dynamic_slice(terms, (dest // n_tp, 0, dest % n_tp * width), (1, length, width))
-        total = block_of(me_plane).astype(jnp.float32)
-        for k in shifts:
-            dest = (me_plane + k) % n_plane
-            total = total + plane_perm(block_of(dest), k).astype(jnp.float32)
-        return total
-
-    segs = gather_plane(segment_ids[:, :, None])[:, :, 0::1].reshape(n_core, length * n_tp)
-    segs = segs.reshape(n_core, length, n_tp)[:, :, 0]
+        terms = terms.reshape(n_core, length, n_tp, width).transpose(0, 2, 1, 3)
+        terms = terms.reshape(n_plane, length, width)
+        got = lax.all_to_all(terms, plane, split_axis=0, concat_axis=0, tiled=True)
+        return jnp.sum(got.astype(jnp.float32), axis=0, keepdims=True)
+
+    other = lax.ppermute(segment_ids, "core", perm=[(i, (i + 1) % n_core) for i in range(n_core)])
+    segs = jnp.where(core == 0, jnp.concatenate([segment_ids, other]), jnp.concatenate([other, segment_ids]))
     rows = n_core
     pos = positions(segs)
     index = jnp.arange(length, dtype=jnp.int32)

time: 703 us -> 669 us (0.952)
  the two profiles are of different devices: /device:TPU:15 before, /device:TPU:9 now
where the time goes in v4:
time: 669 us; the launch traced here: 660 us
  waiting for transfers between devices  340 us (51%)
  local copies, waits for them, and re-layouts  125 us (19%)
  matrix products  83.4 us (12%)
  blocking collectives  52.5 us (8%)
  starting transfers between devices  30.5 us (5%)
  other arithmetic  27.6 us (4%)
    ppermute x6, waiting for transfers between devices, gather_zz(): lax.ppermute(piece, 'zz', perm=[(i, (i + k) % n_zz) for i in range(n_zz)])  191 us
    all_to_all x2, waiting for transfers between devices, gather_plane(): got = lax.all_to_all(spread, plane, split_axis=0, concat_axis=0, tiled=True)  72.3 us
    all_to_all x1, blocking collectives, scatter_plane(): got = lax.all_to_all(terms, plane, split_axis=0, concat_axis=0, tiled=True)  52.5 us
    all_to_all x1, waiting for transfers between devices, scatter_plane(): got = lax.all_to_all(terms, plane, split_axis=0, concat_axis=0, tiled=True)  48.5 us
    dot_general x2, matrix products, shards(): jnp.dot(mlp_in, w_up, preferred_element_type=jnp.float32)  36.8 us
    all_to_all x1, waiting for transfers between devices, shards(): lax.all_to_all(packed, ('tp', 'core'), split_axis=2, concat_axis=1, tiled...  28.3 us
    convert_element_type x2, local copies, waits for them, and re-layouts, shards(): permuted = permuted.reshape(rows * length, full_width).astype(jnp.float32)  24.9 us
    another operation x4, local copies, waits for them, and re-layouts, scatter_plane(): terms = terms.reshape(n_core, length, n_tp, width).transpose(0, 2, 1, 3)  23.7 us
  transfers between devices with their start and end apart: 11, of which 8 were waited for; matrix products, arithmetic and copies ran while one was open for 12% of the time, Pallas kernels for 0%

profile of v4, /device:TPU:9, one launch (start us, length us, event | category | flops | bytes accessed | tf_op | source)
XLA Modules:
  0.0 659.9 jit_solution(3918265506878268806)
XLA Ops:
  0.0 2.6 convert_element_type.149
  2.6 1.4 copy.92
  4.8 2.5 copy.62
  7.4 5.2 all-to-all-start.1
  19.4 4.9 fusion.195
  24.3 28.3 %all-to-all-done.1 = bf16[2,64,8,1792]{3,1,0,2:T(8,128)(2,1)} async-done(((bf16[2,64,8,1792]{3,1,0,2:T(8,128)(2,1)}), bf16[2,64,8,1792]{3,1,0,2:T(8,128)(2,1)}, u32[]{:S(2)}, u32[]{:S(2)}) %all-to-all-start.1) | async-done | bytes 3670048 | tf_op jit(solution)/shard_map/all_to_all | solution.py:96
  52.6 2.4 broadcast_in_dim.52
  55.1 8.2 %all-to-all-start = ((bf16[8,512,512]{1,2,0:T(8,128)(2,1)}), bf16[8,512,512]{1,2,0:T(8,128)(2,1)}, u32[]{:S(2)}, u32[]{:S(2)}) async-start(bf16[8,512,512]{1,2,0:T(8,128)(2,1)} %broadcast_in_dim.52), calls=%async_computation | async-start | bytes 8388608 | tf_op jit(solution)/shard_map/all_to_all | solution.py:115
  63.3 12.1 %fusion.194 = (bf16[1,2048,2048]{2,1,0:T(8,128)(2,1)}, bf16[1,2048,2048]{2,1,0:T(8,128)(2,1)}) fusion(bf16[2,2048,2048]{2,1,0:T(8,128)(2,1)} %param.27), kind=kLoop, calls=%fused_computation.283 | loop fusion | bytes 33554432 | tf_op jit(solution)/shard_map/slice | solution.py:172
  77.0 2.4 copy.107
  79.4 1.5 fusion.196
  80.9 1.3 collective-permute-start
  82.2 1.0 collective-permute-start.1
  83.2 1.5 collective-permute-start.2
  84.7 27.1 %all-to-all-done = bf16[8,512,512]{1,2,0:T(8,128)(2,1)} async-done(((bf16[8,512,512]{1,2,0:T(8,128)(2,1)}), bf16[8,512,512]{1,2,0:T(8,128)(2,1)}, u32[]{:S(2)}, u32[]{:S(2)}) %all-to-all-start) | async-done | bytes 4194336 | tf_op jit(solution)/shard_map/all_to_all | solution.py:115
  111.8 5.1 gather_fusion.1
  116.8 3.6 fusion.19
  120.4 1.6 multiply_reduce_fusion.1
  122.7 12.6 %copy.61 = f32[2,512,32,64]{1,0,3,2:T(2,128)S(1)} copy(f32[2,512,32,64]{1,3,0,2:T(8,128)S(1)} %bitcast_convert_fusion.1) | data formatting | bytes 16777216 | tf_op jit(solution)/shard_map/convert_element_type | solution.py:141
  135.3 2.1 copy.88
  137.4 102.1 %collective-permute-done.1 = bf16[512,1792]{1,0:T(8,128)(2,1)} collective-permute-done((bf16[512,1792]{1,0:T(8,128)(2,1)S(1)}, bf16[512,1792]{1,0:T(8,128)(2,1)}, u32[]{:S(2)}, u32[]{:S(2)}) %collective-permute-start.1) | collective-permute-done | bytes 1835040 | tf_op jit(solution)/shard_map/ppermute | solution.py:106
  239.4 2.4 collective-permute-done.2
  241.8 7.3 %fusion.69 = f32[1024,768]{1,0:T(8,128)} fusion(bf16[512,1792]{1,0:T(8,128)(2,1)} %collective-permute-done.2, bf16[512,1792]{1,0:T(8,128)(2,1)} %collective-permute-done.1, bf16[512,1792]{1,0:T(8,128)(2,1)} %collective-permute-done, bf16[512,1792]{1,0:T(8,128)(2,1)S(1)} %bitcast.187, f32[1024,2048]{0,1:T(8,128)S(1)} %bitcast.163, f32[2048]{0:T(1024)S(1)} %add.212, ...), kind=kOutput, calls=%fused_computation.127 | convolution fusion | flops 3245080576 | bytes 18902016 | tf_op jit(solution)/shard_map/dot_general | solution.py:153
  249.1 2.4 copy.64
  251.4 3.7 reshape.388
  255.2 2.3 fusion.198
  257.4 2.4 slice.215
  261.5 3.7 fusion.147
  265.2 4.2 fusion.202
  269.5 2.2 fusion.72
  271.9 18.4 %fusion.4 = bf16[1024,1024]{1,0:T(8,128)(2,1)S(1)} fusion(bf16[512,1792]{1,0:T(8,128)(2,1)} %collective-permute-done.2, bf16[512,1792]{1,0:T(8,128)(2,1)} %collective-permute-done.1, bf16[512,1792]{1,0:T(8,128)(2,1)} %collective-permute-done, bf16[512,1792]{1,0:T(8,128)(2,1)S(1)} %bitcast.188, f32[1024,2048]{0,1:T(8,128)} %bitcast.164, f32[2048]{0:T(1024)S(1)} %add.223, ...), kind=kOutput, calls=%fused_computation.29 | convolution fusion | flops 4391436288 | bytes 17854464 | tf_op jit(solution)/shard_map/dot_general | solution.py:170
  290.3 6.5 fusion.17
  296.7 3.3 add_convert_fusion.3
  300.1 7.8 %reshape_reshape.13 = bf16[2,512,4,512]{3,2,1,0:T(4,128)(2,1)} reshape(bf16[1024,2048]{1,0:T(8,128)(2,1)} %add_convert_fusion.3) | data formatting | bytes 8388608 | tf_op jit(solution)/shard_map/reshape;reshape | solution.py:121
  307.9 5.0 copy.70
  312.9 5.1 all-to-all-start.2
  318.0 48.5 %all-to-all-done.2 = bf16[8,512,512]{2,1,0:T(8,128)(2,1)} async-done(((bf16[8,512,512]{2,1,0:T(8,128)(2,1)}), bf16[8,512,512]{2,1,0:T(8,128)(2,1)}, u32[]{:S(2)}, u32[]{:S(2)}) %all-to-all-start.2) | async-done | bytes 4194336 | tf_op jit(solution)/shard_map/all_to_all | solution.py:123
  366.5 2.9 convert_reduce_fusion.1
  369.8 2.4 broadcast_in_dim.61
  372.2 4.8 all-to-all-start.3
  377.4 1.4 collective-permute-start.5
  378.8 1.8 collective-permute-start.6
  380.6 45.2 %all-to-all-done.3 = bf16[8,512,512]{1,2,0:T(8,128)(2,1)} async-done(((bf16[8,512,512]{1,2,0:T(8,128)(2,1)}), bf16[8,512,512]{1,2,0:T(8,128)(2,1)}, u32[]{:S(2)}, u32[]{:S(2)}) %all-to-all-start.3) | async-done | bytes 4194336 | tf_op jit(solution)/shard_map/all_to_all | solution.py:115
  425.8 5.0 gather_fusion.6
  430.8 3.6 fusion.16
  434.4 1.6 multiply_reduce_fusion
  436.6 12.4 %copy.72 = f32[2,512,32,64]{1,0,3,2:T(2,128)S(1)} copy(f32[2,512,32,64]{1,3,0,2:T(8,128)S(1)} %bitcast_convert_fusion) | data formatting | bytes 16777216 | tf_op jit(solution)/shard_map/convert_element_type | solution.py:141
  449.0 2.1 copy.94
  451.1 83.8 %collective-permute-done.5 = bf16[512,1792]{1,0:T(8,128)(2,1)} collective-permute-done((bf16[512,1792]{1,0:T(8,128)(2,1)S(1)}, bf16[512,1792]{1,0:T(8,128)(2,1)}, u32[]{:S(2)}, u32[]{:S(2)}) %collective-permute-start.5) | collective-permute-done | bytes 1835040 | tf_op jit(solution)/shard_map/ppermute | solution.py:106
  534.9 2.4 collective-permute-done.6
  537.3 7.3 %fusion.66 = f32[1024,768]{1,0:T(8,128)} fusion(bf16[512,1792]{1,0:T(8,128)(2,1)} %collective-permute-done.6, bf16[512,1792]{1,0:T(8,128)(2,1)} %collective-permute-done.5, bf16[512,1792]{1,0:T(8,128)(2,1)} %collective-permute-done.4, bf16[512,1792]{1,0:T(8,128)(2,1)S(1)} %bitcast.182, f32[1024,2048]{0,1:T(8,128)S(1)} %bitcast.161, f32[2048]{0:T(1024)S(1)} %add.237, ...), kind=kOutput, calls=%fused_computation.126 | convolution fusion | flops 3245080576 | bytes 18902016 | tf_op jit(solution)/shard_map/dot_general | solution.py:153
  544.6 2.4 copy.73
  547.0 3.8 reshape.394
  550.8 2.3 fusion.197
  554.5 3.3 fusion.143
  558.1 1.6 slice.228
  559.7 4.0 fusion.207
  563.7 2.2 fusion.73
  566.1 18.4 %fusion.7 = bf16[1024,1024]{1,0:T(8,128)(2,1)S(1)} fusion(bf16[512,1792]{1,0:T(8,128)(2,1)} %collective-permute-done.6, bf16[512,1792]{1,0:T(8,128)(2,1)} %collective-permute-done.5, bf16[512,1792]{1,0:T(8,128)(2,1)} %collective-permute-done.4, bf16[512,1792]{1,0:T(8,128)(2,1)S(1)} %bitcast.183, f32[1024,2048]{0,1:T(8,128)} %bitcast.162, ...), kind=kOutput, calls=%fused_computation.32 | convolution fusion | flops 4391436288 | bytes 17854464 | tf_op jit(solution)/shard_map/dot_general | solution.py:170
  584.5 6.5 fusion.14
  591.0 3.3 add_convert_fusion
  594.3 7.8 %reshape_reshape.15 = bf16[2,512,4,512]{3,2,1,0:T(4,128)(2,1)} reshape(bf16[1024,2048]{1,0:T(8,128)(2,1)} %add_convert_fusion) | data formatting | bytes 8388608 | tf_op jit(solution)/shard_map/reshape;reshape | solution.py:121
  602.1 3.0 copy.79
  605.2 52.5 %all_to_all.35 = bf16[8,512,512]{2,1,0:T(8,128)(2,1)S(1)} all-to-all(bf16[8,512,512]{2,1,0:T(8,128)(2,1)S(1)} %bitcast.157), channel_id=1, replica_groups=mesh['zz'=4,'core'=2,'tp'=4] {'core','tp'}, dimensions={0} | all-to-all | bytes 8388608 | tf_op jit(solution)/shard_map/all_to_all | solution.py:123
  (136 shorter events, 17.0 us)
Async XLA Ops:
  0.0 13.2 %copy-start = (s32[32]{0:T(128)S(1)}, s32[32]{0:T(128)}, u32[]{:S(2)}) copy-start(s32[32]{0:T(128)} %param.21) | copy-start | bytes 388
  0.0 4.0 copy-start.10
  7.4 5.2 copy-start.23
  7.4 5.5 copy-start.19
  7.4 5.5 copy-start.20
  7.4 5.8 copy-start.24
  7.4 5.8 copy-start.25
  7.4 5.8 copy-start.26
  7.4 11.5 %copy-start.11 = (bf16[1,512,512]{2,1,0:T(8,128)(2,1)S(1)}, bf16[1,512,512]{2,1,0:T(8,128)(2,1)}, u32[]{:S(2)}) copy-start(bf16[1,512,512]{2,1,0:T(8,128)(2,1)} %param.19) | copy-start | bytes 1572868
  7.4 11.8 %copy-start.18 = (bf16[2,2048]{1,0:T(2,128)(2,1)S(1)}, bf16[2,2048]{1,0:T(2,128)(2,1)}, u32[]{:S(2)}) copy-start(bf16[2,2048]{1,0:T(2,128)(2,1)} %param.25) | copy-start | bytes 24580
  7.4 45.2 %all-to-all-start.1 = ((bf16[2,64,8,1792]{3,1,0,2:T(8,128)(2,1)}), bf16[2,64,8,1792]{3,1,0,2:T(8,128)(2,1)}, u32[]{:S(2)}, u32[]{:S(2)}) async-start(bf16[2,64,8,1792]{3,1,0,2:T(8,128)(2,1)} %copy.62), calls=%async_computation.1 | async-start | bytes 7340032 | tf_op jit(solution)/shard_map/all_to_all | solution.py:96
  12.6 63.1 %collective-permute-start.3 = (s32[1,512]{1,0:T(1,128)S(1)}, s32[1,512]{1,0:T(1,128)S(1)}, u32[]{:S(2)}, u32[]{:S(2)}) collective-permute-start(s32[1,512]{1,0:T(1,128)S(1)} %copy-done.23), channel_id=1, source_target_pairs={{0,4},{4,0},{1,5},{5,1},{2,6},{6,2},{3,7},{7,3},{8,12},{12,8},{9,1... | collective-permute-start | bytes 6152 | tf_op jit(solution)/shard_map/ppermute | solution.py:126
  55.1 8.2 %copy-start.21 = (bf16[2,1536]{1,0:T(2,128)(2,1)S(1)}, bf16[2,1536]{1,0:T(2,128)(2,1)}, u32[]{:S(2)}) copy-start(bf16[2,1536]{1,0:T(2,128)(2,1)} %param.24) | copy-start | bytes 18436
  55.1 56.7 %all-to-all-start = ((bf16[8,512,512]{1,2,0:T(8,128)(2,1)}), bf16[8,512,512]{1,2,0:T(8,128)(2,1)}, u32[]{:S(2)}, u32[]{:S(2)}) async-start(bf16[8,512,512]{1,2,0:T(8,128)(2,1)} %broadcast_in_dim.52), calls=%async_computation | async-start | bytes 8388608 | tf_op jit(solution)/shard_map/all_to_all | solution.py:115
  80.9 160.9 %copy-start.15 = (bf16[1,8,64,1,1792]{4,2,1,3,0:T(8,128)(2,1)}, bf16[1,8,64,1,1792]{4,2,1,3,0:T(8,128)(2,1)S(1)}, u32[]{:S(2)}) copy-start(bf16[1,8,64,1,1792]{4,2,1,3,0:T(8,128)(2,1)S(1)} %get-tuple-element.21) | copy-start | bytes 5505028
  80.9 56.5 %collective-permute-start = (bf16[512,1792]{1,0:T(8,128)(2,1)S(1)}, bf16[512,1792]{1,0:T(8,128)(2,1)}, u32[]{:S(2)}, u32[]{:S(2)}) collective-permute-start(bf16[512,1792]{1,0:T(8,128)(2,1)S(1)} %bitcast.184), channel_id=1, source_target_pairs={{0,8},{8,16},{16,24},{24,0},{1,9},{9,17},{17,25},{25,1},{2,10},{10... | collective-permute-start | bytes 5505032 | tf_op jit(solution)/shard_map/ppermute | solution.py:106
  82.2 157.2 %collective-permute-start.1 = (bf16[512,1792]{1,0:T(8,128)(2,1)S(1)}, bf16[512,1792]{1,0:T(8,128)(2,1)}, u32[]{:S(2)}, u32[]{:S(2)}) collective-permute-start(bf16[512,1792]{1,0:T(8,128)(2,1)S(1)} %bitcast.185), channel_id=1, source_target_pairs={{0,16},{8,24},{16,0},{24,8},{1,17},{9,25},{17,1},{25,9},{2,18},{10... | collective-permute-start | bytes 5505032 | tf_op jit(solution)/shard_map/ppermute | solution.py:106
  83.2 158.6 %collective-permute-start.2 = (bf16[512,1792]{1,0:T(8,128)(2,1)S(1)}, bf16[512,1792]{1,0:T(8,128)(2,1)}, u32[]{:S(2)}, u32[]{:S(2)}) collective-permute-start(bf16[512,1792]{1,0:T(8,128)(2,1)S(1)} %bitcast.186), channel_id=1, source_target_pairs={{0,24},{8,0},{16,8},{24,16},{1,25},{9,1},{17,9},{25,17},{2,26},{10... | collective-permute-start | bytes 5505032 | tf_op jit(solution)/shard_map/ppermute | solution.py:106
  116.8 3.6 copy-start.2
  137.3 104.5 %copy-start.5 = (f32[256,8,2,512]{3,1,2,0:T(8,128)}, f32[256,8,2,512]{3,1,2,0:T(8,128)S(1)}, u32[]{:S(2)}) copy-start(f32[256,8,2,512]{3,1,2,0:T(8,128)S(1)} %copy.88) | copy-start | bytes 25165828
  265.2 4.2 copy-start.17
  269.5 2.4 copy-start.16
  290.3 6.5 copy-start.9
  312.9 5.1 copy-start.22
  312.9 53.5 %all-to-all-start.2 = ((bf16[8,512,512]{2,1,0:T(8,128)(2,1)}), bf16[8,512,512]{2,1,0:T(8,128)(2,1)}, u32[]{:S(2)}, u32[]{:S(2)}) async-start(bf16[8,512,512]{2,1,0:T(8,128)(2,1)} %bitcast.156), calls=%async_computation.2 | async-start | bytes 8388608 | tf_op jit(solution)/shard_map/all_to_all | solution.py:123
  318.0 51.4 %copy-start.12 = (bf16[1,512,512]{2,1,0:T(8,128)(2,1)S(1)}, bf16[1,512,512]{2,1,0:T(8,128)(2,1)}, u32[]{:S(2)}) copy-start(bf16[1,512,512]{2,1,0:T(8,128)(2,1)} %param.19) | copy-start | bytes 1572868
  369.6 2.6 copy-start.6
  372.2 5.2 copy-start.13
  372.2 53.6 %all-to-all-start.3 = ((bf16[8,512,512]{1,2,0:T(8,128)(2,1)}), bf16[8,512,512]{1,2,0:T(8,128)(2,1)}, u32[]{:S(2)}, u32[]{:S(2)}) async-start(bf16[8,512,512]{1,2,0:T(8,128)(2,1)} %broadcast_in_dim.61), calls=%async_computation.3 | async-start | bytes 8388608 | tf_op jit(solution)/shard_map/all_to_all | solution.py:115
  377.3 73.8 %collective-permute-start.4 = (bf16[512,1792]{1,0:T(8,128)(2,1)S(1)}, bf16[512,1792]{1,0:T(8,128)(2,1)}, u32[]{:S(2)}, u32[]{:S(2)}) collective-permute-start(bf16[512,1792]{1,0:T(8,128)(2,1)S(1)} %bitcast.179), channel_id=1, source_target_pairs={{0,8},{8,16},{16,24},{24,0},{1,9},{9,17},{17,25},{25,1},{2,10},{10... | collective-permute-start | bytes 5505032 | tf_op jit(solution)/shard_map/ppermute | solution.py:106
  377.4 157.5 %collective-permute-start.5 = (bf16[512,1792]{1,0:T(8,128)(2,1)S(1)}, bf16[512,1792]{1,0:T(8,128)(2,1)}, u32[]{:S(2)}, u32[]{:S(2)}) collective-permute-start(bf16[512,1792]{1,0:T(8,128)(2,1)S(1)} %bitcast.180), channel_id=1, source_target_pairs={{0,16},{8,24},{16,0},{24,8},{1,17},{9,25},{17,1},{25,9},{2,18},{10... | collective-permute-start | bytes 5505032 | tf_op jit(solution)/shard_map/ppermute | solution.py:106
  378.8 158.5 %collective-permute-start.6 = (bf16[512,1792]{1,0:T(8,128)(2,1)S(1)}, bf16[512,1792]{1,0:T(8,128)(2,1)}, u32[]{:S(2)}, u32[]{:S(2)}) collective-permute-start(bf16[512,1792]{1,0:T(8,128)(2,1)S(1)} %bitcast.181), channel_id=1, source_target_pairs={{0,24},{8,0},{16,8},{24,16},{1,25},{9,1},{17,9},{25,17},{2,26},{10... | collective-permute-start | bytes 5505032 | tf_op jit(solution)/shard_map/ppermute | solution.py:106
  430.8 3.6 copy-start.3
  451.1 86.2 %copy-start.4 = (f32[256,8,2,512]{3,1,2,0:T(8,128)}, f32[256,8,2,512]{3,1,2,0:T(8,128)S(1)}, u32[]{:S(2)}) copy-start(f32[256,8,2,512]{3,1,2,0:T(8,128)S(1)} %copy.94) | copy-start | bytes 25165828
  563.7 2.4 copy-start.14
  584.5 6.5 copy-start.8
  605.1 54.5 %copy-start.1 = (s32[32]{0:T(128)S(1)}, s32[32]{0:T(128)}, u32[]{:S(2)}) copy-start(s32[32]{0:T(128)} %param.21) | copy-start | bytes 388
  657.6 1.0 copy-start.7

commit v5 on v4

--- a/solution.py
+++ b/solution.py
@@ -131,10 +131,15 @@
     mask = (index[None, :] <= index[:, None])[None] & (segs[:, :, None] == segs[:, None, :])
     mask = mask[:, None]
 
+    gathered = [gather_zz(packed[0].reshape(n_dest * block, -1))]
+    for layer in range(1, LAYERS):
+        piece, gathered[-1] = lax.optimization_barrier((packed[layer], gathered[-1]))
+        gathered.append(gather_zz(piece.reshape(n_dest * block, -1)))
+
     local = tokens
     for layer in range(LAYERS):
         stream = gather_plane(local)
-        weights = gather_zz(packed[layer].reshape(n_dest * block, -1))
+        weights = gathered[layer]
         w_qkv = weights[:, :qkv_cols]
         w_up = weights[:, qkv_cols:]
         permuted = jnp.take(stream.reshape(rows, length, n_blocks, block), feature_block, axis=2)
@@ -172,6 +177,8 @@
         m_rows = lax.dynamic_slice_in_dim(down_w[layer], core * ff_here, ff_here)
         partial_terms = attn_out + jnp.dot(hidden_units, m_rows, preferred_element_type=jnp.float32)
         partial_terms = partial_terms.astype(jnp.bfloat16).reshape(rows, length, full_width)
+        if layer + 1 < LAYERS:
+            partial_terms, gathered[layer + 1] = lax.optimization_barrier((partial_terms, gathered[layer + 1]))
         summed = scatter_plane(partial_terms)
         local = (local.astype(jnp.float32) + summed + out_bias[layer]).astype(jnp.bfloat16)
     stream = local

time: 669 us -> 695 us (1.039)
  other arithmetic: 27.6 us -> 51.8 us
  waiting for transfers between devices: 340 us -> 358 us
  local copies, waits for them, and re-layouts: 125 us -> 115 us
    concatenate x0 -> x3, other arithmetic: none -> 23.7 us  [the longest x2 21.6 us: gather_zz(): return jnp.concatenate(pieces, axis=0)]
    ppermute x6, waiting for transfers between devices: 191 us -> 207 us  [gather_zz(): lax.ppermute(piece, 'zz', perm=[(i, (i + k) % n_zz) for i in range(n_zz)])]
    another operation x4 -> x2, local copies, waits for them, and re-layouts: 23.7 us -> 10.9 us  [scatter_plane(): terms = terms.reshape(n_core, length, n_tp, width).transpose(0, 2, 1, 3)]
  transfers between devices with their start and end apart: 11 -> 11, of which waited for: 8 -> 8; matrix products, arithmetic and copies ran while one was open for 12% -> 16% of each run, Pallas kernels for 0% -> 0%
where the time goes in v5:
time: 695 us; the launch traced here: 688 us
  waiting for transfers between devices  358 us (52%)
  local copies, waits for them, and re-layouts  115 us (17%)
  matrix products  81 us (12%)
  other arithmetic  51.8 us (7%)
  blocking collectives  51.1 us (7%)
  starting transfers between devices  30.4 us (4%)
    ppermute x6, waiting for transfers between devices, gather_zz(): lax.ppermute(piece, 'zz', perm=[(i, (i + k) % n_zz) for i in range(n_zz)])  207 us
    all_to_all x2, waiting for transfers between devices, gather_plane(): got = lax.all_to_all(spread, plane, split_axis=0, concat_axis=0, tiled=True)  75.3 us
    all_to_all x1, blocking collectives, scatter_plane(): got = lax.all_to_all(terms, plane, split_axis=0, concat_axis=0, tiled=True)  51.1 us
    all_to_all x1, waiting for transfers between devices, scatter_plane(): got = lax.all_to_all(terms, plane, split_axis=0, concat_axis=0, tiled=True)  48.5 us
    dot_general x2, matrix products, shards(): jnp.dot(mlp_in, w_up, preferred_element_type=jnp.float32)  38.9 us
    all_to_all x1, waiting for transfers between devices, shards(): lax.all_to_all(packed, ('tp', 'core'), split_axis=2, concat_axis=1, tiled...  27.9 us
    convert_element_type x2, local copies, waits for them, and re-layouts, shards(): permuted = permuted.reshape(rows * length, full_width).astype(jnp.float32)  24.7 us
    concatenate x2, other arithmetic, gather_zz(): return jnp.concatenate(pieces, axis=0)  21.6 us
  transfers between devices with their start and end apart: 11, of which 8 were waited for; matrix products, arithmetic and copies ran while one was open for 16% of the time, Pallas kernels for 0%

profile of v5, /device:TPU:9, one launch (start us, length us, event | category | flops | bytes accessed | tf_op | source)
XLA Modules:
  0.0 688.5 jit_solution(15030101284560624814)
XLA Ops:
  0.0 2.6 convert_element_type.149
  2.6 1.4 copy.89
  4.8 2.5 copy.60
  7.4 5.2 all-to-all-start.1
  20.0 4.8 fusion.311
  24.8 27.9 %all-to-all-done.1 = bf16[2,64,8,1792]{3,1,0,2:T(8,128)(2,1)} async-done(((bf16[2,64,8,1792]{3,1,0,2:T(8,128)(2,1)}), bf16[2,64,8,1792]{3,1,0,2:T(8,128)(2,1)}, u32[]{:S(2)}, u32[]{:S(2)}) %all-to-all-start.1) | async-done | bytes 3670048 | tf_op jit(solution)/shard_map/all_to_all | solution.py:96
  52.7 2.3 broadcast_in_dim.52
  55.0 8.2 %all-to-all-start = ((bf16[8,512,512]{1,2,0:T(8,128)(2,1)}), bf16[8,512,512]{1,2,0:T(8,128)(2,1)}, u32[]{:S(2)}, u32[]{:S(2)}) async-start(bf16[8,512,512]{1,2,0:T(8,128)(2,1)} %broadcast_in_dim.52), calls=%async_computation | async-start | bytes 8388608 | tf_op jit(solution)/shard_map/all_to_all | solution.py:115
  63.3 11.8 %fusion.310 = (bf16[1,2048,2048]{2,1,0:T(8,128)(2,1)}, bf16[1,2048,2048]{2,1,0:T(8,128)(2,1)}) fusion(bf16[2,2048,2048]{2,1,0:T(8,128)(2,1)} %param.27), kind=kLoop, calls=%fused_computation.386 | loop fusion | bytes 33554432 | tf_op jit(solution)/shard_map/slice | solution.py:177
  76.7 2.4 copy.104
  79.1 1.5 fusion.313
  80.6 1.3 collective-permute-start
  83.0 1.6 collective-permute-start.2
  84.6 27.2 %all-to-all-done = bf16[8,512,512]{1,2,0:T(8,128)(2,1)} async-done(((bf16[8,512,512]{1,2,0:T(8,128)(2,1)}), bf16[8,512,512]{1,2,0:T(8,128)(2,1)}, u32[]{:S(2)}, u32[]{:S(2)}) %all-to-all-start) | async-done | bytes 4194336 | tf_op jit(solution)/shard_map/all_to_all | solution.py:115
  111.7 5.0 gather_fusion.1
  116.7 3.6 fusion.17
  120.3 1.6 multiply_reduce_fusion.1
  122.5 12.4 %copy.59 = f32[2,512,32,64]{1,0,3,2:T(2,128)S(1)} copy(f32[2,512,32,64]{1,3,0,2:T(8,128)S(1)} %bitcast_convert_fusion.1) | data formatting | bytes 16777216 | tf_op jit(solution)/shard_map/convert_element_type | solution.py:146
  134.9 2.1 copy.85
  137.0 102.2 %collective-permute-done.1 = bf16[512,1792]{1,0:T(8,128)(2,1)} collective-permute-done((bf16[512,1792]{1,0:T(8,128)(2,1)S(1)}, bf16[512,1792]{1,0:T(8,128)(2,1)}, u32[]{:S(2)}, u32[]{:S(2)}) %collective-permute-start.1) | collective-permute-done | bytes 1835040 | tf_op jit(solution)/shard_map/ppermute | solution.py:106
  239.2 2.4 collective-permute-done.2
  241.6 10.6 %pad_maximum_fusion = bf16[2048,1792]{1,0:T(8,128)(2,1)S(1)} fusion(bf16[512,1792]{1,0:T(8,128)(2,1)} %collective-permute-done.2, bf16[512,1792]{1,0:T(8,128)(2,1)} %collective-permute-done.1, bf16[512,1792]{1,0:T(8,128)(2,1)} %collective-permute-done, bf16[512,1792]{1,0:T(8,128)(2,1)S(1)} %bitcast.172), kind=kLoop, calls=%fused_computation.25 | loop fusion | flops 29360128 | bytes 14680064 | tf_op jit(solution)/shard_map/concatenate | solution.py:107
  253.1 1.6 collective-permute-start.6
  255.2 5.7 fusion.121
  260.9 2.4 copy.62
  263.3 3.8 reshape.395
  267.1 2.3 fusion.315
  271.1 3.6 fusion.199
  274.7 20.1 %fusion.344 = bf16[1024,1024]{1,0:T(8,128)(2,1)} fusion(f32[1024]{0:T(1024)S(1)} %bitcast.199, bf16[2048,1792]{1,0:T(8,128)(2,1)} %copy-done.6, f32[1024,2048]{0,1:T(8,128)} %bitcast.168, f32[2048]{0:T(1024)S(1)} %add.223, f32[2048]{0:T(1024)S(1)} %mul.236, f32[1024]{0:T(1024)S(1)} %bitcast.191, f32[1024]{0:T(1024)S(1)} %bitcast.193), kind=kOutput, calls=%fused_computation.31.clone.clone | convolution fusion | flops 4374659072 | bytes 14708736 | tf_op jit(solution)/shard_map/dot_general | solution.py:175
  294.9 2.8 fusion.319
  297.7 1.6 slice.232
  299.3 2.2 fusion.124
  301.7 6.5 fusion.15
  308.2 1.4 add_convert_fusion.3
  309.6 100.1 %collective-permute-done.5 = bf16[512,1792]{1,0:T(8,128)(2,1)} collective-permute-done((bf16[512,1792]{1,0:T(8,128)(2,1)}, bf16[512,1792]{1,0:T(8,128)(2,1)}, u32[]{:S(2)}, u32[]{:S(2)}) %collective-permute-start.5) | collective-permute-done | bytes 1835040 | tf_op jit(solution)/shard_map/ppermute | solution.py:106
  409.7 2.1 collective-permute-done.6
  411.9 11.0 %pad_maximum_fusion.1 = bf16[2048,1792]{1,0:T(8,128)(2,1)} fusion(bf16[512,1792]{1,0:T(8,128)(2,1)} %collective-permute-done.6, bf16[512,1792]{1,0:T(8,128)(2,1)} %collective-permute-done.5, bf16[512,1792]{1,0:T(8,128)(2,1)} %collective-permute-done.4, bf16[512,1792]{1,0:T(8,128)(2,1)} %bitcast.26), kind=kLoop, calls=%fused_computation.26 | loop fusion | flops 29360128 | bytes 14680064 | tf_op jit(solution)/shard_map/concatenate | solution.py:107
  423.3 2.1 pad_maximum_fusion.2
  425.4 5.1 all-to-all-start.2
  430.5 48.5 %all-to-all-done.2 = bf16[8,512,512]{2,1,0:T(8,128)(2,1)} async-done(((bf16[8,512,512]{2,1,0:T(8,128)(2,1)}), bf16[8,512,512]{2,1,0:T(8,128)(2,1)}, u32[]{:S(2)}, u32[]{:S(2)}) %all-to-all-start.2) | async-done | bytes 4194336 | tf_op jit(solution)/shard_map/all_to_all | solution.py:123
  479.0 2.9 convert_reduce_fusion.1
  482.3 2.3 broadcast_in_dim.61
  484.6 5.2 all-to-all-start.3
  490.1 48.1 %all-to-all-done.3 = bf16[8,512,512]{1,2,0:T(8,128)(2,1)} async-done(((bf16[8,512,512]{1,2,0:T(8,128)(2,1)}), bf16[8,512,512]{1,2,0:T(8,128)(2,1)}, u32[]{:S(2)}, u32[]{:S(2)}) %all-to-all-start.3) | async-done | bytes 4194336 | tf_op jit(solution)/shard_map/all_to_all | solution.py:115
  538.2 5.0 gather_fusion.6
  543.2 3.6 fusion.14
  547.4 1.6 multiply_reduce_fusion
  549.0 12.4 %copy.69 = f32[2,512,32,64]{1,0,3,2:T(2,128)S(1)} copy(f32[2,512,32,64]{1,3,0,2:T(8,128)S(1)} %bitcast_convert_fusion) | data formatting | bytes 16777216 | tf_op jit(solution)/shard_map/convert_element_type | solution.py:146
  561.4 2.1 copy.91
  563.5 3.2 copy-done.4
  566.7 7.6 %fusion.118 = f32[1024,768]{1,0:T(8,128)} fusion(bf16[2048,1792]{1,0:T(8,128)(2,1)} %pad_maximum_fusion.1, f32[1024,2048]{0,1:T(8,128)S(1)} %bitcast.165, f32[2048]{0:T(1024)S(1)} %add.237, f32[2048]{0:T(1024)S(1)} %mul.246, f32[1024]{0:T(1024)S(1)} %bitcast.194, f32[1024]{0:T(1024)S(1)} %bitcast.196, f32[768]{0:T(1024)S(1)} %get-tuple-element.79), kind=kOutput, calls=%fused_computation.173 | convolution fusion | flops 3232497664 | bytes 14707712 | tf_op jit(solution)/shard_map/dot_general | solution.py:158
  574.3 2.4 copy.70
  576.7 3.7 reshape.403
  580.4 2.3 fusion.314
  584.2 3.3 fusion.195
  587.7 1.6 slice.244
  589.3 4.1 fusion.324
  593.4 2.0 fusion.125
  595.6 18.8 %fusion.341 = bf16[1024,1024]{1,0:T(8,128)(2,1)S(1)} fusion(f32[1024]{0:T(1024)S(1)} %bitcast.198, bf16[2048,1792]{1,0:T(8,128)(2,1)} %pad_maximum_fusion.1, f32[1024,2048]{0,1:T(8,128)} %bitcast.166, f32[2048]{0:T(1024)S(1)} %add.246, f32[2048]{0:T(1024)S(1)} %mul.257, f32[1024]{0:T(1024)S(1)} %bitcast.195, f32[1024]{0:T(1024)S(1)} %bitcast.197), kind=kOutput, calls=%fused_computation.34.clone.clone.2 | convolution fusion | flops 4374659072 | bytes 14708736 | tf_op jit(solution)/shard_map/dot_general | solution.py:175
  614.4 6.5 fusion.12
  620.9 3.3 add_convert_fusion
  624.2 7.8 %reshape_reshape.11 = bf16[2,512,4,512]{3,2,1,0:T(4,128)(2,1)} reshape(bf16[1024,2048]{1,0:T(8,128)(2,1)} %add_convert_fusion) | data formatting | bytes 8388608 | tf_op jit(solution)/shard_map/reshape;reshape | solution.py:121
  632.1 3.0 copy.76
  635.1 51.1 %all_to_all.35 = bf16[8,512,512]{2,1,0:T(8,128)(2,1)S(1)} all-to-all(bf16[8,512,512]{2,1,0:T(8,128)(2,1)S(1)} %bitcast.160), channel_id=1, replica_groups=mesh['zz'=4,'core'=2,'tp'=4] {'core','tp'}, dimensions={0} | all-to-all | bytes 8388608 | tf_op jit(solution)/shard_map/all_to_all | solution.py:123
  (140 shorter events, 20.3 us)
Async XLA Ops:
  0.0 13.3 %copy-start = (s32[32]{0:T(128)S(1)}, s32[32]{0:T(128)}, u32[]{:S(2)}) copy-start(s32[32]{0:T(128)} %param.21) | copy-start | bytes 388
  0.0 4.0 copy-start.11
  7.4 5.3 copy-start.24
  7.4 5.5 copy-start.19
  7.4 5.5 copy-start.20
  7.4 5.8 copy-start.25
  7.4 5.8 copy-start.26
  7.4 5.8 copy-start.27
  7.4 11.6 %copy-start.12 = (bf16[1,512,512]{2,1,0:T(8,128)(2,1)S(1)}, bf16[1,512,512]{2,1,0:T(8,128)(2,1)}, u32[]{:S(2)}) copy-start(bf16[1,512,512]{2,1,0:T(8,128)(2,1)} %param.19) | copy-start | bytes 1572868
  7.4 11.8 %copy-start.18 = (bf16[2,2048]{1,0:T(2,128)(2,1)S(1)}, bf16[2,2048]{1,0:T(2,128)(2,1)}, u32[]{:S(2)}) copy-start(bf16[2,2048]{1,0:T(2,128)(2,1)} %param.25) | copy-start | bytes 24580
  7.4 45.2 %all-to-all-start.1 = ((bf16[2,64,8,1792]{3,1,0,2:T(8,128)(2,1)}), bf16[2,64,8,1792]{3,1,0,2:T(8,128)(2,1)}, u32[]{:S(2)}, u32[]{:S(2)}) async-start(bf16[2,64,8,1792]{3,1,0,2:T(8,128)(2,1)} %copy.60), calls=%async_computation.1 | async-start | bytes 7340032 | tf_op jit(solution)/shard_map/all_to_all | solution.py:96
  12.7 62.7 %collective-permute-start.3 = (s32[1,512]{1,0:T(1,128)S(1)}, s32[1,512]{1,0:T(1,128)S(1)}, u32[]{:S(2)}, u32[]{:S(2)}) collective-permute-start(s32[1,512]{1,0:T(1,128)S(1)} %copy-done.24), channel_id=1, source_target_pairs={{0,4},{4,0},{1,5},{5,1},{2,6},{6,2},{3,7},{7,3},{8,12},{12,8},{9,1... | collective-permute-start | bytes 6152 | tf_op jit(solution)/shard_map/ppermute | solution.py:126
  55.0 8.2 %copy-start.21 = (bf16[2,1536]{1,0:T(2,128)(2,1)S(1)}, bf16[2,1536]{1,0:T(2,128)(2,1)}, u32[]{:S(2)}) copy-start(bf16[2,1536]{1,0:T(2,128)(2,1)} %param.24) | copy-start | bytes 18436
  55.0 56.7 %all-to-all-start = ((bf16[8,512,512]{1,2,0:T(8,128)(2,1)}), bf16[8,512,512]{1,2,0:T(8,128)(2,1)}, u32[]{:S(2)}, u32[]{:S(2)}) async-start(bf16[8,512,512]{1,2,0:T(8,128)(2,1)} %broadcast_in_dim.52), calls=%async_computation | async-start | bytes 8388608 | tf_op jit(solution)/shard_map/all_to_all | solution.py:115
  80.6 56.4 %collective-permute-start = (bf16[512,1792]{1,0:T(8,128)(2,1)S(1)}, bf16[512,1792]{1,0:T(8,128)(2,1)}, u32[]{:S(2)}, u32[]{:S(2)}) collective-permute-start(bf16[512,1792]{1,0:T(8,128)(2,1)S(1)} %bitcast.169), channel_id=1, source_target_pairs={{0,8},{8,16},{16,24},{24,0},{1,9},{9,17},{17,25},{25,1},{2,10},{10... | collective-permute-start | bytes 5505032 | tf_op jit(solution)/shard_map/ppermute | solution.py:106
  81.9 157.2 %collective-permute-start.1 = (bf16[512,1792]{1,0:T(8,128)(2,1)S(1)}, bf16[512,1792]{1,0:T(8,128)(2,1)}, u32[]{:S(2)}, u32[]{:S(2)}) collective-permute-start(bf16[512,1792]{1,0:T(8,128)(2,1)S(1)} %bitcast.170), channel_id=1, source_target_pairs={{0,16},{8,24},{16,0},{24,8},{1,17},{9,25},{17,1},{25,9},{2,18},{10... | collective-permute-start | bytes 5505032 | tf_op jit(solution)/shard_map/ppermute | solution.py:106
  83.0 158.6 %collective-permute-start.2 = (bf16[512,1792]{1,0:T(8,128)(2,1)S(1)}, bf16[512,1792]{1,0:T(8,128)(2,1)}, u32[]{:S(2)}, u32[]{:S(2)}) collective-permute-start(bf16[512,1792]{1,0:T(8,128)(2,1)S(1)} %bitcast.171), channel_id=1, source_target_pairs={{0,24},{8,0},{16,8},{24,16},{1,25},{9,1},{17,9},{25,17},{2,26},{10... | collective-permute-start | bytes 5505032 | tf_op jit(solution)/shard_map/ppermute | solution.py:106
  116.7 3.6 copy-start.2
  137.0 117.7 %copy-start.5 = (f32[256,8,2,512]{3,1,2,0:T(8,128)}, f32[256,8,2,512]{3,1,2,0:T(8,128)S(1)}, u32[]{:S(2)}) copy-start(f32[256,8,2,512]{3,1,2,0:T(8,128)S(1)} %copy.85) | copy-start | bytes 25165828
  252.2 3.0 copy-start.6
  252.2 57.5 %collective-permute-start.4 = (bf16[512,1792]{1,0:T(8,128)(2,1)}, bf16[512,1792]{1,0:T(8,128)(2,1)}, u32[]{:S(2)}, u32[]{:S(2)}) collective-permute-start(bf16[512,1792]{1,0:T(8,128)(2,1)} %bitcast.26), channel_id=1, source_target_pairs={{0,8},{8,16},{16,24},{24,0},{1,9},{9,17},{17,25},{25,1},{2,10},{10... | collective-permute-start | bytes 5505032 | tf_op jit(solution)/shard_map/ppermute | solution.py:106
  252.2 157.5 %collective-permute-start.5 = (bf16[512,1792]{1,0:T(8,128)(2,1)}, bf16[512,1792]{1,0:T(8,128)(2,1)}, u32[]{:S(2)}, u32[]{:S(2)}) collective-permute-start(bf16[512,1792]{1,0:T(8,128)(2,1)} %bitcast.26), channel_id=1, source_target_pairs={{0,16},{8,24},{16,0},{24,8},{1,17},{9,25},{17,1},{25,9},{2,18},{10... | collective-permute-start | bytes 5505032 | tf_op jit(solution)/shard_map/ppermute | solution.py:106
  253.1 158.7 %collective-permute-start.6 = (bf16[512,1792]{1,0:T(8,128)(2,1)}, bf16[512,1792]{1,0:T(8,128)(2,1)}, u32[]{:S(2)}, u32[]{:S(2)}) collective-permute-start(bf16[512,1792]{1,0:T(8,128)(2,1)} %bitcast.26), channel_id=1, source_target_pairs={{0,24},{8,0},{16,8},{24,16},{1,25},{9,1},{17,9},{25,17},{2,26},{10... | collective-permute-start | bytes 5505032 | tf_op jit(solution)/shard_map/ppermute | solution.py:106
  274.7 20.2 %copy-start.14 = (bf16[2,512,32]{2,1,0:T(8,128)(2,1)S(1)}, bf16[2,512,32]{2,1,0:T(8,128)(2,1)}, u32[]{:S(2)}) copy-start(bf16[2,512,32]{2,1,0:T(8,128)(2,1)} %get-tuple-element.43) | copy-start | bytes 196612
  274.7 20.1 %copy-start.15 = (bf16[2,512,32]{2,1,0:T(8,128)(2,1)S(1)}, bf16[2,512,32]{2,1,0:T(8,128)(2,1)}, u32[]{:S(2)}) copy-start(bf16[2,512,32]{2,1,0:T(8,128)(2,1)} %get-tuple-element.44) | copy-start | bytes 196612
  274.7 20.1 %copy-start.16 = (bf16[2,512,32]{2,1,0:T(8,128)(2,1)S(1)}, bf16[2,512,32]{2,1,0:T(8,128)(2,1)}, u32[]{:S(2)}) copy-start(bf16[2,512,32]{2,1,0:T(8,128)(2,1)} %get-tuple-element.53) | copy-start | bytes 196612
  274.7 20.1 %copy-start.17 = (bf16[2,512,32]{2,1,0:T(8,128)(2,1)S(1)}, bf16[2,512,32]{2,1,0:T(8,128)(2,1)}, u32[]{:S(2)}) copy-start(bf16[2,512,32]{2,1,0:T(8,128)(2,1)} %get-tuple-element.54) | copy-start | bytes 196612
  299.3 2.4 copy-start.28
  301.7 6.5 copy-start.10
  425.4 5.1 copy-start.22
  425.4 53.6 %all-to-all-start.2 = ((bf16[8,512,512]{2,1,0:T(8,128)(2,1)}), bf16[8,512,512]{2,1,0:T(8,128)(2,1)}, u32[]{:S(2)}, u32[]{:S(2)}) async-start(bf16[8,512,512]{2,1,0:T(8,128)(2,1)} %bitcast.159), calls=%async_computation.2 | async-start | bytes 8388608 | tf_op jit(solution)/shard_map/all_to_all | solution.py:123
  430.5 51.4 %copy-start.13 = (bf16[1,512,512]{2,1,0:T(8,128)(2,1)S(1)}, bf16[1,512,512]{2,1,0:T(8,128)(2,1)}, u32[]{:S(2)}) copy-start(bf16[1,512,512]{2,1,0:T(8,128)(2,1)} %param.19) | copy-start | bytes 1572868
  482.1 2.6 copy-start.7
  484.6 53.6 %all-to-all-start.3 = ((bf16[8,512,512]{1,2,0:T(8,128)(2,1)}), bf16[8,512,512]{1,2,0:T(8,128)(2,1)}, u32[]{:S(2)}, u32[]{:S(2)}) async-start(bf16[8,512,512]{1,2,0:T(8,128)(2,1)} %broadcast_in_dim.61), calls=%async_computation.3 | async-start | bytes 8388608 | tf_op jit(solution)/shard_map/all_to_all | solution.py:115
  543.2 3.6 copy-start.3
  563.5 3.2 copy-start.4
  593.4 2.3 copy-start.23
  614.4 6.5 copy-start.9
  635.1 53.1 %copy-start.1 = (s32[32]{0:T(128)S(1)}, s32[32]{0:T(128)}, u32[]{:S(2)}) copy-start(s32[32]{0:T(128)} %param.21) | copy-start | bytes 388
  686.2 1.0 copy-start.8

commit v6 on v0

v6 whole, which is shorter than its diff:
```python
import jax
import jax.numpy as jnp
from jax import lax
from jax.sharding import PartitionSpec as P

HD = 256
ROT = 64
LAYERS = 2


def layer_norm(values, gain, shift):
    mean = jnp.mean(values, axis=-1, keepdims=True)
    centred = values - mean
    var = jnp.mean(centred * centred, axis=-1, keepdims=True)
    return centred * lax.rsqrt(var + 1e-05) * gain + shift


def positions(segs):
    length = segs.shape[-1]
    index = jnp.broadcast_to(jnp.arange(length, dtype=jnp.int32), segs.shape)
    first = jnp.ones(segs.shape[:-1] + (1,), dtype=bool)
    flag = jnp.concatenate([first, segs[..., 1:] != segs[..., :-1]], axis=-1)
    start = lax.cummax(jnp.where(flag, index, 0), axis=segs.ndim - 1)
    return index - start


def rotate(values, pos):
    half = ROT // 2
    inverse = 10000.0 ** (-(jnp.arange(half, dtype=jnp.float32) * 2.0 / ROT))
    angle = pos[..., None].astype(jnp.float32) * inverse
    cosine = jnp.cos(angle)[..., None, :]
    sine = jnp.sin(angle)[..., None, :]
    first = values[..., :half]
    second = values[..., half:ROT]
    return jnp.concatenate(
        [first * cosine - second * sine, second * cosine + first * sine, values[..., ROT:]], axis=-1
    )


def shards(
    tokens,
    segment_ids,
    shard_map,
    trainer_qkv,
    trainer_up,
    qkv_bias,
    up_bias,
    dense_w,
    down_w,
    out_bias,
    norm_gain,
    norm_shift,
):
    n_tp = lax.axis_size("tp")
    rows, length, _ = tokens.shape
    block = trainer_qkv.shape[1]
    full_width = block * n_tp * lax.axis_size("seq")
    n_blocks = full_width // block
    heads_here = qkv_bias.shape[1] // (3 * HD)
    qkv_cols = qkv_bias.shape[1]

    wq = trainer_qkv.astype(jnp.bfloat16).reshape(LAYERS, block, n_tp, qkv_cols)
    wu = trainer_up.astype(jnp.bfloat16).reshape(LAYERS, block, n_tp, up_bias.shape[1])
    packed = jnp.concatenate([wq, wu], axis=-1)
    packed = lax.all_to_all(packed, "tp", split_axis=2, concat_axis=1, tiled=True)
    gathered = [lax.all_gather(packed[layer].reshape(n_tp * block, -1), "seq", axis=0, tiled=True) for layer in range(LAYERS)]

    pos = positions(segment_ids)
    index = jnp.arange(length, dtype=jnp.int32)
    mask = (index[None, :] <= index[:, None])[None] & (
        segment_ids[:, :, None] == segment_ids[:, None, :]
    )
    mask = mask[:, None]
    stream = tokens
    for layer in range(LAYERS):
        weights = gathered[layer]
        qkv_mat = weights[:, :qkv_cols]
        up_mat = weights[:, qkv_cols:]
        whole = lax.all_gather(stream, "tp", axis=2, tiled=True)
        permuted = jnp.take(whole.reshape(rows, length, n_blocks, block), shard_map, axis=2)
        permuted = permuted.reshape(rows * length, full_width).astype(jnp.float32)

        def norm_of(i):
            gain = jnp.take(norm_gain[layer, i].reshape(n_blocks, block), shard_map, axis=0)
            shift = jnp.take(norm_shift[layer, i].reshape(n_blocks, block), shard_map, axis=0)
            return layer_norm(permuted, gain.reshape(-1), shift.reshape(-1)).astype(jnp.bfloat16)

        attn_in = norm_of(0)
        mlp_in = norm_of(1)
        qkv = jnp.dot(attn_in, qkv_mat, preferred_element_type=jnp.float32) + qkv_bias[layer].astype(jnp.float32)
        qkv = qkv.reshape(rows, length, heads_here, 3, HD)
        query = rotate(qkv[:, :, :, 0], pos).astype(jnp.bfloat16)
        keys = rotate(qkv[:, :, :, 1], pos).astype(jnp.bfloat16)
        vals = qkv[:, :, :, 2].astype(jnp.bfloat16)
        scores = jnp.einsum(
            "rqhd,rkhd->rhqk", query, keys, preferred_element_type=jnp.float32
        ) / jnp.sqrt(jnp.float32(HD))
        scores = jnp.where(mask, scores, -jnp.inf)
        probs = jax.nn.softmax(scores, axis=-1).astype(jnp.bfloat16)
        ctx = jnp.einsum("rhqk,rkhd->rqhd", probs, vals, preferred_element_type=jnp.float32).astype(
            jnp.bfloat16
        )
        ctx = ctx.reshape(rows * length, heads_here * HD)
        up = jnp.dot(mlp_in, up_mat, preferred_element_type=jnp.float32) + up_bias[layer].astype(jnp.float32)
        hidden_units = jax.nn.gelu(up, approximate=False).astype(jnp.bfloat16)
        partial_terms = jnp.dot(ctx, dense_w[layer], preferred_element_type=jnp.float32) + jnp.dot(
            hidden_units, down_w[layer], preferred_element_type=jnp.float32
        )
        partial_terms = partial_terms.astype(jnp.bfloat16)
        if layer + 1 < LAYERS:
            partial_terms, gathered[layer + 1] = lax.optimization_barrier((partial_terms, gathered[layer + 1]))
        summed = lax.psum_scatter(partial_terms, "tp", scatter_dimension=1, tiled=True).astype(jnp.float32)
        flat_stream = stream.astype(jnp.float32).reshape(rows * length, -1)
        stream = (flat_stream + summed + out_bias[layer]).astype(jnp.bfloat16).reshape(rows, length, -1)
    return stream


def solution(mesh):
    in_specs = (
        P("seq", None, "tp"),
        P("seq", None),
        P(),
        P(None, ("seq", "tp"), None),
        P(None, ("seq", "tp"), None),
        P(None, "tp"),
        P(None, "tp"),
        P(None, "tp", None),
        P(None, "tp", None),
        P(None, "tp"),
        P(),
        P(),
    )
    out_specs = P("seq", None, "tp")
    return jax.shard_map(shards, mesh=mesh, in_specs=in_specs, out_specs=out_specs, check_vma=False)
```

time: 702 us -> 559 us (0.80); the launches traced: 689 us -> 553 us
  local copies, waits for them, and re-layouts: 140 us -> 60.4 us
  waiting for transfers between devices: 397 us -> 339 us
  starting transfers between devices: 22.5 us -> 5.71 us
  matrix products: 89.2 us -> 101 us
    all_gather x6 -> x4, waiting for transfers between devices: 256 us -> 213 us  [the longest x2 178 us: shards(): lax.all_gather(packed[layer].reshape(n_tp * block, -1), 'seq', axis=0, ti...]
    all_to_all x4 -> x1, local copies, waits for them, and re-layouts: 40.1 us -> 2.28 us  [shards(): lax.all_to_all(packed, 'tp', split_axis=2, concat_axis=1, tiled=True)]
    all_gather x4 -> x1, local copies, waits for them, and re-layouts: 41.2 us -> 3.95 us  [shards(): whole = lax.all_gather(stream, 'tp', axis=2, tiled=True)]
    gather x5 -> x10, local copies, waits for them, and re-layouts: 31.2 us -> 9.47 us  [the longest x2 4.87 us: shards(): jnp.take(whole.reshape(rows, length, n_blocks, block), shard_map, axis=2)]
    reduce_scatter x2, waiting for transfers between devices: 89 us -> 71.5 us  [shards(): lax.psum_scatter(partial_terms, 'tp', scatter_dimension=1, tiled=True)]
    all_to_all x4 -> x1, starting transfers between devices: 22.2 us -> 5.29 us  [shards(): lax.all_to_all(packed, 'tp', split_axis=2, concat_axis=1, tiled=True)]
    dot_general x2, matrix products: 47.7 us -> 63 us  [shards(): jnp.dot(hidden_units, down_w[layer], preferred_element_type=jnp.float32)]
    convert_element_type x0 -> x4, other arithmetic: none -> 12.8 us  [the longest x2 5.82 us: norm_of(): layer_norm(permuted, gain.reshape(-1), shift.reshape(-1))]
  transfers between devices with their start and end apart: 12 -> 7, of which waited for: 8 -> 6; matrix products, arithmetic and copies ran while one was open for 27% -> 18% of each run, Pallas kernels for 0% -> 0%
where the time goes in v6:
time: 559 us; the launch traced here: 553 us
  waiting for transfers between devices  339 us (61%)
  matrix products  101 us (18%)
  local copies, waits for them, and re-layouts  60.4 us (11%)
  other arithmetic  32.9 us (6%)
  between operations  14.1 us (3%)
  starting transfers between devices  5.71 us (1%)
    all_gather x2, waiting for transfers between devices, shards(): lax.all_gather(packed[layer].reshape(n_tp * block, -1), 'seq', axis=0, ti...  178 us
    reduce_scatter x2, waiting for transfers between devices, shards(): lax.psum_scatter(partial_terms, 'tp', scatter_dimension=1, tiled=True)  71.5 us
    dot_general x2, matrix products, shards(): jnp.dot(hidden_units, down_w[layer], preferred_element_type=jnp.float32)  63 us
    all_to_all x1, waiting for transfers between devices, shards(): lax.all_to_all(packed, 'tp', split_axis=2, concat_axis=1, tiled=True)  54 us
    all_gather x2, waiting for transfers between devices, shards(): whole = lax.all_gather(stream, 'tp', axis=2, tiled=True)  35 us
    dot_general x2, matrix products, shards(): jnp.dot(attn_in, qkv_mat, preferred_element_type=jnp.float32)  16.4 us
    unnamed x33, local copies, waits for them, and re-layouts  13.2 us
  transfers between devices with their start and end apart: 7, of which 6 were waited for; matrix products, arithmetic and copies ran while one was open for 18% of the time, Pallas kernels for 0%

profile of v6, /device:TPU:0, one launch (start us, length us, event | category | flops | bytes accessed | tf_op | source)
XLA Modules:
  0.0 553.4 jit_solution(5028571515839628539)
XLA Ops:
  6.5 3.8 convert_element_type.147
  10.3 3.3 reshape.470
  13.7 3.2 convert_element_type.146
  16.9 4.5 reshape.469
  21.4 3.2 pad_maximum_fusion
  24.6 2.5 copy.46
  27.1 5.3 all-to-all-start
  32.4 1.0 copy.45
  33.4 54.0 %all-to-all-done = bf16[2,64,4,3584]{3,1,0,2:T(8,128)(2,1)} async-done(((bf16[2,64,4,3584]{3,1,0,2:T(8,128)(2,1)}), bf16[2,64,4,3584]{3,1,0,2:T(8,128)(2,1)}, u32[]{:S(2)}, u32[]{:S(2)}) %all-to-all-start) | async-done | bytes 3670048 | tf_op jit(solution)/shard_map/all_to_all | solution.py:65
  87.4 2.3 copy.76
  89.7 2.0 fusion.227
  91.8 0.7 all-gather.10.cloned.1.call-update
  93.2 0.6 gather_fusion.6
  93.7 0.6 gather_fusion.2
  94.4 0.6 gather_fusion.3
  95.0 0.6 gather_fusion.4
  95.7 0.6 gather_fusion.7
  96.3 0.6 gather_fusion.8
  97.0 0.6 gather_fusion.9
  97.6 0.6 gather_fusion.1
  99.6 0.9 fusion.89
  100.5 1.7 multiply_cosine_fusion
  102.3 2.6 gather_fusion
  104.9 0.7 convert_reduce_fusion
  105.6 0.9 multiply_reduce_fusion.1
  106.6 2.8 add_convert_fusion.5
  109.4 119.0 %all-gather.8.cloned.1.call-done = bf16[2048,3584]{1,0:T(8,128)(2,1)} async-done(((bf16[256,3584]{1,0:T(8,128)(2,1)}), bf16[2048,3584]{1,0:T(8,128)(2,1)}) %all-gather.8.cloned.1.call-update) | async-done | bytes 14680080 | tf_op jit(solution)/shard_map/all_gather | solution.py:66
  228.4 8.5 %fusion.41 = f32[512,1536]{1,0:T(8,128)} fusion(bf16[512,2048]{0,1:T(8,128)(2,1)} %get-tuple-element.29, bf16[2048,3584]{1,0:T(8,128)(2,1)} %all-gather.8.cloned.1.call-done, f32[1536]{0:T(1024)S(1)} %get-tuple-element.20), kind=kOutput, calls=%fused_computation.81 | convolution fusion | flops 3222011904 | bytes 11540480 | tf_op jit(solution)/shard_map/dot_general | solution.py:90
  236.9 3.0 copy.48
  240.0 1.6 fusion.229
  241.5 2.5 copy.62
  244.1 2.6 copy.61
  246.6 2.3 fusion.94
  248.9 2.3 fusion.93
  251.2 3.0 fusion.125
  254.2 4.4 fusion.231
  258.6 2.8 convolution_convert_fusion.1
  261.4 36.6 %fusion.6 = f32[512,2048]{1,0:T(8,128)} fusion(bf16[2,2048,2048]{2,1,0:T(8,128)(2,1)} %param.24, bf16[512,2048]{0,1:T(8,128)(2,1)} %get-tuple-element.30, bf16[2048,3584]{1,0:T(8,128)(2,1)} %all-gather.8.cloned.1.call-done, f32[2048]{0:T(1024)S(1)} %bitcast.163), kind=kOutput, calls=%fused_computation.16 | convolution fusion | flops 8659140608 | bytes 23076864 | tf_op jit(solution)/shard_map/dot_general | solution.py:106
  298.1 5.5 add_convert_fusion.3
  303.6 58.7 %all-gather.10.cloned.1.call-done = bf16[2048,3584]{1,0:T(8,128)(2,1)} async-done(((bf16[256,3584]{1,0:T(8,128)(2,1)}), bf16[2048,3584]{1,0:T(8,128)(2,1)}) %all-gather.10.cloned.1.call-update) | async-done | bytes 14680080 | tf_op jit(solution)/shard_map/all_gather | solution.py:66
  362.3 36.2 %reduce-scatter.3.cloned.1.call-done = bf16[512,512]{1,0:T(8,128)(2,1)} async-done(((bf16[512,2048]{1,0:T(8,128)(2,1)}), bf16[512,512]{1,0:T(8,128)(2,1)}) %reduce-scatter.3.cloned.1.call-update) | async-done | bytes 524304 | tf_op jit(solution)/shard_map/reduce_scatter | solution.py:112
  398.5 2.0 fusion.84
  400.9 35.0 %all-gather.12.cloned.1.call-done = bf16[512,2048]{1,0:T(8,128)(2,1)} async-done(((bf16[512,512]{1,0:T(8,128)(2,1)}), bf16[512,2048]{1,0:T(8,128)(2,1)}) %all-gather.12.cloned.1.call-update) | async-done | bytes 2097168 | tf_op jit(solution)/shard_map/all_gather | solution.py:79
  435.9 3.9 copy.53
  439.8 2.3 gather_fusion.5
  442.1 0.7 convert_reduce_fusion.1
  442.8 0.9 multiply_reduce_fusion
  443.8 3.0 add_convert_fusion.2
  446.7 7.9 %fusion.38 = f32[512,1536]{1,0:T(8,128)} fusion(bf16[512,2048]{0,1:T(8,128)(2,1)S(1)} %get-tuple-element.27, bf16[2048,3584]{1,0:T(8,128)(2,1)} %all-gather.10.cloned.1.call-done, f32[1536]{0:T(1024)S(1)} %get-tuple-element.19), kind=kOutput, calls=%fused_computation.80 | convolution fusion | flops 3222011904 | bytes 11540480 | tf_op jit(solution)/shard_map/dot_general | solution.py:90
  454.6 2.6 copy.54
  457.2 1.5 fusion.228
  458.7 2.5 copy.64
  461.2 2.2 fusion.96
  463.5 2.6 copy.63
  466.0 3.0 fusion.129
  469.0 2.3 fusion.95
  471.3 26.3 %fusion.4 = f32[512,2048]{1,0:T(8,128)} fusion(bf16[2,2048,2048]{2,1,0:T(8,128)(2,1)} %param.24, bf16[512,2048]{0,1:T(8,128)(2,1)} %get-tuple-element.28, bf16[2048,3584]{1,0:T(8,128)(2,1)} %all-gather.10.cloned.1.call-done, f32[2048]{0:T(1024)S(1)} %bitcast.162), kind=kOutput, calls=%fused_computation.14 | convolution fusion | flops 8659140608 | bytes 23076864 | tf_op jit(solution)/shard_map/dot_general | solution.py:106
  497.6 4.3 fusion.236
  502.0 2.2 convolution_convert_fusion
  504.2 0.6 copy-done.1
  504.8 1.3 copy-done.2
  506.1 2.7 add_convert_fusion
  508.8 35.4 %reduce-scatter.5.cloned.1.call-done = bf16[512,512]{1,0:T(8,128)(2,1)} async-done(((bf16[512,2048]{1,0:T(8,128)(2,1)}), bf16[512,512]{1,0:T(8,128)(2,1)}) %reduce-scatter.5.cloned.1.call-update) | async-done | bytes 524304 | tf_op jit(solution)/shard_map/reduce_scatter | solution.py:112
  544.2 2.0 fusion.92
  (76 shorter events, 3.0 us)
Async XLA Ops:
  27.1 5.3 copy-start.3
  27.1 60.4 %all-to-all-start = ((bf16[2,64,4,3584]{3,1,0,2:T(8,128)(2,1)}), bf16[2,64,4,3584]{3,1,0,2:T(8,128)(2,1)}, u32[]{:S(2)}, u32[]{:S(2)}) async-start(bf16[2,64,4,3584]{3,1,0,2:T(8,128)(2,1)} %copy.46), calls=%async_computation | async-start | bytes 7340032 | tf_op jit(solution)/shard_map/all_to_all | solution.py:65
  32.4 69.9 %all-gather.6.cloned.1.call-start = ((), (), s32[]{:S(2)}) async-start(), calls=%async_computation.3 | async-start | bytes 2621440 | tf_op jit(solution)/shard_map/all_gather | solution.py:79
  33.4 195.0 %all-gather.8.cloned.1.call-start = ((), (), s32[]{:S(2)}) async-start(), calls=%async_computation.4 | async-start | bytes 16515072 | tf_op jit(solution)/shard_map/all_gather | solution.py:66
  89.7 3.1 copy-start.9
  89.7 3.1 copy-start.10
  89.7 3.4 copy-start.13
  91.8 6.8 %copy-start.7 = (s32[1,512]{1,0:T(1,128)S(1)}, s32[1,512]{1,0:T(1,128)}, u32[]{:S(2)}) copy-start(s32[1,512]{1,0:T(1,128)} %param.17) | copy-start | bytes 6148
  91.8 7.7 %copy-start.11 = (bf16[2,1536]{1,0:T(2,128)(2,1)S(1)}, bf16[2,1536]{1,0:T(2,128)(2,1)}, u32[]{:S(2)}) copy-start(bf16[2,1536]{1,0:T(2,128)(2,1)} %param.21) | copy-start | bytes 18436
  91.8 10.5 %copy-start.8 = (bf16[2,2048]{1,0:T(2,128)(2,1)S(1)}, bf16[2,2048]{1,0:T(2,128)(2,1)}, u32[]{:S(2)}) copy-start(bf16[2,2048]{1,0:T(2,128)(2,1)} %param.22) | copy-start | bytes 24580
  91.8 270.4 %all-gather.10.cloned.1.call-start = ((), (), s32[]{:S(2)}) async-start(), calls=%async_computation.5 | async-start | bytes 16515072 | tf_op jit(solution)/shard_map/all_gather | solution.py:66
  92.5 306.0 %reduce-scatter.3.cloned.1.call-start = ((), (), s32[]{:S(2)}) async-start(), calls=%async_computation.6 | async-start | bytes 2621440 | tf_op jit(solution)/shard_map/reduce_scatter | solution.py:112
  261.4 36.6 %copy-start.5 = (bf16[2,256,512]{2,1,0:T(8,128)(2,1)S(1)}, bf16[2,256,512]{2,1,0:T(8,128)(2,1)}, u32[]{:S(2)}) copy-start(bf16[2,256,512]{2,1,0:T(8,128)(2,1)} %convolution_convert_fusion.1) | copy-start | bytes 1572868
  298.1 64.2 %copy-start.12 = (f32[2,512]{1,0:T(2,128)S(1)}, f32[2,512]{1,0:T(2,128)}, u32[]{:S(2)}) copy-start(f32[2,512]{1,0:T(2,128)} %param.25) | copy-start | bytes 12292
  298.1 100.4 %copy-start.4 = (bf16[1,512,512]{2,1,0:T(8,128)(2,1)S(1)}, bf16[1,512,512]{2,1,0:T(8,128)(2,1)}, u32[]{:S(2)}) copy-start(bf16[1,512,512]{2,1,0:T(8,128)(2,1)} %param.16) | copy-start | bytes 1572868
  362.3 73.6 %all-gather.12.cloned.1.call-start = ((), (), s32[]{:S(2)}) async-start(), calls=%async_computation.8 | async-start | bytes 2621440 | tf_op jit(solution)/shard_map/all_gather | solution.py:79
  400.5 143.6 %reduce-scatter.5.cloned.1.call-start = ((), (), s32[]{:S(2)}) async-start(), calls=%async_computation.7 | async-start | bytes 2621440 | tf_op jit(solution)/shard_map/reduce_scatter | solution.py:112
  471.3 26.3 %copy-start.6 = (bf16[512,2,32]{2,0,1:T(8,128)(2,1)S(1)}, bf16[512,2,32]{2,0,1:T(8,128)(2,1)}, u32[]{:S(2)}) copy-start(bf16[512,2,32]{2,0,1:T(8,128)(2,1)} %get-tuple-element.31) | copy-start | bytes 196612
  502.0 2.8 copy-start.1
  502.0 4.1 copy-start.2
  506.1 38.1 %copy-start = (bf16[512,512]{1,0:T(8,128)(2,1)S(1)}, bf16[512,512]{1,0:T(8,128)(2,1)}, u32[]{:S(2)}) copy-start(bf16[512,512]{1,0:T(8,128)(2,1)} %fusion.84) | copy-start | bytes 1572868
Sparse Core Ops, SparseCore 0:
  35.0 57.2 all-gather.5
  94.0 134.3 all-gather.7
  230.0 132.1 all-gather.9
  365.0 33.4 reduce-scatter.2
  400.7 35.1 all-gather.11
  508.9 35.1 reduce-scatter.4

commit v7 on v6

--- a/solution.py
+++ b/solution.py
@@ -61,9 +61,24 @@
 
     wq = trainer_qkv.astype(jnp.bfloat16).reshape(LAYERS, block, n_tp, qkv_cols)
     wu = trainer_up.astype(jnp.bfloat16).reshape(LAYERS, block, n_tp, up_bias.shape[1])
-    packed = jnp.concatenate([wq, wu], axis=-1)
-    packed = lax.all_to_all(packed, "tp", split_axis=2, concat_axis=1, tiled=True)
-    gathered = [lax.all_gather(packed[layer].reshape(n_tp * block, -1), "seq", axis=0, tiled=True) for layer in range(LAYERS)]
+    packed = jnp.concatenate([wq, wu], axis=-1).transpose(0, 2, 1, 3).reshape(LAYERS, n_tp, -1)
+    cols = packed.shape[2] // block
+    width_here = tokens.shape[2]
+
+    def exchange(x):
+        return lax.all_to_all(x, "tp", split_axis=0, concat_axis=0, tiled=True)
+
+    def spread(local):
+        return jnp.broadcast_to(local.reshape(1, -1), (n_tp, local.size))
+
+    def joined(got):
+        got = got.reshape(n_tp, rows, length, width_here).transpose(1, 2, 0, 3)
+        return got.reshape(rows, length, n_tp * width_here)
+
+    first = exchange(jnp.concatenate([packed[0], spread(tokens)], axis=1))
+    pieces = [first[:, : block * cols]] + [exchange(packed[layer]) for layer in range(1, LAYERS)]
+    whole = joined(first[:, block * cols :])
+    gathered = [lax.all_gather(piece.reshape(n_tp * block, cols), "seq", axis=0, tiled=True) for piece in pieces]
 
     pos = positions(segment_ids)
     index = jnp.arange(length, dtype=jnp.int32)
@@ -76,7 +91,8 @@
         weights = gathered[layer]
         qkv_mat = weights[:, :qkv_cols]
         up_mat = weights[:, qkv_cols:]
-        whole = lax.all_gather(stream, "tp", axis=2, tiled=True)
+        if layer > 0:
+            whole = joined(exchange(spread(stream)))
         permuted = jnp.take(whole.reshape(rows, length, n_blocks, block), shard_map, axis=2)
         permuted = permuted.reshape(rows * length, full_width).astype(jnp.float32)
 
@@ -108,8 +124,10 @@
         )
         partial_terms = partial_terms.astype(jnp.bfloat16)
         if layer + 1 < LAYERS:
-            partial_terms, gathered[layer + 1] = lax.optimization_barrier((partial_terms, gathered[layer + 1]))
-        summed = lax.psum_scatter(partial_terms, "tp", scatter_dimension=1, tiled=True).astype(jnp.float32)
+            split = partial_terms.reshape(rows * length, n_tp, width_here).transpose(1, 0, 2)
+            summed = jnp.sum(exchange(split).astype(jnp.float32), axis=0)
+        else:
+            summed = lax.psum_scatter(partial_terms, "tp", scatter_dimension=1, tiled=True).astype(jnp.float32)
         flat_stream = stream.astype(jnp.float32).reshape(rows * length, -1)
         stream = (flat_stream + summed + out_bias[layer]).astype(jnp.bfloat16).reshape(rows, length, -1)
     return stream

time: 559 us -> 536 us (0.959)
  waiting for transfers between devices: 339 us -> 125 us
  blocking collectives: 0 us -> 77.9 us
  other arithmetic: 32.9 us -> 101 us
  local copies, waits for them, and re-layouts: 60.4 us -> 112 us
  matrix products: 101 us -> 94 us
    all_gather x4 -> x2, waiting for transfers between devices: 213 us -> 45.3 us  [shards(): lax.all_gather(piece.reshape(n_tp * block, cols), 'seq', axis=0, tiled=True)]
    all_to_all x0 -> x2, blocking collectives: none -> 77.9 us  [exchange(): return lax.all_to_all(x, 'tp', split_axis=0, concat_axis=0, tiled=True)]
    all_to_all x0 -> x5, other arithmetic: none -> 63.2 us  [exchange(): return lax.all_to_all(x, 'tp', split_axis=0, concat_axis=0, tiled=True)]
    unnamed x33 -> x51, local copies, waits for them, and re-layouts: 13.2 us -> 56.8 us
    reduce_scatter x2 -> x1, waiting for transfers between devices: 71.5 us -> 33.1 us  [shards(): lax.psum_scatter(partial_terms, 'tp', scatter_dimension=1, tiled=True)]
    broadcast_in_dim x0 -> x1, other arithmetic: none -> 14.2 us  [spread(): return jnp.broadcast_to(local.reshape(1, -1), (n_tp, local.size))]
    dot_general x2, matrix products: 63 us -> 52.4 us  [shards(): jnp.dot(hidden_units, down_w[layer], preferred_element_type=jnp.float32)]
    reshape x0 -> x3, local copies, waits for them, and re-layouts: none -> 7.22 us  [the longest x2 5.73 us: shards(): piece.reshape(n_tp * block, cols)]
  transfers between devices with their start and end apart: 7 -> 5, of which waited for: 6 -> 4; matrix products, arithmetic and copies ran while one was open for 18% -> 34% of each run, Pallas kernels for 0% -> 0%
where the time goes in v7:
time: 536 us; the launch traced here: 532 us
  waiting for transfers between devices  125 us (23%)
  local copies, waits for them, and re-layouts  112 us (21%)
  other arithmetic  101 us (19%)
  matrix products  94 us (18%)
  blocking collectives  77.9 us (15%)
  between operations  13.7 us (3%)
  starting transfers between devices  7.77 us (1%)
    all_to_all x2, blocking collectives, exchange(): return lax.all_to_all(x, 'tp', split_axis=0, concat_axis=0, tiled=True)  77.9 us
    all_to_all x5, other arithmetic, exchange(): return lax.all_to_all(x, 'tp', split_axis=0, concat_axis=0, tiled=True)  63.2 us
    unnamed x51, local copies, waits for them, and re-layouts  56.8 us
    dot_general x2, matrix products, shards(): jnp.dot(hidden_units, down_w[layer], preferred_element_type=jnp.float32)  52.4 us
    all_to_all x2, waiting for transfers between devices, exchange(): return lax.all_to_all(x, 'tp', split_axis=0, concat_axis=0, tiled=True)  46.9 us
    all_gather x2, waiting for transfers between devices, shards(): lax.all_gather(piece.reshape(n_tp * block, cols), 'seq', axis=0, tiled=True)  45.3 us
    reduce_scatter x1, waiting for transfers between devices, shards(): lax.psum_scatter(partial_terms, 'tp', scatter_dimension=1, tiled=True)  33.1 us
    dot_general x2, matrix products, shards(): jnp.dot(attn_in, qkv_mat, preferred_element_type=jnp.float32)  17.1 us
  transfers between devices with their start and end apart: 5, of which 4 were waited for; matrix products, arithmetic and copies ran while one was open for 34% of the time, Pallas kernels for 0%

profile of v7, /device:TPU:0, one launch (start us, length us, event | category | flops | bytes accessed | tf_op | source)
XLA Modules:
  0.0 532.1 jit_solution(12812199045323885447)
XLA Ops:
  6.5 2.6 convert_element_type.152
  10.3 1.6 fusion.230
  11.9 1.4 copy.91
  13.6 13.5 %maximum_bitcast_fusion = bf16[4,1,491520]{2,0,1:T(4,128)(2,1)} fusion(bf16[4,229376]{1,0:T(4,128)(2,1)S(1)} %bitcast.213, bf16[491520]{0:T(1024)(128)(2,1)S(1)} %pad.15.clone), kind=kLoop, calls=%fused_computation.77 | loop fusion | flops 7864320 | bytes 6750208 | tf_op jit(solution)/shard_map/all_to_all | solution.py:69
  27.7 9.3 %reduce.54 = bf16[4,491520]{1,0:T(4,128)(2,1)} reduce(bf16[4,1,491520]{2,0,1:T(4,128)(2,1)} %maximum_bitcast_fusion, bf16[]{:T(256)} %broadcast.636), dimensions={1}, to_apply=%copy.64.reduce_sub_computation | reduce | bytes 7864322 | tf_op jit(solution)/shard_map/all_to_all | solution.py:69
  37.0 7.9 %reshape.708 = bf16[4,2,245760]{2,1,0:T(2,128)(2,1)} reshape(bf16[4,491520]{1,0:T(4,128)(2,1)} %reduce.54) | data formatting | bytes 7864320
  44.9 52.7 %all_to_all.33 = bf16[4,2,245760]{2,1,0:T(2,128)(2,1)} all-to-all(bf16[4,2,245760]{2,1,0:T(2,128)(2,1)} %reshape.708), channel_id=1, replica_groups=mesh['seq'=8,'tp'=4] {'tp'}, dimensions={0} | all-to-all | bytes 7864320 | tf_op jit(solution)/shard_map/all_to_all | solution.py:69
  97.6 7.1 %reshape.709 = bf16[4,1,491520]{2,1,0:T(2,128)(2,1)} reshape(bf16[4,2,245760]{2,1,0:T(2,128)(2,1)} %all_to_all.33) | data formatting | bytes 7864320
  104.7 9.7 %copy.112 = bf16[4,1,491520]{2,0,1:T(4,128)(2,1)S(1)} copy(bf16[4,1,491520]{2,1,0:T(2,128)(2,1)} %reshape.709) | data formatting | bytes 7864320
  114.4 1.9 copy-done
  116.9 2.9 reshape.517
  119.9 4.4 all_to_all.28
  124.3 14.5 %reduce.56 = bf16[4,229376]{1,0:T(4,128)(2,1)} reduce(bf16[4,1,229376]{2,1,0:T(2,128)(2,1)} %all_to_all.28, bf16[]{:T(256)} %broadcast.636), dimensions={1}, to_apply=%all_to_all.28.reduce_sub_computation | reduce | bytes 3670018 | tf_op jit(solution)/shard_map/all_to_all | solution.py:69
  138.7 3.4 reshape.712
  142.1 25.2 %all_to_all.34 = bf16[4,2,114688]{2,1,0:T(2,128)(2,1)} all-to-all(bf16[4,2,114688]{2,1,0:T(2,128)(2,1)S(1)} %reshape.712), channel_id=1, replica_groups=mesh['seq'=8,'tp'=4] {'tp'}, dimensions={0} | all-to-all | bytes 3670016 | tf_op jit(solution)/shard_map/all_to_all | solution.py:69
  167.3 4.7 reshape.713
  172.1 12.5 %reduce.22 = bf16[4,229376]{1,0:T(4,128)(2,1)S(1)} reduce(bf16[4,1,229376]{2,1,0:T(2,128)(2,1)} %reshape.713, bf16[]{:T(256)} %constant.121), dimensions={1}, to_apply=%all_to_all.27.reduce_sub_computation | reduce | bytes 3670018 | tf_op jit(solution)/shard_map/all_to_all | solution.py:69
  184.6 2.9 reshape.529
  195.2 1.7 multiply_cosine_fusion
  196.9 2.0 slice.221
  199.4 2.4 copy.65
  201.8 2.3 gather_fusion
  205.7 2.8 add_convert_fusion.5
  208.5 45.3 %all-gather.3.cloned.1.call-done = bf16[2048,3584]{1,0:T(8,128)(2,1)} async-done(((bf16[256,3584]{1,0:T(8,128)(2,1)}), bf16[2048,3584]{1,0:T(8,128)(2,1)}) %all-gather.3.cloned.1.call-update) | async-done | bytes 14680080 | tf_op jit(solution)/shard_map/all_gather | solution.py:81
  253.8 8.5 %fusion.38 = f32[512,1536]{1,0:T(8,128)} fusion(bf16[512,2048]{0,1:T(8,128)(2,1)} %get-tuple-element.25, bf16[2048,3584]{1,0:T(8,128)(2,1)} %all-gather.3.cloned.1.call-done, f32[1536]{0:T(1024)S(1)} %get-tuple-element.16), kind=kOutput, calls=%fused_computation.82 | convolution fusion | flops 3222011904 | bytes 11540480 | tf_op jit(solution)/shard_map/dot_general | solution.py:106
  262.4 2.9 copy.66
  265.3 1.5 fusion.232
  266.8 2.5 copy.82
  269.4 2.5 copy.83
  271.9 2.3 fusion.95
  274.2 2.2 fusion.96
  276.4 3.1 fusion.128
  279.5 4.4 fusion.234
  283.9 2.8 convolution_convert_fusion.1
  286.7 26.8 %fusion.8 = f32[512,2048]{1,0:T(8,128)} fusion(bf16[2,2048,2048]{2,1,0:T(8,128)(2,1)} %param.24, bf16[512,2048]{0,1:T(8,128)(2,1)} %get-tuple-element.26, bf16[2048,3584]{1,0:T(8,128)(2,1)} %all-gather.3.cloned.1.call-done, f32[2048]{0:T(1024)S(1)} %bitcast.237), kind=kOutput, calls=%fused_computation.18 | convolution fusion | flops 8659140608 | bytes 23076864 | tf_op jit(solution)/shard_map/dot_general | solution.py:122
  313.6 4.1 add_convert_fusion.3
  317.7 1.5 copy.115
  319.2 4.1 all-to-all-start.1
  323.4 1.2 copy.96
  324.8 1.3 copy.94
  326.1 22.6 %all-to-all-done.1 = bf16[4,512,512]{2,1,0:T(8,128)(2,1)S(1)} async-done(((bf16[4,512,512]{2,1,0:T(8,128)(2,1)}), bf16[4,512,512]{2,1,0:T(8,128)(2,1)S(1)}, u32[]{:S(2)}, u32[]{:S(2)}) %all-to-all-start.1) | async-done | bytes 2097184 | tf_op jit(solution)/shard_map/all_to_all | solution.py:69
  350.4 4.6 broadcast_in_dim.49
  355.0 14.2 %reduce.55 = bf16[4,262144]{1,0:T(4,128)(2,1)S(1)} reduce(bf16[4,1,262144]{2,1,0:T(2,128)(2,1)} %broadcast_in_dim.49, bf16[]{:T(256)} %broadcast.636), dimensions={1}, to_apply=%broadcast_in_dim.49.reduce_sub_computation | reduce | bytes 4194306 | tf_op jit(solution)/shard_map/broadcast_in_dim | solution.py:72
  369.2 3.4 reshape.710
  372.6 3.6 all-to-all-start.2
  376.6 24.3 %all-to-all-done.2 = bf16[4,2,131072]{2,1,0:T(2,128)(2,1)S(1)} async-done(((bf16[4,2,131072]{2,1,0:T(2,128)(2,1)}), bf16[4,2,131072]{2,1,0:T(2,128)(2,1)S(1)}, u32[]{:S(2)}, u32[]{:S(2)}) %all-to-all-start.2) | async-done | bytes 2097184 | tf_op jit(solution)/shard_map/all_to_all | solution.py:69
  400.9 3.5 reshape.711
  404.5 13.5 %reduce.19 = bf16[4,262144]{1,0:T(4,128)(2,1)S(1)} reduce(bf16[4,1,262144]{2,1,0:T(2,128)(2,1)} %reshape.711, bf16[]{:T(256)} %constant.121), dimensions={1}, to_apply=%all_to_all.25.reduce_sub_computation | reduce | bytes 4194306 | tf_op jit(solution)/shard_map/all_to_all | solution.py:69
  418.0 1.7 copy.113
  419.7 4.2 copy.72
  423.9 2.3 gather_fusion.5
  427.8 2.8 add_convert_fusion.2
  430.6 8.5 %fusion.41 = f32[512,1536]{1,0:T(8,128)} fusion(bf16[512,2048]{0,1:T(8,128)(2,1)} %get-tuple-element.23, bf16[2048,3584]{1,0:T(8,128)(2,1)} %all-gather.5.cloned.1.call-done, f32[1536]{0:T(1024)S(1)} %get-tuple-element.15), kind=kOutput, calls=%fused_computation.83 | convolution fusion | flops 3222011904 | bytes 11540480 | tf_op jit(solution)/shard_map/dot_general | solution.py:106
  439.1 3.9 copy.74
  443.1 2.8 fusion.231
  446.2 1.6 copy.85
  447.8 1.0 fusion.97
  448.8 2.4 fusion.132
  451.4 4.2 fusion.239
  455.6 3.3 convolution_convert_fusion
  458.9 25.6 %fusion.6 = f32[512,2048]{1,0:T(8,128)} fusion(bf16[2,2048,2048]{2,1,0:T(8,128)(2,1)} %param.24, bf16[512,2048]{0,1:T(8,128)(2,1)S(1)} %copy-done.7, bf16[2048,3584]{1,0:T(8,128)(2,1)} %all-gather.5.cloned.1.call-done, f32[2048]{0:T(1024)S(1)} %bitcast.236), kind=kOutput, calls=%fused_computation.16 | convolution fusion | flops 8659140608 | bytes 23076864 | tf_op jit(solution)/shard_map/dot_general | solution.py:122
  484.5 5.7 %add_convert_fusion = bf16[512,2048]{1,0:T(8,128)(2,1)} fusion(f32[512,2048]{1,0:T(8,128)} %fusion.6, bf16[512,512]{0,1:T(8,128)(2,1)} %bitcast.229, bf16[2,512,2048]{2,1,0:T(8,128)(2,1)} %param.23), kind=kOutput, calls=%fused_computation.38 | convolution fusion | flops 1075838976 | bytes 8912896 | tf_op jit(solution)/shard_map/dot_general | solution.py:122
  490.2 33.1 %reduce-scatter.2.cloned.1.call-done = bf16[512,512]{1,0:T(8,128)(2,1)} async-done(((bf16[512,2048]{1,0:T(8,128)(2,1)}), bf16[512,512]{1,0:T(8,128)(2,1)}) %reduce-scatter.2.cloned.1.call-update) | async-done | bytes 524304 | tf_op jit(solution)/shard_map/reduce_scatter | solution.py:130
  523.3 2.1 fusion.94
  (105 shorter events, 17.0 us)
Async XLA Ops:
  6.5 3.2 copy-start.6
  6.5 247.3 %all-gather.3.cloned.1.call-start = ((), (), s32[]{:S(2)}) async-start(), calls=%async_computation.5 | async-start | bytes 16515072 | tf_op jit(solution)/shard_map/all_gather | solution.py:81
  10.3 3.1 copy-start.1
  114.4 1.9 copy-start
  119.8 310.8 %all-gather.5.cloned.1.call-start = ((), (), s32[]{:S(2)}) async-start(), calls=%async_computation.6 | async-start | bytes 16515072 | tf_op jit(solution)/shard_map/all_gather | solution.py:81
  172.1 15.4 %copy-start.11 = (f32[2,2,2048]{2,1,0:T(2,128)S(1)}, f32[2,2,2048]{2,1,0:T(2,128)}, u32[]{:S(2)}) copy-start(f32[2,2,2048]{2,1,0:T(2,128)} %param.27) | copy-start | bytes 98308
  172.1 15.4 %copy-start.12 = (f32[2,2,2048]{2,1,0:T(2,128)S(1)}, f32[2,2,2048]{2,1,0:T(2,128)}, u32[]{:S(2)}) copy-start(f32[2,2,2048]{2,1,0:T(2,128)} %param.26) | copy-start | bytes 98308
  184.6 3.3 copy-start.15
  184.6 8.7 %copy-start.9 = (s32[1,512]{1,0:T(1,128)S(1)}, s32[1,512]{1,0:T(1,128)}, u32[]{:S(2)}) copy-start(s32[1,512]{1,0:T(1,128)} %param.17) | copy-start | bytes 6148
  184.6 9.5 %copy-start.13 = (bf16[2,1536]{1,0:T(2,128)(2,1)S(1)}, bf16[2,1536]{1,0:T(2,128)(2,1)}, u32[]{:S(2)}) copy-start(bf16[2,1536]{1,0:T(2,128)(2,1)} %param.21) | copy-start | bytes 18436
  184.6 12.3 %copy-start.10 = (bf16[2,2048]{1,0:T(2,128)(2,1)S(1)}, bf16[2,2048]{1,0:T(2,128)(2,1)}, u32[]{:S(2)}) copy-start(bf16[2,2048]{1,0:T(2,128)(2,1)} %param.22) | copy-start | bytes 24580
  286.7 26.8 %copy-start.8 = (bf16[2,256,512]{2,1,0:T(8,128)(2,1)S(1)}, bf16[2,256,512]{2,1,0:T(8,128)(2,1)}, u32[]{:S(2)}) copy-start(bf16[2,256,512]{2,1,0:T(8,128)(2,1)} %convolution_convert_fusion.1) | copy-start | bytes 1572868
  317.7 5.6 %copy-start.14 = (f32[2,512]{1,0:T(2,128)S(1)}, f32[2,512]{1,0:T(2,128)}, u32[]{:S(2)}) copy-start(f32[2,512]{1,0:T(2,128)} %param.25) | copy-start | bytes 12292
  319.2 5.5 %copy-start.2 = (bf16[1,512,512]{2,1,0:T(8,128)(2,1)S(1)}, bf16[1,512,512]{2,1,0:T(8,128)(2,1)}, u32[]{:S(2)}) copy-start(bf16[1,512,512]{2,1,0:T(8,128)(2,1)} %param.16) | copy-start | bytes 1572868
  319.2 29.5 %all-to-all-start.1 = ((bf16[4,512,512]{2,1,0:T(8,128)(2,1)}), bf16[4,512,512]{2,1,0:T(8,128)(2,1)S(1)}, u32[]{:S(2)}, u32[]{:S(2)}) async-start(bf16[4,512,512]{2,1,0:T(8,128)(2,1)} %bitcast.209), calls=%async_computation.1 | async-start | bytes 4194304 | tf_op jit(solution)/shard_map/all_to_all | solution.py:69
  348.7 1.2 copy-start.4
  348.7 1.6 copy-start.5
  372.6 28.3 %all-to-all-start.2 = ((bf16[4,2,131072]{2,1,0:T(2,128)(2,1)}), bf16[4,2,131072]{2,1,0:T(2,128)(2,1)S(1)}, u32[]{:S(2)}, u32[]{:S(2)}) async-start(bf16[4,2,131072]{2,1,0:T(2,128)(2,1)} %reshape.710), calls=%async_computation.2 | async-start | bytes 4194304 | tf_op jit(solution)/shard_map/all_to_all | solution.py:69
  376.2 147.0 %reduce-scatter.2.cloned.1.call-start = ((), (), s32[]{:S(2)}) async-start(), calls=%async_computation.7 | async-start | bytes 2621440 | tf_op jit(solution)/shard_map/reduce_scatter | solution.py:130
  455.6 3.3 copy-start.7
  484.5 38.8 %copy-start.3 = (bf16[1,512,512]{2,1,0:T(8,128)(2,1)S(1)}, bf16[1,512,512]{2,1,0:T(8,128)(2,1)}, u32[]{:S(2)}) copy-start(bf16[1,512,512]{2,1,0:T(8,128)(2,1)} %param.16) | copy-start | bytes 1572868
Sparse Core Ops, SparseCore 0:
  120.0 133.8 all-gather.2
  255.5 132.1 all-gather.4
  490.3 32.8 reduce-scatter.1

commit v8 on v7

--- a/solution.py
+++ b/solution.py
@@ -75,9 +75,8 @@
         got = got.reshape(n_tp, rows, length, width_here).transpose(1, 2, 0, 3)
         return got.reshape(rows, length, n_tp * width_here)
 
-    first = exchange(jnp.concatenate([packed[0], spread(tokens)], axis=1))
-    pieces = [first[:, : block * cols]] + [exchange(packed[layer]) for layer in range(1, LAYERS)]
-    whole = joined(first[:, block * cols :])
+    pieces = [exchange(packed[layer]) for layer in range(LAYERS)]
+    whole = joined(exchange(spread(tokens)))
     gathered = [lax.all_gather(piece.reshape(n_tp * block, cols), "seq", axis=0, tiled=True) for piece in pieces]
 
     pos = positions(segment_ids)

time: 536 us -> 515 us (0.961)
  other arithmetic: 101 us -> 133 us
  waiting for transfers between devices: 125 us -> 94.4 us
  blocking collectives: 77.9 us -> 52.1 us
    all_gather x2, waiting for transfers between devices: 45.3 us -> 0.01 us  [shards(): lax.all_gather(piece.reshape(n_tp * block, cols), 'seq', axis=0, tiled=True)]
    all_to_all x2, blocking collectives: 77.9 us -> 52.1 us  [exchange(): return lax.all_to_all(x, 'tp', split_axis=0, concat_axis=0, tiled=True)]
    all_to_all x5 -> x6, other arithmetic: 63.2 us -> 80.8 us  [exchange(): return lax.all_to_all(x, 'tp', split_axis=0, concat_axis=0, tiled=True)]
    broadcast_in_dim x1 -> x2, other arithmetic: 14.2 us -> 28.4 us  [spread(): return jnp.broadcast_to(local.reshape(1, -1), (n_tp, local.size))]
    all_to_all x2 -> x3, waiting for transfers between devices: 46.9 us -> 58.9 us  [exchange(): return lax.all_to_all(x, 'tp', split_axis=0, concat_axis=0, tiled=True)]
    unnamed x51 -> x49, local copies, waits for them, and re-layouts: 56.8 us -> 45 us
    all_to_all x2 -> x3, starting transfers between devices: 7.68 us -> 11.4 us  [exchange(): return lax.all_to_all(x, 'tp', split_axis=0, concat_axis=0, tiled=True)]
  transfers between devices with their start and end apart: 5 -> 6, of which waited for: 4 -> 4; matrix products, arithmetic and copies ran while one was open for 34% -> 44% of each run, Pallas kernels for 0% -> 0%
where the time goes in v8:
time: 515 us; the launch traced here: 506 us
  other arithmetic  133 us (26%)
  local copies, waits for them, and re-layouts  107 us (21%)
  waiting for transfers between devices  94.4 us (18%)
  matrix products  94 us (18%)
  blocking collectives  52.1 us (10%)
  between operations  13.7 us (3%)
  starting transfers between devices  12 us (2%)
    all_to_all x6, other arithmetic, exchange(): return lax.all_to_all(x, 'tp', split_axis=0, concat_axis=0, tiled=True)  80.8 us
    all_to_all x3, waiting for transfers between devices, exchange(): return lax.all_to_all(x, 'tp', split_axis=0, concat_axis=0, tiled=True)  58.9 us
    dot_general x2, matrix products, shards(): jnp.dot(hidden_units, down_w[layer], preferred_element_type=jnp.float32)  52.4 us
    all_to_all x2, blocking collectives, exchange(): return lax.all_to_all(x, 'tp', split_axis=0, concat_axis=0, tiled=True)  52.1 us
    unnamed x49, local copies, waits for them, and re-layouts  45 us
    reduce_scatter x1, waiting for transfers between devices, shards(): lax.psum_scatter(partial_terms, 'tp', scatter_dimension=1, tiled=True)  35.5 us
    broadcast_in_dim x2, other arithmetic, spread(): return jnp.broadcast_to(local.reshape(1, -1), (n_tp, local.size))  28.4 us
    dot_general x2, matrix products, shards(): jnp.dot(attn_in, qkv_mat, preferred_element_type=jnp.float32)  17.1 us
  transfers between devices with their start and end apart: 6, of which 4 were waited for; matrix products, arithmetic and copies ran while one was open for 44% of the time, Pallas kernels for 0%

profile of v8, /device:TPU:0, one launch (start us, length us, event | category | flops | bytes accessed | tf_op | source)
XLA Modules:
  0.0 505.8 jit_solution(17558014956738603193)
XLA Ops:
  6.5 2.6 convert_element_type.156
  10.3 1.6 fusion.230
  11.9 2.6 all_to_all.30
  15.1 14.4 %reduce.57 = bf16[4,229376]{1,0:T(4,128)(2,1)} reduce(bf16[4,1,229376]{2,1,0:T(2,128)(2,1)} %all_to_all.30, bf16[]{:T(256)} %broadcast.639), dimensions={1}, to_apply=%all_to_all.30.reduce_sub_computation | reduce | bytes 3670018 | tf_op jit(solution)/shard_map/all_to_all | solution.py:69
  29.5 3.3 reshape.721
  32.8 27.6 %all_to_all.37 = bf16[4,2,114688]{2,1,0:T(2,128)(2,1)} all-to-all(bf16[4,2,114688]{2,1,0:T(2,128)(2,1)S(1)} %reshape.721), channel_id=1, replica_groups=mesh['seq'=8,'tp'=4] {'tp'}, dimensions={0} | all-to-all | bytes 3670016 | tf_op jit(solution)/shard_map/all_to_all | solution.py:69
  60.5 4.7 reshape.722
  65.2 12.5 %reduce.15 = bf16[4,229376]{1,0:T(4,128)(2,1)S(1)} reduce(bf16[4,1,229376]{2,1,0:T(2,128)(2,1)} %reshape.722, bf16[]{:T(256)} %constant.114), dimensions={1}, to_apply=%all_to_all.25.reduce_sub_computation | reduce | bytes 3670018 | tf_op jit(solution)/shard_map/all_to_all | solution.py:69
  77.7 2.9 reshape.527
  81.1 4.4 all_to_all.31
  85.5 14.5 %reduce.59 = bf16[4,229376]{1,0:T(4,128)(2,1)} reduce(bf16[4,1,229376]{2,1,0:T(2,128)(2,1)} %all_to_all.31, bf16[]{:T(256)} %broadcast.639), dimensions={1}, to_apply=%all_to_all.31.reduce_sub_computation | reduce | bytes 3670018 | tf_op jit(solution)/shard_map/all_to_all | solution.py:69
  99.9 3.4 reshape.725
  103.3 24.5 %all_to_all.38 = bf16[4,2,114688]{2,1,0:T(2,128)(2,1)} all-to-all(bf16[4,2,114688]{2,1,0:T(2,128)(2,1)S(1)} %reshape.725), channel_id=1, replica_groups=mesh['seq'=8,'tp'=4] {'tp'}, dimensions={0} | all-to-all | bytes 3670016 | tf_op jit(solution)/shard_map/all_to_all | solution.py:69
  127.7 4.7 reshape.726
  132.5 12.5 %reduce.24 = bf16[4,229376]{1,0:T(4,128)(2,1)S(1)} reduce(bf16[4,1,229376]{2,1,0:T(2,128)(2,1)} %reshape.726, bf16[]{:T(256)} %constant.114), dimensions={1}, to_apply=%all_to_all.29.reduce_sub_computation | reduce | bytes 3670018 | tf_op jit(solution)/shard_map/all_to_all | solution.py:69
  145.0 2.9 reshape.539
  148.1 4.6 broadcast_in_dim.45
  152.7 14.2 %reduce.56 = bf16[4,262144]{1,0:T(4,128)(2,1)S(1)} reduce(bf16[4,1,262144]{2,1,0:T(2,128)(2,1)} %broadcast_in_dim.45, bf16[]{:T(256)} %broadcast.639), dimensions={1}, to_apply=%broadcast_in_dim.45.reduce_sub_computation | reduce | bytes 4194306 | tf_op jit(solution)/shard_map/broadcast_in_dim | solution.py:72
  167.0 3.4 reshape.719
  170.4 3.9 all-to-all-start
  182.0 1.7 multiply_cosine_fusion
  183.8 12.8 %all-to-all-done = bf16[4,2,131072]{2,1,0:T(2,128)(2,1)S(1)} async-done(((bf16[4,2,131072]{2,1,0:T(2,128)(2,1)}), bf16[4,2,131072]{2,1,0:T(2,128)(2,1)S(1)}, u32[]{:S(2)}, u32[]{:S(2)}) %all-to-all-start) | async-done | bytes 2097184 | tf_op jit(solution)/shard_map/all_to_all | solution.py:69
  196.6 3.3 reshape.720
  199.9 13.5 %reduce.12 = bf16[4,262144]{1,0:T(4,128)(2,1)S(1)} reduce(bf16[4,1,262144]{2,1,0:T(2,128)(2,1)} %reshape.720, bf16[]{:T(256)} %constant.114), dimensions={1}, to_apply=%all_to_all.23.reduce_sub_computation | reduce | bytes 4194306 | tf_op jit(solution)/shard_map/all_to_all | solution.py:69
  213.4 1.7 copy.81
  215.1 4.2 copy.33
  219.3 2.4 gather_fusion
  223.3 3.2 add_convert_fusion.5
  226.5 8.6 %fusion.38 = f32[512,1536]{1,0:T(8,128)} fusion(bf16[512,2048]{0,1:T(8,128)(2,1)} %get-tuple-element.25, bf16[2048,3584]{1,0:T(8,128)(2,1)} %all-gather.3.cloned.1.call-done, f32[1536]{0:T(1024)S(1)} %get-tuple-element.16), kind=kOutput, calls=%fused_computation.80 | convolution fusion | flops 3222011904 | bytes 11540480 | tf_op jit(solution)/shard_map/dot_general | solution.py:105
  235.1 2.6 copy.37
  237.7 1.5 fusion.232
  239.1 2.6 copy.52
  241.7 2.6 copy.53
  244.3 2.3 fusion.95
  246.6 2.2 fusion.96
  248.8 3.1 fusion.128
  251.9 4.4 fusion.234
  256.3 2.8 convolution_convert_fusion.1
  259.1 26.8 %fusion.8 = f32[512,2048]{1,0:T(8,128)} fusion(bf16[2,2048,2048]{2,1,0:T(8,128)(2,1)} %param.24, bf16[512,2048]{0,1:T(8,128)(2,1)} %get-tuple-element.26, bf16[2048,3584]{1,0:T(8,128)(2,1)} %all-gather.3.cloned.1.call-done, f32[2048]{0:T(1024)S(1)} %bitcast.227), kind=kOutput, calls=%fused_computation.18 | convolution fusion | flops 8659140608 | bytes 23076864 | tf_op jit(solution)/shard_map/dot_general | solution.py:121
  285.9 4.1 add_convert_fusion.3
  291.5 3.9 all-to-all-start.2
  298.2 22.0 %all-to-all-done.2 = bf16[4,512,512]{2,1,0:T(8,128)(2,1)S(1)} async-done(((bf16[4,512,512]{2,1,0:T(8,128)(2,1)}), bf16[4,512,512]{2,1,0:T(8,128)(2,1)S(1)}, u32[]{:S(2)}, u32[]{:S(2)}) %all-to-all-start.2) | async-done | bytes 2097184 | tf_op jit(solution)/shard_map/all_to_all | solution.py:69
  322.0 4.6 broadcast_in_dim.49
  326.6 14.2 %reduce.58 = bf16[4,262144]{1,0:T(4,128)(2,1)S(1)} reduce(bf16[4,1,262144]{2,1,0:T(2,128)(2,1)} %broadcast_in_dim.49, bf16[]{:T(256)} %broadcast.639), dimensions={1}, to_apply=%broadcast_in_dim.49.reduce_sub_computation | reduce | bytes 4194306 | tf_op jit(solution)/shard_map/broadcast_in_dim | solution.py:72
  340.8 3.4 reshape.723
  344.2 3.6 all-to-all-start.3
  348.2 24.1 %all-to-all-done.3 = bf16[4,2,131072]{2,1,0:T(2,128)(2,1)S(1)} async-done(((bf16[4,2,131072]{2,1,0:T(2,128)(2,1)}), bf16[4,2,131072]{2,1,0:T(2,128)(2,1)S(1)}, u32[]{:S(2)}, u32[]{:S(2)}) %all-to-all-start.3) | async-done | bytes 2097184 | tf_op jit(solution)/shard_map/all_to_all | solution.py:69
  372.3 3.5 reshape.724
  375.8 13.5 %reduce.21 = bf16[4,262144]{1,0:T(4,128)(2,1)S(1)} reduce(bf16[4,1,262144]{2,1,0:T(2,128)(2,1)} %reshape.724, bf16[]{:T(256)} %constant.114), dimensions={1}, to_apply=%all_to_all.27.reduce_sub_computation | reduce | bytes 4194306 | tf_op jit(solution)/shard_map/all_to_all | solution.py:69
  389.3 1.7 copy.80
  391.0 4.2 copy.43
  395.2 2.3 gather_fusion.5
  399.2 2.8 add_convert_fusion.2
  402.0 8.5 %fusion.41 = f32[512,1536]{1,0:T(8,128)} fusion(bf16[512,2048]{0,1:T(8,128)(2,1)} %get-tuple-element.23, bf16[2048,3584]{1,0:T(8,128)(2,1)} %all-gather.5.cloned.1.call-done, f32[1536]{0:T(1024)S(1)} %get-tuple-element.15), kind=kOutput, calls=%fused_computation.81 | convolution fusion | flops 3222011904 | bytes 11540480 | tf_op jit(solution)/shard_map/dot_general | solution.py:105
  410.5 3.9 copy.45
  414.4 2.8 fusion.231
  417.6 1.6 copy.55
  420.2 2.4 fusion.132
  422.8 4.2 fusion.239
  427.0 3.3 convolution_convert_fusion
  430.3 25.6 %fusion.6 = f32[512,2048]{1,0:T(8,128)} fusion(bf16[2,2048,2048]{2,1,0:T(8,128)(2,1)} %param.24, bf16[512,2048]{0,1:T(8,128)(2,1)S(1)} %copy-done.6, bf16[2048,3584]{1,0:T(8,128)(2,1)} %all-gather.5.cloned.1.call-done, f32[2048]{0:T(1024)S(1)} %bitcast.226), kind=kOutput, calls=%fused_computation.16 | convolution fusion | flops 8659140608 | bytes 23076864 | tf_op jit(solution)/shard_map/dot_general | solution.py:121
  455.9 5.7 %add_convert_fusion = bf16[512,2048]{1,0:T(8,128)(2,1)} fusion(f32[512,2048]{1,0:T(8,128)} %fusion.6, bf16[512,512]{0,1:T(8,128)(2,1)} %bitcast.219, bf16[2,512,2048]{2,1,0:T(8,128)(2,1)} %param.23), kind=kOutput, calls=%fused_computation.38 | convolution fusion | flops 1075838976 | bytes 8912896 | tf_op jit(solution)/shard_map/dot_general | solution.py:121
  461.6 35.5 %reduce-scatter.2.cloned.1.call-done = bf16[512,512]{1,0:T(8,128)(2,1)} async-done(((bf16[512,2048]{1,0:T(8,128)(2,1)}), bf16[512,512]{1,0:T(8,128)(2,1)}) %reduce-scatter.2.cloned.1.call-update) | async-done | bytes 524304 | tf_op jit(solution)/shard_map/reduce_scatter | solution.py:129
  497.0 2.1 fusion.94
  (106 shorter events, 21.4 us)
Async XLA Ops:
  6.5 3.2 copy-start.5
  6.5 219.9 %all-gather.3.cloned.1.call-start = ((), (), s32[]{:S(2)}) async-start(), calls=%async_computation.6 | async-start | bytes 16515072 | tf_op jit(solution)/shard_map/all_gather | solution.py:80
  80.6 321.4 %all-gather.5.cloned.1.call-start = ((), (), s32[]{:S(2)}) async-start(), calls=%async_computation.7 | async-start | bytes 16515072 | tf_op jit(solution)/shard_map/all_gather | solution.py:80
  132.5 15.4 %copy-start = (bf16[1,512,512]{2,1,0:T(8,128)(2,1)S(1)}, bf16[1,512,512]{2,1,0:T(8,128)(2,1)}, u32[]{:S(2)}) copy-start(bf16[1,512,512]{2,1,0:T(8,128)(2,1)} %param.16) | copy-start | bytes 1572868
  166.9 7.4 %copy-start.10 = (f32[2,2,2048]{2,1,0:T(2,128)S(1)}, f32[2,2,2048]{2,1,0:T(2,128)}, u32[]{:S(2)}) copy-start(f32[2,2,2048]{2,1,0:T(2,128)} %param.27) | copy-start | bytes 98308
  167.0 7.4 %copy-start.11 = (f32[2,2,2048]{2,1,0:T(2,128)S(1)}, f32[2,2,2048]{2,1,0:T(2,128)}, u32[]{:S(2)}) copy-start(f32[2,2,2048]{2,1,0:T(2,128)} %param.26) | copy-start | bytes 98308
  167.0 7.7 %copy-start.14 = (s32[32]{0:T(128)S(1)}, s32[32]{0:T(128)}, u32[]{:S(2)}) copy-start(s32[32]{0:T(128)} %param.18) | copy-start | bytes 388
  167.0 13.1 %copy-start.8 = (s32[1,512]{1,0:T(1,128)S(1)}, s32[1,512]{1,0:T(1,128)}, u32[]{:S(2)}) copy-start(s32[1,512]{1,0:T(1,128)} %param.17) | copy-start | bytes 6148
  167.0 14.0 %copy-start.12 = (bf16[2,1536]{1,0:T(2,128)(2,1)S(1)}, bf16[2,1536]{1,0:T(2,128)(2,1)}, u32[]{:S(2)}) copy-start(bf16[2,1536]{1,0:T(2,128)(2,1)} %param.21) | copy-start | bytes 18436
  170.4 13.4 %copy-start.9 = (bf16[2,2048]{1,0:T(2,128)(2,1)S(1)}, bf16[2,2048]{1,0:T(2,128)(2,1)}, u32[]{:S(2)}) copy-start(bf16[2,2048]{1,0:T(2,128)(2,1)} %param.22) | copy-start | bytes 24580
  170.4 26.2 %all-to-all-start = ((bf16[4,2,131072]{2,1,0:T(2,128)(2,1)}), bf16[4,2,131072]{2,1,0:T(2,128)(2,1)S(1)}, u32[]{:S(2)}, u32[]{:S(2)}) async-start(bf16[4,2,131072]{2,1,0:T(2,128)(2,1)} %reshape.719), calls=%async_computation | async-start | bytes 4194304 | tf_op jit(solution)/shard_map/all_to_all | solution.py:69
  259.1 26.8 %copy-start.7 = (bf16[2,256,512]{2,1,0:T(8,128)(2,1)S(1)}, bf16[2,256,512]{2,1,0:T(8,128)(2,1)}, u32[]{:S(2)}) copy-start(bf16[2,256,512]{2,1,0:T(8,128)(2,1)} %convolution_convert_fusion.1) | copy-start | bytes 1572868
  290.0 5.4 %copy-start.13 = (f32[2,512]{1,0:T(2,128)S(1)}, f32[2,512]{1,0:T(2,128)}, u32[]{:S(2)}) copy-start(f32[2,512]{1,0:T(2,128)} %param.25) | copy-start | bytes 12292
  291.5 5.3 %copy-start.1 = (bf16[1,512,512]{2,1,0:T(8,128)(2,1)S(1)}, bf16[1,512,512]{2,1,0:T(8,128)(2,1)}, u32[]{:S(2)}) copy-start(bf16[1,512,512]{2,1,0:T(8,128)(2,1)} %param.16) | copy-start | bytes 1572868
  291.5 28.7 %all-to-all-start.2 = ((bf16[4,512,512]{2,1,0:T(8,128)(2,1)}), bf16[4,512,512]{2,1,0:T(8,128)(2,1)S(1)}, u32[]{:S(2)}, u32[]{:S(2)}) async-start(bf16[4,512,512]{2,1,0:T(8,128)(2,1)} %bitcast.201), calls=%async_computation.2 | async-start | bytes 4194304 | tf_op jit(solution)/shard_map/all_to_all | solution.py:69
  320.2 1.3 copy-start.3
  320.2 1.6 copy-start.4
  344.2 28.0 %all-to-all-start.3 = ((bf16[4,2,131072]{2,1,0:T(2,128)(2,1)}), bf16[4,2,131072]{2,1,0:T(2,128)(2,1)S(1)}, u32[]{:S(2)}, u32[]{:S(2)}) async-start(bf16[4,2,131072]{2,1,0:T(2,128)(2,1)} %reshape.723), calls=%async_computation.3 | async-start | bytes 4194304 | tf_op jit(solution)/shard_map/all_to_all | solution.py:69
  347.9 149.2 %reduce-scatter.2.cloned.1.call-start = ((), (), s32[]{:S(2)}) async-start(), calls=%async_computation.8 | async-start | bytes 2621440 | tf_op jit(solution)/shard_map/reduce_scatter | solution.py:129
  427.0 3.3 copy-start.6
  455.9 41.2 %copy-start.2 = (bf16[1,512,512]{2,1,0:T(8,128)(2,1)S(1)}, bf16[1,512,512]{2,1,0:T(8,128)(2,1)}, u32[]{:S(2)}) copy-start(bf16[1,512,512]{2,1,0:T(8,128)(2,1)} %param.16) | copy-start | bytes 1572868
Sparse Core Ops, SparseCore 0:
  80.7 133.6 all-gather.2
  216.0 132.1 all-gather.4
  461.7 35.3 reduce-scatter.1

commit v9 on v8

--- a/solution.py
+++ b/solution.py
@@ -61,21 +61,22 @@
 
     wq = trainer_qkv.astype(jnp.bfloat16).reshape(LAYERS, block, n_tp, qkv_cols)
     wu = trainer_up.astype(jnp.bfloat16).reshape(LAYERS, block, n_tp, up_bias.shape[1])
-    packed = jnp.concatenate([wq, wu], axis=-1).transpose(0, 2, 1, 3).reshape(LAYERS, n_tp, -1)
-    cols = packed.shape[2] // block
+    packed = jnp.concatenate([wq, wu], axis=-1)
+    cols = packed.shape[3]
     width_here = tokens.shape[2]
 
     def exchange(x):
         return lax.all_to_all(x, "tp", split_axis=0, concat_axis=0, tiled=True)
 
     def spread(local):
-        return jnp.broadcast_to(local.reshape(1, -1), (n_tp, local.size))
+        return jnp.broadcast_to(local.reshape(1, rows * length, width_here), (n_tp, rows * length, width_here))
 
     def joined(got):
-        got = got.reshape(n_tp, rows, length, width_here).transpose(1, 2, 0, 3)
-        return got.reshape(rows, length, n_tp * width_here)
+        return got.transpose(1, 0, 2).reshape(rows, length, n_tp * width_here)
 
-    pieces = [exchange(packed[layer]) for layer in range(LAYERS)]
+    pieces = [
+        lax.all_to_all(packed[layer], "tp", split_axis=1, concat_axis=0, tiled=True) for layer in range(LAYERS)
+    ]
     whole = joined(exchange(spread(tokens)))
     gathered = [lax.all_gather(piece.reshape(n_tp * block, cols), "seq", axis=0, tiled=True) for piece in pieces]
 

time: 515 us -> 432 us (0.84)
  other arithmetic: 133 us -> 25.5 us
  waiting for transfers between devices: 94.4 us -> 169 us
  local copies, waits for them, and re-layouts: 107 us -> 60.3 us
    all_to_all x6 -> x0, other arithmetic: 80.8 us -> none  [exchange(): return lax.all_to_all(x, 'tp', split_axis=0, concat_axis=0, tiled=True)]
    all_gather x2, waiting for transfers between devices: 0.01 us -> 73.1 us  [shards(): lax.all_gather(piece.reshape(n_tp * block, cols), 'seq', axis=0, tiled=True)]
    unnamed x49 -> x35, local copies, waits for them, and re-layouts: 45 us -> 14.7 us
    broadcast_in_dim x2 -> x0, other arithmetic: 28.4 us -> none  [spread(): return jnp.broadcast_to(local.reshape(1, -1), (n_tp, local.size))]
    transpose x2 -> x0, local copies, waits for them, and re-layouts: 8.36 us -> none  [joined(): got = got.reshape(n_tp, rows, length, width_here).transpose(1, 2, 0, 3)]
    all_to_all x2 -> x0, local copies, waits for them, and re-layouts: 7.01 us -> none  [exchange(): return lax.all_to_all(x, 'tp', split_axis=0, concat_axis=0, tiled=True)]
    broadcast_in_dim x3, local copies, waits for them, and re-layouts: 9.87 us -> 3.23 us  [spread(): jnp.broadcast_to(local.reshape(1, rows * length, width_here), (n_tp, rows...]
    reshape x2 -> x1, local copies, waits for them, and re-layouts: 5.73 us -> 0.21 us  [shards(): flat_stream = stream.astype(jnp.float32).reshape(rows * length, -1)]
  transfers between devices with their start and end apart: 6 -> 6, of which waited for: 4 -> 6; matrix products, arithmetic and copies ran while one was open for 44% -> 22% of each run, Pallas kernels for 0% -> 0%
where the time goes in v9:
time: 432 us; the launch traced here: 426 us
  waiting for transfers between devices  169 us (39%)
  matrix products  93.9 us (22%)
  local copies, waits for them, and re-layouts  60.3 us (14%)
  blocking collectives  52.2 us (12%)
  other arithmetic  25.5 us (6%)
  between operations  13.6 us (3%)
  starting transfers between devices  11.5 us (3%)
    all_gather x2, waiting for transfers between devices, shards(): lax.all_gather(piece.reshape(n_tp * block, cols), 'seq', axis=0, tiled=True)  73.1 us
    all_to_all x3, waiting for transfers between devices, exchange(): return lax.all_to_all(x, 'tp', split_axis=0, concat_axis=0, tiled=True)  62.7 us
    dot_general x2, matrix products, shards(): jnp.dot(hidden_units, down_w[layer], preferred_element_type=jnp.float32)  52.8 us
    all_to_all x2, blocking collectives, shards(): lax.all_to_all(packed[layer], 'tp', split_axis=1, concat_axis=0, tiled=True)  52.2 us
    reduce_scatter x1, waiting for transfers between devices, shards(): lax.psum_scatter(partial_terms, 'tp', scatter_dimension=1, tiled=True)  33.6 us
    dot_general x2, matrix products, shards(): jnp.dot(attn_in, qkv_mat, preferred_element_type=jnp.float32)  17 us
    unnamed x35, local copies, waits for them, and re-layouts  14.7 us
    all_to_all x3, starting transfers between devices, exchange(): return lax.all_to_all(x, 'tp', split_axis=0, concat_axis=0, tiled=True)  11.4 us
  transfers between devices with their start and end apart: 6, of which 6 were waited for; matrix products, arithmetic and copies ran while one was open for 22% of the time, Pallas kernels for 0%

profile of v9, /device:TPU:0, one launch (start us, length us, event | category | flops | bytes accessed | tf_op | source)
XLA Modules:
  0.0 426.4 jit_solution(7744436386362389550)
XLA Ops:
  6.5 2.1 convert_element_type.150
  8.6 1.2 reshape.478
  9.8 1.7 constant_dynamic-update-slice_fusion.1
  11.6 2.4 convert_element_type.151
  14.0 2.8 reshape.479
  16.8 4.0 constant_dynamic-update-slice_fusion
  20.8 3.3 slice_bitcast_fusion
  24.5 27.6 %all_to_all.45 = bf16[64,4,3584]{2,0,1:T(8,128)(2,1)} all-to-all(bf16[64,4,3584]{2,0,1:T(8,128)(2,1)S(1)} %copy.46), channel_id=1, replica_groups=mesh['seq'=8,'tp'=4] {'tp'}, dimensions={1} | all-to-all | bytes 3670016 | tf_op jit(solution)/shard_map/all_to_all | solution.py:78
  52.5 24.5 %all_to_all.46 = bf16[64,4,3584]{2,0,1:T(8,128)(2,1)} all-to-all(bf16[64,4,3584]{2,0,1:T(8,128)(2,1)S(1)} %copy.54), channel_id=1, replica_groups=mesh['seq'=8,'tp'=4] {'tp'}, dimensions={1} | all-to-all | bytes 3670016 | tf_op jit(solution)/shard_map/all_to_all | solution.py:78
  77.3 1.5 broadcast_in_dim.45
  78.9 3.9 all-to-all-start
  83.1 0.6 gather_fusion.6
  84.4 0.6 gather_fusion.3
  85.0 0.6 gather_fusion.4
  85.6 0.6 gather_fusion.7
  86.3 0.6 gather_fusion.8
  86.9 0.6 gather_fusion.9
  87.6 0.6 gather_fusion.1
  89.6 0.9 fusion.89
  90.5 1.7 multiply_cosine_fusion
  92.2 12.8 %all-to-all-done = bf16[4,512,512]{1,2,0:T(8,128)(2,1)S(1)} async-done(((bf16[4,512,512]{1,2,0:T(8,128)(2,1)}), bf16[4,512,512]{1,2,0:T(8,128)(2,1)S(1)}, u32[]{:S(2)}, u32[]{:S(2)}) %all-to-all-start) | async-done | bytes 2097184 | tf_op jit(solution)/shard_map/all_to_all | solution.py:69
  105.1 1.4 copy-done
  106.4 2.3 gather_fusion
  108.7 0.7 convert_reduce_fusion.1
  109.5 0.9 multiply_reduce_fusion.1
  110.4 2.8 add_convert_fusion.5
  113.2 72.7 %all-gather.3.cloned.1.call-done = bf16[2048,3584]{1,0:T(8,128)(2,1)} async-done(((bf16[256,3584]{1,0:T(8,128)(2,1)}), bf16[2048,3584]{1,0:T(8,128)(2,1)}) %all-gather.3.cloned.1.call-update) | async-done | bytes 14680080 | tf_op jit(solution)/shard_map/all_gather | solution.py:81
  185.9 8.5 %fusion.38 = f32[512,1536]{1,0:T(8,128)} fusion(bf16[512,2048]{0,1:T(8,128)(2,1)} %get-tuple-element.25, bf16[2048,3584]{1,0:T(8,128)(2,1)} %all-gather.3.cloned.1.call-done, f32[1536]{0:T(1024)S(1)} %get-tuple-element.16), kind=kOutput, calls=%fused_computation.79 | convolution fusion | flops 3222011904 | bytes 11540480 | tf_op jit(solution)/shard_map/dot_general | solution.py:106
  194.5 3.2 copy.47
  197.7 1.6 fusion.229
  199.3 2.5 copy.63
  201.8 2.6 copy.62
  204.4 2.3 fusion.95
  206.6 2.3 fusion.94
  208.9 3.0 fusion.126
  211.9 4.4 %fusion.231 = (f32[2,512]{1,0:T(2,128)S(1)}, f32[2,512,512]{1,2,0:T(8,128)}) fusion(pred[512,512]{0,1:T(8,128)(4,1)} %fusion.89, bf16[512,2,192]{2,0,1:T(8,128)(2,1)} %fusion.95, bf16[512,2,32]{2,0,1:T(8,128)(2,1)} %get-tuple-element.32, bf16[512,2,32]{2,0,1:T(8,128)(2,1)} %get-tuple-element.31, bf16[512,2,192]{2,0,1:T(8,128)(2,1)} %fusion.94, ...), kind=kOutput, calls=%fused_computation.300 | convolution fusion | flops 273678848 | bytes 3411968 | tf_op jit(solution)/shard_map/sub | solution.py:115
  216.3 2.8 convolution_convert_fusion.1
  219.2 26.5 %fusion.8 = f32[512,2048]{1,0:T(8,128)} fusion(bf16[2,2048,2048]{2,1,0:T(8,128)(2,1)} %param.24, bf16[512,2048]{0,1:T(8,128)(2,1)} %get-tuple-element.26, bf16[2048,3584]{1,0:T(8,128)(2,1)} %all-gather.3.cloned.1.call-done, f32[2048]{0:T(1024)S(1)} %bitcast.191), kind=kOutput, calls=%fused_computation.18 | convolution fusion | flops 8659140608 | bytes 23076864 | tf_op jit(solution)/shard_map/dot_general | solution.py:122
  245.7 4.1 add_convert_fusion.3
  249.8 1.5 copy.78
  251.3 3.9 all-to-all-start.2
  255.2 25.5 %all-to-all-done.2 = bf16[4,512,512]{2,1,0:T(8,128)(2,1)S(1)} async-done(((bf16[4,512,512]{2,1,0:T(8,128)(2,1)}), bf16[4,512,512]{2,1,0:T(8,128)(2,1)S(1)}, u32[]{:S(2)}, u32[]{:S(2)}) %all-to-all-start.2) | async-done | bytes 2097184 | tf_op jit(solution)/shard_map/all_to_all | solution.py:69
  281.4 1.5 broadcast_in_dim.49
  282.9 3.6 all-to-all-start.3
  286.9 24.4 %all-to-all-done.3 = bf16[4,512,512]{1,2,0:T(8,128)(2,1)S(1)} async-done(((bf16[4,512,512]{1,2,0:T(8,128)(2,1)}), bf16[4,512,512]{1,2,0:T(8,128)(2,1)S(1)}, u32[]{:S(2)}, u32[]{:S(2)}) %all-to-all-start.3) | async-done | bytes 2097184 | tf_op jit(solution)/shard_map/all_to_all | solution.py:69
  311.3 1.3 copy-done.1
  312.6 2.3 gather_fusion.5
  314.9 0.7 convert_reduce_fusion.2
  315.6 0.9 multiply_reduce_fusion
  316.5 2.8 add_convert_fusion.2
  319.7 8.5 %fusion.41 = f32[512,1536]{1,0:T(8,128)} fusion(bf16[512,2048]{0,1:T(8,128)(2,1)} %get-tuple-element.23, bf16[2048,3584]{1,0:T(8,128)(2,1)} %all-gather.5.cloned.1.call-done, f32[1536]{0:T(1024)S(1)} %get-tuple-element.15), kind=kOutput, calls=%fused_computation.80 | convolution fusion | flops 3222011904 | bytes 11540480 | tf_op jit(solution)/shard_map/dot_general | solution.py:106
  328.2 2.8 copy.55
  331.0 1.5 fusion.228
  332.5 2.5 copy.65
  335.0 2.2 fusion.97
  337.3 2.6 copy.64
  339.8 3.0 fusion.130
  342.8 2.2 fusion.96
  345.1 4.4 %fusion.236 = (f32[2,512]{1,0:T(2,128)S(1)}, f32[2,512,512]{1,2,0:T(8,128)}) fusion(pred[512,512]{0,1:T(8,128)(4,1)} %fusion.89, bf16[512,2,192]{2,0,1:T(8,128)(2,1)} %fusion.97, bf16[512,2,32]{2,0,1:T(8,128)(2,1)} %get-tuple-element.28, bf16[512,2,32]{2,0,1:T(8,128)(2,1)} %get-tuple-element.27, bf16[512,2,192]{2,0,1:T(8,128)(2,1)} %fusion.96, ...), kind=kOutput, calls=%fused_computation.301 | convolution fusion | flops 273678848 | bytes 3411968 | tf_op jit(solution)/shard_map/sub | solution.py:115
  349.5 2.8 convolution_convert_fusion
  352.3 26.3 %fusion.6 = f32[512,2048]{1,0:T(8,128)} fusion(bf16[2,2048,2048]{2,1,0:T(8,128)(2,1)} %param.24, bf16[512,2048]{0,1:T(8,128)(2,1)} %get-tuple-element.24, bf16[2048,3584]{1,0:T(8,128)(2,1)} %all-gather.5.cloned.1.call-done, f32[2048]{0:T(1024)S(1)} %bitcast.190), kind=kOutput, calls=%fused_computation.16 | convolution fusion | flops 8659140608 | bytes 23076864 | tf_op jit(solution)/shard_map/dot_general | solution.py:122
  378.6 5.5 %add_convert_fusion = bf16[512,2048]{1,0:T(8,128)(2,1)} fusion(f32[512,2048]{1,0:T(8,128)} %fusion.6, bf16[512,512]{0,1:T(8,128)(2,1)S(1)} %bitcast.184, bf16[2,512,2048]{2,1,0:T(8,128)(2,1)} %param.23), kind=kOutput, calls=%fused_computation.38 | convolution fusion | flops 1075838976 | bytes 8912896 | tf_op jit(solution)/shard_map/dot_general | solution.py:122
  384.1 33.6 %reduce-scatter.2.cloned.1.call-done = bf16[512,512]{1,0:T(8,128)(2,1)} async-done(((bf16[512,2048]{1,0:T(8,128)(2,1)}), bf16[512,512]{1,0:T(8,128)(2,1)}) %reduce-scatter.2.cloned.1.call-update) | async-done | bytes 524304 | tf_op jit(solution)/shard_map/reduce_scatter | solution.py:130
  417.7 2.0 fusion.92
  (80 shorter events, 5.1 us)
Async XLA Ops:
  6.5 179.4 %all-gather.3.cloned.1.call-start = ((), (), s32[]{:S(2)}) async-start(), calls=%async_computation.6 | async-start | bytes 16515072 | tf_op jit(solution)/shard_map/all_gather | solution.py:81
  52.1 267.6 %all-gather.5.cloned.1.call-start = ((), (), s32[]{:S(2)}) async-start(), calls=%async_computation.7 | async-start | bytes 16515072 | tf_op jit(solution)/shard_map/all_gather | solution.py:81
  52.2 24.9 %copy-start.4 = (bf16[1,512,512]{2,1,0:T(8,128)(2,1)S(1)}, bf16[1,512,512]{2,1,0:T(8,128)(2,1)}, u32[]{:S(2)}) copy-start(bf16[1,512,512]{2,1,0:T(8,128)(2,1)} %param.16) | copy-start | bytes 1572868
  77.0 5.7 %copy-start.10 = (f32[2,2,2048]{2,1,0:T(2,128)S(1)}, f32[2,2,2048]{2,1,0:T(2,128)}, u32[]{:S(2)}) copy-start(f32[2,2,2048]{2,1,0:T(2,128)} %param.27) | copy-start | bytes 98308
  77.1 5.7 %copy-start.11 = (f32[2,2,2048]{2,1,0:T(2,128)S(1)}, f32[2,2,2048]{2,1,0:T(2,128)}, u32[]{:S(2)}) copy-start(f32[2,2,2048]{2,1,0:T(2,128)} %param.26) | copy-start | bytes 98308
  77.1 6.0 %copy-start.14 = (s32[32]{0:T(128)S(1)}, s32[32]{0:T(128)}, u32[]{:S(2)}) copy-start(s32[32]{0:T(128)} %param.18) | copy-start | bytes 388
  77.3 11.2 %copy-start.8 = (s32[1,512]{1,0:T(1,128)S(1)}, s32[1,512]{1,0:T(1,128)}, u32[]{:S(2)}) copy-start(s32[1,512]{1,0:T(1,128)} %param.17) | copy-start | bytes 6148
  77.3 12.1 %copy-start.12 = (bf16[2,1536]{1,0:T(2,128)(2,1)S(1)}, bf16[2,1536]{1,0:T(2,128)(2,1)}, u32[]{:S(2)}) copy-start(bf16[2,1536]{1,0:T(2,128)(2,1)} %param.21) | copy-start | bytes 18436
  77.3 14.9 %copy-start.9 = (bf16[2,2048]{1,0:T(2,128)(2,1)S(1)}, bf16[2,2048]{1,0:T(2,128)(2,1)}, u32[]{:S(2)}) copy-start(bf16[2,2048]{1,0:T(2,128)(2,1)} %param.22) | copy-start | bytes 24580
  78.9 26.2 %all-to-all-start = ((bf16[4,512,512]{1,2,0:T(8,128)(2,1)}), bf16[4,512,512]{1,2,0:T(8,128)(2,1)S(1)}, u32[]{:S(2)}, u32[]{:S(2)}) async-start(bf16[4,512,512]{1,2,0:T(8,128)(2,1)} %broadcast_in_dim.45), calls=%async_computation | async-start | bytes 4194304 | tf_op jit(solution)/shard_map/all_to_all | solution.py:69
  105.1 1.4 copy-start
  219.2 26.5 %copy-start.7 = (bf16[2,256,512]{2,1,0:T(8,128)(2,1)S(1)}, bf16[2,256,512]{2,1,0:T(8,128)(2,1)}, u32[]{:S(2)}) copy-start(bf16[2,256,512]{2,1,0:T(8,128)(2,1)} %convolution_convert_fusion.1) | copy-start | bytes 1572868
  249.8 5.4 %copy-start.13 = (f32[2,512]{1,0:T(2,128)S(1)}, f32[2,512]{1,0:T(2,128)}, u32[]{:S(2)}) copy-start(f32[2,512]{1,0:T(2,128)} %param.25) | copy-start | bytes 12292
  251.3 29.7 %copy-start.5 = (bf16[1,512,512]{2,1,0:T(8,128)(2,1)S(1)}, bf16[1,512,512]{2,1,0:T(8,128)(2,1)}, u32[]{:S(2)}) copy-start(bf16[1,512,512]{2,1,0:T(8,128)(2,1)} %param.16) | copy-start | bytes 1572868
  251.3 29.4 %all-to-all-start.2 = ((bf16[4,512,512]{2,1,0:T(8,128)(2,1)}), bf16[4,512,512]{2,1,0:T(8,128)(2,1)S(1)}, u32[]{:S(2)}, u32[]{:S(2)}) async-start(bf16[4,512,512]{2,1,0:T(8,128)(2,1)} %bitcast.172), calls=%async_computation.2 | async-start | bytes 4194304 | tf_op jit(solution)/shard_map/all_to_all | solution.py:69
  281.2 1.7 copy-start.2
  282.9 28.3 %all-to-all-start.3 = ((bf16[4,512,512]{1,2,0:T(8,128)(2,1)}), bf16[4,512,512]{1,2,0:T(8,128)(2,1)S(1)}, u32[]{:S(2)}, u32[]{:S(2)}) async-start(bf16[4,512,512]{1,2,0:T(8,128)(2,1)} %broadcast_in_dim.49), calls=%async_computation.3 | async-start | bytes 4194304 | tf_op jit(solution)/shard_map/all_to_all | solution.py:69
  286.5 131.1 %reduce-scatter.2.cloned.1.call-start = ((), (), s32[]{:S(2)}) async-start(), calls=%async_computation.8 | async-start | bytes 2621440 | tf_op jit(solution)/shard_map/reduce_scatter | solution.py:130
  311.2 1.3 copy-start.1
  352.3 26.3 %copy-start.6 = (bf16[2,256,512]{2,1,0:T(8,128)(2,1)S(1)}, bf16[2,256,512]{2,1,0:T(8,128)(2,1)}, u32[]{:S(2)}) copy-start(bf16[2,256,512]{2,1,0:T(8,128)(2,1)} %convolution_convert_fusion) | copy-start | bytes 1572868
  378.6 39.1 %copy-start.3 = (bf16[512,512]{1,0:T(8,128)(2,1)S(1)}, bf16[512,512]{1,0:T(8,128)(2,1)}, u32[]{:S(2)}) copy-start(bf16[512,512]{1,0:T(8,128)(2,1)} %copy-done.2) | copy-start | bytes 1572868
Sparse Core Ops, SparseCore 0:
  52.2 133.6 all-gather.2
  187.6 132.1 all-gather.4
  384.2 33.3 reduce-scatter.1

commit v10 on v9

--- a/solution.py
+++ b/solution.py
@@ -78,7 +78,12 @@
         lax.all_to_all(packed[layer], "tp", split_axis=1, concat_axis=0, tiled=True) for layer in range(LAYERS)
     ]
     whole = joined(exchange(spread(tokens)))
-    gathered = [lax.all_gather(piece.reshape(n_tp * block, cols), "seq", axis=0, tiled=True) for piece in pieces]
+    gathered = []
+    for piece in pieces:
+        piece = piece.reshape(n_tp * block, cols)
+        gathered.append(
+            [lax.all_gather(part, "seq", axis=0, tiled=True) for part in (piece[:, :qkv_cols], piece[:, qkv_cols:])]
+        )
 
     pos = positions(segment_ids)
     index = jnp.arange(length, dtype=jnp.int32)
@@ -88,9 +93,7 @@
     mask = mask[:, None]
     stream = tokens
     for layer in range(LAYERS):
-        weights = gathered[layer]
-        qkv_mat = weights[:, :qkv_cols]
-        up_mat = weights[:, qkv_cols:]
+        qkv_mat, up_mat = gathered[layer]
         if layer > 0:
             whole = joined(exchange(spread(stream)))
         permuted = jnp.take(whole.reshape(rows, length, n_blocks, block), shard_map, axis=2)
@@ -123,11 +126,8 @@
             hidden_units, down_w[layer], preferred_element_type=jnp.float32
         )
         partial_terms = partial_terms.astype(jnp.bfloat16)
-        if layer + 1 < LAYERS:
-            split = partial_terms.reshape(rows * length, n_tp, width_here).transpose(1, 0, 2)
-            summed = jnp.sum(exchange(split).astype(jnp.float32), axis=0)
-        else:
-            summed = lax.psum_scatter(partial_terms, "tp", scatter_dimension=1, tiled=True).astype(jnp.float32)
+        split = partial_terms.reshape(rows * length, n_tp, width_here).transpose(1, 0, 2)
+        summed = jnp.sum(exchange(split).astype(jnp.float32), axis=0)
         flat_stream = stream.astype(jnp.float32).reshape(rows * length, -1)
         stream = (flat_stream + summed + out_bias[layer]).astype(jnp.bfloat16).reshape(rows, length, -1)
     return stream

time: 432 us -> 422 us (0.977)
  waiting for transfers between devices: 169 us -> 123 us
  blocking collectives: 52.2 us -> 80.7 us
  local copies, waits for them, and re-layouts: 60.3 us -> 70.1 us
    reduce_scatter x1 -> x0, waiting for transfers between devices: 33.6 us -> none  [shards(): lax.psum_scatter(partial_terms, 'tp', scatter_dimension=1, tiled=True)]
    all_to_all x0 -> x1, blocking collectives: none -> 29.4 us  [exchange(): return lax.all_to_all(x, 'tp', split_axis=0, concat_axis=0, tiled=True)]
    all_gather x2 -> x4, waiting for transfers between devices: 73.1 us -> 62.6 us  [shards(): lax.all_gather(part, 'seq', axis=0, tiled=True)]
    slice x1 -> x5, local copies, waits for them, and re-layouts: 0.19 us -> 6.72 us  [the longest x2 4.67 us: shards(): piece[:, qkv_cols:]]
    unnamed x35 -> x39, local copies, waits for them, and re-layouts: 14.7 us -> 17.3 us
  transfers between devices with their start and end apart: 6 -> 7, of which waited for: 6 -> 5; matrix products, arithmetic and copies ran while one was open for 22% -> 32% of each run, Pallas kernels for 0% -> 0%
where the time goes in v10:
time: 422 us; the launch traced here: 416 us
  waiting for transfers between devices  123 us (29%)
  matrix products  92.8 us (22%)
  blocking collectives  80.7 us (19%)
  local copies, waits for them, and re-layouts  70.1 us (17%)
  other arithmetic  24.9 us (6%)
  between operations  13.6 us (3%)
  starting transfers between devices  11.4 us (3%)
    all_gather x4, waiting for transfers between devices, shards(): lax.all_gather(part, 'seq', axis=0, tiled=True)  62.6 us
    all_to_all x3, waiting for transfers between devices, exchange(): return lax.all_to_all(x, 'tp', split_axis=0, concat_axis=0, tiled=True)  60 us
    dot_general x2, matrix products, shards(): jnp.dot(hidden_units, down_w[layer], preferred_element_type=jnp.float32)  52.6 us
    all_to_all x2, blocking collectives, shards(): lax.all_to_all(packed[layer], 'tp', split_axis=1, concat_axis=0, tiled=True)  51.3 us
    all_to_all x1, blocking collectives, exchange(): return lax.all_to_all(x, 'tp', split_axis=0, concat_axis=0, tiled=True)  29.4 us
    unnamed x39, local copies, waits for them, and re-layouts  17.3 us
    dot_general x2, matrix products, shards(): jnp.dot(attn_in, qkv_mat, preferred_element_type=jnp.float32)  17.3 us
    all_to_all x3, starting transfers between devices, exchange(): return lax.all_to_all(x, 'tp', split_axis=0, concat_axis=0, tiled=True)  11 us
  transfers between devices with their start and end apart: 7, of which 5 were waited for; matrix products, arithmetic and copies ran while one was open for 32% of the time, Pallas kernels for 0%

profile of v10, /device:TPU:0, one launch (start us, length us, event | category | flops | bytes accessed | tf_op | source)
XLA Modules:
  0.0 416.4 jit_solution(3960116228591842403)
XLA Ops:
  6.5 2.1 convert_element_type.153
  8.6 1.2 reshape.481
  9.8 1.7 constant_dynamic-update-slice_fusion.1
  11.6 2.4 convert_element_type.154
  14.0 2.8 reshape.482
  16.8 4.0 constant_dynamic-update-slice_fusion
  20.8 3.3 slice_bitcast_fusion
  24.5 27.5 %all_to_all.50 = bf16[64,4,3584]{2,0,1:T(8,128)(2,1)S(1)} all-to-all(bf16[64,4,3584]{2,0,1:T(8,128)(2,1)S(1)} %copy.46), channel_id=1, replica_groups=mesh['seq'=8,'tp'=4] {'tp'}, dimensions={1} | all-to-all | bytes 3670016 | tf_op jit(solution)/shard_map/all_to_all | solution.py:78
  52.0 1.3 copy-done.3
  53.2 0.9 slice.211
  54.3 2.3 slice.221
  56.9 23.8 %all_to_all.51 = bf16[64,4,3584]{2,0,1:T(8,128)(2,1)S(1)} all-to-all(bf16[64,4,3584]{2,0,1:T(8,128)(2,1)S(1)} %copy.54), channel_id=1, replica_groups=mesh['seq'=8,'tp'=4] {'tp'}, dimensions={1} | all-to-all | bytes 3670016 | tf_op jit(solution)/shard_map/all_to_all | solution.py:78
  80.7 1.3 copy-done.2
  82.0 0.9 slice.223
  83.2 1.5 broadcast_in_dim.47
  84.7 3.6 all-to-all-start
  95.4 0.9 fusion.44
  96.4 1.7 multiply_cosine_fusion
  98.1 2.4 slice.233
  100.5 10.2 %all-to-all-done = bf16[4,512,512]{1,2,0:T(8,128)(2,1)S(1)} async-done(((bf16[4,512,512]{1,2,0:T(8,128)(2,1)}), bf16[4,512,512]{1,2,0:T(8,128)(2,1)S(1)}, u32[]{:S(2)}, u32[]{:S(2)}) %all-to-all-start) | async-done | bytes 2097184 | tf_op jit(solution)/shard_map/all_to_all | solution.py:69
  110.8 1.4 copy-done
  112.1 2.3 gather_fusion
  114.4 0.7 convert_reduce_fusion.2
  115.1 0.9 multiply_reduce_fusion.1
  116.1 2.8 add_convert_fusion.5
  118.8 8.5 %convolution_add_fusion.1 = f32[512,1536]{1,0:T(8,128)} fusion(bf16[512,2048]{0,1:T(8,128)(2,1)} %get-tuple-element.25, bf16[2048,1536]{1,0:T(8,128)(2,1)} %all-gather.5.cloned.1.call-done, f32[1536]{0:T(1024)S(1)} %get-tuple-element.16), kind=kOutput, calls=%fused_computation.73 | convolution fusion | flops 3222011904 | bytes 11540480 | tf_op jit(solution)/shard_map/dot_general | solution.py:109
  127.4 3.5 copy.47
  130.9 1.5 fusion.182
  132.5 2.6 copy.63
  135.0 2.5 copy.64
  137.6 2.3 fusion.47
  139.9 2.3 fusion.48
  142.1 3.1 fusion.79
  145.2 4.5 %fusion.184 = (f32[2,512]{1,0:T(2,128)S(1)}, f32[2,512,512]{1,2,0:T(8,128)}) fusion(pred[512,512]{0,1:T(8,128)(4,1)} %fusion.44, bf16[512,2,192]{2,0,1:T(8,128)(2,1)} %fusion.48, bf16[512,2,32]{2,0,1:T(8,128)(2,1)} %get-tuple-element.32, bf16[512,2,32]{2,0,1:T(8,128)(2,1)} %get-tuple-element.31, bf16[512,2,192]{2,0,1:T(8,128)(2,1)} %fusion.47, ...), kind=kOutput, calls=%fused_computation.269 | convolution fusion | flops 273678848 | bytes 3411968 | tf_op jit(solution)/shard_map/sub | solution.py:118
  149.7 2.9 convolution_convert_fusion.1
  152.5 48.7 %all-gather.7.cloned.1.call-done = bf16[2048,2048]{1,0:T(8,128)(2,1)} async-done(((bf16[256,2048]{1,0:T(8,128)(2,1)}), bf16[2048,2048]{1,0:T(8,128)(2,1)}) %all-gather.7.cloned.1.call-update) | async-done | bytes 8388624 | tf_op jit(solution)/shard_map/all_gather | solution.py:85
  201.2 26.3 %fusion.4 = f32[512,2048]{1,0:T(8,128)} fusion(bf16[2,2048,2048]{2,1,0:T(8,128)(2,1)} %param.24, bf16[512,2048]{0,1:T(8,128)(2,1)} %get-tuple-element.26, bf16[2048,2048]{1,0:T(8,128)(2,1)} %all-gather.7.cloned.1.call-done, f32[2048]{0:T(1024)S(1)} %bitcast.208), kind=kOutput, calls=%fused_computation.14 | convolution fusion | flops 8659140608 | bytes 23076864 | tf_op jit(solution)/shard_map/dot_general | solution.py:125
  227.5 4.2 %add_convert_fusion.3 = bf16[512,2048]{1,0:T(8,128)(2,1)S(1)} fusion(f32[512,2048]{1,0:T(8,128)} %fusion.4, bf16[512,512]{0,1:T(8,128)(2,1)S(1)} %bitcast.202, bf16[2,512,2048]{2,1,0:T(8,128)(2,1)} %param.23), kind=kOutput, calls=%fused_computation.49 | convolution fusion | flops 1075838976 | bytes 8912896 | tf_op jit(solution)/shard_map/dot_general | solution.py:125
  231.7 1.6 copy.82
  233.3 3.8 all-to-all-start.2
  237.1 25.4 %all-to-all-done.2 = bf16[4,512,512]{2,1,0:T(8,128)(2,1)S(1)} async-done(((bf16[4,512,512]{2,1,0:T(8,128)(2,1)}), bf16[4,512,512]{2,1,0:T(8,128)(2,1)S(1)}, u32[]{:S(2)}, u32[]{:S(2)}) %all-to-all-start.2) | async-done | bytes 2097184 | tf_op jit(solution)/shard_map/all_to_all | solution.py:69
  263.2 1.6 broadcast_in_dim.52
  264.8 3.6 all-to-all-start.3
  268.7 24.4 %all-to-all-done.3 = bf16[4,512,512]{1,2,0:T(8,128)(2,1)S(1)} async-done(((bf16[4,512,512]{1,2,0:T(8,128)(2,1)}), bf16[4,512,512]{1,2,0:T(8,128)(2,1)S(1)}, u32[]{:S(2)}, u32[]{:S(2)}) %all-to-all-start.3) | async-done | bytes 2097184 | tf_op jit(solution)/shard_map/all_to_all | solution.py:69
  293.1 1.4 copy-done.1
  294.5 2.3 gather_fusion.5
  296.7 0.7 convert_reduce_fusion.3
  297.5 0.9 multiply_reduce_fusion
  298.4 2.8 add_convert_fusion.2
  301.2 8.8 %convolution_add_fusion = f32[512,1536]{1,0:T(8,128)} fusion(bf16[512,2048]{0,1:T(8,128)(2,1)} %get-tuple-element.23, bf16[2048,1536]{1,0:T(8,128)(2,1)} %all-gather.9.cloned.1.call-done, f32[1536]{0:T(1024)S(1)} %get-tuple-element.15), kind=kOutput, calls=%fused_computation.72 | convolution fusion | flops 3222011904 | bytes 11540480 | tf_op jit(solution)/shard_map/dot_general | solution.py:109
  310.0 2.8 copy.55
  312.8 1.5 fusion.181
  314.3 2.6 copy.65
  316.9 2.5 copy.66
  319.4 2.3 fusion.49
  321.7 2.2 fusion.50
  324.0 3.2 fusion.83
  327.1 4.5 %fusion.189 = (f32[2,512]{1,0:T(2,128)S(1)}, f32[2,512,512]{1,2,0:T(8,128)}) fusion(pred[512,512]{0,1:T(8,128)(4,1)} %fusion.44, bf16[512,2,192]{2,0,1:T(8,128)(2,1)} %fusion.50, bf16[512,2,32]{2,0,1:T(8,128)(2,1)} %get-tuple-element.28, bf16[512,2,32]{2,0,1:T(8,128)(2,1)} %get-tuple-element.27, bf16[512,2,192]{2,0,1:T(8,128)(2,1)} %fusion.49, ...), kind=kOutput, calls=%fused_computation.270 | convolution fusion | flops 273678848 | bytes 3411968 | tf_op jit(solution)/shard_map/sub | solution.py:118
  331.6 2.9 convolution_convert_fusion
  334.5 13.9 %all-gather.11.cloned.1.call-done = bf16[2048,2048]{1,0:T(8,128)(2,1)} async-done(((bf16[256,2048]{1,0:T(8,128)(2,1)}), bf16[2048,2048]{1,0:T(8,128)(2,1)}) %all-gather.11.cloned.1.call-update) | async-done | bytes 8388624 | tf_op jit(solution)/shard_map/all_gather | solution.py:85
  348.4 26.3 %fusion.2 = f32[512,2048]{1,0:T(8,128)} fusion(bf16[2,2048,2048]{2,1,0:T(8,128)(2,1)} %param.24, bf16[512,2048]{0,1:T(8,128)(2,1)} %get-tuple-element.24, bf16[2048,2048]{1,0:T(8,128)(2,1)} %all-gather.11.cloned.1.call-done, f32[2048]{0:T(1024)S(1)} %bitcast.207), kind=kOutput, calls=%fused_computation.12 | convolution fusion | flops 8659140608 | bytes 23076864 | tf_op jit(solution)/shard_map/dot_general | solution.py:125
  374.7 4.1 add_convert_fusion
  378.9 29.4 %all_to_all.52 = bf16[4,512,512]{2,1,0:T(8,128)(2,1)S(1)} all-to-all(bf16[4,512,512]{2,1,0:T(8,128)(2,1)S(1)} %bitcast.186), channel_id=1, replica_groups=mesh['seq'=8,'tp'=4] {'tp'}, dimensions={0} | all-to-all | bytes 4194304 | tf_op jit(solution)/shard_map/all_to_all | solution.py:69
  408.7 1.0 fusion.37
  (94 shorter events, 9.6 us)
Async XLA Ops:
  6.5 112.3 %all-gather.5.cloned.1.call-start = ((), (), s32[]{:S(2)}) async-start(), calls=%async_computation.6 | async-start | bytes 7077888 | tf_op jit(solution)/shard_map/all_gather | solution.py:85
  52.0 1.3 copy-start.3
  54.2 147.0 %all-gather.7.cloned.1.call-start = ((), (), s32[]{:S(2)}) async-start(), calls=%async_computation.7 | async-start | bytes 9437184 | tf_op jit(solution)/shard_map/all_gather | solution.py:85
  56.6 244.6 %all-gather.9.cloned.1.call-start = ((), (), s32[]{:S(2)}) async-start(), calls=%async_computation.8 | async-start | bytes 7077888 | tf_op jit(solution)/shard_map/all_gather | solution.py:85
  56.6 26.3 %copy-start.6 = (bf16[1,512,512]{2,1,0:T(8,128)(2,1)S(1)}, bf16[1,512,512]{2,1,0:T(8,128)(2,1)}, u32[]{:S(2)}) copy-start(bf16[1,512,512]{2,1,0:T(8,128)(2,1)} %param.16) | copy-start | bytes 1572868
  80.7 1.3 copy-start.2
  82.9 5.8 %copy-start.12 = (f32[2,2,2048]{2,1,0:T(2,128)S(1)}, f32[2,2,2048]{2,1,0:T(2,128)}, u32[]{:S(2)}) copy-start(f32[2,2,2048]{2,1,0:T(2,128)} %param.27) | copy-start | bytes 98308
  82.9 5.8 %copy-start.13 = (f32[2,2,2048]{2,1,0:T(2,128)S(1)}, f32[2,2,2048]{2,1,0:T(2,128)}, u32[]{:S(2)}) copy-start(f32[2,2,2048]{2,1,0:T(2,128)} %param.26) | copy-start | bytes 98308
  82.9 6.1 %copy-start.16 = (s32[32]{0:T(128)S(1)}, s32[32]{0:T(128)}, u32[]{:S(2)}) copy-start(s32[32]{0:T(128)} %param.18) | copy-start | bytes 388
  83.2 11.3 %copy-start.10 = (s32[1,512]{1,0:T(1,128)S(1)}, s32[1,512]{1,0:T(1,128)}, u32[]{:S(2)}) copy-start(s32[1,512]{1,0:T(1,128)} %param.17) | copy-start | bytes 6148
  83.2 12.1 %copy-start.14 = (bf16[2,1536]{1,0:T(2,128)(2,1)S(1)}, bf16[2,1536]{1,0:T(2,128)(2,1)}, u32[]{:S(2)}) copy-start(bf16[2,1536]{1,0:T(2,128)(2,1)} %param.21) | copy-start | bytes 18436
  83.2 14.9 %copy-start.11 = (bf16[2,2048]{1,0:T(2,128)(2,1)S(1)}, bf16[2,2048]{1,0:T(2,128)(2,1)}, u32[]{:S(2)}) copy-start(bf16[2,2048]{1,0:T(2,128)(2,1)} %param.22) | copy-start | bytes 24580
  84.7 26.0 %all-to-all-start = ((bf16[4,512,512]{1,2,0:T(8,128)(2,1)}), bf16[4,512,512]{1,2,0:T(8,128)(2,1)S(1)}, u32[]{:S(2)}, u32[]{:S(2)}) async-start(bf16[4,512,512]{1,2,0:T(8,128)(2,1)} %broadcast_in_dim.47), calls=%async_computation | async-start | bytes 4194304 | tf_op jit(solution)/shard_map/all_to_all | solution.py:69
  88.3 260.1 %all-gather.11.cloned.1.call-start = ((), (), s32[]{:S(2)}) async-start(), calls=%async_computation.9 | async-start | bytes 9437184 | tf_op jit(solution)/shard_map/all_gather | solution.py:85
  110.7 1.4 copy-start
  201.2 26.3 %copy-start.9 = (bf16[2,256,512]{2,1,0:T(8,128)(2,1)S(1)}, bf16[2,256,512]{2,1,0:T(8,128)(2,1)}, u32[]{:S(2)}) copy-start(bf16[2,256,512]{2,1,0:T(8,128)(2,1)} %convolution_convert_fusion.1) | copy-start | bytes 1572868
  231.7 5.4 %copy-start.15 = (f32[2,512]{1,0:T(2,128)S(1)}, f32[2,512]{1,0:T(2,128)}, u32[]{:S(2)}) copy-start(f32[2,512]{1,0:T(2,128)} %param.25) | copy-start | bytes 12292
  233.3 29.6 %copy-start.7 = (bf16[1,512,512]{2,1,0:T(8,128)(2,1)S(1)}, bf16[1,512,512]{2,1,0:T(8,128)(2,1)}, u32[]{:S(2)}) copy-start(bf16[1,512,512]{2,1,0:T(8,128)(2,1)} %param.16) | copy-start | bytes 1572868
  233.3 29.2 %all-to-all-start.2 = ((bf16[4,512,512]{2,1,0:T(8,128)(2,1)}), bf16[4,512,512]{2,1,0:T(8,128)(2,1)S(1)}, u32[]{:S(2)}, u32[]{:S(2)}) async-start(bf16[4,512,512]{2,1,0:T(8,128)(2,1)} %bitcast.185), calls=%async_computation.2 | async-start | bytes 4194304 | tf_op jit(solution)/shard_map/all_to_all | solution.py:69
  263.0 1.8 copy-start.4
  264.8 28.3 %all-to-all-start.3 = ((bf16[4,512,512]{1,2,0:T(8,128)(2,1)}), bf16[4,512,512]{1,2,0:T(8,128)(2,1)S(1)}, u32[]{:S(2)}, u32[]{:S(2)}) async-start(bf16[4,512,512]{1,2,0:T(8,128)(2,1)} %broadcast_in_dim.52), calls=%async_computation.3 | async-start | bytes 4194304 | tf_op jit(solution)/shard_map/all_to_all | solution.py:69
  293.1 1.4 copy-start.1
  348.4 26.3 %copy-start.8 = (bf16[2,256,512]{2,1,0:T(8,128)(2,1)S(1)}, bf16[2,256,512]{2,1,0:T(8,128)(2,1)}, u32[]{:S(2)}) copy-start(bf16[2,256,512]{2,1,0:T(8,128)(2,1)} %convolution_convert_fusion) | copy-start | bytes 1572868
  378.9 29.7 %copy-start.5 = (bf16[1,512,512]{2,1,0:T(8,128)(2,1)S(1)}, bf16[1,512,512]{2,1,0:T(8,128)(2,1)}, u32[]{:S(2)}) copy-start(bf16[1,512,512]{2,1,0:T(8,128)(2,1)} %copy-done.4) | copy-start | bytes 1572868
Sparse Core Ops, SparseCore 0:
  54.3 64.4 all-gather.4
  120.4 80.7 all-gather.6
  202.8 63.2 all-gather.8
  267.6 80.7 all-gather.10

commit v11 on v10

--- a/solution.py
+++ b/solution.py
@@ -61,8 +61,6 @@
 
     wq = trainer_qkv.astype(jnp.bfloat16).reshape(LAYERS, block, n_tp, qkv_cols)
     wu = trainer_up.astype(jnp.bfloat16).reshape(LAYERS, block, n_tp, up_bias.shape[1])
-    packed = jnp.concatenate([wq, wu], axis=-1)
-    cols = packed.shape[3]
     width_here = tokens.shape[2]
 
     def exchange(x):
@@ -74,16 +72,14 @@
     def joined(got):
         return got.transpose(1, 0, 2).reshape(rows, length, n_tp * width_here)
 
-    pieces = [
-        lax.all_to_all(packed[layer], "tp", split_axis=1, concat_axis=0, tiled=True) for layer in range(LAYERS)
-    ]
+    gathered = []
+    for layer in range(LAYERS):
+        parts = []
+        for part in (wq[layer], wu[layer]):
+            part = lax.all_to_all(part, "tp", split_axis=1, concat_axis=0, tiled=True)
+            parts.append(lax.all_gather(part.reshape(n_tp * block, -1), "seq", axis=0, tiled=True))
+        gathered.append(parts)
     whole = joined(exchange(spread(tokens)))
-    gathered = []
-    for piece in pieces:
-        piece = piece.reshape(n_tp * block, cols)
-        gathered.append(
-            [lax.all_gather(part, "seq", axis=0, tiled=True) for part in (piece[:, :qkv_cols], piece[:, qkv_cols:])]
-        )
 
     pos = positions(segment_ids)
     index = jnp.arange(length, dtype=jnp.int32)

time: 422 us -> 395 us (0.936)
  local copies, waits for them, and re-layouts: 70.1 us -> 54.4 us
  waiting for transfers between devices: 123 us -> 114 us
  blocking collectives: 80.7 us -> 73.9 us
    all_gather x4, waiting for transfers between devices: 62.6 us -> 45.1 us  [shards(): lax.all_gather(part.reshape(n_tp * block, -1), 'seq', axis=0, tiled=True)]
    all_to_all x3, waiting for transfers between devices: 60 us -> 66.9 us  [exchange(): return lax.all_to_all(x, 'tp', split_axis=0, concat_axis=0, tiled=True)]
    all_to_all x2 -> x3, blocking collectives: 51.3 us -> 44.5 us  [shards(): part = lax.all_to_all(part, 'tp', split_axis=1, concat_axis=0, tiled=True)]
    slice x5 -> x3, local copies, waits for them, and re-layouts: 6.72 us -> 1.4 us  [the longest x1 1.03 us: shards(): wq[layer]]
    unnamed x39 -> x36, local copies, waits for them, and re-layouts: 17.3 us -> 13.1 us
  transfers between devices with their start and end apart: 7 -> 8, of which waited for: 5 -> 6; matrix products, arithmetic and copies ran while one was open for 32% -> 34% of each run, Pallas kernels for 0% -> 0%
where the time goes in v11:
time: 395 us; the launch traced here: 389 us
  waiting for transfers between devices  114 us (29%)
  matrix products  92.9 us (24%)
  blocking collectives  73.9 us (19%)
  local copies, waits for them, and re-layouts  54.4 us (14%)
  other arithmetic  24.9 us (6%)
  starting transfers between devices  15 us (4%)
  between operations  13.7 us (3%)
    all_to_all x3, waiting for transfers between devices, exchange(): return lax.all_to_all(x, 'tp', split_axis=0, concat_axis=0, tiled=True)  66.9 us
    dot_general x2, matrix products, shards(): jnp.dot(hidden_units, down_w[layer], preferred_element_type=jnp.float32)  52.6 us
    all_gather x4, waiting for transfers between devices, shards(): lax.all_gather(part.reshape(n_tp * block, -1), 'seq', axis=0, tiled=True)  45.1 us
    all_to_all x3, blocking collectives, shards(): part = lax.all_to_all(part, 'tp', split_axis=1, concat_axis=0, tiled=True)  44.5 us
    all_to_all x1, blocking collectives, exchange(): return lax.all_to_all(x, 'tp', split_axis=0, concat_axis=0, tiled=True)  29.4 us
    dot_general x2, matrix products, shards(): jnp.dot(attn_in, qkv_mat, preferred_element_type=jnp.float32)  17.4 us
    unnamed x36, local copies, waits for them, and re-layouts  13.1 us
    all_to_all x3, starting transfers between devices, exchange(): return lax.all_to_all(x, 'tp', split_axis=0, concat_axis=0, tiled=True)  11 us
  transfers between devices with their start and end apart: 8, of which 6 were waited for; matrix products, arithmetic and copies ran while one was open for 34% of the time, Pallas kernels for 0%

profile of v11, /device:TPU:0, one launch (start us, length us, event | category | flops | bytes accessed | tf_op | source)
XLA Modules:
  0.0 388.9 jit_solution(17570129192269081183)
XLA Ops:
  6.5 2.1 convert_element_type.153
  8.6 1.0 fusion.184
  10.4 16.4 %all_to_all.80 = bf16[64,4,1536]{2,0,1:T(8,128)(2,1)} all-to-all(bf16[64,4,1536]{2,0,1:T(8,128)(2,1)S(1)} %copy.48), channel_id=1, replica_groups=mesh['seq'=8,'tp'=4] {'tp'}, dimensions={1} | all-to-all | bytes 1572864 | tf_op jit(solution)/shard_map/all_to_all | solution.py:79
  26.8 2.4 convert_element_type.161
  29.5 0.8 squeeze.46
  30.3 0.6 copy.54
  30.9 16.0 %all_to_all.81 = bf16[64,4,2048]{2,0,1:T(8,128)(2,1)} all-to-all(bf16[64,4,2048]{2,0,1:T(8,128)(2,1)S(1)} %copy.54), channel_id=1, replica_groups=mesh['seq'=8,'tp'=4] {'tp'}, dimensions={1} | all-to-all | bytes 2097152 | tf_op jit(solution)/shard_map/all_to_all | solution.py:79
  47.0 0.6 squeeze.48
  47.7 12.1 %all_to_all.82 = bf16[64,4,1536]{2,0,1:T(8,128)(2,1)} all-to-all(bf16[64,4,1536]{2,0,1:T(8,128)(2,1)S(1)} %copy.57), channel_id=1, replica_groups=mesh['seq'=8,'tp'=4] {'tp'}, dimensions={1} | all-to-all | bytes 1572864 | tf_op jit(solution)/shard_map/all_to_all | solution.py:79
  59.8 0.8 squeeze.52
  60.6 1.6 copy.63
  62.2 3.5 all-to-all-start.6
  68.6 0.6 gather_fusion.6
  71.5 1.3 copy.47
  73.6 2.1 all-to-all-done.6
  75.7 1.6 broadcast_in_dim.47
  77.4 3.6 all-to-all-start
  81.5 0.9 fusion.44
  82.4 1.7 multiply_cosine_fusion
  84.2 17.2 %all-to-all-done = bf16[4,512,512]{1,2,0:T(8,128)(2,1)S(1)} async-done(((bf16[4,512,512]{1,2,0:T(8,128)(2,1)}), bf16[4,512,512]{1,2,0:T(8,128)(2,1)S(1)}, u32[]{:S(2)}, u32[]{:S(2)}) %all-to-all-start) | async-done | bytes 2097184 | tf_op jit(solution)/shard_map/all_to_all | solution.py:67
  101.3 1.4 copy-done
  102.7 2.3 gather_fusion
  105.0 0.7 convert_reduce_fusion.2
  105.7 0.9 multiply_reduce_fusion.1
  106.7 2.8 add_convert_fusion.5
  109.4 8.6 %convolution_add_fusion.1 = f32[512,1536]{1,0:T(8,128)} fusion(bf16[512,2048]{0,1:T(8,128)(2,1)} %get-tuple-element.23, bf16[2048,1536]{1,0:T(8,128)(2,1)} %all-gather.5.cloned.1.call-done, f32[1536]{0:T(1024)S(1)} %get-tuple-element.16), kind=kOutput, calls=%fused_computation.73 | convolution fusion | flops 3222011904 | bytes 11540480 | tf_op jit(solution)/shard_map/dot_general | solution.py:105
  118.1 2.9 copy.49
  121.0 1.5 fusion.182
  122.5 2.6 copy.67
  125.1 2.5 copy.68
  127.6 2.3 fusion.47
  130.0 2.3 fusion.48
  132.2 3.1 fusion.79
  135.3 4.4 %fusion.186 = (f32[2,512]{1,0:T(2,128)S(1)}, f32[2,512,512]{1,2,0:T(8,128)}) fusion(pred[512,512]{0,1:T(8,128)(4,1)} %fusion.44, bf16[512,2,192]{2,0,1:T(8,128)(2,1)} %fusion.48, bf16[512,2,32]{2,0,1:T(8,128)(2,1)} %get-tuple-element.34, bf16[512,2,32]{2,0,1:T(8,128)(2,1)} %get-tuple-element.33, bf16[512,2,192]{2,0,1:T(8,128)(2,1)} %fusion.47, ...), kind=kOutput, calls=%fused_computation.267 | convolution fusion | flops 273678848 | bytes 3411968 | tf_op jit(solution)/shard_map/sub | solution.py:114
  139.7 2.9 convolution_convert_fusion.1
  142.6 31.1 %all-gather.7.cloned.1.call-done = bf16[2048,2048]{1,0:T(8,128)(2,1)} async-done(((bf16[256,2048]{1,0:T(8,128)(2,1)}), bf16[2048,2048]{1,0:T(8,128)(2,1)}) %all-gather.7.cloned.1.call-update) | async-done | bytes 8388624 | tf_op jit(solution)/shard_map/all_gather | solution.py:80
  173.8 26.3 %fusion.4 = f32[512,2048]{1,0:T(8,128)} fusion(bf16[2,2048,2048]{2,1,0:T(8,128)(2,1)} %param.24, bf16[512,2048]{0,1:T(8,128)(2,1)} %get-tuple-element.24, bf16[2048,2048]{1,0:T(8,128)(2,1)} %all-gather.7.cloned.1.call-done, f32[2048]{0:T(1024)S(1)} %bitcast.214), kind=kOutput, calls=%fused_computation.14 | convolution fusion | flops 8659140608 | bytes 23076864 | tf_op jit(solution)/shard_map/dot_general | solution.py:121
  200.1 4.2 %add_convert_fusion.3 = bf16[512,2048]{1,0:T(8,128)(2,1)S(1)} fusion(f32[512,2048]{1,0:T(8,128)} %fusion.4, bf16[512,512]{0,1:T(8,128)(2,1)S(1)} %bitcast.208, bf16[2,512,2048]{2,1,0:T(8,128)(2,1)} %param.23), kind=kOutput, calls=%fused_computation.49 | convolution fusion | flops 1075838976 | bytes 8912896 | tf_op jit(solution)/shard_map/dot_general | solution.py:121
  204.3 1.6 copy.86
  205.8 3.8 all-to-all-start.3
  209.7 25.4 %all-to-all-done.3 = bf16[4,512,512]{2,1,0:T(8,128)(2,1)S(1)} async-done(((bf16[4,512,512]{2,1,0:T(8,128)(2,1)}), bf16[4,512,512]{2,1,0:T(8,128)(2,1)S(1)}, u32[]{:S(2)}, u32[]{:S(2)}) %all-to-all-start.3) | async-done | bytes 2097184 | tf_op jit(solution)/shard_map/all_to_all | solution.py:67
  235.8 1.6 broadcast_in_dim.52
  237.4 3.6 all-to-all-start.4
  241.3 24.4 %all-to-all-done.4 = bf16[4,512,512]{1,2,0:T(8,128)(2,1)S(1)} async-done(((bf16[4,512,512]{1,2,0:T(8,128)(2,1)}), bf16[4,512,512]{1,2,0:T(8,128)(2,1)S(1)}, u32[]{:S(2)}, u32[]{:S(2)}) %all-to-all-start.4) | async-done | bytes 2097184 | tf_op jit(solution)/shard_map/all_to_all | solution.py:67
  265.6 1.4 copy-done.1
  267.0 2.3 gather_fusion.5
  269.3 0.7 convert_reduce_fusion.3
  270.1 0.9 multiply_reduce_fusion
  271.0 2.8 add_convert_fusion.2
  273.8 8.8 %convolution_add_fusion = f32[512,1536]{1,0:T(8,128)} fusion(bf16[512,2048]{0,1:T(8,128)(2,1)} %get-tuple-element.21, bf16[2048,1536]{1,0:T(8,128)(2,1)} %all-gather.9.cloned.1.call-done, f32[1536]{0:T(1024)S(1)} %get-tuple-element.15), kind=kOutput, calls=%fused_computation.72 | convolution fusion | flops 3222011904 | bytes 11540480 | tf_op jit(solution)/shard_map/dot_general | solution.py:105
  282.5 2.8 copy.58
  285.3 1.5 fusion.181
  286.8 2.6 copy.69
  289.5 2.5 copy.70
  292.0 2.3 fusion.49
  294.3 2.2 fusion.50
  296.5 3.2 fusion.83
  299.7 4.5 %fusion.191 = (f32[2,512]{1,0:T(2,128)S(1)}, f32[2,512,512]{1,2,0:T(8,128)}) fusion(pred[512,512]{0,1:T(8,128)(4,1)} %fusion.44, bf16[512,2,192]{2,0,1:T(8,128)(2,1)} %fusion.50, bf16[512,2,32]{2,0,1:T(8,128)(2,1)} %get-tuple-element.28, bf16[512,2,32]{2,0,1:T(8,128)(2,1)} %get-tuple-element.27, bf16[512,2,192]{2,0,1:T(8,128)(2,1)} %fusion.49, ...), kind=kOutput, calls=%fused_computation.268 | convolution fusion | flops 273678848 | bytes 3411968 | tf_op jit(solution)/shard_map/sub | solution.py:114
  304.2 2.9 convolution_convert_fusion
  307.0 13.9 %all-gather.11.cloned.1.call-done = bf16[2048,2048]{1,0:T(8,128)(2,1)} async-done(((bf16[256,2048]{1,0:T(8,128)(2,1)}), bf16[2048,2048]{1,0:T(8,128)(2,1)}) %all-gather.11.cloned.1.call-update) | async-done | bytes 8388624 | tf_op jit(solution)/shard_map/all_gather | solution.py:80
  321.0 26.2 %fusion.2 = f32[512,2048]{1,0:T(8,128)} fusion(bf16[2,2048,2048]{2,1,0:T(8,128)(2,1)} %param.24, bf16[512,2048]{0,1:T(8,128)(2,1)} %get-tuple-element.22, bf16[2048,2048]{1,0:T(8,128)(2,1)} %all-gather.11.cloned.1.call-done, f32[2048]{0:T(1024)S(1)} %bitcast.213), kind=kOutput, calls=%fused_computation.12 | convolution fusion | flops 8659140608 | bytes 23076864 | tf_op jit(solution)/shard_map/dot_general | solution.py:121
  347.2 4.1 %add_convert_fusion = bf16[512,2048]{1,0:T(8,128)(2,1)S(1)} fusion(f32[512,2048]{1,0:T(8,128)} %fusion.2, bf16[512,512]{0,1:T(8,128)(2,1)S(1)} %bitcast.207, bf16[2,512,2048]{2,1,0:T(8,128)(2,1)} %param.23), kind=kOutput, calls=%fused_computation.31 | convolution fusion | flops 1075838976 | bytes 8912896 | tf_op jit(solution)/shard_map/dot_general | solution.py:121
  351.5 29.4 %all_to_all.83 = bf16[4,512,512]{2,1,0:T(8,128)(2,1)S(1)} all-to-all(bf16[4,512,512]{2,1,0:T(8,128)(2,1)S(1)} %bitcast.192), channel_id=1, replica_groups=mesh['seq'=8,'tp'=4] {'tp'}, dimensions={0} | all-to-all | bytes 4194304 | tf_op jit(solution)/shard_map/all_to_all | solution.py:67
  381.2 1.0 fusion.37
  (94 shorter events, 9.2 us)
Async XLA Ops:
  6.5 102.9 %all-gather.5.cloned.1.call-start = ((), (), s32[]{:S(2)}) async-start(), calls=%async_computation.8 | async-start | bytes 7077888 | tf_op jit(solution)/shard_map/all_gather | solution.py:80
  26.8 147.0 %all-gather.7.cloned.1.call-start = ((), (), s32[]{:S(2)}) async-start(), calls=%async_computation.9 | async-start | bytes 9437184 | tf_op jit(solution)/shard_map/all_gather | solution.py:80
  30.3 16.7 %copy-start.5 = (bf16[1,64,6144]{2,1,0:T(8,128)(2,1)S(1)}, bf16[1,64,6144]{2,1,0:T(8,128)(2,1)}, u32[]{:S(2)}) copy-start(bf16[1,64,6144]{2,1,0:T(8,128)(2,1)} %get-tuple-element.31) | copy-start | bytes 2359300
  46.9 226.8 %all-gather.9.cloned.1.call-start = ((), (), s32[]{:S(2)}) async-start(), calls=%async_computation.10 | async-start | bytes 7077888 | tf_op jit(solution)/shard_map/all_gather | solution.py:80
  47.7 18.0 %copy-start.11 = (f32[2,2,2048]{2,1,0:T(2,128)S(1)}, f32[2,2,2048]{2,1,0:T(2,128)}, u32[]{:S(2)}) copy-start(f32[2,2,2048]{2,1,0:T(2,128)} %param.27) | copy-start | bytes 98308
  47.7 18.0 %copy-start.12 = (f32[2,2,2048]{2,1,0:T(2,128)S(1)}, f32[2,2,2048]{2,1,0:T(2,128)}, u32[]{:S(2)}) copy-start(f32[2,2,2048]{2,1,0:T(2,128)} %param.26) | copy-start | bytes 98308
  47.7 18.3 %copy-start.15 = (s32[32]{0:T(128)S(1)}, s32[32]{0:T(128)}, u32[]{:S(2)}) copy-start(s32[32]{0:T(128)} %param.18) | copy-start | bytes 388
  59.8 13.0 %copy-start.9 = (s32[1,512]{1,0:T(1,128)S(1)}, s32[1,512]{1,0:T(1,128)}, u32[]{:S(2)}) copy-start(s32[1,512]{1,0:T(1,128)} %param.17) | copy-start | bytes 6148
  62.2 13.5 %all-to-all-start.6 = ((bf16[64,4,2048]{2,0,1:T(8,128)(2,1)}), bf16[64,4,2048]{2,0,1:T(8,128)(2,1)S(1)}, u32[]{:S(2)}, u32[]{:S(2)}) async-start(bf16[64,4,2048]{2,0,1:T(8,128)(2,1)} %copy.63), calls=%async_computation.6 | async-start | bytes 2097152 | tf_op jit(solution)/shard_map/all_to_all | solution.py:79
  70.5 10.8 %copy-start.13 = (bf16[2,1536]{1,0:T(2,128)(2,1)S(1)}, bf16[2,1536]{1,0:T(2,128)(2,1)}, u32[]{:S(2)}) copy-start(bf16[2,1536]{1,0:T(2,128)(2,1)} %param.21) | copy-start | bytes 18436
  71.5 12.6 %copy-start.10 = (bf16[2,2048]{1,0:T(2,128)(2,1)S(1)}, bf16[2,2048]{1,0:T(2,128)(2,1)}, u32[]{:S(2)}) copy-start(bf16[2,2048]{1,0:T(2,128)(2,1)} %param.22) | copy-start | bytes 24580
  75.7 8.4 %copy-start.4 = (bf16[64,4,2048]{2,0,1:T(8,128)(2,1)}, bf16[64,4,2048]{2,0,1:T(8,128)(2,1)S(1)}, u32[]{:S(2)}) copy-start(bf16[64,4,2048]{2,0,1:T(8,128)(2,1)S(1)} %all-to-all-done.6) | copy-start | bytes 3145732
  77.4 24.0 %all-to-all-start = ((bf16[4,512,512]{1,2,0:T(8,128)(2,1)}), bf16[4,512,512]{1,2,0:T(8,128)(2,1)S(1)}, u32[]{:S(2)}, u32[]{:S(2)}) async-start(bf16[4,512,512]{1,2,0:T(8,128)(2,1)} %broadcast_in_dim.47), calls=%async_computation | async-start | bytes 4194304 | tf_op jit(solution)/shard_map/all_to_all | solution.py:67
  81.0 240.0 %all-gather.11.cloned.1.call-start = ((), (), s32[]{:S(2)}) async-start(), calls=%async_computation.11 | async-start | bytes 9437184 | tf_op jit(solution)/shard_map/all_gather | solution.py:80
  101.3 1.4 copy-start
  173.8 26.3 %copy-start.8 = (bf16[2,256,512]{2,1,0:T(8,128)(2,1)S(1)}, bf16[2,256,512]{2,1,0:T(8,128)(2,1)}, u32[]{:S(2)}) copy-start(bf16[2,256,512]{2,1,0:T(8,128)(2,1)} %convolution_convert_fusion.1) | copy-start | bytes 1572868
  204.3 5.4 %copy-start.14 = (f32[2,512]{1,0:T(2,128)S(1)}, f32[2,512]{1,0:T(2,128)}, u32[]{:S(2)}) copy-start(f32[2,512]{1,0:T(2,128)} %param.25) | copy-start | bytes 12292
  205.8 29.6 %copy-start.6 = (bf16[1,512,512]{2,1,0:T(8,128)(2,1)S(1)}, bf16[1,512,512]{2,1,0:T(8,128)(2,1)}, u32[]{:S(2)}) copy-start(bf16[1,512,512]{2,1,0:T(8,128)(2,1)} %param.16) | copy-start | bytes 1572868
  205.8 29.2 %all-to-all-start.3 = ((bf16[4,512,512]{2,1,0:T(8,128)(2,1)}), bf16[4,512,512]{2,1,0:T(8,128)(2,1)S(1)}, u32[]{:S(2)}, u32[]{:S(2)}) async-start(bf16[4,512,512]{2,1,0:T(8,128)(2,1)} %bitcast.191), calls=%async_computation.3 | async-start | bytes 4194304 | tf_op jit(solution)/shard_map/all_to_all | solution.py:67
  235.6 1.8 copy-start.2
  237.4 28.3 %all-to-all-start.4 = ((bf16[4,512,512]{1,2,0:T(8,128)(2,1)}), bf16[4,512,512]{1,2,0:T(8,128)(2,1)S(1)}, u32[]{:S(2)}, u32[]{:S(2)}) async-start(bf16[4,512,512]{1,2,0:T(8,128)(2,1)} %broadcast_in_dim.52), calls=%async_computation.4 | async-start | bytes 4194304 | tf_op jit(solution)/shard_map/all_to_all | solution.py:67
  265.6 1.4 copy-start.1
  321.0 26.2 %copy-start.7 = (bf16[2,256,512]{2,1,0:T(8,128)(2,1)S(1)}, bf16[2,256,512]{2,1,0:T(8,128)(2,1)}, u32[]{:S(2)}) copy-start(bf16[2,256,512]{2,1,0:T(8,128)(2,1)} %convolution_convert_fusion) | copy-start | bytes 1572868
  351.5 29.8 %copy-start.3 = (bf16[1,512,512]{2,1,0:T(8,128)(2,1)S(1)}, bf16[1,512,512]{2,1,0:T(8,128)(2,1)}, u32[]{:S(2)}) copy-start(bf16[1,512,512]{2,1,0:T(8,128)(2,1)} %copy-done.2) | copy-start | bytes 1572868
Sparse Core Ops, SparseCore 0:
  26.9 64.4 all-gather.4
  93.0 80.6 all-gather.6
  175.4 63.2 all-gather.8
  240.2 80.7 all-gather.10

commit v12 on v11

--- a/solution.py
+++ b/solution.py
@@ -116,14 +116,19 @@
             jnp.bfloat16
         )
         ctx = ctx.reshape(rows * length, heads_here * HD)
-        up = jnp.dot(mlp_in, up_mat, preferred_element_type=jnp.float32) + up_bias[layer].astype(jnp.float32)
-        hidden_units = jax.nn.gelu(up, approximate=False).astype(jnp.bfloat16)
-        partial_terms = jnp.dot(ctx, dense_w[layer], preferred_element_type=jnp.float32) + jnp.dot(
-            hidden_units, down_w[layer], preferred_element_type=jnp.float32
-        )
-        partial_terms = partial_terms.astype(jnp.bfloat16)
-        split = partial_terms.reshape(rows * length, n_tp, width_here).transpose(1, 0, 2)
-        summed = jnp.sum(exchange(split).astype(jnp.float32), axis=0)
+        chunks = 2 if layer + 1 == LAYERS else 1
+        size = rows * length // chunks
+        sums = []
+        for chunk in range(chunks):
+            rows_here = slice(chunk * size, (chunk + 1) * size)
+            up = jnp.dot(mlp_in[rows_here], up_mat, preferred_element_type=jnp.float32)
+            hidden_units = jax.nn.gelu(up + up_bias[layer].astype(jnp.float32), approximate=False).astype(jnp.bfloat16)
+            partial_terms = jnp.dot(ctx[rows_here], dense_w[layer], preferred_element_type=jnp.float32) + jnp.dot(
+                hidden_units, down_w[layer], preferred_element_type=jnp.float32
+            )
+            split = partial_terms.astype(jnp.bfloat16).reshape(size, n_tp, width_here).transpose(1, 0, 2)
+            sums.append(jnp.sum(exchange(split).astype(jnp.float32), axis=0))
+        summed = jnp.concatenate(sums, axis=0) if chunks > 1 else sums[0]
         flat_stream = stream.astype(jnp.float32).reshape(rows * length, -1)
         stream = (flat_stream + summed + out_bias[layer]).astype(jnp.bfloat16).reshape(rows, length, -1)
     return stream

time: 395 us -> 395 us (level)
  blocking collectives: 73.9 us -> 44.5 us
  waiting for transfers between devices: 114 us -> 130 us
  starting transfers between devices: 15 us -> 23 us
  matrix products: 92.9 us -> 98.2 us
    all_to_all x1 -> x0, blocking collectives: 29.4 us -> none  [exchange(): return lax.all_to_all(x, 'tp', split_axis=0, concat_axis=0, tiled=True)]
    all_to_all x3 -> x5, waiting for transfers between devices: 66.9 us -> 80.4 us  [exchange(): return lax.all_to_all(x, 'tp', split_axis=0, concat_axis=0, tiled=True)]
    all_to_all x3 -> x5, starting transfers between devices: 11 us -> 18.9 us  [exchange(): return lax.all_to_all(x, 'tp', split_axis=0, concat_axis=0, tiled=True)]
    dot_general x2 -> x3, matrix products: 52.6 us -> 57.6 us  [shards(): jnp.dot(hidden_units, down_w[layer], preferred_element_type=jnp.float32)]
    dot_general x2 -> x3, matrix products: 8.28 us -> 9.45 us  [shards(): jnp.dot(ctx[rows_here], dense_w[layer], preferred_element_type=jnp.float32)]
    unnamed x36 -> x44, local copies, waits for them, and re-layouts: 13.1 us -> 13.2 us
  transfers between devices with their start and end apart: 8 -> 10, of which waited for: 6 -> 7; matrix products, arithmetic and copies ran while one was open for 34% -> 39% of each run, Pallas kernels for 0% -> 0%
where the time goes in v12:
time: 395 us; the launch traced here: 389 us
  waiting for transfers between devices  130 us (33%)
  matrix products  98.2 us (25%)
  local copies, waits for them, and re-layouts  55.8 us (14%)
  blocking collectives  44.5 us (11%)
  other arithmetic  23.5 us (6%)
  starting transfers between devices  23 us (6%)
  between operations  13.7 us (3%)
    all_to_all x5, waiting for transfers between devices, exchange(): return lax.all_to_all(x, 'tp', split_axis=0, concat_axis=0, tiled=True)  80.4 us
    dot_general x3, matrix products, shards(): jnp.dot(hidden_units, down_w[layer], preferred_element_type=jnp.float32)  57.6 us
    all_gather x4, waiting for transfers between devices, shards(): lax.all_gather(part.reshape(n_tp * block, -1), 'seq', axis=0, tiled=True)  46.9 us
    all_to_all x3, blocking collectives, shards(): part = lax.all_to_all(part, 'tp', split_axis=1, concat_axis=0, tiled=True)  44.5 us
    all_to_all x5, starting transfers between devices, exchange(): return lax.all_to_all(x, 'tp', split_axis=0, concat_axis=0, tiled=True)  18.9 us
    dot_general x2, matrix products, shards(): jnp.dot(attn_in, qkv_mat, preferred_element_type=jnp.float32)  17.4 us
    unnamed x44, local copies, waits for them, and re-layouts  13.2 us
    dot_general x3, matrix products, shards(): jnp.dot(ctx[rows_here], dense_w[layer], preferred_element_type=jnp.float32)  9.45 us
  transfers between devices with their start and end apart: 10, of which 7 were waited for; matrix products, arithmetic and copies ran while one was open for 39% of the time, Pallas kernels for 0%

profile of v12, /device:TPU:0, one launch (start us, length us, event | category | flops | bytes accessed | tf_op | source)
XLA Modules:
  0.0 389.1 jit_solution(16863292146262231671)
XLA Ops:
  6.5 2.1 convert_element_type.163
  8.6 1.0 fusion.300
  10.4 16.4 %all_to_all.85 = bf16[64,4,1536]{2,0,1:T(8,128)(2,1)} all-to-all(bf16[64,4,1536]{2,0,1:T(8,128)(2,1)S(1)} %copy.48), channel_id=1, replica_groups=mesh['seq'=8,'tp'=4] {'tp'}, dimensions={1} | all-to-all | bytes 1572864 | tf_op jit(solution)/shard_map/all_to_all | solution.py:79
  26.8 2.4 convert_element_type.171
  29.5 0.8 squeeze.49
  30.9 16.2 %all_to_all.86 = bf16[64,4,2048]{2,0,1:T(8,128)(2,1)} all-to-all(bf16[64,4,2048]{2,0,1:T(8,128)(2,1)S(1)} %copy.54), channel_id=1, replica_groups=mesh['seq'=8,'tp'=4] {'tp'}, dimensions={1} | all-to-all | bytes 2097152 | tf_op jit(solution)/shard_map/all_to_all | solution.py:79
  47.8 11.9 %all_to_all.87 = bf16[64,4,1536]{2,0,1:T(8,128)(2,1)} all-to-all(bf16[64,4,1536]{2,0,1:T(8,128)(2,1)S(1)} %copy.57), channel_id=1, replica_groups=mesh['seq'=8,'tp'=4] {'tp'}, dimensions={1} | all-to-all | bytes 1572864 | tf_op jit(solution)/shard_map/all_to_all | solution.py:79
  59.8 0.8 squeeze.55
  60.6 1.6 copy.63
  62.2 3.6 all-to-all-start.6
  72.7 3.1 all-to-all-done.6
  75.8 1.6 broadcast_in_dim.47
  77.5 3.6 all-to-all-start
  81.6 0.9 fusion.130
  82.6 1.7 multiply_cosine_fusion
  84.3 17.2 %all-to-all-done = bf16[4,512,512]{1,2,0:T(8,128)(2,1)S(1)} async-done(((bf16[4,512,512]{1,2,0:T(8,128)(2,1)}), bf16[4,512,512]{1,2,0:T(8,128)(2,1)S(1)}, u32[]{:S(2)}, u32[]{:S(2)}) %all-to-all-start) | async-done | bytes 2097184 | tf_op jit(solution)/shard_map/all_to_all | solution.py:67
  101.5 1.4 copy-done
  102.9 2.3 gather_fusion
  105.9 0.9 multiply_reduce_fusion.1
  106.8 2.8 add_convert_fusion.4
  109.6 8.6 %convolution_add_fusion.1 = f32[512,1536]{1,0:T(8,128)} fusion(bf16[512,2048]{0,1:T(8,128)(2,1)} %get-tuple-element.23, bf16[2048,1536]{1,0:T(8,128)(2,1)} %all-gather.5.cloned.1.call-done, f32[1536]{0:T(1024)S(1)} %get-tuple-element.16), kind=kOutput, calls=%fused_computation.55 | convolution fusion | flops 3222011904 | bytes 11540480 | tf_op jit(solution)/shard_map/dot_general | solution.py:105
  118.2 2.9 copy.49
  121.2 1.5 fusion.298
  122.7 2.6 copy.68
  125.3 2.6 copy.69
  127.8 2.4 fusion.133
  130.2 2.2 fusion.134
  132.5 2.4 fusion.165
  134.9 4.4 %fusion.303 = (f32[2,512]{1,0:T(2,128)S(1)}, f32[2,512,512]{1,2,0:T(8,128)}) fusion(pred[512,512]{0,1:T(8,128)(4,1)} %fusion.130, bf16[512,2,192]{2,0,1:T(8,128)(2,1)} %fusion.134, bf16[512,2,32]{2,0,1:T(8,128)(2,1)} %get-tuple-element.34, bf16[512,2,32]{2,0,1:T(8,128)(2,1)} %get-tuple-element.33, bf16[512,2,192]{2,0,1:T(8,128)(2,1)} %fusion.133, ...), kind=kOutput, calls=%fused_computation.394 | convolution fusion | flops 273678848 | bytes 3411968 | tf_op jit(solution)/shard_map/sub | solution.py:114
  139.3 2.9 convolution_convert_fusion.1
  142.2 31.6 %all-gather.7.cloned.1.call-done = bf16[2048,2048]{1,0:T(8,128)(2,1)} async-done(((bf16[256,2048]{1,0:T(8,128)(2,1)}), bf16[2048,2048]{1,0:T(8,128)(2,1)}) %all-gather.7.cloned.1.call-update) | async-done | bytes 8388624 | tf_op jit(solution)/shard_map/all_gather | solution.py:80
  173.8 26.3 %fusion.6 = f32[512,2048]{1,0:T(8,128)} fusion(bf16[2,2048,2048]{2,1,0:T(8,128)(2,1)} %param.24, bf16[512,2048]{0,1:T(8,128)(2,1)} %get-tuple-element.24, bf16[2048,2048]{1,0:T(8,128)(2,1)} %all-gather.7.cloned.1.call-done, f32[2048]{0:T(1024)S(1)} %bitcast.227), kind=kOutput, calls=%fused_computation.16 | convolution fusion | flops 8659140608 | bytes 23076864 | tf_op jit(solution)/shard_map/dot_general | solution.py:126
  200.1 4.2 %add_convert_fusion.2 = bf16[512,2048]{1,0:T(8,128)(2,1)S(1)} fusion(f32[512,2048]{1,0:T(8,128)} %fusion.6, bf16[512,512]{0,1:T(8,128)(2,1)S(1)} %bitcast.220, bf16[2,512,2048]{2,1,0:T(8,128)(2,1)} %param.23), kind=kOutput, calls=%fused_computation.33 | convolution fusion | flops 1075838976 | bytes 8912896 | tf_op jit(solution)/shard_map/dot_general | solution.py:126
  204.3 1.6 copy.88
  205.8 3.8 all-to-all-start.3
  209.6 25.4 %all-to-all-done.3 = bf16[4,512,512]{2,1,0:T(8,128)(2,1)S(1)} async-done(((bf16[4,512,512]{2,1,0:T(8,128)(2,1)}), bf16[4,512,512]{2,1,0:T(8,128)(2,1)S(1)}, u32[]{:S(2)}, u32[]{:S(2)}) %all-to-all-start.3) | async-done | bytes 2097184 | tf_op jit(solution)/shard_map/all_to_all | solution.py:67
  235.8 1.6 broadcast_in_dim.52
  237.4 3.6 all-to-all-start.4
  241.3 24.4 %all-to-all-done.4 = bf16[4,512,512]{1,2,0:T(8,128)(2,1)S(1)} async-done(((bf16[4,512,512]{1,2,0:T(8,128)(2,1)}), bf16[4,512,512]{1,2,0:T(8,128)(2,1)S(1)}, u32[]{:S(2)}, u32[]{:S(2)}) %all-to-all-start.4) | async-done | bytes 2097184 | tf_op jit(solution)/shard_map/all_to_all | solution.py:67
  265.6 1.4 copy-done.1
  267.0 2.3 gather_fusion.5
  270.1 0.9 multiply_reduce_fusion
  271.0 2.8 add_convert_fusion.1
  273.8 8.8 %convolution_add_fusion = f32[512,1536]{1,0:T(8,128)} fusion(bf16[512,2048]{0,1:T(8,128)(2,1)} %get-tuple-element.21, bf16[2048,1536]{1,0:T(8,128)(2,1)} %all-gather.9.cloned.1.call-done, f32[1536]{0:T(1024)S(1)} %get-tuple-element.15), kind=kOutput, calls=%fused_computation.54 | convolution fusion | flops 3222011904 | bytes 11540480 | tf_op jit(solution)/shard_map/dot_general | solution.py:105
  282.6 2.8 copy.58
  285.4 1.5 fusion.297
  286.9 2.6 copy.70
  289.5 2.5 copy.71
  292.1 2.4 fusion.135
  294.5 2.2 fusion.136
  296.7 2.4 fusion.169
  299.1 4.5 %fusion.308 = (f32[2,512]{1,0:T(2,128)S(1)}, f32[2,512,512]{1,2,0:T(8,128)}) fusion(pred[512,512]{0,1:T(8,128)(4,1)} %fusion.130, bf16[512,2,192]{2,0,1:T(8,128)(2,1)} %fusion.136, bf16[512,2,32]{2,0,1:T(8,128)(2,1)} %get-tuple-element.28, bf16[512,2,32]{2,0,1:T(8,128)(2,1)} %get-tuple-element.27, bf16[512,2,192]{2,0,1:T(8,128)(2,1)} %fusion.135, ...), kind=kOutput, calls=%fused_computation.395 | convolution fusion | flops 273678848 | bytes 3411968 | tf_op jit(solution)/shard_map/sub | solution.py:114
  303.6 2.0 fusion.53
  305.7 15.3 %all-gather.11.cloned.1.call-done = bf16[2048,2048]{1,0:T(8,128)(2,1)} async-done(((bf16[256,2048]{1,0:T(8,128)(2,1)}), bf16[2048,2048]{1,0:T(8,128)(2,1)}) %all-gather.11.cloned.1.call-update) | async-done | bytes 8388624 | tf_op jit(solution)/shard_map/all_gather | solution.py:80
  320.9 14.9 %fusion.4 = f32[256,2048]{1,0:T(8,128)S(1)} fusion(bf16[2,2048,2048]{2,1,0:T(8,128)(2,1)} %param.24, bf16[2048,2048]{1,0:T(8,128)(2,1)} %all-gather.11.cloned.1.call-done, bf16[512,2048]{0,1:T(8,128)(2,1)} %get-tuple-element.22, f32[2048]{0:T(1024)S(1)} %bitcast.225), kind=kOutput, calls=%fused_computation.14 | convolution fusion | flops 4329570304 | bytes 19931136 | tf_op jit(solution)/shard_map/dot_general | solution.py:126
  335.9 2.3 fusion.23
  338.2 1.2 copy.90
  339.4 3.7 all-to-all-start.7
  343.1 16.3 %fusion.2 = f32[256,2048]{1,0:T(8,128)} fusion(bf16[2,2048,2048]{2,1,0:T(8,128)(2,1)} %param.24, bf16[2048,2048]{1,0:T(8,128)(2,1)} %all-gather.11.cloned.1.call-done, bf16[512,2048]{0,1:T(8,128)(2,1)} %get-tuple-element.22, f32[2048]{0:T(1024)S(1)} %bitcast.226), kind=kOutput, calls=%fused_computation.12 | convolution fusion | flops 4329570304 | bytes 19931136 | tf_op jit(solution)/shard_map/dot_general | solution.py:126
  359.5 3.0 fusion.24
  362.4 1.1 copy.89
  363.5 4.2 %all-to-all-start.8 = ((bf16[4,256,512]{2,1,0:T(8,128)(2,1)}), bf16[4,256,512]{2,1,0:T(8,128)(2,1)S(1)}, u32[]{:S(2)}, u32[]{:S(2)}) async-start(bf16[4,256,512]{2,1,0:T(8,128)(2,1)} %bitcast.189), calls=%async_computation.8 | async-start | bytes 2097152 | tf_op jit(solution)/shard_map/all_to_all | solution.py:67
  367.8 13.4 %all-to-all-done.8 = bf16[4,256,512]{2,1,0:T(8,128)(2,1)S(1)} async-done(((bf16[4,256,512]{2,1,0:T(8,128)(2,1)}), bf16[4,256,512]{2,1,0:T(8,128)(2,1)S(1)}, u32[]{:S(2)}, u32[]{:S(2)}) %all-to-all-start.8) | async-done | bytes 1048608 | tf_op jit(solution)/shard_map/all_to_all | solution.py:67
  381.4 1.0 fusion.61
  (110 shorter events, 12.5 us)
Async XLA Ops:
  6.5 103.1 %all-gather.5.cloned.1.call-start = ((), (), s32[]{:S(2)}) async-start(), calls=%async_computation.9 | async-start | bytes 7077888 | tf_op jit(solution)/shard_map/all_gather | solution.py:80
  26.8 147.0 %all-gather.7.cloned.1.call-start = ((), (), s32[]{:S(2)}) async-start(), calls=%async_computation.10 | async-start | bytes 9437184 | tf_op jit(solution)/shard_map/all_gather | solution.py:80
  30.9 16.2 %copy-start.9 = (bf16[1,64,6144]{2,1,0:T(8,128)(2,1)S(1)}, bf16[1,64,6144]{2,1,0:T(8,128)(2,1)}, u32[]{:S(2)}) copy-start(bf16[1,64,6144]{2,1,0:T(8,128)(2,1)} %get-tuple-element.31) | copy-start | bytes 2359300
  47.1 226.8 %all-gather.9.cloned.1.call-start = ((), (), s32[]{:S(2)}) async-start(), calls=%async_computation.11 | async-start | bytes 7077888 | tf_op jit(solution)/shard_map/all_gather | solution.py:80
  60.6 5.3 %copy-start.15 = (f32[2,2,2048]{2,1,0:T(2,128)S(1)}, f32[2,2,2048]{2,1,0:T(2,128)}, u32[]{:S(2)}) copy-start(f32[2,2,2048]{2,1,0:T(2,128)} %param.27) | copy-start | bytes 98308
  60.6 5.3 %copy-start.16 = (f32[2,2,2048]{2,1,0:T(2,128)S(1)}, f32[2,2,2048]{2,1,0:T(2,128)}, u32[]{:S(2)}) copy-start(f32[2,2,2048]{2,1,0:T(2,128)} %param.26) | copy-start | bytes 98308
  60.6 5.6 %copy-start.19 = (s32[32]{0:T(128)S(1)}, s32[32]{0:T(128)}, u32[]{:S(2)}) copy-start(s32[32]{0:T(128)} %param.18) | copy-start | bytes 388
  62.2 9.4 %copy-start.10 = (bf16[1,512,512]{2,1,0:T(8,128)(2,1)S(1)}, bf16[1,512,512]{2,1,0:T(8,128)(2,1)}, u32[]{:S(2)}) copy-start(bf16[1,512,512]{2,1,0:T(8,128)(2,1)} %param.16) | copy-start | bytes 1572868
  62.2 9.6 %copy-start.13 = (s32[1,512]{1,0:T(1,128)S(1)}, s32[1,512]{1,0:T(1,128)}, u32[]{:S(2)}) copy-start(s32[1,512]{1,0:T(1,128)} %param.17) | copy-start | bytes 6148
  62.2 13.6 %all-to-all-start.6 = ((bf16[64,4,2048]{2,0,1:T(8,128)(2,1)}), bf16[64,4,2048]{2,0,1:T(8,128)(2,1)S(1)}, u32[]{:S(2)}, u32[]{:S(2)}) async-start(bf16[64,4,2048]{2,0,1:T(8,128)(2,1)} %copy.63), calls=%async_computation.6 | async-start | bytes 2097152 | tf_op jit(solution)/shard_map/all_to_all | solution.py:79
  75.8 1.7 copy-start.8
  77.5 4.0 %copy-start.17 = (bf16[2,1536]{1,0:T(2,128)(2,1)S(1)}, bf16[2,1536]{1,0:T(2,128)(2,1)}, u32[]{:S(2)}) copy-start(bf16[2,1536]{1,0:T(2,128)(2,1)} %param.21) | copy-start | bytes 18436
  77.5 6.8 %copy-start.14 = (bf16[2,2048]{1,0:T(2,128)(2,1)S(1)}, bf16[2,2048]{1,0:T(2,128)(2,1)}, u32[]{:S(2)}) copy-start(bf16[2,2048]{1,0:T(2,128)(2,1)} %param.22) | copy-start | bytes 24580
  77.5 24.0 %all-to-all-start = ((bf16[4,512,512]{1,2,0:T(8,128)(2,1)}), bf16[4,512,512]{1,2,0:T(8,128)(2,1)S(1)}, u32[]{:S(2)}, u32[]{:S(2)}) async-start(bf16[4,512,512]{1,2,0:T(8,128)(2,1)} %broadcast_in_dim.47), calls=%async_computation | async-start | bytes 4194304 | tf_op jit(solution)/shard_map/all_to_all | solution.py:67
  81.1 239.8 %all-gather.11.cloned.1.call-start = ((), (), s32[]{:S(2)}) async-start(), calls=%async_computation.12 | async-start | bytes 9437184 | tf_op jit(solution)/shard_map/all_gather | solution.py:80
  101.5 1.4 copy-start
  127.8 4.7 %copy-start.3 = (f32[1,512,2,1,256]{4,1,2,3,0:T(8,128)S(1)}, f32[1,512,2,1,256]{4,1,2,3,0:T(8,128)}, u32[]{:S(2)}) copy-start(f32[1,512,2,1,256]{4,1,2,3,0:T(8,128)} %copy.68) | copy-start | bytes 3145732
  127.8 4.7 %copy-start.5 = (f32[1,512,2,1,256]{4,1,2,3,0:T(8,128)S(1)}, f32[1,512,2,1,256]{4,1,2,3,0:T(8,128)}, u32[]{:S(2)}) copy-start(f32[1,512,2,1,256]{4,1,2,3,0:T(8,128)} %copy.69) | copy-start | bytes 3145732
  173.8 26.3 %copy-start.12 = (bf16[2,256,512]{2,1,0:T(8,128)(2,1)S(1)}, bf16[2,256,512]{2,1,0:T(8,128)(2,1)}, u32[]{:S(2)}) copy-start(bf16[2,256,512]{2,1,0:T(8,128)(2,1)} %convolution_convert_fusion.1) | copy-start | bytes 1572868
  205.8 3.8 copy-start.18
  205.8 29.2 %all-to-all-start.3 = ((bf16[4,512,512]{2,1,0:T(8,128)(2,1)}), bf16[4,512,512]{2,1,0:T(8,128)(2,1)S(1)}, u32[]{:S(2)}, u32[]{:S(2)}) async-start(bf16[4,512,512]{2,1,0:T(8,128)(2,1)} %bitcast.199), calls=%async_computation.3 | async-start | bytes 4194304 | tf_op jit(solution)/shard_map/all_to_all | solution.py:67
  209.6 25.8 %copy-start.11 = (bf16[1,512,512]{2,1,0:T(8,128)(2,1)S(1)}, bf16[1,512,512]{2,1,0:T(8,128)(2,1)}, u32[]{:S(2)}) copy-start(bf16[1,512,512]{2,1,0:T(8,128)(2,1)} %param.16) | copy-start | bytes 1572868
  235.6 1.8 copy-start.6
  237.4 28.3 %all-to-all-start.4 = ((bf16[4,512,512]{1,2,0:T(8,128)(2,1)}), bf16[4,512,512]{1,2,0:T(8,128)(2,1)S(1)}, u32[]{:S(2)}, u32[]{:S(2)}) async-start(bf16[4,512,512]{1,2,0:T(8,128)(2,1)} %broadcast_in_dim.52), calls=%async_computation.4 | async-start | bytes 4194304 | tf_op jit(solution)/shard_map/all_to_all | solution.py:67
  265.6 1.4 copy-start.1
  292.1 4.6 %copy-start.2 = (f32[1,512,2,1,256]{4,1,2,3,0:T(8,128)S(1)}, f32[1,512,2,1,256]{4,1,2,3,0:T(8,128)}, u32[]{:S(2)}) copy-start(f32[1,512,2,1,256]{4,1,2,3,0:T(8,128)} %copy.70) | copy-start | bytes 3145732
  292.1 4.6 %copy-start.4 = (f32[1,512,2,1,256]{4,1,2,3,0:T(8,128)S(1)}, f32[1,512,2,1,256]{4,1,2,3,0:T(8,128)}, u32[]{:S(2)}) copy-start(f32[1,512,2,1,256]{4,1,2,3,0:T(8,128)} %copy.71) | copy-start | bytes 3145732
  339.4 24.1 %all-to-all-start.7 = ((bf16[4,256,512]{2,1,0:T(8,128)(2,1)}), bf16[4,256,512]{2,1,0:T(8,128)(2,1)S(1)}, u32[]{:S(2)}, u32[]{:S(2)}) async-start(bf16[4,256,512]{2,1,0:T(8,128)(2,1)} %bitcast.191), calls=%async_computation.7 | async-start | bytes 2097152 | tf_op jit(solution)/shard_map/all_to_all | solution.py:67
  363.5 17.8 %all-to-all-start.8 = ((bf16[4,256,512]{2,1,0:T(8,128)(2,1)}), bf16[4,256,512]{2,1,0:T(8,128)(2,1)S(1)}, u32[]{:S(2)}, u32[]{:S(2)}) async-start(bf16[4,256,512]{2,1,0:T(8,128)(2,1)} %bitcast.189), calls=%async_computation.8 | async-start | bytes 2097152 | tf_op jit(solution)/shard_map/all_to_all | solution.py:67
  367.7 13.7 %copy-start.7 = (bf16[1,512,512]{2,1,0:T(8,128)(2,1)S(1)}, bf16[1,512,512]{2,1,0:T(8,128)(2,1)}, u32[]{:S(2)}) copy-start(bf16[1,512,512]{2,1,0:T(8,128)(2,1)} %copy-done.6) | copy-start | bytes 1572868
Sparse Core Ops, SparseCore 0:
  26.9 64.4 all-gather.4
  93.0 80.6 all-gather.6
  175.4 63.2 all-gather.8
  240.2 80.7 all-gather.10

commit v13 on v11

--- a/solution.py
+++ b/solution.py
@@ -72,13 +72,18 @@
     def joined(got):
         return got.transpose(1, 0, 2).reshape(rows, length, n_tp * width_here)
 
+    ff_here = up_bias.shape[1]
+    halves = [1] * (LAYERS - 1) + [2]
+
+    def over_rows(part):
+        part = lax.all_to_all(part, "tp", split_axis=1, concat_axis=0, tiled=True)
+        return lax.all_gather(part.reshape(n_tp * block, -1), "seq", axis=0, tiled=True)
+
     gathered = []
     for layer in range(LAYERS):
-        parts = []
-        for part in (wq[layer], wu[layer]):
-            part = lax.all_to_all(part, "tp", split_axis=1, concat_axis=0, tiled=True)
-            parts.append(lax.all_gather(part.reshape(n_tp * block, -1), "seq", axis=0, tiled=True))
-        gathered.append(parts)
+        size = ff_here // halves[layer]
+        ups = [over_rows(wu[layer][:, :, h * size : (h + 1) * size]) for h in range(halves[layer])]
+        gathered.append((over_rows(wq[layer]), ups))
     whole = joined(exchange(spread(tokens)))
 
     pos = positions(segment_ids)
@@ -116,11 +121,13 @@
             jnp.bfloat16
         )
         ctx = ctx.reshape(rows * length, heads_here * HD)
-        up = jnp.dot(mlp_in, up_mat, preferred_element_type=jnp.float32) + up_bias[layer].astype(jnp.float32)
-        hidden_units = jax.nn.gelu(up, approximate=False).astype(jnp.bfloat16)
-        partial_terms = jnp.dot(ctx, dense_w[layer], preferred_element_type=jnp.float32) + jnp.dot(
-            hidden_units, down_w[layer], preferred_element_type=jnp.float32
-        )
+        partial_terms = jnp.dot(ctx, dense_w[layer], preferred_element_type=jnp.float32)
+        size = ff_here // halves[layer]
+        for h, up_part in enumerate(up_mat):
+            units = slice(h * size, (h + 1) * size)
+            up = jnp.dot(mlp_in, up_part, preferred_element_type=jnp.float32) + up_bias[layer, units].astype(jnp.float32)
+            hidden_units = jax.nn.gelu(up, approximate=False).astype(jnp.bfloat16)
+            partial_terms = partial_terms + jnp.dot(hidden_units, down_w[layer, units], preferred_element_type=jnp.float32)
         partial_terms = partial_terms.astype(jnp.bfloat16)
         split = partial_terms.reshape(rows * length, n_tp, width_here).transpose(1, 0, 2)
         summed = jnp.sum(exchange(split).astype(jnp.float32), axis=0)

time: 395 us -> 398 us (level)
  waiting for transfers between devices: 114 us -> 108 us
  matrix products: 92.9 us -> 97.6 us
  starting transfers between devices: 15 us -> 19.1 us
    all_gather x4 -> x5, waiting for transfers between devices: 45.1 us -> 35.3 us  [over_rows(): lax.all_gather(part.reshape(n_tp * block, -1), 'seq', axis=0, tiled=True)]
    all_to_all x1 -> x2, waiting for transfers between devices: 2.09 us -> 7.08 us  [over_rows(): part = lax.all_to_all(part, 'tp', split_axis=1, concat_axis=0, tiled=True)]
    dot_general x2 -> x3, matrix products: 52.6 us -> 56.1 us  [shards(): jnp.dot(hidden_units, down_w[layer, units], preferred_element_type=jnp.fl...]
    unnamed x36 -> x52, local copies, waits for them, and re-layouts: 13.1 us -> 13.8 us
  transfers between devices with their start and end apart: 8 -> 10, of which waited for: 6 -> 6; matrix products, arithmetic and copies ran while one was open for 34% -> 38% of each run, Pallas kernels for 0% -> 0%
where the time goes in v13:
time: 398 us; the launch traced here: 391 us
  waiting for transfers between devices  108 us (27%)
  matrix products  97.6 us (25%)
  blocking collectives  73.7 us (19%)
  local copies, waits for them, and re-layouts  56.1 us (14%)
  other arithmetic  23.5 us (6%)
  starting transfers between devices  19.1 us (5%)
  between operations  13.7 us (3%)
    all_to_all x3, waiting for transfers between devices, exchange(): return lax.all_to_all(x, 'tp', split_axis=0, concat_axis=0, tiled=True)  64.9 us
    dot_general x3, matrix products, shards(): jnp.dot(hidden_units, down_w[layer, units], preferred_element_type=jnp.fl...  56.1 us
    all_to_all x3, blocking collectives, over_rows(): part = lax.all_to_all(part, 'tp', split_axis=1, concat_axis=0, tiled=True)  44.5 us
    all_gather x5, waiting for transfers between devices, over_rows(): lax.all_gather(part.reshape(n_tp * block, -1), 'seq', axis=0, tiled=True)  35.3 us
    all_to_all x1, blocking collectives, exchange(): return lax.all_to_all(x, 'tp', split_axis=0, concat_axis=0, tiled=True)  29.2 us
    dot_general x2, matrix products, shards(): jnp.dot(attn_in, qkv_mat, preferred_element_type=jnp.float32)  17.2 us
    unnamed x52, local copies, waits for them, and re-layouts  13.8 us
    all_to_all x3, starting transfers between devices, exchange(): return lax.all_to_all(x, 'tp', split_axis=0, concat_axis=0, tiled=True)  11.7 us
  transfers between devices with their start and end apart: 10, of which 6 were waited for; matrix products, arithmetic and copies ran while one was open for 38% of the time, Pallas kernels for 0%

profile of v13, /device:TPU:0, one launch (start us, length us, event | category | flops | bytes accessed | tf_op | source)
XLA Modules:
  0.0 391.5 jit_solution(8181063750373113969)
XLA Ops:
  6.5 2.1 convert_element_type.158
  8.6 1.0 fusion.289
  10.3 16.4 %all_to_all.95 = bf16[64,4,1536]{2,0,1:T(8,128)(2,1)} all-to-all(bf16[64,4,1536]{2,0,1:T(8,128)(2,1)S(1)} %copy.49), channel_id=1, replica_groups=mesh['seq'=8,'tp'=4] {'tp'}, dimensions={1} | all-to-all | bytes 1572864 | tf_op jit(solution)/shard_map/all_to_all | solution.py:79
  26.8 2.4 convert_element_type.166
  29.4 0.8 squeeze.51
  30.8 16.2 %all_to_all.96 = bf16[64,4,2048]{2,0,1:T(8,128)(2,1)} all-to-all(bf16[64,4,2048]{2,0,1:T(8,128)(2,1)S(1)} %copy.55), channel_id=1, replica_groups=mesh['seq'=8,'tp'=4] {'tp'}, dimensions={1} | all-to-all | bytes 2097152 | tf_op jit(solution)/shard_map/all_to_all | solution.py:79
  47.8 11.9 %all_to_all.97 = bf16[64,4,1536]{2,0,1:T(8,128)(2,1)} all-to-all(bf16[64,4,1536]{2,0,1:T(8,128)(2,1)S(1)} %copy.58), channel_id=1, replica_groups=mesh['seq'=8,'tp'=4] {'tp'}, dimensions={1} | all-to-all | bytes 1572864 | tf_op jit(solution)/shard_map/all_to_all | solution.py:79
  59.7 0.8 squeeze.57
  60.6 1.2 fusion.290
  61.8 1.0 copy.64
  62.7 3.5 all-to-all-start.6
  73.1 1.6 broadcast_in_dim.47
  74.6 4.3 %all-to-all-start = ((bf16[4,512,512]{1,2,0:T(8,128)(2,1)}), bf16[4,512,512]{1,2,0:T(8,128)(2,1)S(1)}, u32[]{:S(2)}, u32[]{:S(2)}) async-start(bf16[4,512,512]{1,2,0:T(8,128)(2,1)} %broadcast_in_dim.47), calls=%async_computation | async-start | bytes 4194304 | tf_op jit(solution)/shard_map/all_to_all | solution.py:67
  79.4 0.9 fusion.119
  80.3 1.7 multiply_cosine_fusion
  82.0 17.5 %all-to-all-done = bf16[4,512,512]{1,2,0:T(8,128)(2,1)S(1)} async-done(((bf16[4,512,512]{1,2,0:T(8,128)(2,1)}), bf16[4,512,512]{1,2,0:T(8,128)(2,1)S(1)}, u32[]{:S(2)}, u32[]{:S(2)}) %all-to-all-start) | async-done | bytes 2097184 | tf_op jit(solution)/shard_map/all_to_all | solution.py:67
  99.6 1.4 copy-done
  101.0 2.5 gather_fusion
  103.4 0.7 convert_reduce_fusion.2
  104.2 0.9 multiply_reduce_fusion.1
  105.1 2.8 add_convert_fusion.5
  107.9 8.6 %convolution_add_fusion.1 = f32[512,1536]{1,0:T(8,128)} fusion(bf16[512,2048]{0,1:T(8,128)(2,1)} %get-tuple-element.23, bf16[2048,1536]{1,0:T(8,128)(2,1)} %all-gather.6.cloned.1.call-done, f32[1536]{0:T(1024)S(1)} %get-tuple-element.16), kind=kOutput, calls=%fused_computation.57 | convolution fusion | flops 3222011904 | bytes 11540480 | tf_op jit(solution)/shard_map/dot_general | solution.py:110
  116.6 2.9 copy.50
  119.5 1.6 fusion.287
  121.1 2.5 copy.69
  123.6 2.6 copy.70
  126.2 2.4 fusion.122
  128.7 2.3 fusion.123
  131.0 2.4 fusion.154
  133.3 4.5 %fusion.292 = (f32[2,512]{1,0:T(2,128)S(1)}, f32[2,512,512]{1,2,0:T(8,128)}) fusion(pred[512,512]{0,1:T(8,128)(4,1)} %fusion.119, bf16[512,2,192]{2,0,1:T(8,128)(2,1)} %fusion.123, bf16[512,2,32]{2,0,1:T(8,128)(2,1)} %get-tuple-element.34, bf16[512,2,32]{2,0,1:T(8,128)(2,1)} %get-tuple-element.33, bf16[512,2,192]{2,0,1:T(8,128)(2,1)} %fusion.122, ...), kind=kOutput, calls=%fused_computation.383 | convolution fusion | flops 273678848 | bytes 3411968 | tf_op jit(solution)/shard_map/sub | solution.py:119
  137.8 2.8 convolution_convert_fusion.1
  140.6 33.1 %all-gather.8.cloned.1.call-done = bf16[2048,2048]{1,0:T(8,128)(2,1)} async-done(((bf16[256,2048]{1,0:T(8,128)(2,1)}), bf16[2048,2048]{1,0:T(8,128)(2,1)}) %all-gather.8.cloned.1.call-update) | async-done | bytes 8388624 | tf_op jit(solution)/shard_map/all_gather | solution.py:80
  173.7 26.2 %fusion.2 = f32[512,2048]{1,0:T(8,128)} fusion(bf16[2,2048,2048]{2,1,0:T(8,128)(2,1)} %param.24, bf16[512,2048]{0,1:T(8,128)(2,1)} %get-tuple-element.24, bf16[2048,2048]{1,0:T(8,128)(2,1)} %all-gather.8.cloned.1.call-done, f32[2048]{0:T(1024)S(1)} %bitcast.225), kind=kOutput, calls=%fused_computation.12 | convolution fusion | flops 8659140608 | bytes 23076864 | tf_op jit(solution)/shard_map/dot_general | solution.py:130
  200.0 4.2 %add_convert_fusion.3 = bf16[512,2048]{1,0:T(8,128)(2,1)S(1)} fusion(f32[512,2048]{1,0:T(8,128)} %fusion.2, bf16[512,512]{0,1:T(8,128)(2,1)S(1)} %bitcast.220, bf16[2,512,2048]{2,1,0:T(8,128)(2,1)} %param.23), kind=kOutput, calls=%fused_computation.35 | convolution fusion | flops 1075838976 | bytes 8912896 | tf_op jit(solution)/shard_map/dot_general | solution.py:124
  204.1 1.5 copy.88
  205.6 3.8 all-to-all-start.3
  209.5 1.0 copy.65
  210.5 24.5 %all-to-all-done.3 = bf16[4,512,512]{2,1,0:T(8,128)(2,1)S(1)} async-done(((bf16[4,512,512]{2,1,0:T(8,128)(2,1)}), bf16[4,512,512]{2,1,0:T(8,128)(2,1)S(1)}, u32[]{:S(2)}, u32[]{:S(2)}) %all-to-all-start.3) | async-done | bytes 2097184 | tf_op jit(solution)/shard_map/all_to_all | solution.py:67
  234.9 3.5 all-to-all-start.7
  239.1 7.1 %all-to-all-done.7 = bf16[64,4,1024]{2,0,1:T(8,128)(2,1)S(1)} async-done(((bf16[64,4,1024]{2,0,1:T(8,128)(2,1)}), bf16[64,4,1024]{2,0,1:T(8,128)(2,1)S(1)}, u32[]{:S(2)}, u32[]{:S(2)}) %all-to-all-start.7) | async-done | bytes 524320 | tf_op jit(solution)/shard_map/all_to_all | solution.py:79
  246.2 1.5 broadcast_in_dim.52
  247.7 3.6 all-to-all-start.4
  252.2 22.9 %all-to-all-done.4 = bf16[4,512,512]{1,2,0:T(8,128)(2,1)S(1)} async-done(((bf16[4,512,512]{1,2,0:T(8,128)(2,1)}), bf16[4,512,512]{1,2,0:T(8,128)(2,1)S(1)}, u32[]{:S(2)}, u32[]{:S(2)}) %all-to-all-start.4) | async-done | bytes 2097184 | tf_op jit(solution)/shard_map/all_to_all | solution.py:67
  275.1 1.3 copy-done.1
  276.4 2.3 gather_fusion.5
  278.7 0.7 convert_reduce_fusion.3
  279.4 0.9 multiply_reduce_fusion
  280.4 2.8 add_convert_fusion.2
  283.2 8.6 %convolution_add_fusion = f32[512,1536]{1,0:T(8,128)} fusion(bf16[512,2048]{0,1:T(8,128)(2,1)} %get-tuple-element.21, bf16[2048,1536]{1,0:T(8,128)(2,1)} %all-gather.10.cloned.1.call-done, f32[1536]{0:T(1024)S(1)} %get-tuple-element.15), kind=kOutput, calls=%fused_computation.56 | convolution fusion | flops 3222011904 | bytes 11540480 | tf_op jit(solution)/shard_map/dot_general | solution.py:110
  291.7 3.0 copy.59
  294.7 1.5 fusion.286
  296.2 2.5 copy.71
  298.8 2.6 copy.72
  301.4 2.4 fusion.124
  303.8 2.3 fusion.125
  306.1 2.4 fusion.158
  308.5 4.4 %fusion.297 = (f32[2,512]{1,0:T(2,128)S(1)}, f32[2,512,512]{1,2,0:T(8,128)}) fusion(pred[512,512]{0,1:T(8,128)(4,1)} %fusion.119, bf16[512,2,192]{2,0,1:T(8,128)(2,1)} %fusion.125, bf16[512,2,32]{2,0,1:T(8,128)(2,1)} %get-tuple-element.28, bf16[512,2,32]{2,0,1:T(8,128)(2,1)} %get-tuple-element.27, bf16[512,2,192]{2,0,1:T(8,128)(2,1)} %fusion.124, ...), kind=kOutput, calls=%fused_computation.384 | convolution fusion | flops 273678848 | bytes 3411968 | tf_op jit(solution)/shard_map/sub | solution.py:119
  312.9 2.9 convolution_convert_fusion
  315.8 15.2 %fusion.10 = f32[512,2048]{1,0:T(8,128)} fusion(bf16[2,2048,2048]{2,1,0:T(8,128)(2,1)} %param.24, bf16[512,2048]{0,1:T(8,128)(2,1)} %get-tuple-element.22, bf16[2048,1024]{1,0:T(8,128)(2,1)} %all-gather.12.cloned.1.call-done, f32[1024]{0:T(1024)S(1)} %bitcast.227), kind=kOutput, calls=%fused_computation.21 | convolution fusion | flops 4329570304 | bytes 14684160 | tf_op jit(solution)/shard_map/dot_general | solution.py:130
  331.0 2.3 all-gather.14.cloned.1.call-done
  333.3 14.6 %fusion.8 = f32[512,2048]{1,0:T(8,128)} fusion(bf16[2,2048,2048]{2,1,0:T(8,128)(2,1)} %param.24, bf16[512,2048]{0,1:T(8,128)(2,1)S(1)} %copy-done.14, bf16[2048,1024]{1,0:T(8,128)(2,1)} %all-gather.14.cloned.1.call-done, f32[1024]{0:T(1024)S(1)} %bitcast.226), kind=kOutput, calls=%fused_computation.19 | convolution fusion | flops 4329570304 | bytes 14684160 | tf_op jit(solution)/shard_map/dot_general | solution.py:130
  347.9 5.4 %add_convert_fusion = bf16[512,2048]{1,0:T(8,128)(2,1)S(1)} fusion(f32[512,2048]{1,0:T(8,128)} %fusion.8, f32[512,2048]{1,0:T(8,128)} %fusion.10, bf16[512,512]{0,1:T(8,128)(2,1)S(1)} %bitcast.219, bf16[2,512,2048]{2,1,0:T(8,128)(2,1)} %param.23), kind=kOutput, calls=%fused_computation.28 | convolution fusion | flops 1076887552 | bytes 13107200 | tf_op jit(solution)/shard_map/dot_general | solution.py:124
  353.5 29.2 %all_to_all.98 = bf16[4,512,512]{2,1,0:T(8,128)(2,1)S(1)} all-to-all(bf16[4,512,512]{2,1,0:T(8,128)(2,1)S(1)} %bitcast.203), channel_id=1, replica_groups=mesh['seq'=8,'tp'=4] {'tp'}, dimensions={0} | all-to-all | bytes 4194304 | tf_op jit(solution)/shard_map/all_to_all | solution.py:67
  383.8 1.0 fusion.50
  (119 shorter events, 12.4 us)
Async XLA Ops:
  6.5 101.4 %all-gather.6.cloned.1.call-start = ((), (), s32[]{:S(2)}) async-start(), calls=%async_computation.9 | async-start | bytes 7077888 | tf_op jit(solution)/shard_map/all_gather | solution.py:80
  26.7 147.0 %all-gather.8.cloned.1.call-start = ((), (), s32[]{:S(2)}) async-start(), calls=%async_computation.10 | async-start | bytes 9437184 | tf_op jit(solution)/shard_map/all_gather | solution.py:80
  30.8 16.2 %copy-start.8 = (bf16[1,64,6144]{2,1,0:T(8,128)(2,1)S(1)}, bf16[1,64,6144]{2,1,0:T(8,128)(2,1)}, u32[]{:S(2)}) copy-start(bf16[1,64,6144]{2,1,0:T(8,128)(2,1)} %get-tuple-element.31) | copy-start | bytes 2359300
  47.0 236.2 %all-gather.10.cloned.1.call-start = ((), (), s32[]{:S(2)}) async-start(), calls=%async_computation.11 | async-start | bytes 7077888 | tf_op jit(solution)/shard_map/all_gather | solution.py:80
  60.5 5.7 %copy-start.19 = (f32[2,2,2048]{2,1,0:T(2,128)S(1)}, f32[2,2,2048]{2,1,0:T(2,128)}, u32[]{:S(2)}) copy-start(f32[2,2,2048]{2,1,0:T(2,128)} %param.27) | copy-start | bytes 98308
  60.6 5.7 %copy-start.20 = (f32[2,2,2048]{2,1,0:T(2,128)S(1)}, f32[2,2,2048]{2,1,0:T(2,128)}, u32[]{:S(2)}) copy-start(f32[2,2,2048]{2,1,0:T(2,128)} %param.26) | copy-start | bytes 98308
  60.6 6.0 %copy-start.23 = (s32[32]{0:T(128)S(1)}, s32[32]{0:T(128)}, u32[]{:S(2)}) copy-start(s32[32]{0:T(128)} %param.18) | copy-start | bytes 388
  61.8 9.9 %copy-start.17 = (s32[1,512]{1,0:T(1,128)S(1)}, s32[1,512]{1,0:T(1,128)}, u32[]{:S(2)}) copy-start(s32[1,512]{1,0:T(1,128)} %param.17) | copy-start | bytes 6148
  61.8 10.3 %copy-start.9 = (bf16[1,512,512]{2,1,0:T(8,128)(2,1)S(1)}, bf16[1,512,512]{2,1,0:T(8,128)(2,1)}, u32[]{:S(2)}) copy-start(bf16[1,512,512]{2,1,0:T(8,128)(2,1)} %param.16) | copy-start | bytes 1572868
  62.7 10.3 %all-to-all-start.6 = ((bf16[64,4,1024]{2,0,1:T(8,128)(2,1)}), bf16[64,4,1024]{2,0,1:T(8,128)(2,1)S(1)}, u32[]{:S(2)}, u32[]{:S(2)}) async-start(bf16[64,4,1024]{2,0,1:T(8,128)(2,1)} %copy.64), calls=%async_computation.6 | async-start | bytes 1048576 | tf_op jit(solution)/shard_map/all_to_all | solution.py:79
  73.1 1.6 copy-start.11
  74.6 4.6 %copy-start.21 = (bf16[2,1536]{1,0:T(2,128)(2,1)S(1)}, bf16[2,1536]{1,0:T(2,128)(2,1)}, u32[]{:S(2)}) copy-start(bf16[2,1536]{1,0:T(2,128)(2,1)} %param.21) | copy-start | bytes 18436
  74.6 7.4 %copy-start.18 = (bf16[2,2048]{1,0:T(2,128)(2,1)S(1)}, bf16[2,2048]{1,0:T(2,128)(2,1)}, u32[]{:S(2)}) copy-start(bf16[2,2048]{1,0:T(2,128)(2,1)} %param.22) | copy-start | bytes 24580
  74.6 24.9 %all-to-all-start = ((bf16[4,512,512]{1,2,0:T(8,128)(2,1)}), bf16[4,512,512]{1,2,0:T(8,128)(2,1)S(1)}, u32[]{:S(2)}, u32[]{:S(2)}) async-start(bf16[4,512,512]{1,2,0:T(8,128)(2,1)} %broadcast_in_dim.47), calls=%async_computation | async-start | bytes 4194304 | tf_op jit(solution)/shard_map/all_to_all | solution.py:67
  78.9 236.9 %all-gather.12.cloned.1.call-start = ((), (), s32[]{:S(2)}) async-start(), calls=%async_computation.12 | async-start | bytes 4718592 | tf_op jit(solution)/shard_map/all_gather | solution.py:80
  99.6 1.4 copy-start
  126.2 4.7 %copy-start.3 = (f32[1,512,2,1,256]{4,1,2,3,0:T(8,128)S(1)}, f32[1,512,2,1,256]{4,1,2,3,0:T(8,128)}, u32[]{:S(2)}) copy-start(f32[1,512,2,1,256]{4,1,2,3,0:T(8,128)} %copy.69) | copy-start | bytes 3145732
  126.2 4.7 %copy-start.5 = (f32[1,512,2,1,256]{4,1,2,3,0:T(8,128)S(1)}, f32[1,512,2,1,256]{4,1,2,3,0:T(8,128)}, u32[]{:S(2)}) copy-start(f32[1,512,2,1,256]{4,1,2,3,0:T(8,128)} %copy.70) | copy-start | bytes 3145732
  173.7 26.2 %copy-start.16 = (bf16[2,256,512]{2,1,0:T(8,128)(2,1)S(1)}, bf16[2,256,512]{2,1,0:T(8,128)(2,1)}, u32[]{:S(2)}) copy-start(bf16[2,256,512]{2,1,0:T(8,128)(2,1)} %convolution_convert_fusion.1) | copy-start | bytes 1572868
  205.6 3.8 copy-start.13
  205.6 4.8 %copy-start.22 = (f32[2,512]{1,0:T(2,128)S(1)}, f32[2,512]{1,0:T(2,128)}, u32[]{:S(2)}) copy-start(f32[2,512]{1,0:T(2,128)} %param.25) | copy-start | bytes 12292
  205.6 29.3 %all-to-all-start.3 = ((bf16[4,512,512]{2,1,0:T(8,128)(2,1)}), bf16[4,512,512]{2,1,0:T(8,128)(2,1)S(1)}, u32[]{:S(2)}, u32[]{:S(2)}) async-start(bf16[4,512,512]{2,1,0:T(8,128)(2,1)} %bitcast.202), calls=%async_computation.3 | async-start | bytes 4194304 | tf_op jit(solution)/shard_map/all_to_all | solution.py:67
  210.4 28.3 %copy-start.10 = (bf16[1,512,512]{2,1,0:T(8,128)(2,1)S(1)}, bf16[1,512,512]{2,1,0:T(8,128)(2,1)}, u32[]{:S(2)}) copy-start(bf16[1,512,512]{2,1,0:T(8,128)(2,1)} %param.16) | copy-start | bytes 1572868
  234.9 11.3 %all-to-all-start.7 = ((bf16[64,4,1024]{2,0,1:T(8,128)(2,1)}), bf16[64,4,1024]{2,0,1:T(8,128)(2,1)S(1)}, u32[]{:S(2)}, u32[]{:S(2)}) async-start(bf16[64,4,1024]{2,0,1:T(8,128)(2,1)} %copy.65), calls=%async_computation.7 | async-start | bytes 1048576 | tf_op jit(solution)/shard_map/all_to_all | solution.py:79
  238.9 8.8 %copy-start.6 = (bf16[1,512,512]{2,1,0:T(8,128)(2,1)}, bf16[1,512,512]{2,1,0:T(8,128)(2,1)S(1)}, u32[]{:S(2)}) copy-start(bf16[1,512,512]{2,1,0:T(8,128)(2,1)S(1)} %fusion.52) | copy-start | bytes 1572868
  246.2 1.5 copy-start.12
  247.7 27.4 %all-to-all-start.4 = ((bf16[4,512,512]{1,2,0:T(8,128)(2,1)}), bf16[4,512,512]{1,2,0:T(8,128)(2,1)S(1)}, u32[]{:S(2)}, u32[]{:S(2)}) async-start(bf16[4,512,512]{1,2,0:T(8,128)(2,1)} %broadcast_in_dim.52), calls=%async_computation.4 | async-start | bytes 4194304 | tf_op jit(solution)/shard_map/all_to_all | solution.py:67
  251.3 82.0 %all-gather.14.cloned.1.call-start = ((), (), s32[]{:S(2)}) async-start(), calls=%async_computation.13 | async-start | bytes 4718592 | tf_op jit(solution)/shard_map/all_gather | solution.py:80
  275.1 1.3 copy-start.1
  301.4 4.7 %copy-start.2 = (f32[1,512,2,1,256]{4,1,2,3,0:T(8,128)S(1)}, f32[1,512,2,1,256]{4,1,2,3,0:T(8,128)}, u32[]{:S(2)}) copy-start(f32[1,512,2,1,256]{4,1,2,3,0:T(8,128)} %copy.71) | copy-start | bytes 3145732
  301.4 4.7 %copy-start.4 = (f32[1,512,2,1,256]{4,1,2,3,0:T(8,128)S(1)}, f32[1,512,2,1,256]{4,1,2,3,0:T(8,128)}, u32[]{:S(2)}) copy-start(f32[1,512,2,1,256]{4,1,2,3,0:T(8,128)} %copy.72) | copy-start | bytes 3145732
  315.8 17.5 %copy-start.14 = (bf16[512,2048]{0,1:T(8,128)(2,1)S(1)}, bf16[512,2048]{0,1:T(8,128)(2,1)}, u32[]{:S(2)}) copy-start(bf16[512,2048]{0,1:T(8,128)(2,1)} %get-tuple-element.22) | copy-start | bytes 6291460
  333.3 14.6 %copy-start.15 = (bf16[2,256,512]{2,1,0:T(8,128)(2,1)S(1)}, bf16[2,256,512]{2,1,0:T(8,128)(2,1)}, u32[]{:S(2)}) copy-start(bf16[2,256,512]{2,1,0:T(8,128)(2,1)} %convolution_convert_fusion) | copy-start | bytes 1572868
  382.7 1.0 copy-start.7
Sparse Core Ops, SparseCore 0:
  26.9 64.4 all-gather.5
  93.0 80.6 all-gather.7
  175.4 63.2 all-gather.9
  240.1 45.7 all-gather.11
  287.4 45.8 all-gather.13

commit v14 on v11

--- a/solution.py
+++ b/solution.py
@@ -118,12 +118,12 @@
         ctx = ctx.reshape(rows * length, heads_here * HD)
         up = jnp.dot(mlp_in, up_mat, preferred_element_type=jnp.float32) + up_bias[layer].astype(jnp.float32)
         hidden_units = jax.nn.gelu(up, approximate=False).astype(jnp.bfloat16)
-        partial_terms = jnp.dot(ctx, dense_w[layer], preferred_element_type=jnp.float32) + jnp.dot(
-            hidden_units, down_w[layer], preferred_element_type=jnp.float32
+        d_view = dense_w[layer].reshape(-1, n_tp, width_here)
+        m_view = down_w[layer].reshape(-1, n_tp, width_here)
+        split = jnp.einsum("tc,cgd->gtd", ctx, d_view, preferred_element_type=jnp.float32) + jnp.einsum(
+            "th,hgd->gtd", hidden_units, m_view, preferred_element_type=jnp.float32
         )
-        partial_terms = partial_terms.astype(jnp.bfloat16)
-        split = partial_terms.reshape(rows * length, n_tp, width_here).transpose(1, 0, 2)
-        summed = jnp.sum(exchange(split).astype(jnp.float32), axis=0)
+        summed = jnp.sum(exchange(split.astype(jnp.bfloat16)).astype(jnp.float32), axis=0)
         flat_stream = stream.astype(jnp.float32).reshape(rows * length, -1)
         stream = (flat_stream + summed + out_bias[layer]).astype(jnp.bfloat16).reshape(rows, length, -1)
     return stream

time: 395 us -> 396 us (level)
  waiting for transfers between devices: 114 us -> 66.5 us
  local copies, waits for them, and re-layouts: 54.4 us -> 101 us
    unnamed x36 -> x46, local copies, waits for them, and re-layouts: 13.1 us -> 44.3 us
    all_gather x4, waiting for transfers between devices: 45.1 us -> 15.8 us  [shards(): lax.all_gather(part.reshape(n_tp * block, -1), 'seq', axis=0, tiled=True)]
    all_to_all x3, waiting for transfers between devices: 66.9 us -> 50.6 us  [exchange(): return lax.all_to_all(x, 'tp', split_axis=0, concat_axis=0, tiled=True)]
    slice x1 -> x3, local copies, waits for them, and re-layouts: 0.19 us -> 16.5 us  [the longest x1 11.9 us: shards(): m_view = down_w[layer].reshape(-1, n_tp, width_here)]
  transfers between devices with their start and end apart: 8 -> 8, of which waited for: 6 -> 5; matrix products, arithmetic and copies ran while one was open for 34% -> 47% of each run, Pallas kernels for 0% -> 0%
where the time goes in v14:
time: 396 us; the launch traced here: 388 us
  local copies, waits for them, and re-layouts  101 us (26%)
  matrix products  93.2 us (24%)
  blocking collectives  73.9 us (19%)
  waiting for transfers between devices  66.5 us (17%)
  other arithmetic  24.9 us (6%)
  starting transfers between devices  15.4 us (4%)
  between operations  13.7 us (3%)
    dot_general x2, matrix products, shards(): jnp.einsum('th,hgd->gtd', hidden_units, m_view, preferred_element_type=jn...  53 us
    all_to_all x3, waiting for transfers between devices, exchange(): return lax.all_to_all(x, 'tp', split_axis=0, concat_axis=0, tiled=True)  50.6 us
    all_to_all x3, blocking collectives, shards(): part = lax.all_to_all(part, 'tp', split_axis=1, concat_axis=0, tiled=True)  44.5 us
    unnamed x46, local copies, waits for them, and re-layouts  44.3 us
    all_to_all x1, blocking collectives, exchange(): return lax.all_to_all(x, 'tp', split_axis=0, concat_axis=0, tiled=True)  29.4 us
    dot_general x2, matrix products, shards(): jnp.dot(attn_in, qkv_mat, preferred_element_type=jnp.float32)  17.3 us
    all_gather x4, waiting for transfers between devices, shards(): lax.all_gather(part.reshape(n_tp * block, -1), 'seq', axis=0, tiled=True)  15.8 us
    slice x1, local copies, waits for them, and re-layouts, shards(): m_view = down_w[layer].reshape(-1, n_tp, width_here)  11.9 us
  transfers between devices with their start and end apart: 8, of which 5 were waited for; matrix products, arithmetic and copies ran while one was open for 47% of the time, Pallas kernels for 0%

profile of v14, /device:TPU:0, one launch (start us, length us, event | category | flops | bytes accessed | tf_op | source)
XLA Modules:
  0.0 388.2 jit_solution(4442292201224726295)
XLA Ops:
  6.5 2.1 convert_element_type.159
  8.6 1.0 fusion.184
  10.3 16.4 %all_to_all.80 = bf16[64,4,1536]{2,0,1:T(8,128)(2,1)} all-to-all(bf16[64,4,1536]{2,0,1:T(8,128)(2,1)S(1)} %copy.70), channel_id=1, replica_groups=mesh['seq'=8,'tp'=4] {'tp'}, dimensions={1} | all-to-all | bytes 1572864 | tf_op jit(solution)/shard_map/all_to_all | solution.py:79
  26.8 2.4 convert_element_type.167
  29.5 0.8 squeeze.33
  30.9 16.0 %all_to_all.81 = bf16[64,4,2048]{2,0,1:T(8,128)(2,1)} all-to-all(bf16[64,4,2048]{2,0,1:T(8,128)(2,1)S(1)} %copy.79), channel_id=1, replica_groups=mesh['seq'=8,'tp'=4] {'tp'}, dimensions={1} | all-to-all | bytes 2097152 | tf_op jit(solution)/shard_map/all_to_all | solution.py:79
  47.7 12.0 %all_to_all.82 = bf16[64,4,1536]{2,0,1:T(8,128)(2,1)} all-to-all(bf16[64,4,1536]{2,0,1:T(8,128)(2,1)S(1)} %copy.83), channel_id=1, replica_groups=mesh['seq'=8,'tp'=4] {'tp'}, dimensions={1} | all-to-all | bytes 1572864 | tf_op jit(solution)/shard_map/all_to_all | solution.py:79
  59.8 0.8 squeeze.37
  60.6 1.6 copy.92
  62.2 3.5 all-to-all-start.6
  71.3 11.9 %fusion.179 = (bf16[1,2048,2048]{2,1,0:T(8,128)(2,1)}, bf16[1,2048,2048]{2,1,0:T(8,128)(2,1)}) fusion(bf16[2,2048,2048]{2,1,0:T(8,128)(2,1)} %param.24), kind=kLoop, calls=%fused_computation.258 | loop fusion | bytes 33554432 | tf_op jit(solution)/shard_map/slice | solution.py:122
  83.2 12.4 %copy.108 = bf16[1,2048,2048]{1,2,0:T(8,128)(2,1)} copy(bf16[1,2048,2048]{2,1,0:T(8,128)(2,1)} %get-tuple-element.17) | data formatting | bytes 16777216
  95.8 1.0 copy.69
  97.6 4.4 %fusion.180 = (bf16[1,512,2048]{2,1,0:T(8,128)(2,1)}, bf16[1,512,2048]{2,1,0:T(8,128)(2,1)S(1)}) fusion(bf16[2,512,2048]{2,1,0:T(8,128)(2,1)} %param.23), kind=kLoop, calls=%fused_computation.259 | loop fusion | bytes 8388608 | tf_op jit(solution)/shard_map/slice | solution.py:121
  102.0 2.5 copy.107
  104.5 3.0 broadcast_in_dim.47
  107.5 4.2 %all-to-all-start = ((bf16[4,512,512]{1,2,0:T(8,128)(2,1)}), bf16[4,512,512]{1,2,0:T(8,128)(2,1)S(1)}, u32[]{:S(2)}, u32[]{:S(2)}) async-start(bf16[4,512,512]{1,2,0:T(8,128)(2,1)} %broadcast_in_dim.47), calls=%async_computation | async-start | bytes 4194304 | tf_op jit(solution)/shard_map/all_to_all | solution.py:67
  112.0 0.9 fusion.42
  112.9 1.7 multiply_cosine_fusion
  114.7 17.2 %all-to-all-done = bf16[4,512,512]{1,2,0:T(8,128)(2,1)S(1)} async-done(((bf16[4,512,512]{1,2,0:T(8,128)(2,1)}), bf16[4,512,512]{1,2,0:T(8,128)(2,1)S(1)}, u32[]{:S(2)}, u32[]{:S(2)}) %all-to-all-start) | async-done | bytes 2097184 | tf_op jit(solution)/shard_map/all_to_all | solution.py:67
  131.9 1.4 copy-done
  133.3 2.3 gather_fusion
  135.6 0.7 convert_reduce_fusion.2
  136.4 0.9 multiply_reduce_fusion.1
  137.3 2.8 add_convert_fusion.5
  140.1 8.6 %convolution_add_fusion.1 = f32[512,1536]{1,0:T(8,128)} fusion(bf16[512,2048]{0,1:T(8,128)(2,1)} %get-tuple-element.27, bf16[2048,1536]{1,0:T(8,128)(2,1)} %all-gather.5.cloned.1.call-done, f32[1536]{0:T(1024)S(1)} %get-tuple-element.16), kind=kOutput, calls=%fused_computation.67 | convolution fusion | flops 3222011904 | bytes 11540480 | tf_op jit(solution)/shard_map/dot_general | solution.py:105
  148.7 2.6 copy.71
  151.3 1.6 fusion.182
  152.9 2.5 copy.106
  155.4 2.6 copy.105
  157.9 2.2 fusion.46
  160.2 2.3 fusion.45
  162.4 3.0 fusion.77
  165.5 4.4 %fusion.186 = (f32[2,512]{1,0:T(2,128)S(1)}, f32[2,512,512]{1,2,0:T(8,128)}) fusion(pred[512,512]{0,1:T(8,128)(4,1)} %fusion.42, bf16[512,2,192]{2,0,1:T(8,128)(2,1)} %fusion.46, bf16[512,2,32]{2,0,1:T(8,128)(2,1)} %get-tuple-element.38, bf16[512,2,32]{2,0,1:T(8,128)(2,1)} %get-tuple-element.37, bf16[512,2,192]{2,0,1:T(8,128)(2,1)} %fusion.45, ...), kind=kOutput, calls=%fused_computation.265 | convolution fusion | flops 273678848 | bytes 3411968 | tf_op jit(solution)/shard_map/sub | solution.py:114
  169.8 2.8 convolution_convert_fusion.1
  172.7 1.1 all-gather.7.cloned.1.call-done
  173.7 26.6 %fusion.28 = f32[512,4,512]{2,0,1:T(8,128)} fusion(bf16[2048,4,512]{0,2,1:T(8,128)(2,1)} %bitcast.189, bf16[512,2048]{0,1:T(8,128)(2,1)} %get-tuple-element.28, bf16[2048,2048]{1,0:T(8,128)(2,1)} %all-gather.7.cloned.1.call-done, f32[2048]{0:T(1024)S(1)} %bitcast.212), kind=kOutput, calls=%fused_computation.77 | convolution fusion | flops 8659140608 | bytes 23076864 | tf_op jit(solution)/shard_map/th,hgd->gtd/dot_general | solution.py:123
  200.4 4.9 %fusion.32 = bf16[4,512,512]{2,1,0:T(8,128)(2,1)} fusion(f32[512,4,512]{2,0,1:T(8,128)} %fusion.28, bf16[512,512,1]{0,1,2:T(8,128)(2,1)S(1)} %bitcast.206, bf16[512,4,512]{0,2,1:T(8,128)(2,1)S(1)} %bitcast.187), kind=kOutput, calls=%fused_computation.84 | convolution fusion | flops 1075838976 | bytes 8912896 | tf_op jit(solution)/shard_map/tc,cgd->gtd/dot_general | solution.py:123
  205.2 3.8 all-to-all-start.3
  209.1 25.4 %all-to-all-done.3 = bf16[4,512,512]{2,1,0:T(8,128)(2,1)S(1)} async-done(((bf16[4,512,512]{2,1,0:T(8,128)(2,1)}), bf16[4,512,512]{2,1,0:T(8,128)(2,1)S(1)}, u32[]{:S(2)}, u32[]{:S(2)}) %all-to-all-start.3) | async-done | bytes 2097184 | tf_op jit(solution)/shard_map/all_to_all | solution.py:67
  235.2 1.6 broadcast_in_dim.52
  236.8 3.6 all-to-all-start.4
  240.4 12.4 %copy.112 = bf16[1,2048,2048]{1,2,0:T(8,128)(2,1)} copy(bf16[1,2048,2048]{2,1,0:T(8,128)(2,1)} %get-tuple-element.18) | data formatting | bytes 16777216
  253.1 3.9 %copy.111 = bf16[1,512,2048]{1,2,0:T(8,128)(2,1)} copy(bf16[1,512,2048]{2,1,0:T(8,128)(2,1)} %get-tuple-element.19) | data formatting | bytes 4194304
  257.1 8.0 %all-to-all-done.4 = bf16[4,512,512]{1,2,0:T(8,128)(2,1)S(1)} async-done(((bf16[4,512,512]{1,2,0:T(8,128)(2,1)}), bf16[4,512,512]{1,2,0:T(8,128)(2,1)S(1)}, u32[]{:S(2)}, u32[]{:S(2)}) %all-to-all-start.4) | async-done | bytes 2097184 | tf_op jit(solution)/shard_map/all_to_all | solution.py:67
  265.1 1.3 copy-done.1
  266.4 2.3 gather_fusion.5
  269.5 0.9 multiply_reduce_fusion
  270.4 2.8 add_convert_fusion.2
  273.2 8.7 %convolution_add_fusion = f32[512,1536]{1,0:T(8,128)} fusion(bf16[512,2048]{0,1:T(8,128)(2,1)} %get-tuple-element.25, bf16[2048,1536]{1,0:T(8,128)(2,1)} %all-gather.9.cloned.1.call-done, f32[1536]{0:T(1024)S(1)} %get-tuple-element.15), kind=kOutput, calls=%fused_computation.66 | convolution fusion | flops 3222011904 | bytes 11540480 | tf_op jit(solution)/shard_map/dot_general | solution.py:105
  281.9 2.6 copy.84
  284.5 1.5 fusion.181
  286.0 2.7 copy.110
  288.6 2.5 copy.109
  291.2 2.2 fusion.48
  293.4 2.3 fusion.47
  295.7 3.1 fusion.81
  298.8 4.5 %fusion.191 = (f32[2,512]{1,0:T(2,128)S(1)}, f32[2,512,512]{1,2,0:T(8,128)}) fusion(pred[512,512]{0,1:T(8,128)(4,1)} %fusion.42, bf16[512,2,192]{2,0,1:T(8,128)(2,1)} %fusion.48, bf16[512,2,32]{2,0,1:T(8,128)(2,1)} %get-tuple-element.32, bf16[512,2,32]{2,0,1:T(8,128)(2,1)} %get-tuple-element.31, bf16[512,2,192]{2,0,1:T(8,128)(2,1)} %fusion.47, ...), kind=kOutput, calls=%fused_computation.266 | convolution fusion | flops 273678848 | bytes 3411968 | tf_op jit(solution)/shard_map/sub | solution.py:114
  303.3 2.8 convolution_convert_fusion
  306.1 14.8 %all-gather.11.cloned.1.call-done = bf16[2048,2048]{1,0:T(8,128)(2,1)} async-done(((bf16[256,2048]{1,0:T(8,128)(2,1)}), bf16[2048,2048]{1,0:T(8,128)(2,1)}) %all-gather.11.cloned.1.call-update) | async-done | bytes 8388624 | tf_op jit(solution)/shard_map/all_gather | solution.py:80
  320.9 26.4 %fusion.26 = f32[512,4,512]{2,0,1:T(8,128)} fusion(bf16[2048,4,512]{0,2,1:T(8,128)(2,1)} %bitcast.190, bf16[512,2048]{0,1:T(8,128)(2,1)} %get-tuple-element.26, bf16[2048,2048]{1,0:T(8,128)(2,1)} %all-gather.11.cloned.1.call-done, f32[2048]{0:T(1024)S(1)} %bitcast.211), kind=kOutput, calls=%fused_computation.75 | convolution fusion | flops 8659140608 | bytes 23076864 | tf_op jit(solution)/shard_map/th,hgd->gtd/dot_general | solution.py:123
  347.3 3.5 fusion.33
  350.8 29.4 %all_to_all.83 = bf16[4,512,512]{2,1,0:T(8,128)(2,1)S(1)} all-to-all(bf16[4,512,512]{2,1,0:T(8,128)(2,1)S(1)} %fusion.33), channel_id=1, replica_groups=mesh['seq'=8,'tp'=4] {'tp'}, dimensions={0} | all-to-all | bytes 4194304 | tf_op jit(solution)/shard_map/all_to_all | solution.py:67
  380.5 1.0 fusion.35
  (104 shorter events, 11.4 us)
Async XLA Ops:
  6.5 133.5 %all-gather.5.cloned.1.call-start = ((), (), s32[]{:S(2)}) async-start(), calls=%async_computation.8 | async-start | bytes 7077888 | tf_op jit(solution)/shard_map/all_gather | solution.py:80
  26.8 147.0 %all-gather.7.cloned.1.call-start = ((), (), s32[]{:S(2)}) async-start(), calls=%async_computation.9 | async-start | bytes 9437184 | tf_op jit(solution)/shard_map/all_gather | solution.py:80
  30.3 16.7 %copy-start.7 = (bf16[1,64,6144]{2,1,0:T(8,128)(2,1)S(1)}, bf16[1,64,6144]{2,1,0:T(8,128)(2,1)}, u32[]{:S(2)}) copy-start(bf16[1,64,6144]{2,1,0:T(8,128)(2,1)} %get-tuple-element.35) | copy-start | bytes 2359300
  46.9 226.3 %all-gather.9.cloned.1.call-start = ((), (), s32[]{:S(2)}) async-start(), calls=%async_computation.10 | async-start | bytes 7077888 | tf_op jit(solution)/shard_map/all_gather | solution.py:80
  47.7 18.0 %copy-start.14 = (f32[2,2,2048]{2,1,0:T(2,128)S(1)}, f32[2,2,2048]{2,1,0:T(2,128)}, u32[]{:S(2)}) copy-start(f32[2,2,2048]{2,1,0:T(2,128)} %param.27) | copy-start | bytes 98308
  47.7 18.0 %copy-start.15 = (f32[2,2,2048]{2,1,0:T(2,128)S(1)}, f32[2,2,2048]{2,1,0:T(2,128)}, u32[]{:S(2)}) copy-start(f32[2,2,2048]{2,1,0:T(2,128)} %param.26) | copy-start | bytes 98308
  47.7 18.3 %copy-start.18 = (s32[32]{0:T(128)S(1)}, s32[32]{0:T(128)}, u32[]{:S(2)}) copy-start(s32[32]{0:T(128)} %param.18) | copy-start | bytes 388
  59.8 11.3 %copy-start.12 = (s32[1,512]{1,0:T(1,128)S(1)}, s32[1,512]{1,0:T(1,128)}, u32[]{:S(2)}) copy-start(s32[1,512]{1,0:T(1,128)} %param.17) | copy-start | bytes 6148
  62.2 42.4 %all-to-all-start.6 = ((bf16[64,4,2048]{2,0,1:T(8,128)(2,1)}), bf16[64,4,2048]{2,0,1:T(8,128)(2,1)S(1)}, u32[]{:S(2)}, u32[]{:S(2)}) async-start(bf16[64,4,2048]{2,0,1:T(8,128)(2,1)} %copy.92), calls=%async_computation.6 | async-start | bytes 2097152 | tf_op jit(solution)/shard_map/all_to_all | solution.py:79
  83.2 12.6 %copy-start.8 = (bf16[1,512,512]{2,1,0:T(8,128)(2,1)S(1)}, bf16[1,512,512]{2,1,0:T(8,128)(2,1)}, u32[]{:S(2)}) copy-start(bf16[1,512,512]{2,1,0:T(8,128)(2,1)} %param.16) | copy-start | bytes 1572868
  104.5 7.3 %copy-start.16 = (bf16[2,1536]{1,0:T(2,128)(2,1)S(1)}, bf16[2,1536]{1,0:T(2,128)(2,1)}, u32[]{:S(2)}) copy-start(bf16[2,1536]{1,0:T(2,128)(2,1)} %param.21) | copy-start | bytes 18436
  104.5 10.2 %copy-start.13 = (bf16[2,2048]{1,0:T(2,128)(2,1)S(1)}, bf16[2,2048]{1,0:T(2,128)(2,1)}, u32[]{:S(2)}) copy-start(bf16[2,2048]{1,0:T(2,128)(2,1)} %param.22) | copy-start | bytes 24580
  104.5 10.2 %copy-start.6 = (bf16[64,4,2048]{2,0,1:T(8,128)(2,1)}, bf16[64,4,2048]{2,0,1:T(8,128)(2,1)S(1)}, u32[]{:S(2)}) copy-start(bf16[64,4,2048]{2,0,1:T(8,128)(2,1)S(1)} %all-to-all-done.6) | copy-start | bytes 3145732
  107.5 24.4 %all-to-all-start = ((bf16[4,512,512]{1,2,0:T(8,128)(2,1)}), bf16[4,512,512]{1,2,0:T(8,128)(2,1)S(1)}, u32[]{:S(2)}, u32[]{:S(2)}) async-start(bf16[4,512,512]{1,2,0:T(8,128)(2,1)} %broadcast_in_dim.47), calls=%async_computation | async-start | bytes 4194304 | tf_op jit(solution)/shard_map/all_to_all | solution.py:67
  111.7 209.2 %all-gather.11.cloned.1.call-start = ((), (), s32[]{:S(2)}) async-start(), calls=%async_computation.11 | async-start | bytes 9437184 | tf_op jit(solution)/shard_map/all_gather | solution.py:80
  131.9 1.4 copy-start
  173.7 26.6 %copy-start.2 = (bf16[1,512,2048]{1,2,0:T(8,128)(2,1)S(1)}, bf16[1,512,2048]{1,2,0:T(8,128)(2,1)}, u32[]{:S(2)}) copy-start(bf16[1,512,2048]{1,2,0:T(8,128)(2,1)} %copy.107) | copy-start | bytes 6291460
  173.7 26.6 %copy-start.11 = (bf16[2,256,512]{2,1,0:T(8,128)(2,1)S(1)}, bf16[2,256,512]{2,1,0:T(8,128)(2,1)}, u32[]{:S(2)}) copy-start(bf16[2,256,512]{2,1,0:T(8,128)(2,1)} %convolution_convert_fusion.1) | copy-start | bytes 1572868
  205.2 3.8 copy-start.17
  205.2 29.6 %copy-start.9 = (bf16[1,512,512]{2,1,0:T(8,128)(2,1)S(1)}, bf16[1,512,512]{2,1,0:T(8,128)(2,1)}, u32[]{:S(2)}) copy-start(bf16[1,512,512]{2,1,0:T(8,128)(2,1)} %param.16) | copy-start | bytes 1572868
  205.2 29.3 %all-to-all-start.3 = ((bf16[4,512,512]{2,1,0:T(8,128)(2,1)}), bf16[4,512,512]{2,1,0:T(8,128)(2,1)S(1)}, u32[]{:S(2)}, u32[]{:S(2)}) async-start(bf16[4,512,512]{2,1,0:T(8,128)(2,1)} %fusion.32), calls=%async_computation.3 | async-start | bytes 4194304 | tf_op jit(solution)/shard_map/all_to_all | solution.py:67
  235.0 1.8 copy-start.4
  236.8 28.3 %all-to-all-start.4 = ((bf16[4,512,512]{1,2,0:T(8,128)(2,1)}), bf16[4,512,512]{1,2,0:T(8,128)(2,1)S(1)}, u32[]{:S(2)}, u32[]{:S(2)}) async-start(bf16[4,512,512]{1,2,0:T(8,128)(2,1)} %broadcast_in_dim.52), calls=%async_computation.4 | async-start | bytes 4194304 | tf_op jit(solution)/shard_map/all_to_all | solution.py:67
  265.1 1.3 copy-start.1
  320.9 26.4 %copy-start.3 = (bf16[1,512,2048]{1,2,0:T(8,128)(2,1)S(1)}, bf16[1,512,2048]{1,2,0:T(8,128)(2,1)}, u32[]{:S(2)}) copy-start(bf16[1,512,2048]{1,2,0:T(8,128)(2,1)} %copy.111) | copy-start | bytes 6291460
  320.9 26.4 %copy-start.10 = (bf16[2,256,512]{2,1,0:T(8,128)(2,1)S(1)}, bf16[2,256,512]{2,1,0:T(8,128)(2,1)}, u32[]{:S(2)}) copy-start(bf16[2,256,512]{2,1,0:T(8,128)(2,1)} %convolution_convert_fusion) | copy-start | bytes 1572868
  350.8 29.7 %copy-start.5 = (bf16[1,512,512]{2,1,0:T(8,128)(2,1)S(1)}, bf16[1,512,512]{2,1,0:T(8,128)(2,1)}, u32[]{:S(2)}) copy-start(bf16[1,512,512]{2,1,0:T(8,128)(2,1)} %copy-done.4) | copy-start | bytes 1572868
Sparse Core Ops, SparseCore 0:
  26.9 64.4 all-gather.4
  93.0 80.6 all-gather.6
  175.4 63.2 all-gather.8
  240.2 80.6 all-gather.10

commit v15 on v12

--- a/solution.py
+++ b/solution.py
@@ -116,15 +116,15 @@
             jnp.bfloat16
         )
         ctx = ctx.reshape(rows * length, heads_here * HD)
+        up = jnp.dot(mlp_in, up_mat, preferred_element_type=jnp.float32) + up_bias[layer].astype(jnp.float32)
+        hidden_units = jax.nn.gelu(up, approximate=False).astype(jnp.bfloat16)
         chunks = 2 if layer + 1 == LAYERS else 1
         size = rows * length // chunks
         sums = []
         for chunk in range(chunks):
-            rows_here = slice(chunk * size, (chunk + 1) * size)
-            up = jnp.dot(mlp_in[rows_here], up_mat, preferred_element_type=jnp.float32)
-            hidden_units = jax.nn.gelu(up + up_bias[layer].astype(jnp.float32), approximate=False).astype(jnp.bfloat16)
-            partial_terms = jnp.dot(ctx[rows_here], dense_w[layer], preferred_element_type=jnp.float32) + jnp.dot(
-                hidden_units, down_w[layer], preferred_element_type=jnp.float32
+            part = slice(chunk * size, (chunk + 1) * size)
+            partial_terms = jnp.dot(ctx[part], dense_w[layer], preferred_element_type=jnp.float32) + jnp.dot(
+                hidden_units[part], down_w[layer], preferred_element_type=jnp.float32
             )
             split = partial_terms.astype(jnp.bfloat16).reshape(size, n_tp, width_here).transpose(1, 0, 2)
             sums.append(jnp.sum(exchange(split).astype(jnp.float32), axis=0))

time: 395 us -> 404 us (1.023)
  waiting for transfers between devices: 130 us -> 141 us
  matrix products: 98.2 us -> 93.5 us
    all_gather x4, waiting for transfers between devices: 46.9 us -> 52.7 us  [shards(): lax.all_gather(part.reshape(n_tp * block, -1), 'seq', axis=0, tiled=True)]
    all_to_all x5, waiting for transfers between devices: 80.4 us -> 85.8 us  [exchange(): return lax.all_to_all(x, 'tp', split_axis=0, concat_axis=0, tiled=True)]
    dot_general x6 -> x7, matrix products: 67 us -> 62.3 us  [the longest x3 40.3 us: shards(): jnp.dot(hidden_units[part], down_w[layer], preferred_element_type=jnp.flo...]
  transfers between devices with their start and end apart: 10 -> 10, of which waited for: 7 -> 8; matrix products, arithmetic and copies ran while one was open for 39% -> 34% of each run, Pallas kernels for 0% -> 0%
where the time goes in v15:
time: 404 us; the launch traced here: 397 us
  waiting for transfers between devices  141 us (35%)
  matrix products  93.5 us (23%)
  local copies, waits for them, and re-layouts  56.9 us (14%)
  blocking collectives  44.5 us (11%)
  other arithmetic  24.9 us (6%)
  starting transfers between devices  23 us (6%)
  between operations  13.8 us (3%)
    all_to_all x5, waiting for transfers between devices, exchange(): return lax.all_to_all(x, 'tp', split_axis=0, concat_axis=0, tiled=True)  85.8 us
    all_gather x4, waiting for transfers between devices, shards(): lax.all_gather(part.reshape(n_tp * block, -1), 'seq', axis=0, tiled=True)  52.7 us
    all_to_all x3, blocking collectives, shards(): part = lax.all_to_all(part, 'tp', split_axis=1, concat_axis=0, tiled=True)  44.5 us
    dot_general x3, matrix products, shards(): jnp.dot(hidden_units[part], down_w[layer], preferred_element_type=jnp.flo...  40.3 us
    all_to_all x5, starting transfers between devices, exchange(): return lax.all_to_all(x, 'tp', split_axis=0, concat_axis=0, tiled=True)  18.9 us
    dot_general x2, matrix products, shards(): jnp.dot(attn_in, qkv_mat, preferred_element_type=jnp.float32)  17.4 us
    dot_general x1, matrix products, shards(): jnp.dot(mlp_in, up_mat, preferred_element_type=jnp.float32)  16.4 us
    unnamed x44, local copies, waits for them, and re-layouts  14.4 us
  transfers between devices with their start and end apart: 10, of which 8 were waited for; matrix products, arithmetic and copies ran while one was open for 34% of the time, Pallas kernels for 0%

profile of v15, /device:TPU:0, one launch (start us, length us, event | category | flops | bytes accessed | tf_op | source)
XLA Modules:
  0.0 397.4 jit_solution(15098961882116632569)
XLA Ops:
  6.5 2.1 convert_element_type.159
  8.6 1.0 fusion.164
  10.4 16.4 %all_to_all.85 = bf16[64,4,1536]{2,0,1:T(8,128)(2,1)} all-to-all(bf16[64,4,1536]{2,0,1:T(8,128)(2,1)S(1)} %copy.48), channel_id=1, replica_groups=mesh['seq'=8,'tp'=4] {'tp'}, dimensions={1} | all-to-all | bytes 1572864 | tf_op jit(solution)/shard_map/all_to_all | solution.py:79
  26.8 2.4 convert_element_type.167
  29.5 0.8 squeeze.48
  30.9 16.0 %all_to_all.86 = bf16[64,4,2048]{2,0,1:T(8,128)(2,1)} all-to-all(bf16[64,4,2048]{2,0,1:T(8,128)(2,1)S(1)} %copy.54), channel_id=1, replica_groups=mesh['seq'=8,'tp'=4] {'tp'}, dimensions={1} | all-to-all | bytes 2097152 | tf_op jit(solution)/shard_map/all_to_all | solution.py:79
  47.7 12.1 %all_to_all.87 = bf16[64,4,1536]{2,0,1:T(8,128)(2,1)} all-to-all(bf16[64,4,1536]{2,0,1:T(8,128)(2,1)S(1)} %copy.57), channel_id=1, replica_groups=mesh['seq'=8,'tp'=4] {'tp'}, dimensions={1} | all-to-all | bytes 1572864 | tf_op jit(solution)/shard_map/all_to_all | solution.py:79
  60.6 1.6 copy.63
  62.2 3.5 all-to-all-start.6
  71.3 1.3 copy.47
  73.6 2.1 all-to-all-done.6
  75.7 1.6 broadcast_in_dim.47
  77.4 3.6 all-to-all-start
  81.7 0.9 fusion.54
  82.6 1.7 multiply_cosine_fusion
  84.4 16.9 %all-to-all-done = bf16[4,512,512]{1,2,0:T(8,128)(2,1)S(1)} async-done(((bf16[4,512,512]{1,2,0:T(8,128)(2,1)}), bf16[4,512,512]{1,2,0:T(8,128)(2,1)S(1)}, u32[]{:S(2)}, u32[]{:S(2)}) %all-to-all-start) | async-done | bytes 2097184 | tf_op jit(solution)/shard_map/all_to_all | solution.py:67
  101.3 1.4 copy-done
  102.7 2.3 gather_fusion
  105.7 0.9 multiply_reduce_fusion.1
  106.7 2.8 add_convert_fusion.4
  109.4 8.6 %convolution_add_fusion.1 = f32[512,1536]{1,0:T(8,128)} fusion(bf16[512,2048]{0,1:T(8,128)(2,1)} %get-tuple-element.23, bf16[2048,1536]{1,0:T(8,128)(2,1)} %all-gather.5.cloned.1.call-done, f32[1536]{0:T(1024)S(1)} %get-tuple-element.16), kind=kOutput, calls=%fused_computation.74 | convolution fusion | flops 3222011904 | bytes 11540480 | tf_op jit(solution)/shard_map/dot_general | solution.py:105
  118.1 2.6 copy.49
  120.6 1.5 fusion.162
  122.2 2.6 copy.69
  124.7 2.5 copy.68
  127.3 2.2 fusion.58
  129.5 2.3 fusion.57
  131.8 3.1 fusion.89
  134.9 4.4 %fusion.167 = (f32[2,512]{1,0:T(2,128)S(1)}, f32[2,512,512]{1,2,0:T(8,128)}) fusion(pred[512,512]{0,1:T(8,128)(4,1)} %fusion.54, bf16[512,2,192]{2,0,1:T(8,128)(2,1)} %fusion.58, bf16[512,2,32]{2,0,1:T(8,128)(2,1)} %get-tuple-element.34, bf16[512,2,32]{2,0,1:T(8,128)(2,1)} %get-tuple-element.33, bf16[512,2,192]{2,0,1:T(8,128)(2,1)} %fusion.57, ...), kind=kOutput, calls=%fused_computation.251 | convolution fusion | flops 273678848 | bytes 3411968 | tf_op jit(solution)/shard_map/sub | solution.py:114
  139.3 2.9 convolution_convert_fusion.1
  142.2 31.6 %all-gather.7.cloned.1.call-done = bf16[2048,2048]{1,0:T(8,128)(2,1)} async-done(((bf16[256,2048]{1,0:T(8,128)(2,1)}), bf16[2048,2048]{1,0:T(8,128)(2,1)}) %all-gather.7.cloned.1.call-update) | async-done | bytes 8388624 | tf_op jit(solution)/shard_map/all_gather | solution.py:80
  173.8 26.3 %fusion.6 = f32[512,2048]{1,0:T(8,128)} fusion(bf16[2,2048,2048]{2,1,0:T(8,128)(2,1)} %param.24, bf16[512,2048]{0,1:T(8,128)(2,1)} %get-tuple-element.24, bf16[2048,2048]{1,0:T(8,128)(2,1)} %all-gather.7.cloned.1.call-done, f32[2048]{0:T(1024)S(1)} %bitcast.226), kind=kOutput, calls=%fused_computation.16 | convolution fusion | flops 8659140608 | bytes 23076864 | tf_op jit(solution)/shard_map/dot_general | solution.py:126
  200.1 4.2 %add_convert_fusion.2 = bf16[512,2048]{1,0:T(8,128)(2,1)S(1)} fusion(f32[512,2048]{1,0:T(8,128)} %fusion.6, bf16[512,512]{0,1:T(8,128)(2,1)S(1)} %bitcast.220, bf16[2,512,2048]{2,1,0:T(8,128)(2,1)} %param.23), kind=kOutput, calls=%fused_computation.50 | convolution fusion | flops 1075838976 | bytes 8912896 | tf_op jit(solution)/shard_map/dot_general | solution.py:126
  204.3 1.6 copy.88
  205.9 3.8 all-to-all-start.3
  209.7 25.4 %all-to-all-done.3 = bf16[4,512,512]{2,1,0:T(8,128)(2,1)S(1)} async-done(((bf16[4,512,512]{2,1,0:T(8,128)(2,1)}), bf16[4,512,512]{2,1,0:T(8,128)(2,1)S(1)}, u32[]{:S(2)}, u32[]{:S(2)}) %all-to-all-start.3) | async-done | bytes 2097184 | tf_op jit(solution)/shard_map/all_to_all | solution.py:67
  235.8 1.6 broadcast_in_dim.52
  237.4 4.0 %all-to-all-start.4 = ((bf16[4,512,512]{1,2,0:T(8,128)(2,1)}), bf16[4,512,512]{1,2,0:T(8,128)(2,1)S(1)}, u32[]{:S(2)}, u32[]{:S(2)}) async-start(bf16[4,512,512]{1,2,0:T(8,128)(2,1)} %broadcast_in_dim.52), calls=%async_computation.4 | async-start | bytes 4194304 | tf_op jit(solution)/shard_map/all_to_all | solution.py:67
  241.7 24.3 %all-to-all-done.4 = bf16[4,512,512]{1,2,0:T(8,128)(2,1)S(1)} async-done(((bf16[4,512,512]{1,2,0:T(8,128)(2,1)}), bf16[4,512,512]{1,2,0:T(8,128)(2,1)S(1)}, u32[]{:S(2)}, u32[]{:S(2)}) %all-to-all-start.4) | async-done | bytes 2097184 | tf_op jit(solution)/shard_map/all_to_all | solution.py:67
  266.0 1.4 copy-done.1
  267.4 2.3 gather_fusion.5
  270.5 0.9 multiply_reduce_fusion
  271.4 2.8 add_convert_fusion.1
  274.2 8.8 %convolution_add_fusion = f32[512,1536]{1,0:T(8,128)} fusion(bf16[512,2048]{0,1:T(8,128)(2,1)} %get-tuple-element.21, bf16[2048,1536]{1,0:T(8,128)(2,1)} %all-gather.9.cloned.1.call-done, f32[1536]{0:T(1024)S(1)} %get-tuple-element.15), kind=kOutput, calls=%fused_computation.73 | convolution fusion | flops 3222011904 | bytes 11540480 | tf_op jit(solution)/shard_map/dot_general | solution.py:105
  283.0 2.4 copy.58
  285.4 1.5 fusion.161
  286.9 2.6 copy.71
  289.6 2.5 copy.70
  292.1 2.3 fusion.60
  294.3 2.3 fusion.59
  296.6 3.2 fusion.93
  299.8 21.1 %all-gather.11.cloned.1.call-done = bf16[2048,2048]{1,0:T(8,128)(2,1)} async-done(((bf16[256,2048]{1,0:T(8,128)(2,1)}), bf16[2048,2048]{1,0:T(8,128)(2,1)}) %all-gather.11.cloned.1.call-update) | async-done | bytes 8388624 | tf_op jit(solution)/shard_map/all_gather | solution.py:80
  320.9 16.4 %fusion.16 = bf16[512,2048]{1,0:T(8,128)(2,1)S(1)} fusion(bf16[512,2048]{0,1:T(8,128)(2,1)} %get-tuple-element.22, bf16[2048,2048]{1,0:T(8,128)(2,1)} %all-gather.11.cloned.1.call-done, f32[2048]{0:T(1024)S(1)} %bitcast.225), kind=kOutput, calls=%fused_computation.28 | convolution fusion | flops 4364173312 | bytes 12591104 | tf_op jit(solution)/shard_map/dot_general | solution.py:119
  337.3 7.8 %fusion.2 = f32[256,2048]{1,0:T(8,128)} fusion(bf16[2,2048,2048]{2,1,0:T(8,128)(2,1)} %param.24, bf16[512,2048]{1,0:T(8,128)(2,1)S(1)} %fusion.16), kind=kOutput, calls=%fused_computation.12 | convolution fusion | flops 2147483648 | bytes 11534336 | tf_op jit(solution)/shard_map/dot_general | solution.py:126
  345.1 4.3 %fusion.172 = (f32[2,512]{1,0:T(2,128)S(1)}, f32[2,512,512]{1,2,0:T(8,128)}) fusion(pred[512,512]{0,1:T(8,128)(4,1)} %fusion.54, bf16[512,2,192]{2,0,1:T(8,128)(2,1)} %fusion.60, bf16[512,2,32]{2,0,1:T(8,128)(2,1)} %get-tuple-element.28, bf16[512,2,32]{2,0,1:T(8,128)(2,1)S(1)} %copy-done.11, bf16[512,2,192]{2,0,1:T(8,128)(2,1)} %fusion.59, ...), kind=kOutput, calls=%fused_computation.252 | convolution fusion | flops 273678848 | bytes 3411968 | tf_op jit(solution)/shard_map/sub | solution.py:114
  349.4 2.2 fusion.43
  353.7 1.1 copy.89
  354.8 3.9 all-to-all-start.8
  358.7 6.2 %fusion.4 = f32[256,2048]{1,0:T(8,128)S(1)} fusion(bf16[2,2048,2048]{2,1,0:T(8,128)(2,1)} %param.24, bf16[512,2048]{1,0:T(8,128)(2,1)} %copy-done.19), kind=kOutput, calls=%fused_computation.14 | convolution fusion | flops 2147483648 | bytes 11534336 | tf_op jit(solution)/shard_map/dot_general | solution.py:126
  365.6 1.1 copy.90
  366.7 6.1 %all-to-all-done.8 = bf16[4,256,512]{2,1,0:T(8,128)(2,1)S(1)} async-done(((bf16[4,256,512]{2,1,0:T(8,128)(2,1)}), bf16[4,256,512]{2,1,0:T(8,128)(2,1)S(1)}, u32[]{:S(2)}, u32[]{:S(2)}) %all-to-all-start.8) | async-done | bytes 1048608 | tf_op jit(solution)/shard_map/all_to_all | solution.py:67
  372.8 3.5 all-to-all-start.7
  376.4 13.1 %all-to-all-done.7 = bf16[4,256,512]{2,1,0:T(8,128)(2,1)S(1)} async-done(((bf16[4,256,512]{2,1,0:T(8,128)(2,1)}), bf16[4,256,512]{2,1,0:T(8,128)(2,1)S(1)}, u32[]{:S(2)}, u32[]{:S(2)}) %all-to-all-start.7) | async-done | bytes 1048608 | tf_op jit(solution)/shard_map/all_to_all | solution.py:67
  389.7 1.0 fusion.47
  (111 shorter events, 16.0 us)
Async XLA Ops:
  6.5 102.9 %all-gather.5.cloned.1.call-start = ((), (), s32[]{:S(2)}) async-start(), calls=%async_computation.9 | async-start | bytes 7077888 | tf_op jit(solution)/shard_map/all_gather | solution.py:80
  26.8 147.0 %all-gather.7.cloned.1.call-start = ((), (), s32[]{:S(2)}) async-start(), calls=%async_computation.10 | async-start | bytes 9437184 | tf_op jit(solution)/shard_map/all_gather | solution.py:80
  30.3 16.7 %copy-start.7 = (bf16[1,64,6144]{2,1,0:T(8,128)(2,1)S(1)}, bf16[1,64,6144]{2,1,0:T(8,128)(2,1)}, u32[]{:S(2)}) copy-start(bf16[1,64,6144]{2,1,0:T(8,128)(2,1)} %get-tuple-element.31) | copy-start | bytes 2359300
  46.9 227.3 %all-gather.9.cloned.1.call-start = ((), (), s32[]{:S(2)}) async-start(), calls=%async_computation.11 | async-start | bytes 7077888 | tf_op jit(solution)/shard_map/all_gather | solution.py:80
  47.7 18.0 %copy-start.14 = (f32[2,2,2048]{2,1,0:T(2,128)S(1)}, f32[2,2,2048]{2,1,0:T(2,128)}, u32[]{:S(2)}) copy-start(f32[2,2,2048]{2,1,0:T(2,128)} %param.27) | copy-start | bytes 98308
  47.7 18.0 %copy-start.15 = (f32[2,2,2048]{2,1,0:T(2,128)S(1)}, f32[2,2,2048]{2,1,0:T(2,128)}, u32[]{:S(2)}) copy-start(f32[2,2,2048]{2,1,0:T(2,128)} %param.26) | copy-start | bytes 98308
  47.7 18.3 %copy-start.18 = (s32[32]{0:T(128)S(1)}, s32[32]{0:T(128)}, u32[]{:S(2)}) copy-start(s32[32]{0:T(128)} %param.18) | copy-start | bytes 388
  59.8 12.9 %copy-start.12 = (s32[1,512]{1,0:T(1,128)S(1)}, s32[1,512]{1,0:T(1,128)}, u32[]{:S(2)}) copy-start(s32[1,512]{1,0:T(1,128)} %param.17) | copy-start | bytes 6148
  62.2 13.5 %all-to-all-start.6 = ((bf16[64,4,2048]{2,0,1:T(8,128)(2,1)}), bf16[64,4,2048]{2,0,1:T(8,128)(2,1)S(1)}, u32[]{:S(2)}, u32[]{:S(2)}) async-start(bf16[64,4,2048]{2,0,1:T(8,128)(2,1)} %copy.63), calls=%async_computation.6 | async-start | bytes 2097152 | tf_op jit(solution)/shard_map/all_to_all | solution.py:79
  70.5 11.0 %copy-start.16 = (bf16[2,1536]{1,0:T(2,128)(2,1)S(1)}, bf16[2,1536]{1,0:T(2,128)(2,1)}, u32[]{:S(2)}) copy-start(bf16[2,1536]{1,0:T(2,128)(2,1)} %param.21) | copy-start | bytes 18436
  71.3 13.0 %copy-start.13 = (bf16[2,2048]{1,0:T(2,128)(2,1)S(1)}, bf16[2,2048]{1,0:T(2,128)(2,1)}, u32[]{:S(2)}) copy-start(bf16[2,2048]{1,0:T(2,128)(2,1)} %param.22) | copy-start | bytes 24580
  75.7 8.7 %copy-start.6 = (bf16[64,4,2048]{2,0,1:T(8,128)(2,1)}, bf16[64,4,2048]{2,0,1:T(8,128)(2,1)S(1)}, u32[]{:S(2)}) copy-start(bf16[64,4,2048]{2,0,1:T(8,128)(2,1)S(1)} %all-to-all-done.6) | copy-start | bytes 3145732
  77.4 24.0 %all-to-all-start = ((bf16[4,512,512]{1,2,0:T(8,128)(2,1)}), bf16[4,512,512]{1,2,0:T(8,128)(2,1)S(1)}, u32[]{:S(2)}, u32[]{:S(2)}) async-start(bf16[4,512,512]{1,2,0:T(8,128)(2,1)} %broadcast_in_dim.47), calls=%async_computation | async-start | bytes 4194304 | tf_op jit(solution)/shard_map/all_to_all | solution.py:67
  81.0 239.9 %all-gather.11.cloned.1.call-start = ((), (), s32[]{:S(2)}) async-start(), calls=%async_computation.12 | async-start | bytes 9437184 | tf_op jit(solution)/shard_map/all_gather | solution.py:80
  101.3 1.4 copy-start
  173.8 26.4 %copy-start.10 = (bf16[2,256,512]{2,1,0:T(8,128)(2,1)S(1)}, bf16[2,256,512]{2,1,0:T(8,128)(2,1)}, u32[]{:S(2)}) copy-start(bf16[2,256,512]{2,1,0:T(8,128)(2,1)} %convolution_convert_fusion.1) | copy-start | bytes 1572868
  204.3 5.4 %copy-start.17 = (f32[2,512]{1,0:T(2,128)S(1)}, f32[2,512]{1,0:T(2,128)}, u32[]{:S(2)}) copy-start(f32[2,512]{1,0:T(2,128)} %param.25) | copy-start | bytes 12292
  205.9 29.6 %copy-start.8 = (bf16[1,512,512]{2,1,0:T(8,128)(2,1)S(1)}, bf16[1,512,512]{2,1,0:T(8,128)(2,1)}, u32[]{:S(2)}) copy-start(bf16[1,512,512]{2,1,0:T(8,128)(2,1)} %param.16) | copy-start | bytes 1572868
  205.9 29.2 %all-to-all-start.3 = ((bf16[4,512,512]{2,1,0:T(8,128)(2,1)}), bf16[4,512,512]{2,1,0:T(8,128)(2,1)S(1)}, u32[]{:S(2)}, u32[]{:S(2)}) async-start(bf16[4,512,512]{2,1,0:T(8,128)(2,1)} %bitcast.199), calls=%async_computation.3 | async-start | bytes 4194304 | tf_op jit(solution)/shard_map/all_to_all | solution.py:67
  235.6 1.8 copy-start.4
  237.4 28.7 %all-to-all-start.4 = ((bf16[4,512,512]{1,2,0:T(8,128)(2,1)}), bf16[4,512,512]{1,2,0:T(8,128)(2,1)S(1)}, u32[]{:S(2)}, u32[]{:S(2)}) async-start(bf16[4,512,512]{1,2,0:T(8,128)(2,1)} %broadcast_in_dim.52), calls=%async_computation.4 | async-start | bytes 4194304 | tf_op jit(solution)/shard_map/all_to_all | solution.py:67
  266.0 1.4 copy-start.1
  337.3 7.8 %copy-start.19 = (bf16[512,2048]{1,0:T(8,128)(2,1)}, bf16[512,2048]{1,0:T(8,128)(2,1)S(1)}, u32[]{:S(2)}) copy-start(bf16[512,2048]{1,0:T(8,128)(2,1)S(1)} %fusion.16) | copy-start | bytes 6291460
  337.3 7.8 %copy-start.11 = (bf16[512,2,32]{2,0,1:T(8,128)(2,1)S(1)}, bf16[512,2,32]{2,0,1:T(8,128)(2,1)}, u32[]{:S(2)}) copy-start(bf16[512,2,32]{2,0,1:T(8,128)(2,1)} %get-tuple-element.27) | copy-start | bytes 196612
  349.4 2.8 copy-start.2
  349.4 3.5 copy-start.9
  354.8 18.0 %all-to-all-start.8 = ((bf16[4,256,512]{2,1,0:T(8,128)(2,1)}), bf16[4,256,512]{2,1,0:T(8,128)(2,1)S(1)}, u32[]{:S(2)}, u32[]{:S(2)}) async-start(bf16[4,256,512]{2,1,0:T(8,128)(2,1)} %bitcast.189), calls=%async_computation.8 | async-start | bytes 2097152 | tf_op jit(solution)/shard_map/all_to_all | solution.py:67
  358.7 6.2 %copy-start.3 = (bf16[2,512,2048]{2,1,0:T(8,128)(2,1)S(1)}, bf16[2,512,2048]{2,1,0:T(8,128)(2,1)}, u32[]{:S(2)}) copy-start(bf16[2,512,2048]{2,1,0:T(8,128)(2,1)} %param.23) | copy-start | bytes 12582916
  365.6 24.1 %copy-start.5 = (bf16[1,512,512]{2,1,0:T(8,128)(2,1)S(1)}, bf16[1,512,512]{2,1,0:T(8,128)(2,1)}, u32[]{:S(2)}) copy-start(bf16[1,512,512]{2,1,0:T(8,128)(2,1)} %copy-done.4) | copy-start | bytes 1572868
  372.8 16.8 %all-to-all-start.7 = ((bf16[4,256,512]{2,1,0:T(8,128)(2,1)}), bf16[4,256,512]{2,1,0:T(8,128)(2,1)S(1)}, u32[]{:S(2)}, u32[]{:S(2)}) async-start(bf16[4,256,512]{2,1,0:T(8,128)(2,1)} %bitcast.191), calls=%async_computation.7 | async-start | bytes 2097152 | tf_op jit(solution)/shard_map/all_to_all | solution.py:67
Sparse Core Ops, SparseCore 0:
  26.9 64.4 all-gather.4
  93.0 80.6 all-gather.6
  175.4 63.2 all-gather.8
  240.2 80.6 all-gather.10
